TPU v7x, 32 devices: a whole 2x2x4 slice. The times are simulated.
32 devices in a mesh: grp: 2 (over x), seg: 16 (over z, y, core).
Axes of the slice: x: 2, y: 2, z: 4, core: 2. Of those that a mesh axis runs over, the one named last changes fastest.
Arguments:
- strain: float32 [2097152], P(('grp', 'seg')), parts along dimension 0, may hold values from -6 to 6
- gate_mask: int32 [2097152], P(('grp', 'seg')), parts along dimension 0, may hold values 0 or 1
- template_bank: bfloat16 [32, 2, 32768], P('grp', None, 'seg'), parts along dimension 0, may hold values from -6 to 6
Outputs:
- peak_power: float32 [16, 8192], P(None, ('grp', 'seg')), parts along dimension 1
There are 2 independent parts, one for each index of `grp`. A program takes and returns all parts, laid end to end along the dimension named above; each array names one. Nothing has to cross between parts.
All inputs are finite; a program needn't handle non-finite values. No bound on the sum of `gate_mask` on one device may be relied on, other than what follows from the above.
Results may differ from a plain program's by a relative error of at most 0.0003.
Values may be sent and summed in bfloat16 or wider, within the bound.
No kernel may reach another device: no remote copies, remote signals or barrier semaphores. Data moves between devices by JAX's collectives and lax.ppermute only.
A program may use at most 128 MiB of HBM per device.

v0:
```python
import math

import jax
import jax.numpy as jnp
from jax import lax
from jax.experimental import pallas as pl
from jax.experimental.pallas import tpu as pltpu
from jax.sharding import PartitionSpec as P

RADIX = 256
BLOCK = 32768
SUBBANK = 16


PRECISE = lax.Precision.HIGH
EPSILON = 1e-06


def passed_along(value, axis, by):
    count = lax.axis_size(axis)
    pairs = [(i, i + by) for i in range(count) if 0 <= i + by < count]
    return lax.ppermute(value, axis, pairs)


def angle_table(row_count, col_count, period):
    row_index = lax.broadcasted_iota(jnp.int32, (row_count, col_count), 0)
    col_index = lax.broadcasted_iota(jnp.int32, (row_count, col_count), 1)
    phase_step = row_index * col_index % period
    angle_value = phase_step.astype(jnp.float32) * (2.0 * math.pi / period)
    return (jnp.cos(angle_value), jnp.sin(angle_value))


def forward(windows):
    half_radix = RADIX // 2
    window_total = windows.shape[0]
    rows = windows.shape[1] // RADIX
    block_grid = windows.reshape(window_total, rows, RADIX)
    cos_first, sin_first = angle_table(rows, RADIX, RADIX)
    first_table = jnp.concatenate([cos_first, -sin_first], axis=1)
    first_section = jnp.einsum("bnm,nf->bmf", block_grid, first_table, precision=PRECISE)
    cos_twist, sin_twist = angle_table(RADIX, RADIX, RADIX * RADIX)
    real_part = first_section[..., :RADIX]
    imag_part = first_section[..., RADIX:]
    turned = jnp.concatenate(
        [
            real_part * cos_twist + imag_part * sin_twist,
            imag_part * cos_twist - real_part * sin_twist,
        ],
        axis=-1,
    )
    cos_second, sin_second = angle_table(RADIX, half_radix, RADIX)
    cosine_part = jnp.einsum("bnf,nk->bkf", turned, cos_second, precision=PRECISE)
    sine_part = jnp.einsum("bnf,nk->bkf", turned, sin_second, precision=PRECISE)
    return jnp.concatenate(
        [
            cosine_part[..., :RADIX] + sine_part[..., RADIX:],
            cosine_part[..., RADIX:] - sine_part[..., :RADIX],
        ],
        axis=-1,
    )


def split_pair(value):
    high = value.astype(jnp.bfloat16)
    low = (value - high.astype(jnp.float32)).astype(jnp.bfloat16)
    return high, low


def table_pair(value):
    high = lax.reduce_precision(value, exponent_bits=8, mantissa_bits=7)
    return high.astype(jnp.bfloat16), (value - high).astype(jnp.bfloat16)


def triple_dot(left_high, left_low, right_high, right_low):
    total = jnp.dot(left_high, right_high, preferred_element_type=jnp.float32)
    total = total + jnp.dot(left_high, right_low, preferred_element_type=jnp.float32)
    return total + jnp.dot(left_low, right_high, preferred_element_type=jnp.float32)


def inverse_tables(k_rows):
    half_radix = RADIX // 2
    cos_first, sin_first = angle_table(RADIX, k_rows, RADIX)
    first = jnp.concatenate(
        [
            jnp.concatenate([cos_first, -sin_first], axis=1),
            jnp.concatenate([sin_first, cos_first], axis=1),
        ],
        axis=0,
    )
    cos_twist, sin_twist = angle_table(RADIX, RADIX, RADIX * RADIX)
    cos_out, sin_out = angle_table(RADIX, RADIX, RADIX)
    real_cols = jnp.concatenate([cos_out, -sin_out], axis=0)
    imag_cols = jnp.concatenate([sin_out, cos_out], axis=0)
    second = jnp.concatenate([real_cols[:, half_radix:], imag_cols[:, half_radix:]], axis=1)
    first_high, first_low = table_pair(first)
    second_high, second_low = table_pair(second)
    return first_high, first_low, cos_twist, sin_twist, second_high, second_low


def peaks_kernel(spec_ref, bank_ref, fh_ref, fl_ref, tc_ref, ts_ref, sh_ref, sl_ref, out_ref):
    half_radix = RADIX // 2
    wave_real = bank_ref[0, 0].astype(jnp.float32)
    wave_imag = bank_ref[0, 1].astype(jnp.float32)
    for block in range(spec_ref.shape[0]):
        spec_real = spec_ref[block, :, :RADIX]
        spec_imag = spec_ref[block, :, RADIX:]
        prod_real = spec_real * wave_real + spec_imag * wave_imag
        prod_imag = spec_imag * wave_real - spec_real * wave_imag
        stacked = jnp.concatenate([prod_real, prod_imag], axis=0)
        stacked_high, stacked_low = split_pair(stacked)
        first = triple_dot(fh_ref[...], fl_ref[...], stacked_high, stacked_low)
        real_part = first[:RADIX]
        imag_part = first[RADIX:]
        cos_twist = tc_ref[...]
        sin_twist = ts_ref[...]
        turned = jnp.concatenate(
            [
                real_part * cos_twist - imag_part * sin_twist,
                real_part * sin_twist + imag_part * cos_twist,
            ],
            axis=1,
        )
        turned_high, turned_low = split_pair(turned)
        series = triple_dot(turned_high, turned_low, sh_ref[...], sl_ref[...])
        power_series = (
            series[:, :half_radix] * series[:, :half_radix]
            + series[:, half_radix:] * series[:, half_radix:]
        )
        out_ref[0, block : block + 1, :] = jnp.max(power_series, axis=0, keepdims=True)


def window_peaks(spectra, bank, tables):
    block_total, k_rows, _ = spectra.shape
    template_total = bank.shape[0]
    fixed = lambda k: (0, 0)
    pair_flops = 6 * (2 * RADIX) * (2 * k_rows) * RADIX + 6 * RADIX * (2 * RADIX) * RADIX
    return pl.pallas_call(
        peaks_kernel,
        out_shape=jax.ShapeDtypeStruct((template_total, block_total, RADIX // 2), jnp.float32),
        grid=(template_total,),
        in_specs=[
            pl.BlockSpec((block_total, k_rows, 2 * RADIX), lambda k: (0, 0, 0)),
            pl.BlockSpec((1, 2, k_rows, RADIX), lambda k: (k, 0, 0, 0)),
            pl.BlockSpec((2 * RADIX, 2 * k_rows), fixed),
            pl.BlockSpec((2 * RADIX, 2 * k_rows), fixed),
            pl.BlockSpec((RADIX, RADIX), fixed),
            pl.BlockSpec((RADIX, RADIX), fixed),
            pl.BlockSpec((2 * RADIX, RADIX), fixed),
            pl.BlockSpec((2 * RADIX, RADIX), fixed),
        ],
        out_specs=pl.BlockSpec((1, block_total, RADIX // 2), lambda k: (k, 0, 0)),
        compiler_params=pltpu.CompilerParams(dimension_semantics=("arbitrary",)),
        cost_estimate=pl.CostEstimate(
            flops=pair_flops * template_total * block_total,
            transcendentals=0,
            bytes_accessed=spectra.size * 4 + bank.size * 2 + template_total * block_total * RADIX * 2,
        ),
    )(spectra, bank, *tables)


def gathered_bank(bank_rows):
    seg_total = lax.axis_size("seg")
    me = lax.axis_index("seg")
    rows, parts, local_bins = bank_rows.shape
    held = bank_rows[None]
    distance = seg_total // 2
    steps = 0
    while distance >= 1:
        pairs = [(i, i ^ distance) for i in range(seg_total)]
        arrived = lax.ppermute(held, "seg", pairs)
        upper = (me & distance) != 0
        held = jnp.stack([jnp.where(upper, arrived, held), jnp.where(upper, held, arrived)], axis=0)
        distance //= 2
        steps += 1
    held = held.reshape((2,) * steps + (rows, parts, local_bins // RADIX, RADIX))
    order = tuple(reversed(range(steps)))
    held = jnp.transpose(held, (steps, steps + 1) + order + (steps + 2, steps + 3))
    return held.reshape(rows, parts, seg_total * local_bins // RADIX, RADIX)


def local(strain, gate_mask, template_bank):
    gated = strain * gate_mask.astype(jnp.float32)
    local_blocks = gated.reshape(-1, BLOCK)
    block_total = local_blocks.shape[0]
    earlier = passed_along(local_blocks[block_total - 1], "seg", 1)
    before = jnp.concatenate([earlier[None], local_blocks[:-1]], axis=0)
    windows = jnp.concatenate([before, local_blocks], axis=1)
    spectra = forward(windows)
    wide_bank = template_bank.astype(jnp.float32)
    power_sum = lax.psum(jnp.sum(wide_bank * wide_bank, axis=(1, 2)), "seg")
    norm_scale = 1.0 / jnp.sqrt(BLOCK * power_sum + EPSILON)
    tables = inverse_tables(spectra.shape[1])
    template_total = template_bank.shape[0]
    results = []
    for start in range(0, template_total, SUBBANK):
        bank = gathered_bank(template_bank[start : start + SUBBANK])
        peaks = window_peaks(spectra, bank, tables)
        results.append(peaks.reshape(bank.shape[0], block_total * (RADIX // 2)))
    peaks = jnp.concatenate(results, axis=0)
    return peaks * (norm_scale * norm_scale)[:, None]


def solution(mesh):
    in_specs = (P(("grp", "seg")), P(("grp", "seg")), P("grp", None, "seg"))
    out_specs = P(None, ("grp", "seg"))
    return jax.shard_map(local, mesh=mesh, in_specs=in_specs, out_specs=out_specs, check_vma=False)
```

profile of v0, /device:TPU:1, one launch (start us, length us, event | category | flops | bytes accessed | tf_op | source)
XLA Modules:
  0.0 104.6 jit_solution(14282154102799709890)
XLA Ops:
  0.0 0.0 copy-start.2
  0.0 3.1 %collective-permute-start.1 = (bf16[1,16,2,2048]{3,2,1,0:T(2,128)(2,1)}, bf16[1,16,2,2048]{3,2,1,0:T(2,128)(2,1)S(1)}, u32[]{:S(2)}, u32[]{:S(2)}) collective-permute-start(bf16[1,16,2,2048]{3,2,1,0:T(2,128)(2,1)} %bitcast.59), channel_id=1, source_target_pairs={{0,8},{1,9},{2,10},{3,11},{4,12},{5,13},{6,14},{7,15},{8,0},{9,1},... | collective-permute-start | bytes 393224 | tf_op jit(solution)/shard_map/ppermute | solution.py:170
  3.1 1.1 %convert_multiply_fusion = f32[65536]{0:T(1024)S(1)} fusion(f32[65536]{0:T(1024)} %param.3, s32[65536]{0:T(1024)} %param.4), kind=kLoop, calls=%fused_computation.58 | loop fusion | flops 131072 | bytes 786432 | tf_op jit(solution)/shard_map/mul | solution.py:182
  4.2 0.7 fusion.59
  4.9 4.0 %collective-permute-start = (f32[32768]{0:T(1024)}, f32[32768]{0:T(1024)}, u32[]{:S(2)}, u32[]{:S(2)}) collective-permute-start(f32[32768]{0:T(1024)} %get-tuple-element.17), channel_id=1, source_target_pairs={{0,1},{1,2},{2,3},{3,4},{4,5},{5,6},{6,7},{7,8},{8,9},{9,10},{10,1... | collective-permute-start | bytes 393224 | tf_op jit(solution)/shard_map/ppermute | solution.py:22
  8.9 1.0 fusion.35
  9.9 0.0 collective-permute-done.1
  9.9 1.1 %fusion.29 = (bf16[1,1,16,2,2048]{4,3,2,1,0:T(2,128)(2,1)S(1)}, bf16[1,1,16,2,2048]{4,3,2,1,0:T(2,128)(2,1)S(1)}) fusion(bf16[1,16,2,2048]{3,2,1,0:T(2,128)(2,1)S(1)} %collective-permute-done.1, pred[]{:T(512)S(6)} %ne.92, bf16[16,2,2048]{2,1,0:T(2,128)(2,1)} %param.5), kind=kLoop, calls=%fused_computation.69 | loop fusion | flops 131072 | bytes 524289 | tf_op jit(solution)/shard_map/stack | solution.py:172
  11.0 0.4 fusion.57
  11.4 1.4 %collective-permute-start.2 = (bf16[2,1,16,2,2048]{4,3,2,0,1:T(2,128)(2,1)S(1)}, bf16[2,1,16,2,2048]{4,3,2,0,1:T(2,128)(2,1)S(1)}, u32[]{:S(2)}, u32[]{:S(2)}) collective-permute-start(bf16[2,1,16,2,2048]{4,3,2,0,1:T(2,128)(2,1)S(1)} %fusion.57), channel_id=1, source_target_pairs={{0,4},{1,5},{2,6},{3,7},{4,0},{5,1},{6,2},{7,3},{8,12},{9,13},{10,... | collective-permute-start | bytes 786440 | tf_op jit(solution)/shard_map/ppermute | solution.py:170
  12.8 1.2 %fusion.41 = (f32[256,128]{1,0:T(8,128)S(1)}, f32[256,128]{1,0:T(8,128)}) fusion(), kind=kLoop, calls=%fused_computation.81 | loop fusion | flops 458752 | bytes 262144 | tf_op jit(solution)/shard_map/sin | solution.py:30
  14.0 1.0 fusion.36
  15.0 0.0 copy-done.2
  15.0 0.3 multiply_reduce_fusion
  15.3 3.3 %collective-permute-done.2 = bf16[2,1,16,2,2048]{4,3,2,0,1:T(2,128)(2,1)S(1)} collective-permute-done((bf16[2,1,16,2,2048]{4,3,2,0,1:T(2,128)(2,1)S(1)}, bf16[2,1,16,2,2048]{4,3,2,0,1:T(2,128)(2,1)S(1)}, u32[]{:S(2)}, u32[]{:S(2)}) %collective-permute-start.2) | collective-permute-done | bytes 262176 | tf_op jit(solution)/shard_map/ppermute | solution.py:170
  18.6 0.5 fusion.17
  19.0 0.5 fusion.18
  19.5 0.7 fusion.58
  20.2 1.3 %collective-permute-start.3 = (bf16[2,2,1,16,2,2048]{5,4,3,1,0,2:T(2,128)(2,1)S(1)}, bf16[2,2,1,16,2,2048]{5,4,3,1,0,2:T(2,128)(2,1)S(1)}, u32[]{:S(2)}, u32[]{:S(2)}) collective-permute-start(bf16[2,2,1,16,2,2048]{5,4,3,1,0,2:T(2,128)(2,1)S(1)} %fusion.58), channel_id=1, source_target_pairs={{0,2},{1,3},{2,0},{3,1},{4,6},{5,7},{6,4},{7,5},{8,10},{9,11},{10,... | collective-permute-start | bytes 1572872 | tf_op jit(solution)/shard_map/ppermute | solution.py:170
  21.5 1.1 %fusion.43 = f32[256,128]{1,0:T(8,128)} fusion(), kind=kLoop, calls=%fused_computation.83 | loop fusion | flops 491520 | bytes 131072 | tf_op jit(solution)/shard_map/neg | solution.py:85
  22.6 31.9 %psum.7 = f32[16]{0:T(128)S(1)} all-reduce(f32[16]{0:T(128)S(1)} %multiply_reduce_fusion), channel_id=1, replica_groups=mesh['grp'=2,'seg'=16] {'seg'}, use_global_device_ids=true, to_apply=%region_1.2 | all-reduce | flops 16 | bytes 128 | tf_op jit(solution)/shard_map/psum | solution.py:190
  54.6 1.0 fusion.33
  55.6 0.0 copy-start
  55.6 0.0 copy-start.1
  55.6 1.0 fusion.1
  56.6 0.0 collective-permute-done.3
  56.6 0.9 fusion.2
  57.5 0.0 copy-start.3
  57.5 0.0 copy-start.4
  57.5 0.9 fusion.3
  58.4 0.0 copy-start.5
  58.5 2.5 %pad_maximum_fusion.2 = bf16[2,2,2,1,16,2,2048]{6,5,4,2,1,3,0:T(2,128)(2,1)} fusion(bf16[1,2,2,1,16,2,2048]{6,5,4,2,1,3,0:T(2,128)(2,1)S(1)} %fusion.3, bf16[1,2,2,1,16,2,2048]{6,5,4,2,1,3,0:T(2,128)(2,1)S(1)} %fusion.2), kind=kLoop, calls=%fused_computation.7 | loop fusion | flops 524288 | bytes 2097152 | tf_op jit(solution)/shard_map/stack | solution.py:172
  61.0 3.1 %collective-permute-start.4 = (bf16[2,2,2,1,16,2,2048]{6,5,4,2,1,3,0:T(2,128)(2,1)}, bf16[2,2,2,1,16,2,2048]{6,5,4,2,1,3,0:T(2,128)(2,1)}, u32[]{:S(2)}, u32[]{:S(2)}) collective-permute-start(bf16[2,2,2,1,16,2,2048]{6,5,4,2,1,3,0:T(2,128)(2,1)} %pad_maximum_fusion.2), channel_id=1, source_target_pairs={{0,1},{1,0},{2,3},{3,2},{4,5},{5,4},{6,7},{7,6},{8,9},{9,8},{10,11... | collective-permute-start | bytes 3145736 | tf_op jit(solution)/shard_map/ppermute | solution.py:170
  64.1 0.0 copy-done.3
  64.1 0.0 copy-done.4
  64.1 0.9 fusion
  64.9 0.1 concatenate.42
  65.0 0.0 copy-done.5
  65.1 0.1 copy.17
  65.2 0.1 copy.18
  65.3 0.0 collective-permute-done
  65.3 0.9 concatenate.40
  66.2 0.1 copy.16
  66.3 0.6 fusion.5
  66.9 0.0 copy-done
  67.0 0.0 copy-done.1
  67.0 0.1 multiply_add_fusion
  67.1 0.9 convolution_bitcast_fusion.1
  68.0 0.9 convolution_bitcast_fusion
  68.9 0.1 slice_add_fusion
  69.0 0.9 pad_maximum_fusion.6.spec_ref
  69.9 0.0 collective-permute-done.4
  69.9 3.5 %broadcast_select_fusion.1 = (bf16[2,2,2,1,16,2,2048]{6,5,4,2,1,3,0:T(2,128)(2,1)S(1)}, bf16[2,2,2,1,16,2,2048]{6,5,4,2,1,3,0:T(2,128)(2,1)S(1)}) fusion(bf16[2,2,2,1,16,2,2048]{6,5,4,2,1,3,0:T(2,128)(2,1)} %collective-permute-done.4, pred[]{:T(512)S(6)} %ne.89, bf16[1,2,2,1,16,2,2048]{6,5,4,2,1,3,0:T(2,128)(2,1)S(1)} %fusion.3, ...), kind=kLoop, calls=%fused_computation.3 | loop fusion | flops 1572864 | bytes 4194305 | tf_op jit(solution)/shard_map/jit(_where)/select_n | solution.py:172
  73.4 0.7 stack.45
  74.1 0.7 stack.46
  74.9 0.2 pad_maximum_fusion
  75.1 1.6 %copy.35 = bf16[2,2,2,2,16,2,8,256]{7,6,0,1,2,3,5,4:T(8,128)(2,1)} copy(bf16[2,2,2,2,16,2,8,256]{7,6,5,4,3,2,1,0:T(8,128)(2,1)S(1)} %pad_maximum_fusion) | data formatting | bytes 4194304 | tf_op jit(solution)/shard_map/stack | solution.py:172
  76.7 26.5 %shard_map.37 = f32[16,2,128]{2,1,0:T(2,128)} custom-call(f32[2,128,512]{2,1,0:T(8,128)} %pad_maximum_fusion.6.spec_ref, bf16[16,2,128,256]{3,2,1,0:T(8,128)(2,1)} %bitcast.58, bf16[512,256]{1,0:T(8,128)(2,1)} %get-tuple-element.14.fh_ref, bf16[512,256]{1,0:T(8,128)(2,1)} %get-tuple-element.13.fl_ref, f32[256,256]{1,0:T(8,128)} %copy-done.1, ...), custom_call_target="tpu_custom_call" | custom-call | flops 12884901888 | bytes 2637824 | tf_op jit(solution)/shard_map/pallas_call | solution.py:137
  103.2 1.4 %bitcast_multiply_fusion = f32[16,256]{1,0:T(8,128)} fusion(f32[2,8,2,128]{3,2,1,0:T(2,128)} %bitcast.60, f32[16]{0:T(128)S(1)} %rsqrt_multiply_fusion), kind=kLoop, calls=%fused_computation.84 | loop fusion | flops 4096 | bytes 32832 | tf_op jit(solution)/shard_map/mul | solution.py:200
  (2 shorter events, 0.0 us)
Async XLA Ops:
  0.0 15.0 %copy-start.2 = (bf16[16,2,2048]{2,1,0:T(2,128)(2,1)S(1)}, bf16[16,2,2048]{2,1,0:T(2,128)(2,1)}, u32[]{:S(2)}) copy-start(bf16[16,2,2048]{2,1,0:T(2,128)(2,1)} %param.5) | copy-start | bytes 393220
  0.0 9.9 %collective-permute-start.1 = (bf16[1,16,2,2048]{3,2,1,0:T(2,128)(2,1)}, bf16[1,16,2,2048]{3,2,1,0:T(2,128)(2,1)S(1)}, u32[]{:S(2)}, u32[]{:S(2)}) collective-permute-start(bf16[1,16,2,2048]{3,2,1,0:T(2,128)(2,1)} %bitcast.59), channel_id=1, source_target_pairs={{0,8},{1,9},{2,10},{3,11},{4,12},{5,13},{6,14},{7,15},{8,0},{9,1},... | collective-permute-start | bytes 393224 | tf_op jit(solution)/shard_map/ppermute | solution.py:170
  4.9 60.4 %collective-permute-start = (f32[32768]{0:T(1024)}, f32[32768]{0:T(1024)}, u32[]{:S(2)}, u32[]{:S(2)}) collective-permute-start(f32[32768]{0:T(1024)} %get-tuple-element.17), channel_id=1, source_target_pairs={{0,1},{1,2},{2,3},{3,4},{4,5},{5,6},{6,7},{7,8},{8,9},{9,10},{10,1... | collective-permute-start | bytes 393224 | tf_op jit(solution)/shard_map/ppermute | solution.py:22
  11.4 7.2 %collective-permute-start.2 = (bf16[2,1,16,2,2048]{4,3,2,0,1:T(2,128)(2,1)S(1)}, bf16[2,1,16,2,2048]{4,3,2,0,1:T(2,128)(2,1)S(1)}, u32[]{:S(2)}, u32[]{:S(2)}) collective-permute-start(bf16[2,1,16,2,2048]{4,3,2,0,1:T(2,128)(2,1)S(1)} %fusion.57), channel_id=1, source_target_pairs={{0,4},{1,5},{2,6},{3,7},{4,0},{5,1},{6,2},{7,3},{8,12},{9,13},{10,... | collective-permute-start | bytes 786440 | tf_op jit(solution)/shard_map/ppermute | solution.py:170
  20.2 36.4 %collective-permute-start.3 = (bf16[2,2,1,16,2,2048]{5,4,3,1,0,2:T(2,128)(2,1)S(1)}, bf16[2,2,1,16,2,2048]{5,4,3,1,0,2:T(2,128)(2,1)S(1)}, u32[]{:S(2)}, u32[]{:S(2)}) collective-permute-start(bf16[2,2,1,16,2,2048]{5,4,3,1,0,2:T(2,128)(2,1)S(1)} %fusion.58), channel_id=1, source_target_pairs={{0,2},{1,3},{2,0},{3,1},{4,6},{5,7},{6,4},{7,5},{8,10},{9,11},{10,... | collective-permute-start | bytes 1572872 | tf_op jit(solution)/shard_map/ppermute | solution.py:170
  55.6 11.3 %copy-start = (f32[256,256]{1,0:T(8,128)}, f32[256,256]{1,0:T(8,128)S(1)}, u32[]{:S(2)}) copy-start(f32[256,256]{1,0:T(8,128)S(1)} %get-tuple-element.21.ts_ref) | copy-start | bytes 786436
  55.6 11.3 %copy-start.1 = (f32[256,256]{1,0:T(8,128)}, f32[256,256]{1,0:T(8,128)S(1)}, u32[]{:S(2)}) copy-start(f32[256,256]{1,0:T(8,128)S(1)} %get-tuple-element.22.tc_ref) | copy-start | bytes 786436
  57.5 6.6 %copy-start.3 = (f32[256,128]{1,0:T(8,128)S(1)}, f32[256,128]{1,0:T(8,128)}, u32[]{:S(2)}) copy-start(f32[256,128]{1,0:T(8,128)} %get-tuple-element.24) | copy-start | bytes 393220
  57.5 6.5 %copy-start.4 = (f32[256,128]{1,0:T(8,128)S(1)}, f32[256,128]{1,0:T(8,128)}, u32[]{:S(2)}) copy-start(f32[256,128]{1,0:T(8,128)} %fusion.43) | copy-start | bytes 393220
  58.4 6.6 %copy-start.5 = (f32[32768]{0:T(1024)S(1)}, f32[32768]{0:T(1024)}, u32[]{:S(2)}) copy-start(f32[32768]{0:T(1024)} %get-tuple-element.18) | copy-start | bytes 393220
  61.0 8.9 %collective-permute-start.4 = (bf16[2,2,2,1,16,2,2048]{6,5,4,2,1,3,0:T(2,128)(2,1)}, bf16[2,2,2,1,16,2,2048]{6,5,4,2,1,3,0:T(2,128)(2,1)}, u32[]{:S(2)}, u32[]{:S(2)}) collective-permute-start(bf16[2,2,2,1,16,2,2048]{6,5,4,2,1,3,0:T(2,128)(2,1)} %pad_maximum_fusion.2), channel_id=1, source_target_pairs={{0,1},{1,0},{2,3},{3,2},{4,5},{5,4},{6,7},{7,6},{8,9},{9,8},{10,11... | collective-permute-start | bytes 3145736 | tf_op jit(solution)/shard_map/ppermute | solution.py:170
where the time goes:
time: 105 us
  blocking collectives  31.9 us (30%)
  Pallas kernels  26.5 us (25%)
  other arithmetic  22.2 us (21%)
  starting transfers between devices  12.9 us (12%)
  local copies, waits for them, and re-layouts  5.15 us (5%)
  waiting for transfers between devices  3.3 us (3%)
  matrix products  2.41 us (2%)
    psum x1, blocking collectives, local(): power_sum = lax.psum(jnp.sum(wide_bank * wide_bank, axis=(1, 2)), 'seg')  31.9 us
    pallas_call x1, Pallas kernels, window_peaks(): pl.pallas_call(peaks_kernel, out_shape=jax.ShapeDtypeStruct((template_tot...  26.5 us
    ppermute x4, starting transfers between devices, gathered_bank(): arrived = lax.ppermute(held, 'seg', pairs)  8.87 us
    another operation x9, other arithmetic, gathered_bank(): jnp.stack([jnp.where(upper, arrived, held), jnp.where(upper, held, arrive...  7.67 us
    ppermute x1, starting transfers between devices, passed_along(): return lax.ppermute(value, axis, pairs)  3.98 us
    select_n x1, other arithmetic, gathered_bank(): jnp.where(upper, arrived, held)  3.55 us
    ppermute x4, waiting for transfers between devices, gathered_bank(): arrived = lax.ppermute(held, 'seg', pairs)  3.3 us
    sin x3, other arithmetic, angle_table(): return (jnp.cos(angle_value), jnp.sin(angle_value))  3.19 us
  transfers between devices with their start and end apart: 5, of which 1 were waited for; matrix products, arithmetic and copies ran while one was open for 21% of the time, Pallas kernels for 0%

commit v1 on v0

--- a/solution.py
+++ b/solution.py
@@ -101,6 +101,8 @@
     half_radix = RADIX // 2
     wave_real = bank_ref[0, 0].astype(jnp.float32)
     wave_imag = bank_ref[0, 1].astype(jnp.float32)
+    power_sum = jnp.sum(wave_real * wave_real + wave_imag * wave_imag, keepdims=True)
+    norm_scale = 1.0 / jnp.sqrt(BLOCK * power_sum + EPSILON)
     for block in range(spec_ref.shape[0]):
         spec_real = spec_ref[block, :, :RADIX]
         spec_imag = spec_ref[block, :, RADIX:]
@@ -126,7 +128,8 @@
             series[:, :half_radix] * series[:, :half_radix]
             + series[:, half_radix:] * series[:, half_radix:]
         )
-        out_ref[0, block : block + 1, :] = jnp.max(power_series, axis=0, keepdims=True)
+        peak = jnp.max(power_series, axis=0, keepdims=True)
+        out_ref[0, block : block + 1, :] = peak * (norm_scale * norm_scale)
 
 
 def window_peaks(spectra, bank, tables):
@@ -186,9 +189,6 @@
     before = jnp.concatenate([earlier[None], local_blocks[:-1]], axis=0)
     windows = jnp.concatenate([before, local_blocks], axis=1)
     spectra = forward(windows)
-    wide_bank = template_bank.astype(jnp.float32)
-    power_sum = lax.psum(jnp.sum(wide_bank * wide_bank, axis=(1, 2)), "seg")
-    norm_scale = 1.0 / jnp.sqrt(BLOCK * power_sum + EPSILON)
     tables = inverse_tables(spectra.shape[1])
     template_total = template_bank.shape[0]
     results = []
@@ -196,8 +196,7 @@
         bank = gathered_bank(template_bank[start : start + SUBBANK])
         peaks = window_peaks(spectra, bank, tables)
         results.append(peaks.reshape(bank.shape[0], block_total * (RADIX // 2)))
-    peaks = jnp.concatenate(results, axis=0)
-    return peaks * (norm_scale * norm_scale)[:, None]
+    return jnp.concatenate(results, axis=0)
 
 
 def solution(mesh):

time: 105 us -> 79.9 us (0.76)
  blocking collectives: 31.9 us -> 0 us
  waiting for transfers between devices: 3.3 us -> 11.7 us
  other arithmetic: 22.2 us -> 19.3 us
  local copies, waits for them, and re-layouts: 5.15 us -> 6.48 us
    psum x1 -> x0, blocking collectives: 31.9 us -> none  [local(): power_sum = lax.psum(jnp.sum(wide_bank * wide_bank, axis=(1, 2)), 'seg')]
    ppermute x4, waiting for transfers between devices: 3.3 us -> 11.7 us  [gathered_bank(): arrived = lax.ppermute(held, 'seg', pairs)]
    mul x2 -> x0, other arithmetic: 1.4 us -> none  [local(): return peaks * (norm_scale * norm_scale)[:, None]]
    unnamed x12 -> x7, local copies, waits for them, and re-layouts: 0.02 us -> 1.34 us
  transfers between devices with their start and end apart: 5 -> 5, of which waited for: 1 -> 2; matrix products, arithmetic and copies ran while one was open for 21% -> 24% of each run, Pallas kernels for 0% -> 0%
where the time goes in v1:
time: 79.9 us; the launch traced here: 78.9 us
  Pallas kernels  26.6 us (33%)
  other arithmetic  19.3 us (24%)
  starting transfers between devices  12.1 us (15%)
  waiting for transfers between devices  11.7 us (15%)
  local copies, waits for them, and re-layouts  6.48 us (8%)
  matrix products  2.58 us (3%)
    pallas_call x1, Pallas kernels, window_peaks(): pl.pallas_call(peaks_kernel, out_shape=jax.ShapeDtypeStruct((template_tot...  26.6 us
    ppermute x4, waiting for transfers between devices, gathered_bank(): arrived = lax.ppermute(held, 'seg', pairs)  11.7 us
    ppermute x4, starting transfers between devices, gathered_bank(): arrived = lax.ppermute(held, 'seg', pairs)  8.28 us
    another operation x9, other arithmetic, gathered_bank(): jnp.stack([jnp.where(upper, arrived, held), jnp.where(upper, held, arrive...  7.67 us
    ppermute x1, starting transfers between devices, passed_along(): return lax.ppermute(value, axis, pairs)  3.79 us
    select_n x1, other arithmetic, gathered_bank(): jnp.where(upper, arrived, held)  3.55 us
    another operation x3, local copies, waits for them, and re-layouts, gathered_bank(): jnp.stack([jnp.where(upper, arrived, held), jnp.where(upper, held, arrive...  3.06 us
    sin x3, other arithmetic, angle_table(): return (jnp.cos(angle_value), jnp.sin(angle_value))  2.54 us
  transfers between devices with their start and end apart: 5, of which 2 were waited for; matrix products, arithmetic and copies ran while one was open for 24% of the time, Pallas kernels for 0%

profile of v1, /device:TPU:1, one launch (start us, length us, event | category | flops | bytes accessed | tf_op | source)
XLA Modules:
  0.0 78.9 jit_solution(2937370314579966578)
XLA Ops:
  0.0 3.1 %collective-permute-start.1 = (bf16[1,16,2,2048]{3,2,1,0:T(2,128)(2,1)}, bf16[1,16,2,2048]{3,2,1,0:T(2,128)(2,1)S(1)}, u32[]{:S(2)}, u32[]{:S(2)}) collective-permute-start(bf16[1,16,2,2048]{3,2,1,0:T(2,128)(2,1)} %bitcast.60), channel_id=1, source_target_pairs={{0,8},{1,9},{2,10},{3,11},{4,12},{5,13},{6,14},{7,15},{8,0},{9,1},... | collective-permute-start | bytes 393224 | tf_op jit(solution)/shard_map/ppermute | solution.py:173
  3.1 1.1 %convert_multiply_fusion = f32[65536]{0:T(1024)S(1)} fusion(f32[65536]{0:T(1024)} %param.3, s32[65536]{0:T(1024)} %param.4), kind=kLoop, calls=%fused_computation.57 | loop fusion | flops 131072 | bytes 786432 | tf_op jit(solution)/shard_map/mul | solution.py:185
  4.2 5.2 %collective-permute-done.1 = bf16[1,16,2,2048]{3,2,1,0:T(2,128)(2,1)S(1)} collective-permute-done((bf16[1,16,2,2048]{3,2,1,0:T(2,128)(2,1)}, bf16[1,16,2,2048]{3,2,1,0:T(2,128)(2,1)S(1)}, u32[]{:S(2)}, u32[]{:S(2)}) %collective-permute-start.1) | collective-permute-done | bytes 131104 | tf_op jit(solution)/shard_map/ppermute | solution.py:173
  9.4 1.1 %fusion.29 = (bf16[1,1,16,2,2048]{4,3,2,1,0:T(2,128)(2,1)S(1)}, bf16[1,1,16,2,2048]{4,3,2,1,0:T(2,128)(2,1)S(1)}) fusion(bf16[1,16,2,2048]{3,2,1,0:T(2,128)(2,1)S(1)} %collective-permute-done.1, pred[]{:T(512)S(6)} %ne.92, bf16[16,2,2048]{2,1,0:T(2,128)(2,1)} %param.5), kind=kLoop, calls=%fused_computation.68 | loop fusion | flops 131072 | bytes 524289 | tf_op jit(solution)/shard_map/stack | solution.py:175
  10.5 0.4 fusion.57
  10.9 1.4 %collective-permute-start.2 = (bf16[2,1,16,2,2048]{4,3,2,0,1:T(2,128)(2,1)S(1)}, bf16[2,1,16,2,2048]{4,3,2,0,1:T(2,128)(2,1)S(1)}, u32[]{:S(2)}, u32[]{:S(2)}) collective-permute-start(bf16[2,1,16,2,2048]{4,3,2,0,1:T(2,128)(2,1)S(1)} %fusion.57), channel_id=1, source_target_pairs={{0,4},{1,5},{2,6},{3,7},{4,0},{5,1},{6,2},{7,3},{8,12},{9,13},{10,... | collective-permute-start | bytes 786440 | tf_op jit(solution)/shard_map/ppermute | solution.py:173
  12.2 0.7 fusion.59
  13.0 3.8 %collective-permute-start = (f32[32768]{0:T(1024)}, f32[32768]{0:T(1024)}, u32[]{:S(2)}, u32[]{:S(2)}) collective-permute-start(f32[32768]{0:T(1024)} %get-tuple-element.17), channel_id=1, source_target_pairs={{0,1},{1,2},{2,3},{3,4},{4,5},{5,6},{6,7},{7,8},{8,9},{9,10},{10,1... | collective-permute-start | bytes 393224 | tf_op jit(solution)/shard_map/ppermute | solution.py:22
  16.8 1.0 %fusion.35 = f32[256,256]{1,0:T(8,128)S(1)} fusion(), kind=kLoop, calls=%fused_computation.74 | loop fusion | flops 917504 | bytes 262144 | tf_op jit(solution)/shard_map/sin | solution.py:30
  17.8 0.0 collective-permute-done.2
  17.8 0.5 fusion.17
  18.2 0.5 fusion.18
  18.7 0.7 fusion.58
  19.4 1.0 %collective-permute-start.3 = (bf16[2,2,1,16,2,2048]{5,4,3,1,0,2:T(2,128)(2,1)S(1)}, bf16[2,2,1,16,2,2048]{5,4,3,1,0,2:T(2,128)(2,1)S(1)}, u32[]{:S(2)}, u32[]{:S(2)}) collective-permute-start(bf16[2,2,1,16,2,2048]{5,4,3,1,0,2:T(2,128)(2,1)S(1)} %fusion.58), channel_id=1, source_target_pairs={{0,2},{1,3},{2,0},{3,1},{4,6},{5,7},{6,4},{7,5},{8,10},{9,11},{10,... | collective-permute-start | bytes 1572872 | tf_op jit(solution)/shard_map/ppermute | solution.py:173
  20.4 0.5 fusion.43
  20.9 0.5 fusion.41
  21.4 1.0 %fusion.36 = (f32[256,256]{1,0:T(8,128)S(1)}, f32[256,256]{1,0:T(8,128)S(1)}) fusion(), kind=kLoop, calls=%fused_computation.75 | loop fusion | flops 983040 | bytes 524288 | tf_op jit(solution)/shard_map/cos | solution.py:30
  22.5 1.0 %fusion.33 = (f32[256,256]{1,0:T(8,128)S(1)}, f32[256,256]{1,0:T(8,128)S(1)}) fusion(), kind=kLoop, calls=%fused_computation.72 | loop fusion | flops 917504 | bytes 524288 | tf_op jit(solution)/shard_map/sin | solution.py:30
  23.5 0.0 copy-start
  23.5 0.0 copy-start.1
  23.5 1.0 %fusion.1 = (bf16[512,256]{1,0:T(8,128)(2,1)}, bf16[512,256]{1,0:T(8,128)(2,1)}) fusion(f32[256,256]{1,0:T(8,128)S(1)} %get-tuple-element.19, f32[256,256]{1,0:T(8,128)S(1)} %fusion.35, f32[256,256]{1,0:T(8,128)S(1)} %get-tuple-element.20), kind=kLoop, calls=%fused_computation.15 | loop fusion | flops 1310720 | bytes 1310720 | tf_op jit(solution)/shard_map/convert_element_type | solution.py:71
  24.5 6.5 %collective-permute-done.3 = bf16[2,2,1,16,2,2048]{5,4,3,1,0,2:T(2,128)(2,1)S(1)} collective-permute-done((bf16[2,2,1,16,2,2048]{5,4,3,1,0,2:T(2,128)(2,1)S(1)}, bf16[2,2,1,16,2,2048]{5,4,3,1,0,2:T(2,128)(2,1)S(1)}, u32[]{:S(2)}, u32[]{:S(2)}) %collective-permute-start.3) | collective-permute-done | bytes 524320 | tf_op jit(solution)/shard_map/ppermute | solution.py:173
  31.0 0.9 %fusion.2 = bf16[1,2,2,1,16,2,2048]{6,5,4,2,1,3,0:T(2,128)(2,1)S(1)} fusion(bf16[2,2,1,16,2,2048]{5,4,3,1,0,2:T(2,128)(2,1)S(1)} %collective-permute-done.3, pred[]{:T(512)S(6)} %ne.90, bf16[1,2,1,16,2,2048]{5,4,3,1,2,0:T(2,128)(2,1)S(1)} %fusion.18, bf16[1,2,1,16,2,2048]{5,4,3,1,2,0:T(2,128)(2,1)S(1)} %fusion.17), kind=kLoop, calls=%fused_computation.16 | loop fusion | flops 524288 | bytes 1572865 | tf_op jit(solution)/shard_map/stack | solution.py:175
  31.9 0.9 %fusion.3 = bf16[1,2,2,1,16,2,2048]{6,5,4,2,1,3,0:T(2,128)(2,1)S(1)} fusion(pred[]{:T(512)S(6)} %ne.90, bf16[2,2,1,16,2,2048]{5,4,3,1,0,2:T(2,128)(2,1)S(1)} %collective-permute-done.3, bf16[1,2,1,16,2,2048]{5,4,3,1,2,0:T(2,128)(2,1)S(1)} %fusion.18, bf16[1,2,1,16,2,2048]{5,4,3,1,2,0:T(2,128)(2,1)S(1)} %fusion.17), kind=kLoop, calls=%fused_computation.17 | loop fusion | flops 524288 | bytes 1572865 | tf_op jit(solution)/shard_map/stack | solution.py:175
  32.8 0.0 copy-start.2
  32.8 2.5 %pad_maximum_fusion.2 = bf16[2,2,2,1,16,2,2048]{6,5,4,2,1,3,0:T(2,128)(2,1)} fusion(bf16[1,2,2,1,16,2,2048]{6,5,4,2,1,3,0:T(2,128)(2,1)S(1)} %fusion.3, bf16[1,2,2,1,16,2,2048]{6,5,4,2,1,3,0:T(2,128)(2,1)S(1)} %fusion.2), kind=kLoop, calls=%fused_computation.7 | loop fusion | flops 524288 | bytes 2097152 | tf_op jit(solution)/shard_map/stack | solution.py:175
  35.4 2.8 %collective-permute-start.4 = (bf16[2,2,2,1,16,2,2048]{6,5,4,2,1,3,0:T(2,128)(2,1)}, bf16[2,2,2,1,16,2,2048]{6,5,4,2,1,3,0:T(2,128)(2,1)}, u32[]{:S(2)}, u32[]{:S(2)}) collective-permute-start(bf16[2,2,2,1,16,2,2048]{6,5,4,2,1,3,0:T(2,128)(2,1)} %pad_maximum_fusion.2), channel_id=1, source_target_pairs={{0,1},{1,0},{2,3},{3,2},{4,5},{5,4},{6,7},{7,6},{8,9},{9,8},{10,11... | collective-permute-start | bytes 3145736 | tf_op jit(solution)/shard_map/ppermute | solution.py:173
  38.2 0.9 %fusion = (bf16[512,256]{1,0:T(8,128)(2,1)}, bf16[512,256]{1,0:T(8,128)(2,1)}) fusion(f32[256,128]{1,0:T(8,128)S(1)} %get-tuple-element.24, f32[256,128]{1,0:T(8,128)S(1)} %get-tuple-element.23, f32[256,128]{1,0:T(8,128)S(1)} %fusion.43), kind=kLoop, calls=%fused_computation.14 | loop fusion | flops 917504 | bytes 917504 | tf_op jit(solution)/shard_map/convert_element_type | solution.py:71
  39.1 0.1 concatenate.42
  39.1 0.0 copy-done.2
  39.2 0.1 copy.17
  39.3 0.1 copy.18
  39.4 0.0 collective-permute-done
  39.4 0.9 %concatenate.40 = f32[1,128,256]{2,1,0:T(8,128)S(1)} reshape(f32[32768]{0:T(1024)} %collective-permute-done) | data formatting | bytes 262144 | tf_op jit(solution)/shard_map/concatenate | solution.py:189
  40.4 0.1 copy.16
  40.5 0.6 fusion.5
  41.1 0.0 copy-done
  41.1 0.0 copy-done.1
  41.1 0.1 multiply_add_fusion
  41.2 0.9 %convolution_bitcast_fusion.1 = f32[2,128,512]{2,1,0:T(8,128)S(1)} fusion(f32[2,256,256]{2,1,0:T(8,128)S(1)} %get-tuple-element.8, f32[2,256,256]{2,1,0:T(8,128)S(1)} %get-tuple-element.7), kind=kOutput, calls=%fused_computation.5 | convolution fusion | flops 202047488 | bytes 1572864 | tf_op jit(solution)/shard_map/bnf,nk->bkf/dot_general | solution.py:52
  42.1 1.1 %convolution_bitcast_fusion = f32[2,128,512]{2,1,0:T(8,128)S(1)} fusion(f32[2,256,256]{2,1,0:T(8,128)S(1)} %get-tuple-element.8, f32[2,256,256]{2,1,0:T(8,128)S(1)} %get-tuple-element.7), kind=kOutput, calls=%fused_computation.4 | convolution fusion | flops 202047488 | bytes 1572864 | tf_op jit(solution)/shard_map/bnf,nk->bkf/dot_general | solution.py:53
  43.2 0.1 slice_add_fusion
  43.3 0.9 %pad_maximum_fusion.6.spec_ref = f32[2,128,512]{2,1,0:T(8,128)} fusion(f32[2,128,256]{2,1,0:T(8,128)S(1)} %get-tuple-element.10, f32[2,128,256]{2,1,0:T(8,128)S(1)} %get-tuple-element.9), kind=kLoop, calls=%fused_computation.31 | loop fusion | flops 131072 | bytes 1048576 | tf_op jit(solution)/shard_map/concatenate | solution.py:54
  44.2 0.0 collective-permute-done.4
  44.2 3.5 %broadcast_select_fusion.1 = (bf16[2,2,2,1,16,2,2048]{6,5,4,2,1,3,0:T(2,128)(2,1)S(1)}, bf16[2,2,2,1,16,2,2048]{6,5,4,2,1,3,0:T(2,128)(2,1)S(1)}) fusion(bf16[2,2,2,1,16,2,2048]{6,5,4,2,1,3,0:T(2,128)(2,1)} %collective-permute-done.4, pred[]{:T(512)S(6)} %ne.89, bf16[1,2,2,1,16,2,2048]{6,5,4,2,1,3,0:T(2,128)(2,1)S(1)} %fusion.3, ...), kind=kLoop, calls=%fused_computation.3 | loop fusion | flops 1572864 | bytes 4194305 | tf_op jit(solution)/shard_map/jit(_where)/select_n | solution.py:175
  47.7 0.7 stack.45
  48.5 0.7 stack.46
  49.2 0.2 pad_maximum_fusion
  49.4 1.6 %copy.35 = bf16[2,2,2,2,16,2,8,256]{7,6,0,1,2,3,5,4:T(8,128)(2,1)} copy(bf16[2,2,2,2,16,2,8,256]{7,6,5,4,3,2,1,0:T(8,128)(2,1)S(1)} %pad_maximum_fusion) | data formatting | bytes 4194304 | tf_op jit(solution)/shard_map/stack | solution.py:175
  51.0 26.6 %shard_map.37 = f32[16,2,128]{2,1,0:T(2,128)} custom-call(f32[2,128,512]{2,1,0:T(8,128)} %pad_maximum_fusion.6.spec_ref, bf16[16,2,128,256]{3,2,1,0:T(8,128)(2,1)} %bitcast.59, bf16[512,256]{1,0:T(8,128)(2,1)} %get-tuple-element.14.fh_ref, bf16[512,256]{1,0:T(8,128)(2,1)} %get-tuple-element.13.fl_ref, f32[256,256]{1,0:T(8,128)} %copy-done.1, ...), custom_call_target="tpu_custom_call" | custom-call | flops 12884901888 | bytes 2637824 | tf_op jit(solution)/shard_map/pallas_call | solution.py:140
  77.6 1.3 %copy.38 = f32[2,8,2,128]{3,1,2,0:T(8,128)} copy(f32[2,8,2,128]{3,2,1,0:T(2,128)} %bitcast.61) | data formatting | bytes 32768
  (1 shorter events, 0.0 us)
Async XLA Ops:
  0.0 9.4 %collective-permute-start.1 = (bf16[1,16,2,2048]{3,2,1,0:T(2,128)(2,1)}, bf16[1,16,2,2048]{3,2,1,0:T(2,128)(2,1)S(1)}, u32[]{:S(2)}, u32[]{:S(2)}) collective-permute-start(bf16[1,16,2,2048]{3,2,1,0:T(2,128)(2,1)} %bitcast.60), channel_id=1, source_target_pairs={{0,8},{1,9},{2,10},{3,11},{4,12},{5,13},{6,14},{7,15},{8,0},{9,1},... | collective-permute-start | bytes 393224 | tf_op jit(solution)/shard_map/ppermute | solution.py:173
  10.9 6.9 %collective-permute-start.2 = (bf16[2,1,16,2,2048]{4,3,2,0,1:T(2,128)(2,1)S(1)}, bf16[2,1,16,2,2048]{4,3,2,0,1:T(2,128)(2,1)S(1)}, u32[]{:S(2)}, u32[]{:S(2)}) collective-permute-start(bf16[2,1,16,2,2048]{4,3,2,0,1:T(2,128)(2,1)S(1)} %fusion.57), channel_id=1, source_target_pairs={{0,4},{1,5},{2,6},{3,7},{4,0},{5,1},{6,2},{7,3},{8,12},{9,13},{10,... | collective-permute-start | bytes 786440 | tf_op jit(solution)/shard_map/ppermute | solution.py:173
  13.0 26.5 %collective-permute-start = (f32[32768]{0:T(1024)}, f32[32768]{0:T(1024)}, u32[]{:S(2)}, u32[]{:S(2)}) collective-permute-start(f32[32768]{0:T(1024)} %get-tuple-element.17), channel_id=1, source_target_pairs={{0,1},{1,2},{2,3},{3,4},{4,5},{5,6},{6,7},{7,8},{8,9},{9,10},{10,1... | collective-permute-start | bytes 393224 | tf_op jit(solution)/shard_map/ppermute | solution.py:22
  19.4 11.6 %collective-permute-start.3 = (bf16[2,2,1,16,2,2048]{5,4,3,1,0,2:T(2,128)(2,1)S(1)}, bf16[2,2,1,16,2,2048]{5,4,3,1,0,2:T(2,128)(2,1)S(1)}, u32[]{:S(2)}, u32[]{:S(2)}) collective-permute-start(bf16[2,2,1,16,2,2048]{5,4,3,1,0,2:T(2,128)(2,1)S(1)} %fusion.58), channel_id=1, source_target_pairs={{0,2},{1,3},{2,0},{3,1},{4,6},{5,7},{6,4},{7,5},{8,10},{9,11},{10,... | collective-permute-start | bytes 1572872 | tf_op jit(solution)/shard_map/ppermute | solution.py:173
  23.5 17.6 %copy-start = (f32[256,256]{1,0:T(8,128)}, f32[256,256]{1,0:T(8,128)S(1)}, u32[]{:S(2)}) copy-start(f32[256,256]{1,0:T(8,128)S(1)} %get-tuple-element.21.ts_ref) | copy-start | bytes 786436
  23.5 17.6 %copy-start.1 = (f32[256,256]{1,0:T(8,128)}, f32[256,256]{1,0:T(8,128)S(1)}, u32[]{:S(2)}) copy-start(f32[256,256]{1,0:T(8,128)S(1)} %get-tuple-element.22.tc_ref) | copy-start | bytes 786436
  32.8 6.3 %copy-start.2 = (f32[32768]{0:T(1024)S(1)}, f32[32768]{0:T(1024)}, u32[]{:S(2)}) copy-start(f32[32768]{0:T(1024)} %get-tuple-element.18) | copy-start | bytes 393220
  35.4 8.8 %collective-permute-start.4 = (bf16[2,2,2,1,16,2,2048]{6,5,4,2,1,3,0:T(2,128)(2,1)}, bf16[2,2,2,1,16,2,2048]{6,5,4,2,1,3,0:T(2,128)(2,1)}, u32[]{:S(2)}, u32[]{:S(2)}) collective-permute-start(bf16[2,2,2,1,16,2,2048]{6,5,4,2,1,3,0:T(2,128)(2,1)} %pad_maximum_fusion.2), channel_id=1, source_target_pairs={{0,1},{1,0},{2,3},{3,2},{4,5},{5,4},{6,7},{7,6},{8,9},{9,8},{10,11... | collective-permute-start | bytes 3145736 | tf_op jit(solution)/shard_map/ppermute | solution.py:173

commit v2 on v1

--- a/solution.py
+++ b/solution.py
@@ -163,22 +163,12 @@
 
 def gathered_bank(bank_rows):
     seg_total = lax.axis_size("seg")
-    me = lax.axis_index("seg")
     rows, parts, local_bins = bank_rows.shape
-    held = bank_rows[None]
-    distance = seg_total // 2
-    steps = 0
-    while distance >= 1:
-        pairs = [(i, i ^ distance) for i in range(seg_total)]
-        arrived = lax.ppermute(held, "seg", pairs)
-        upper = (me & distance) != 0
-        held = jnp.stack([jnp.where(upper, arrived, held), jnp.where(upper, held, arrived)], axis=0)
-        distance //= 2
-        steps += 1
-    held = held.reshape((2,) * steps + (rows, parts, local_bins // RADIX, RADIX))
-    order = tuple(reversed(range(steps)))
-    held = jnp.transpose(held, (steps, steps + 1) + order + (steps + 2, steps + 3))
-    return held.reshape(rows, parts, seg_total * local_bins // RADIX, RADIX)
+    copies = jnp.broadcast_to(bank_rows[None], (seg_total, rows, parts, local_bins))
+    every = lax.all_to_all(copies, "seg", 0, 0, tiled=True)
+    every = every.reshape(seg_total, rows, parts, local_bins // RADIX, RADIX)
+    every = jnp.transpose(every, (1, 2, 0, 3, 4))
+    return every.reshape(rows, parts, seg_total * local_bins // RADIX, RADIX)
 
 
 def local(strain, gate_mask, template_bank):

time: 79.9 us -> 101 us (1.26)
  the two profiles are of different devices: /device:TPU:1 before, /device:TPU:18 now
where the time goes in v2:
time: 101 us
  waiting for transfers between devices  35.2 us (35%)
  Pallas kernels  26.6 us (26%)
  local copies, waits for them, and re-layouts  18.4 us (18%)
  other arithmetic  8.7 us (9%)
  starting transfers between devices  8.36 us (8%)
  matrix products  3.3 us (3%)
    ppermute x1, waiting for transfers between devices, passed_along(): return lax.ppermute(value, axis, pairs)  35.2 us
    pallas_call x1, Pallas kernels, window_peaks(): pl.pallas_call(peaks_kernel, out_shape=jax.ShapeDtypeStruct((template_tot...  26.6 us
    all_to_all x1, starting transfers between devices, gathered_bank(): every = lax.all_to_all(copies, 'seg', 0, 0, tiled=True)  6.32 us
    reshape x2, local copies, waits for them, and re-layouts, gathered_bank(): every = every.reshape(seg_total, rows, parts, local_bins // RADIX, RADIX)  5.78 us
    broadcast_in_dim x1, local copies, waits for them, and re-layouts, gathered_bank(): jnp.broadcast_to(bank_rows[None], (seg_total, rows, parts, local_bins))  3.86 us
    sin x3, other arithmetic, angle_table(): return (jnp.cos(angle_value), jnp.sin(angle_value))  3.25 us
    concatenate x2, local copies, waits for them, and re-layouts, local(): before = jnp.concatenate([earlier[None], local_blocks[:-1]], axis=0)  3.24 us
    convert_element_type x2, other arithmetic, table_pair(): return (high.astype(jnp.bfloat16), (value - high).astype(jnp.bfloat16))  2.82 us
  transfers between devices with their start and end apart: 2, of which 1 were waited for; matrix products, arithmetic and copies ran while one was open for 19% of the time, Pallas kernels for 0%

profile of v2, /device:TPU:18, one launch (start us, length us, event | category | flops | bytes accessed | tf_op | source)
XLA Modules:
  0.0 100.7 jit_solution(734805613884274044)
XLA Ops:
  0.0 3.9 %broadcast_in_dim.2 = bf16[16,16,2,2048]{3,2,1,0:T(2,128)(2,1)} broadcast(bf16[16,2,2048]{2,1,0:T(2,128)(2,1)} %param.5), dimensions={1,2,3} | broadcast | bytes 2228224 | tf_op jit(solution)/shard_map/broadcast_in_dim | solution.py:167
  3.9 0.0 copy-start.2
  3.9 0.0 copy-start.3
  3.9 6.3 %all-to-all-start = ((bf16[16,16,2,2048]{3,2,1,0:T(2,128)(2,1)}), bf16[16,16,2,2048]{3,2,1,0:T(2,128)(2,1)S(1)}, u32[]{:S(2)}, u32[]{:S(2)}) async-start(bf16[16,16,2,2048]{3,2,1,0:T(2,128)(2,1)} %broadcast_in_dim.2), calls=%async_computation | async-start | bytes 4194304 | tf_op jit(solution)/shard_map/all_to_all | solution.py:168
  10.2 0.0 copy-done.2
  10.2 0.0 copy-done.3
  10.2 0.7 fusion.51
  10.9 2.0 %collective-permute-start = (f32[32768]{0:T(1024)}, f32[32768]{0:T(1024)}, u32[]{:S(2)}, u32[]{:S(2)}) collective-permute-start(f32[32768]{0:T(1024)} %get-tuple-element.13), channel_id=1, source_target_pairs={{0,1},{1,2},{2,3},{3,4},{4,5},{5,6},{6,7},{7,8},{8,9},{9,10},{10,1... | collective-permute-start | bytes 393224 | tf_op jit(solution)/shard_map/ppermute | solution.py:22
  13.0 0.5 fusion.37
  13.5 0.5 fusion.35
  14.0 1.0 %fusion.30 = (f32[256,256]{1,0:T(8,128)S(1)}, f32[256,256]{1,0:T(8,128)S(1)}) fusion(), kind=kLoop, calls=%fused_computation.58 | loop fusion | flops 983040 | bytes 524288 | tf_op jit(solution)/shard_map/cos | solution.py:30
  15.1 1.0 %fusion.27 = (f32[256,256]{1,0:T(8,128)S(1)}, f32[256,256]{1,0:T(8,128)S(1)}) fusion(), kind=kLoop, calls=%fused_computation.55 | loop fusion | flops 917504 | bytes 524288 | tf_op jit(solution)/shard_map/sin | solution.py:30
  16.1 0.0 copy-start
  16.1 0.0 copy-start.1
  16.1 1.0 fusion
  17.1 1.7 %fusion.29 = f32[256,256]{1,0:T(8,128)} fusion(), kind=kLoop, calls=%fused_computation.57 | loop fusion | flops 917504 | bytes 262144 | tf_op jit(solution)/shard_map/sin | solution.py:30
  18.8 0.8 concatenate.41
  19.6 1.1 %copy.13 = f32[2,128,256]{1,2,0:T(8,128)S(1)} copy(f32[2,128,256]{2,1,0:T(8,128)} %concatenate.41) | data formatting | bytes 524288 | tf_op jit(solution)/shard_map/concatenate | solution.py:180
  20.7 0.7 slice.42
  21.3 1.0 copy.12
  22.3 1.8 %fusion.1 = (bf16[512,256]{1,0:T(8,128)(2,1)}, bf16[512,256]{1,0:T(8,128)(2,1)}) fusion(f32[256,256]{1,0:T(8,128)S(1)} %get-tuple-element.15, f32[256,256]{1,0:T(8,128)} %fusion.29, f32[256,256]{1,0:T(8,128)S(1)} %get-tuple-element.16), kind=kLoop, calls=%fused_computation.9 | loop fusion | flops 1310720 | bytes 1310720 | tf_op jit(solution)/shard_map/convert_element_type | solution.py:71
  24.2 35.2 %collective-permute-done = f32[32768]{0:T(1024)} collective-permute-done((f32[32768]{0:T(1024)}, f32[32768]{0:T(1024)}, u32[]{:S(2)}, u32[]{:S(2)}) %collective-permute-start) | collective-permute-done | bytes 131104 | tf_op jit(solution)/shard_map/ppermute | solution.py:22
  59.3 1.6 %concatenate.39 = f32[1,128,256]{2,1,0:T(8,128)} reshape(f32[32768]{0:T(1024)} %collective-permute-done) | data formatting | bytes 262144 | tf_op jit(solution)/shard_map/concatenate | solution.py:179
  60.9 1.7 %copy.11 = f32[1,128,256]{1,2,0:T(8,128)} copy(f32[1,128,256]{2,1,0:T(8,128)} %concatenate.39) | data formatting | bytes 262144 | tf_op jit(solution)/shard_map/concatenate | solution.py:179
  62.6 1.5 %fusion.3 = f32[2,256,512]{2,1,0:T(8,128)S(1)} fusion(f32[2,128,256]{1,2,0:T(8,128)S(1)} %copy.13, f32[1,128,256]{1,2,0:T(8,128)S(1)} %copy.12, f32[1,128,256]{1,2,0:T(8,128)} %copy.11, f32[256,256]{1,0:T(8,128)S(1)} %get-tuple-element.16, f32[256,256]{1,0:T(8,128)S(1)} %get-tuple-element.15), kind=kOutput, calls=%fused_computation.14 | convolution fusion | flops 403046400 | bytes 2097152 | tf_op jit(solution)/shard_map/bnm,nf->bmf/dot_general | solution.py:40
  64.1 0.0 copy-done
  64.1 0.0 copy-done.1
  64.1 0.1 multiply_add_fusion
  64.2 0.9 convolution_bitcast_fusion
  65.1 0.9 convolution_bitcast_fusion.1
  66.1 0.1 slice_add_fusion
  66.1 0.9 pad_maximum_fusion.4.spec_ref
  67.0 0.0 all-to-all-done
  67.0 2.6 %reshape.54 = bf16[16,16,2,8,256]{4,3,2,1,0:T(8,128)(2,1)} reshape(bf16[16,16,2,2048]{3,2,1,0:T(2,128)(2,1)S(1)} %all-to-all-done) | data formatting | bytes 4194304 | tf_op jit(solution)/shard_map/reshape | solution.py:169
  69.6 3.2 %copy.24 = bf16[16,16,2,8,256]{4,3,0,2,1:T(8,128)(2,1)} copy(bf16[16,16,2,8,256]{4,3,2,1,0:T(8,128)(2,1)} %reshape.54) | data formatting | bytes 4194304 | tf_op jit(solution)/shard_map/reshape | solution.py:169
  72.8 26.6 %shard_map.37 = f32[16,2,128]{2,1,0:T(2,128)} custom-call(f32[2,128,512]{2,1,0:T(8,128)} %pad_maximum_fusion.4.spec_ref, bf16[16,2,128,256]{3,2,1,0:T(8,128)(2,1)} %bitcast.22, bf16[512,256]{1,0:T(8,128)(2,1)} %get-tuple-element.12.fh_ref, bf16[512,256]{1,0:T(8,128)(2,1)} %get-tuple-element.11.fl_ref, f32[256,256]{1,0:T(8,128)} %copy-done.1, ...), custom_call_target="tpu_custom_call" | custom-call | flops 12884901888 | bytes 2637824 | tf_op jit(solution)/shard_map/pallas_call | solution.py:140
  99.4 1.3 %copy.25 = f32[2,8,2,128]{3,1,2,0:T(8,128)} copy(f32[2,8,2,128]{3,2,1,0:T(2,128)} %bitcast.23) | data formatting | bytes 32768
  (1 shorter events, 0.0 us)
Async XLA Ops:
  3.9 6.3 %copy-start.2 = (f32[65536]{0:T(1024)S(1)}, f32[65536]{0:T(1024)}, u32[]{:S(2)}) copy-start(f32[65536]{0:T(1024)} %param.3) | copy-start | bytes 786436
  3.9 6.3 %copy-start.3 = (s32[65536]{0:T(1024)S(1)}, s32[65536]{0:T(1024)}, u32[]{:S(2)}) copy-start(s32[65536]{0:T(1024)} %param.4) | copy-start | bytes 786436
  3.9 63.1 %all-to-all-start = ((bf16[16,16,2,2048]{3,2,1,0:T(2,128)(2,1)}), bf16[16,16,2,2048]{3,2,1,0:T(2,128)(2,1)S(1)}, u32[]{:S(2)}, u32[]{:S(2)}) async-start(bf16[16,16,2,2048]{3,2,1,0:T(2,128)(2,1)} %broadcast_in_dim.2), calls=%async_computation | async-start | bytes 4194304 | tf_op jit(solution)/shard_map/all_to_all | solution.py:168
  10.9 48.4 %collective-permute-start = (f32[32768]{0:T(1024)}, f32[32768]{0:T(1024)}, u32[]{:S(2)}, u32[]{:S(2)}) collective-permute-start(f32[32768]{0:T(1024)} %get-tuple-element.13), channel_id=1, source_target_pairs={{0,1},{1,2},{2,3},{3,4},{4,5},{5,6},{6,7},{7,8},{8,9},{9,10},{10,1... | collective-permute-start | bytes 393224 | tf_op jit(solution)/shard_map/ppermute | solution.py:22
  16.1 48.0 %copy-start = (f32[256,256]{1,0:T(8,128)}, f32[256,256]{1,0:T(8,128)S(1)}, u32[]{:S(2)}) copy-start(f32[256,256]{1,0:T(8,128)S(1)} %get-tuple-element.17.ts_ref) | copy-start | bytes 786436
  16.1 48.0 %copy-start.1 = (f32[256,256]{1,0:T(8,128)}, f32[256,256]{1,0:T(8,128)S(1)}, u32[]{:S(2)}) copy-start(f32[256,256]{1,0:T(8,128)S(1)} %get-tuple-element.18.tc_ref) | copy-start | bytes 786436

commit v3 on v1

--- a/solution.py
+++ b/solution.py
@@ -9,7 +9,7 @@
 
 RADIX = 256
 BLOCK = 32768
-SUBBANK = 16
+SUBBANK = 8
 
 
 PRECISE = lax.Precision.HIGH

time: 79.9 us -> 74.5 us (0.932)
  waiting for transfers between devices: 11.7 us -> 3.85 us
  starting transfers between devices: 12.1 us -> 16.8 us
  other arithmetic: 19.3 us -> 16.5 us
  Pallas kernels: 26.6 us -> 28.7 us
  local copies, waits for them, and re-layouts: 6.48 us -> 5.59 us
    ppermute x4 -> x8, waiting for transfers between devices: 11.7 us -> 3.84 us  [gathered_bank(): arrived = lax.ppermute(held, 'seg', pairs)]
    ppermute x4 -> x8, starting transfers between devices: 8.28 us -> 12.2 us  [gathered_bank(): arrived = lax.ppermute(held, 'seg', pairs)]
    another operation x9 -> x15, other arithmetic: 7.67 us -> 5.46 us  [gathered_bank(): jnp.stack([jnp.where(upper, arrived, held), jnp.where(upper, held, arrive...]
    pallas_call x1 -> x2, Pallas kernels: 26.6 us -> 28.7 us  [window_peaks(): pl.pallas_call(peaks_kernel, out_shape=jax.ShapeDtypeStruct((template_tot...]
    select_n x1 -> x2, other arithmetic: 3.55 us -> 2.46 us  [gathered_bank(): jnp.where(upper, arrived, held)]
    concatenate x2, local copies, waits for them, and re-layouts: 1.03 us -> 0.13 us  [local(): before = jnp.concatenate([earlier[None], local_blocks[:-1]], axis=0)]
    ppermute x1, starting transfers between devices: 3.79 us -> 4.67 us  [passed_along(): return lax.ppermute(value, axis, pairs)]
    another operation x3 -> x6, local copies, waits for them, and re-layouts: 3.06 us -> 3.62 us  [gathered_bank(): jnp.stack([jnp.where(upper, arrived, held), jnp.where(upper, held, arrive...]
  transfers between devices with their start and end apart: 5 -> 9, of which waited for: 2 -> 3; matrix products, arithmetic and copies ran while one was open for 24% -> 26% of each run, Pallas kernels for 0% -> 19%
where the time goes in v3:
time: 74.5 us; the launch traced here: 74.2 us
  Pallas kernels  28.7 us (39%)
  starting transfers between devices  16.8 us (23%)
  other arithmetic  16.5 us (22%)
  local copies, waits for them, and re-layouts  5.59 us (8%)
  waiting for transfers between devices  3.85 us (5%)
  matrix products  2.4 us (3%)
    pallas_call x2, Pallas kernels, window_peaks(): pl.pallas_call(peaks_kernel, out_shape=jax.ShapeDtypeStruct((template_tot...  28.7 us
    ppermute x8, starting transfers between devices, gathered_bank(): arrived = lax.ppermute(held, 'seg', pairs)  12.2 us
    another operation x15, other arithmetic, gathered_bank(): jnp.stack([jnp.where(upper, arrived, held), jnp.where(upper, held, arrive...  5.46 us
    ppermute x1, starting transfers between devices, passed_along(): return lax.ppermute(value, axis, pairs)  4.67 us
    ppermute x8, waiting for transfers between devices, gathered_bank(): arrived = lax.ppermute(held, 'seg', pairs)  3.84 us
    another operation x6, local copies, waits for them, and re-layouts, gathered_bank(): jnp.stack([jnp.where(upper, arrived, held), jnp.where(upper, held, arrive...  3.62 us
    sin x3, other arithmetic, angle_table(): return (jnp.cos(angle_value), jnp.sin(angle_value))  2.54 us
    select_n x2, other arithmetic, gathered_bank(): jnp.where(upper, arrived, held)  2.46 us
  transfers between devices with their start and end apart: 9, of which 3 were waited for; matrix products, arithmetic and copies ran while one was open for 26% of the time, Pallas kernels for 19%

profile of v3, /device:TPU:1, one launch (start us, length us, event | category | flops | bytes accessed | tf_op | source)
XLA Modules:
  0.0 74.2 jit_solution(5780643528955379030)
XLA Ops:
  0.0 1.1 %convert_multiply_fusion = f32[65536]{0:T(1024)S(1)} fusion(f32[65536]{0:T(1024)} %param.3, s32[65536]{0:T(1024)} %param.4), kind=kLoop, calls=%fused_computation.62 | loop fusion | flops 131072 | bytes 786432 | tf_op jit(solution)/shard_map/mul | solution.py:185
  1.1 0.0 copy-start.2
  1.1 4.7 %collective-permute-start = (f32[32768]{0:T(1024)S(1)}, f32[32768]{0:T(1024)S(1)}, u32[]{:S(2)}, u32[]{:S(2)}) collective-permute-start(f32[32768]{0:T(1024)S(1)} %get-tuple-element.21), channel_id=1, source_target_pairs={{0,1},{1,2},{2,3},{3,4},{4,5},{5,6},{6,7},{7,8},{8,9},{9,10},{10,1... | collective-permute-start | bytes 393224 | tf_op jit(solution)/shard_map/ppermute | solution.py:22
  5.8 0.1 slice_bitcast_fusion.1
  5.9 2.4 %collective-permute-start.1 = (bf16[1,8,2,2048]{3,2,1,0:T(2,128)(2,1)S(1)}, bf16[1,8,2,2048]{3,2,1,0:T(2,128)(2,1)S(1)}, u32[]{:S(2)}, u32[]{:S(2)}) collective-permute-start(bf16[1,8,2,2048]{3,2,1,0:T(2,128)(2,1)S(1)} %get-tuple-element.29), channel_id=1, source_target_pairs={{0,8},{1,9},{2,10},{3,11},{4,12},{5,13},{6,14},{7,15},{8,0},{9,1},... | collective-permute-start | bytes 196616 | tf_op jit(solution)/shard_map/ppermute | solution.py:173
  8.3 0.1 collective-permute-start.5
  8.3 0.1 concatenate.46
  8.4 1.0 %fusion.38 = (f32[256,256]{1,0:T(8,128)S(1)}, f32[256,256]{1,0:T(8,128)S(1)}) fusion(), kind=kLoop, calls=%fused_computation.85 | loop fusion | flops 983040 | bytes 524288 | tf_op jit(solution)/shard_map/cos | solution.py:30
  9.5 1.0 %fusion.35 = (f32[256,256]{1,0:T(8,128)S(1)}, f32[256,256]{1,0:T(8,128)S(1)}) fusion(), kind=kLoop, calls=%fused_computation.82 | loop fusion | flops 917504 | bytes 524288 | tf_op jit(solution)/shard_map/sin | solution.py:30
  10.5 0.5 fusion.47
  11.1 0.5 fusion.49
  11.6 1.0 %fusion.37 = f32[256,256]{1,0:T(8,128)S(1)} fusion(), kind=kLoop, calls=%fused_computation.84 | loop fusion | flops 917504 | bytes 262144 | tf_op jit(solution)/shard_map/sin | solution.py:30
  12.5 0.1 copy.22
  12.7 0.1 copy.21
  12.8 0.9 %fusion = (bf16[512,256]{1,0:T(8,128)(2,1)}, bf16[512,256]{1,0:T(8,128)(2,1)}) fusion(f32[256,128]{1,0:T(8,128)S(1)} %get-tuple-element.36, f32[256,128]{1,0:T(8,128)S(1)} %get-tuple-element.35, f32[256,128]{1,0:T(8,128)S(1)} %fusion.49), kind=kLoop, calls=%fused_computation.14 | loop fusion | flops 917504 | bytes 917504 | tf_op jit(solution)/shard_map/convert_element_type | solution.py:71
  13.7 0.9 %fusion.1 = (bf16[512,256]{1,0:T(8,128)(2,1)}, bf16[512,256]{1,0:T(8,128)(2,1)}) fusion(f32[256,256]{1,0:T(8,128)S(1)} %get-tuple-element.31, f32[256,256]{1,0:T(8,128)S(1)} %fusion.37, f32[256,256]{1,0:T(8,128)S(1)} %get-tuple-element.32), kind=kLoop, calls=%fused_computation.15 | loop fusion | flops 1310720 | bytes 1310720 | tf_op jit(solution)/shard_map/convert_element_type | solution.py:71
  14.6 0.0 collective-permute-done.1
  14.6 0.0 collective-permute-done.5
  14.6 0.2 fusion.43
  14.8 0.2 fusion.63
  15.0 1.4 %collective-permute-start.6 = (bf16[2,1,8,2,2048]{4,3,2,0,1:T(2,128)(2,1)S(1)}, bf16[2,1,8,2,2048]{4,3,2,0,1:T(2,128)(2,1)S(1)}, u32[]{:S(2)}, u32[]{:S(2)}) collective-permute-start(bf16[2,1,8,2,2048]{4,3,2,0,1:T(2,128)(2,1)S(1)} %fusion.63), channel_id=1, source_target_pairs={{0,4},{1,5},{2,6},{3,7},{4,0},{5,1},{6,2},{7,3},{8,12},{9,13},{10,... | collective-permute-start | bytes 393224 | tf_op jit(solution)/shard_map/ppermute | solution.py:173
  16.4 0.2 pad_maximum_fusion.11
  16.6 0.2 collective-permute-start.2
  16.8 0.0 collective-permute-done
  16.9 0.1 copy.20
  16.9 0.6 fusion.3
  17.6 0.1 multiply_add_fusion
  17.7 0.9 %convolution_bitcast_fusion = f32[2,128,512]{2,1,0:T(8,128)S(1)} fusion(f32[2,256,256]{2,1,0:T(8,128)S(1)} %get-tuple-element.6, f32[2,256,256]{2,1,0:T(8,128)S(1)} %get-tuple-element.5), kind=kOutput, calls=%fused_computation | convolution fusion | flops 202047488 | bytes 1572864 | tf_op jit(solution)/shard_map/bnf,nk->bkf/dot_general | solution.py:53
  18.6 0.9 %convolution_bitcast_fusion.1 = f32[2,128,512]{2,1,0:T(8,128)S(1)} fusion(f32[2,256,256]{2,1,0:T(8,128)S(1)} %get-tuple-element.6, f32[2,256,256]{2,1,0:T(8,128)S(1)} %get-tuple-element.5), kind=kOutput, calls=%fused_computation.1 | convolution fusion | flops 202047488 | bytes 1572864 | tf_op jit(solution)/shard_map/bnf,nk->bkf/dot_general | solution.py:52
  19.5 0.1 slice_add_fusion
  19.6 0.9 %pad_maximum_fusion.6.spec_ref = f32[2,128,512]{2,1,0:T(8,128)} fusion(f32[2,128,256]{2,1,0:T(8,128)S(1)} %get-tuple-element.12, f32[2,128,256]{2,1,0:T(8,128)S(1)} %get-tuple-element.11), kind=kLoop, calls=%fused_computation.29 | loop fusion | flops 131072 | bytes 1048576 | tf_op jit(solution)/shard_map/concatenate | solution.py:54
  20.5 0.2 fusion.32
  20.7 0.2 fusion.31
  20.9 0.4 fusion.64
  21.3 1.3 %collective-permute-start.7 = (bf16[2,2,1,8,2,2048]{5,4,3,1,0,2:T(2,128)(2,1)S(1)}, bf16[2,2,1,8,2,2048]{5,4,3,1,0,2:T(2,128)(2,1)S(1)}, u32[]{:S(2)}, u32[]{:S(2)}) collective-permute-start(bf16[2,2,1,8,2,2048]{5,4,3,1,0,2:T(2,128)(2,1)S(1)} %fusion.64), channel_id=1, source_target_pairs={{0,2},{1,3},{2,0},{3,1},{4,6},{5,7},{6,4},{7,5},{8,10},{9,11},{10,... | collective-permute-start | bytes 786440 | tf_op jit(solution)/shard_map/ppermute | solution.py:173
  22.6 0.3 collective-permute-done.2
  22.9 0.3 fusion.29
  23.3 0.4 pad_maximum_fusion.9
  23.6 1.3 %collective-permute-start.3 = (bf16[2,2,1,8,2,2048]{5,4,3,1,0,2:T(2,128)(2,1)S(1)}, bf16[2,2,1,8,2,2048]{5,4,3,1,0,2:T(2,128)(2,1)S(1)}, u32[]{:S(2)}, u32[]{:S(2)}) collective-permute-start(bf16[2,2,1,8,2,2048]{5,4,3,1,0,2:T(2,128)(2,1)S(1)} %pad_maximum_fusion.9), channel_id=1, source_target_pairs={{0,2},{1,3},{2,0},{3,1},{4,6},{5,7},{6,4},{7,5},{8,10},{9,11},{10,... | collective-permute-start | bytes 786440 | tf_op jit(solution)/shard_map/ppermute | solution.py:173
  24.9 3.2 %collective-permute-done.7 = bf16[2,2,1,8,2,2048]{5,4,3,1,0,2:T(2,128)(2,1)S(1)} collective-permute-done((bf16[2,2,1,8,2,2048]{5,4,3,1,0,2:T(2,128)(2,1)S(1)}, bf16[2,2,1,8,2,2048]{5,4,3,1,0,2:T(2,128)(2,1)S(1)}, u32[]{:S(2)}, u32[]{:S(2)}) %collective-permute-start.7) | collective-permute-done | bytes 262176 | tf_op jit(solution)/shard_map/ppermute | solution.py:173
  28.2 0.5 fusion.18
  28.6 0.5 fusion.17
  29.1 0.9 %pad_maximum_fusion.8 = bf16[2,2,2,1,8,2,2048]{6,5,4,2,1,3,0:T(2,128)(2,1)S(1)} fusion(bf16[1,2,2,1,8,2,2048]{6,5,4,2,1,3,0:T(2,128)(2,1)S(1)} %fusion.18, bf16[1,2,2,1,8,2,2048]{6,5,4,2,1,3,0:T(2,128)(2,1)S(1)} %fusion.17), kind=kLoop, calls=%fused_computation.32 | loop fusion | flops 262144 | bytes 1048576 | tf_op jit(solution)/shard_map/stack | solution.py:175
  30.0 3.5 %collective-permute-start.8 = (bf16[2,2,2,1,8,2,2048]{6,5,4,2,1,3,0:T(2,128)(2,1)S(1)}, bf16[2,2,2,1,8,2,2048]{6,5,4,2,1,3,0:T(2,128)(2,1)S(1)}, u32[]{:S(2)}, u32[]{:S(2)}) collective-permute-start(bf16[2,2,2,1,8,2,2048]{6,5,4,2,1,3,0:T(2,128)(2,1)S(1)} %pad_maximum_fusion.8), channel_id=1, source_target_pairs={{0,1},{1,0},{2,3},{3,2},{4,5},{5,4},{6,7},{7,6},{8,9},{9,8},{10,11... | collective-permute-start | bytes 1572872 | tf_op jit(solution)/shard_map/ppermute | solution.py:173
  33.5 0.3 collective-permute-done.3
  33.8 0.6 fusion.15
  34.4 0.7 pad_maximum_fusion.7
  35.2 2.0 %collective-permute-start.4 = (bf16[2,2,2,1,8,2,2048]{6,5,4,2,1,3,0:T(2,128)(2,1)S(1)}, bf16[2,2,2,1,8,2,2048]{6,5,4,2,1,3,0:T(2,128)(2,1)S(1)}, u32[]{:S(2)}, u32[]{:S(2)}) collective-permute-start(bf16[2,2,2,1,8,2,2048]{6,5,4,2,1,3,0:T(2,128)(2,1)S(1)} %pad_maximum_fusion.7), channel_id=1, source_target_pairs={{0,1},{1,0},{2,3},{3,2},{4,5},{5,4},{6,7},{7,6},{8,9},{9,8},{10,11... | collective-permute-start | bytes 1572872 | tf_op jit(solution)/shard_map/ppermute | solution.py:173
  37.1 0.0 collective-permute-done.8
  37.1 1.2 %broadcast_select_fusion.1 = (bf16[2,2,2,1,8,2,2048]{6,5,4,2,1,3,0:T(2,128)(2,1)S(1)}, bf16[2,2,2,1,8,2,2048]{6,5,4,2,1,3,0:T(2,128)(2,1)S(1)}) fusion(bf16[2,2,2,1,8,2,2048]{6,5,4,2,1,3,0:T(2,128)(2,1)S(1)} %collective-permute-done.8, pred[]{:T(512)S(6)} %ne.97, bf16[1,2,2,1,8,2,2048]{6,5,4,2,1,3,0:T(2,128)(2,1)S(1)} %fusion.18, ...), kind=kLoop, calls=%fused_computation.7 | loop fusion | flops 786432 | bytes 2097153 | tf_op jit(solution)/shard_map/jit(_where)/select_n | solution.py:175
  38.4 0.3 stack.94
  38.7 0.3 stack.93
  39.1 0.1 pad_maximum_fusion.2
  39.2 1.1 %copy.44 = bf16[2,2,2,2,8,2,8,256]{7,6,0,1,2,3,5,4:T(8,128)(2,1)} copy(bf16[2,2,2,2,8,2,8,256]{7,6,5,4,3,2,1,0:T(8,128)(2,1)S(1)} %pad_maximum_fusion.2) | data formatting | bytes 2097152 | tf_op jit(solution)/shard_map/stack | solution.py:175
  40.3 14.4 %shard_map.38 = f32[8,2,128]{2,1,0:T(2,128)} custom-call(f32[2,128,512]{2,1,0:T(8,128)} %pad_maximum_fusion.6.spec_ref, bf16[8,2,128,256]{3,2,1,0:T(8,128)(2,1)} %bitcast.96, bf16[512,256]{1,0:T(8,128)(2,1)} %get-tuple-element.18.fh_ref, bf16[512,256]{1,0:T(8,128)(2,1)} %get-tuple-element.17.fl_ref, f32[256,256]{1,0:T(8,128)} %copy-done.1, ...), custom_call_target="tpu_custom_call" | custom-call | flops 6442450944 | bytes 1581056 | tf_op jit(solution)/shard_map/pallas_call | solution.py:140
  54.7 0.7 copy.49
  55.4 1.2 %broadcast_select_fusion.3 = (bf16[2,2,2,1,8,2,2048]{6,5,4,2,1,3,0:T(2,128)(2,1)S(1)}, bf16[2,2,2,1,8,2,2048]{6,5,4,2,1,3,0:T(2,128)(2,1)S(1)}) fusion(bf16[2,2,2,1,8,2,2048]{6,5,4,2,1,3,0:T(2,128)(2,1)S(1)} %collective-permute-done.4, pred[]{:T(512)S(6)} %ne.97, bf16[1,2,2,1,8,2,2048]{6,5,4,2,1,3,0:T(2,128)(2,1)S(1)} %get-tuple-element.16, ...), kind=kLoop, calls=%fused_computation.9 | loop fusion | flops 786432 | bytes 2097153 | tf_op jit(solution)/shard_map/jit(_where)/select_n | solution.py:175
  56.6 0.3 stack.82
  56.9 0.3 stack.81
  57.3 0.1 pad_maximum_fusion.1
  57.4 1.1 %copy.43 = bf16[2,2,2,2,8,2,8,256]{7,6,0,1,2,3,5,4:T(8,128)(2,1)} copy(bf16[2,2,2,2,8,2,8,256]{7,6,5,4,3,2,1,0:T(8,128)(2,1)S(1)} %pad_maximum_fusion.1) | data formatting | bytes 2097152 | tf_op jit(solution)/shard_map/stack | solution.py:175
  58.5 14.4 %shard_map.37 = f32[8,2,128]{2,1,0:T(2,128)} custom-call(f32[2,128,512]{2,1,0:T(8,128)} %pad_maximum_fusion.6.spec_ref, bf16[8,2,128,256]{3,2,1,0:T(8,128)(2,1)} %bitcast.95, bf16[512,256]{1,0:T(8,128)(2,1)} %get-tuple-element.18.fh_ref, bf16[512,256]{1,0:T(8,128)(2,1)} %get-tuple-element.17.fl_ref, f32[256,256]{1,0:T(8,128)} %copy-done.1, ...), custom_call_target="tpu_custom_call" | custom-call | flops 6442450944 | bytes 1581056 | tf_op jit(solution)/shard_map/pallas_call | solution.py:140
  72.9 0.7 copy.50
  73.6 0.6 pad_maximum_fusion.13
  (10 shorter events, 0.1 us)
Async XLA Ops:
  1.1 4.7 %copy-start.2 = (bf16[16,2,2048]{2,1,0:T(2,128)(2,1)S(1)}, bf16[16,2,2048]{2,1,0:T(2,128)(2,1)}, u32[]{:S(2)}) copy-start(bf16[16,2,2048]{2,1,0:T(2,128)(2,1)} %param.5) | copy-start | bytes 393220
  1.1 15.7 %collective-permute-start = (f32[32768]{0:T(1024)S(1)}, f32[32768]{0:T(1024)S(1)}, u32[]{:S(2)}, u32[]{:S(2)}) collective-permute-start(f32[32768]{0:T(1024)S(1)} %get-tuple-element.21), channel_id=1, source_target_pairs={{0,1},{1,2},{2,3},{3,4},{4,5},{5,6},{6,7},{7,8},{8,9},{9,10},{10,1... | collective-permute-start | bytes 393224 | tf_op jit(solution)/shard_map/ppermute | solution.py:22
  5.9 8.7 %collective-permute-start.1 = (bf16[1,8,2,2048]{3,2,1,0:T(2,128)(2,1)S(1)}, bf16[1,8,2,2048]{3,2,1,0:T(2,128)(2,1)S(1)}, u32[]{:S(2)}, u32[]{:S(2)}) collective-permute-start(bf16[1,8,2,2048]{3,2,1,0:T(2,128)(2,1)S(1)} %get-tuple-element.29), channel_id=1, source_target_pairs={{0,8},{1,9},{2,10},{3,11},{4,12},{5,13},{6,14},{7,15},{8,0},{9,1},... | collective-permute-start | bytes 196616 | tf_op jit(solution)/shard_map/ppermute | solution.py:173
  8.3 6.3 %collective-permute-start.5 = (bf16[1,8,2,2048]{3,2,1,0:T(2,128)(2,1)S(1)}, bf16[1,8,2,2048]{3,2,1,0:T(2,128)(2,1)S(1)}, u32[]{:S(2)}, u32[]{:S(2)}) collective-permute-start(bf16[1,8,2,2048]{3,2,1,0:T(2,128)(2,1)S(1)} %get-tuple-element.30), channel_id=1, source_target_pairs={{0,8},{1,9},{2,10},{3,11},{4,12},{5,13},{6,14},{7,15},{8,0},{9,1},... | collective-permute-start | bytes 196616 | tf_op jit(solution)/shard_map/ppermute | solution.py:173
  10.5 7.0 %copy-start = (f32[256,256]{1,0:T(8,128)}, f32[256,256]{1,0:T(8,128)S(1)}, u32[]{:S(2)}) copy-start(f32[256,256]{1,0:T(8,128)S(1)} %get-tuple-element.33.ts_ref) | copy-start | bytes 786436
  10.5 7.0 %copy-start.1 = (f32[256,256]{1,0:T(8,128)}, f32[256,256]{1,0:T(8,128)S(1)}, u32[]{:S(2)}) copy-start(f32[256,256]{1,0:T(8,128)S(1)} %get-tuple-element.34.tc_ref) | copy-start | bytes 786436
  15.0 5.4 %collective-permute-start.6 = (bf16[2,1,8,2,2048]{4,3,2,0,1:T(2,128)(2,1)S(1)}, bf16[2,1,8,2,2048]{4,3,2,0,1:T(2,128)(2,1)S(1)}, u32[]{:S(2)}, u32[]{:S(2)}) collective-permute-start(bf16[2,1,8,2,2048]{4,3,2,0,1:T(2,128)(2,1)S(1)} %fusion.63), channel_id=1, source_target_pairs={{0,4},{1,5},{2,6},{3,7},{4,0},{5,1},{6,2},{7,3},{8,12},{9,13},{10,... | collective-permute-start | bytes 393224 | tf_op jit(solution)/shard_map/ppermute | solution.py:173
  16.6 6.4 %collective-permute-start.2 = (bf16[2,1,8,2,2048]{4,3,2,0,1:T(2,128)(2,1)S(1)}, bf16[2,1,8,2,2048]{4,3,2,0,1:T(2,128)(2,1)S(1)}, u32[]{:S(2)}, u32[]{:S(2)}) collective-permute-start(bf16[2,1,8,2,2048]{4,3,2,0,1:T(2,128)(2,1)S(1)} %pad_maximum_fusion.11), channel_id=1, source_target_pairs={{0,4},{1,5},{2,6},{3,7},{4,0},{5,1},{6,2},{7,3},{8,12},{9,13},{10,... | collective-permute-start | bytes 393224 | tf_op jit(solution)/shard_map/ppermute | solution.py:173
  21.3 6.9 %collective-permute-start.7 = (bf16[2,2,1,8,2,2048]{5,4,3,1,0,2:T(2,128)(2,1)S(1)}, bf16[2,2,1,8,2,2048]{5,4,3,1,0,2:T(2,128)(2,1)S(1)}, u32[]{:S(2)}, u32[]{:S(2)}) collective-permute-start(bf16[2,2,1,8,2,2048]{5,4,3,1,0,2:T(2,128)(2,1)S(1)} %fusion.64), channel_id=1, source_target_pairs={{0,2},{1,3},{2,0},{3,1},{4,6},{5,7},{6,4},{7,5},{8,10},{9,11},{10,... | collective-permute-start | bytes 786440 | tf_op jit(solution)/shard_map/ppermute | solution.py:173
  23.6 10.2 %collective-permute-start.3 = (bf16[2,2,1,8,2,2048]{5,4,3,1,0,2:T(2,128)(2,1)S(1)}, bf16[2,2,1,8,2,2048]{5,4,3,1,0,2:T(2,128)(2,1)S(1)}, u32[]{:S(2)}, u32[]{:S(2)}) collective-permute-start(bf16[2,2,1,8,2,2048]{5,4,3,1,0,2:T(2,128)(2,1)S(1)} %pad_maximum_fusion.9), channel_id=1, source_target_pairs={{0,2},{1,3},{2,0},{3,1},{4,6},{5,7},{6,4},{7,5},{8,10},{9,11},{10,... | collective-permute-start | bytes 786440 | tf_op jit(solution)/shard_map/ppermute | solution.py:173
  30.0 7.1 %collective-permute-start.8 = (bf16[2,2,2,1,8,2,2048]{6,5,4,2,1,3,0:T(2,128)(2,1)S(1)}, bf16[2,2,2,1,8,2,2048]{6,5,4,2,1,3,0:T(2,128)(2,1)S(1)}, u32[]{:S(2)}, u32[]{:S(2)}) collective-permute-start(bf16[2,2,2,1,8,2,2048]{6,5,4,2,1,3,0:T(2,128)(2,1)S(1)} %pad_maximum_fusion.8), channel_id=1, source_target_pairs={{0,1},{1,0},{2,3},{3,2},{4,5},{5,4},{6,7},{7,6},{8,9},{9,8},{10,11... | collective-permute-start | bytes 1572872 | tf_op jit(solution)/shard_map/ppermute | solution.py:173
  35.2 20.2 %collective-permute-start.4 = (bf16[2,2,2,1,8,2,2048]{6,5,4,2,1,3,0:T(2,128)(2,1)S(1)}, bf16[2,2,2,1,8,2,2048]{6,5,4,2,1,3,0:T(2,128)(2,1)S(1)}, u32[]{:S(2)}, u32[]{:S(2)}) collective-permute-start(bf16[2,2,2,1,8,2,2048]{6,5,4,2,1,3,0:T(2,128)(2,1)S(1)} %pad_maximum_fusion.7), channel_id=1, source_target_pairs={{0,1},{1,0},{2,3},{3,2},{4,5},{5,4},{6,7},{7,6},{8,9},{9,8},{10,11... | collective-permute-start | bytes 1572872 | tf_op jit(solution)/shard_map/ppermute | solution.py:173

commit v4 on v3

--- a/solution.py
+++ b/solution.py
@@ -9,7 +9,7 @@
 
 RADIX = 256
 BLOCK = 32768
-SUBBANK = 8
+SUBBANK = 4
 
 
 PRECISE = lax.Precision.HIGH

time: 74.5 us -> 82.6 us (1.11)
  Pallas kernels: 28.7 us -> 32.9 us
  starting transfers between devices: 16.8 us -> 20.2 us
  waiting for transfers between devices: 3.85 us -> 1.2 us
  local copies, waits for them, and re-layouts: 5.59 us -> 8.19 us
    pallas_call x2 -> x4, Pallas kernels: 28.7 us -> 32.9 us  [window_peaks(): pl.pallas_call(peaks_kernel, out_shape=jax.ShapeDtypeStruct((template_tot...]
    ppermute x8 -> x16, starting transfers between devices: 12.2 us -> 15.5 us  [gathered_bank(): arrived = lax.ppermute(held, 'seg', pairs)]
    ppermute x8 -> x16, waiting for transfers between devices: 3.84 us -> 1.2 us  [gathered_bank(): arrived = lax.ppermute(held, 'seg', pairs)]
    unnamed x8 -> x10, local copies, waits for them, and re-layouts: 1.41 us -> 2.77 us
    another operation x6 -> x12, local copies, waits for them, and re-layouts: 3.62 us -> 4.86 us  [gathered_bank(): jnp.stack([jnp.where(upper, arrived, held), jnp.where(upper, held, arrive...]
    another operation x15 -> x28, other arithmetic: 5.46 us -> 5.47 us  [gathered_bank(): jnp.stack([jnp.where(upper, arrived, held), jnp.where(upper, held, arrive...]
    select_n x2 -> x4, other arithmetic: 2.46 us -> 2.45 us  [gathered_bank(): jnp.where(upper, arrived, held)]
  transfers between devices with their start and end apart: 9 -> 17, of which waited for: 3 -> 2; matrix products, arithmetic and copies ran while one was open for 26% -> 28% of each run, Pallas kernels for 19% -> 30%
where the time goes in v4:
time: 82.6 us; the launch traced here: 81.9 us
  Pallas kernels  32.9 us (40%)
  starting transfers between devices  20.2 us (24%)
  other arithmetic  16.4 us (20%)
  local copies, waits for them, and re-layouts  8.19 us (10%)
  matrix products  2.41 us (3%)
  waiting for transfers between devices  1.2 us (1%)
    pallas_call x4, Pallas kernels, window_peaks(): pl.pallas_call(peaks_kernel, out_shape=jax.ShapeDtypeStruct((template_tot...  32.9 us
    ppermute x16, starting transfers between devices, gathered_bank(): arrived = lax.ppermute(held, 'seg', pairs)  15.5 us
    another operation x28, other arithmetic, gathered_bank(): jnp.stack([jnp.where(upper, arrived, held), jnp.where(upper, held, arrive...  5.47 us
    another operation x12, local copies, waits for them, and re-layouts, gathered_bank(): jnp.stack([jnp.where(upper, arrived, held), jnp.where(upper, held, arrive...  4.86 us
    ppermute x1, starting transfers between devices, passed_along(): return lax.ppermute(value, axis, pairs)  4.67 us
    unnamed x10, local copies, waits for them, and re-layouts  2.77 us
    sin x3, other arithmetic, angle_table(): return (jnp.cos(angle_value), jnp.sin(angle_value))  2.54 us
    select_n x4, other arithmetic, gathered_bank(): jnp.where(upper, arrived, held)  2.45 us
  transfers between devices with their start and end apart: 17, of which 2 were waited for; matrix products, arithmetic and copies ran while one was open for 28% of the time, Pallas kernels for 30%

profile of v4, /device:TPU:1, one launch (start us, length us, event | category | flops | bytes accessed | tf_op | source)
XLA Modules:
  0.0 81.9 jit_solution(15917095740051068618)
XLA Ops:
  0.0 1.1 %convert_multiply_fusion = f32[65536]{0:T(1024)S(1)} fusion(f32[65536]{0:T(1024)} %param.3, s32[65536]{0:T(1024)} %param.4), kind=kLoop, calls=%fused_computation.63 | loop fusion | flops 131072 | bytes 786432 | tf_op jit(solution)/shard_map/mul | solution.py:185
  1.1 4.7 %collective-permute-start = (f32[32768]{0:T(1024)S(1)}, f32[32768]{0:T(1024)S(1)}, u32[]{:S(2)}, u32[]{:S(2)}) collective-permute-start(f32[32768]{0:T(1024)S(1)} %get-tuple-element.25), channel_id=1, source_target_pairs={{0,1},{1,2},{2,3},{3,4},{4,5},{5,6},{6,7},{7,8},{8,9},{9,10},{10,1... | collective-permute-start | bytes 393224 | tf_op jit(solution)/shard_map/ppermute | solution.py:22
  5.9 2.4 %collective-permute-start.1 = (bf16[1,4,2,2048]{3,2,1,0:T(2,128)(2,1)S(1)}, bf16[1,4,2,2048]{3,2,1,0:T(2,128)(2,1)S(1)}, u32[]{:S(2)}, u32[]{:S(2)}) collective-permute-start(bf16[1,4,2,2048]{3,2,1,0:T(2,128)(2,1)S(1)} %get-tuple-element.43), channel_id=1, source_target_pairs={{0,8},{1,9},{2,10},{3,11},{4,12},{5,13},{6,14},{7,15},{8,0},{9,1},... | collective-permute-start | bytes 98312 | tf_op jit(solution)/shard_map/ppermute | solution.py:173
  8.3 2.3 %collective-permute-start.9 = (bf16[1,4,2,2048]{3,2,1,0:T(2,128)(2,1)S(1)}, bf16[1,4,2,2048]{3,2,1,0:T(2,128)(2,1)S(1)}, u32[]{:S(2)}, u32[]{:S(2)}) collective-permute-start(bf16[1,4,2,2048]{3,2,1,0:T(2,128)(2,1)S(1)} %get-tuple-element.46), channel_id=1, source_target_pairs={{0,8},{1,9},{2,10},{3,11},{4,12},{5,13},{6,14},{7,15},{8,0},{9,1},... | collective-permute-start | bytes 98312 | tf_op jit(solution)/shard_map/ppermute | solution.py:173
  10.7 1.0 %fusion.38 = (f32[256,256]{1,0:T(8,128)S(1)}, f32[256,256]{1,0:T(8,128)S(1)}) fusion(), kind=kLoop, calls=%fused_computation.95 | loop fusion | flops 983040 | bytes 524288 | tf_op jit(solution)/shard_map/cos | solution.py:30
  11.8 1.0 %fusion.35 = (f32[256,256]{1,0:T(8,128)S(1)}, f32[256,256]{1,0:T(8,128)S(1)}) fusion(), kind=kLoop, calls=%fused_computation.92 | loop fusion | flops 917504 | bytes 524288 | tf_op jit(solution)/shard_map/sin | solution.py:30
  12.8 0.5 fusion.51
  13.3 0.5 fusion.53
  13.9 1.0 %fusion.37 = f32[256,256]{1,0:T(8,128)S(1)} fusion(), kind=kLoop, calls=%fused_computation.94 | loop fusion | flops 917504 | bytes 262144 | tf_op jit(solution)/shard_map/sin | solution.py:30
  14.8 0.9 %fusion = (bf16[512,256]{1,0:T(8,128)(2,1)}, bf16[512,256]{1,0:T(8,128)(2,1)}) fusion(f32[256,128]{1,0:T(8,128)S(1)} %get-tuple-element.56, f32[256,128]{1,0:T(8,128)S(1)} %get-tuple-element.55, f32[256,128]{1,0:T(8,128)S(1)} %fusion.53), kind=kLoop, calls=%fused_computation.9 | loop fusion | flops 917504 | bytes 917504 | tf_op jit(solution)/shard_map/convert_element_type | solution.py:71
  15.7 0.9 %fusion.1 = (bf16[512,256]{1,0:T(8,128)(2,1)}, bf16[512,256]{1,0:T(8,128)(2,1)}) fusion(f32[256,256]{1,0:T(8,128)S(1)} %get-tuple-element.49, f32[256,256]{1,0:T(8,128)S(1)} %fusion.37, f32[256,256]{1,0:T(8,128)S(1)} %get-tuple-element.50), kind=kLoop, calls=%fused_computation.10 | loop fusion | flops 1310720 | bytes 1310720 | tf_op jit(solution)/shard_map/convert_element_type | solution.py:71
  17.0 0.2 fusion.56
  17.3 1.4 %collective-permute-start.2 = (bf16[2,1,4,2,2048]{4,3,2,0,1:T(2,128)(2,1)S(1)}, bf16[2,1,4,2,2048]{4,3,2,0,1:T(2,128)(2,1)S(1)}, u32[]{:S(2)}, u32[]{:S(2)}) collective-permute-start(bf16[2,1,4,2,2048]{4,3,2,0,1:T(2,128)(2,1)S(1)} %pad_maximum_fusion.17), channel_id=1, source_target_pairs={{0,4},{1,5},{2,6},{3,7},{4,0},{5,1},{6,2},{7,3},{8,12},{9,13},{10,... | collective-permute-start | bytes 196616 | tf_op jit(solution)/shard_map/ppermute | solution.py:173
  18.8 0.2 collective-permute-start.14
  19.1 1.4 %collective-permute-start.10 = (bf16[2,1,4,2,2048]{4,3,2,0,1:T(2,128)(2,1)S(1)}, bf16[2,1,4,2,2048]{4,3,2,0,1:T(2,128)(2,1)S(1)}, u32[]{:S(2)}, u32[]{:S(2)}) collective-permute-start(bf16[2,1,4,2,2048]{4,3,2,0,1:T(2,128)(2,1)S(1)} %fusion.75), channel_id=1, source_target_pairs={{0,4},{1,5},{2,6},{3,7},{4,0},{5,1},{6,2},{7,3},{8,12},{9,13},{10,... | collective-permute-start | bytes 196616 | tf_op jit(solution)/shard_map/ppermute | solution.py:173
  20.5 0.2 collective-permute-start.6
  20.8 0.5 collective-permute-done.2
  21.3 0.7 collective-permute-done.14
  21.9 0.3 fusion.43
  22.3 0.2 pad_maximum_fusion.16
  22.5 1.3 %collective-permute-start.15 = (bf16[2,2,1,4,2,2048]{5,4,3,1,0,2:T(2,128)(2,1)S(1)}, bf16[2,2,1,4,2,2048]{5,4,3,1,0,2:T(2,128)(2,1)S(1)}, u32[]{:S(2)}, u32[]{:S(2)}) collective-permute-start(bf16[2,2,1,4,2,2048]{5,4,3,1,0,2:T(2,128)(2,1)S(1)} %pad_maximum_fusion.16), channel_id=1, source_target_pairs={{0,2},{1,3},{2,0},{3,1},{4,6},{5,7},{6,4},{7,5},{8,10},{9,11},{10,... | collective-permute-start | bytes 393224 | tf_op jit(solution)/shard_map/ppermute | solution.py:173
  24.0 0.2 fusion.77
  24.2 1.2 %collective-permute-start.11 = (bf16[2,2,1,4,2,2048]{5,4,3,1,0,2:T(2,128)(2,1)S(1)}, bf16[2,2,1,4,2,2048]{5,4,3,1,0,2:T(2,128)(2,1)S(1)}, u32[]{:S(2)}, u32[]{:S(2)}) collective-permute-start(bf16[2,2,1,4,2,2048]{5,4,3,1,0,2:T(2,128)(2,1)S(1)} %fusion.77), channel_id=1, source_target_pairs={{0,2},{1,3},{2,0},{3,1},{4,6},{5,7},{6,4},{7,5},{8,10},{9,11},{10,... | collective-permute-start | bytes 393224 | tf_op jit(solution)/shard_map/ppermute | solution.py:173
  25.6 0.2 fusion.78
  25.8 1.0 %collective-permute-start.7 = (bf16[2,2,1,4,2,2048]{5,4,3,1,0,2:T(2,128)(2,1)S(1)}, bf16[2,2,1,4,2,2048]{5,4,3,1,0,2:T(2,128)(2,1)S(1)}, u32[]{:S(2)}, u32[]{:S(2)}) collective-permute-start(bf16[2,2,1,4,2,2048]{5,4,3,1,0,2:T(2,128)(2,1)S(1)} %fusion.78), channel_id=1, source_target_pairs={{0,2},{1,3},{2,0},{3,1},{4,6},{5,7},{6,4},{7,5},{8,10},{9,11},{10,... | collective-permute-start | bytes 393224 | tf_op jit(solution)/shard_map/ppermute | solution.py:173
  26.7 0.2 pad_maximum_fusion.13
  26.9 0.6 collective-permute-start.3
  27.7 0.6 fusion.3
  28.4 0.9 %convolution_bitcast_fusion = f32[2,128,512]{2,1,0:T(8,128)S(1)} fusion(f32[2,256,256]{2,1,0:T(8,128)S(1)} %get-tuple-element.6, f32[2,256,256]{2,1,0:T(8,128)S(1)} %get-tuple-element.5), kind=kOutput, calls=%fused_computation | convolution fusion | flops 202047488 | bytes 1572864 | tf_op jit(solution)/shard_map/bnf,nk->bkf/dot_general | solution.py:53
  29.4 0.9 %convolution_bitcast_fusion.1 = f32[2,128,512]{2,1,0:T(8,128)S(1)} fusion(f32[2,256,256]{2,1,0:T(8,128)S(1)} %get-tuple-element.6, f32[2,256,256]{2,1,0:T(8,128)S(1)} %get-tuple-element.5), kind=kOutput, calls=%fused_computation.1 | convolution fusion | flops 202047488 | bytes 1572864 | tf_op jit(solution)/shard_map/bnf,nk->bkf/dot_general | solution.py:52
  30.3 0.9 %pad_maximum_fusion.4.spec_ref = f32[2,128,512]{2,1,0:T(8,128)} fusion(f32[2,128,256]{2,1,0:T(8,128)S(1)} %get-tuple-element.8, f32[2,128,256]{2,1,0:T(8,128)S(1)} %get-tuple-element.7), kind=kLoop, calls=%fused_computation.24 | loop fusion | flops 131072 | bytes 1048576 | tf_op jit(solution)/shard_map/concatenate | solution.py:54
  31.2 0.3 fusion.30
  31.5 0.4 pad_maximum_fusion.12
  31.9 2.7 %collective-permute-start.16 = (bf16[2,2,2,1,4,2,2048]{6,5,4,2,1,3,0:T(2,128)(2,1)S(1)}, bf16[2,2,2,1,4,2,2048]{6,5,4,2,1,3,0:T(2,128)(2,1)S(1)}, u32[]{:S(2)}, u32[]{:S(2)}) collective-permute-start(bf16[2,2,2,1,4,2,2048]{6,5,4,2,1,3,0:T(2,128)(2,1)S(1)} %pad_maximum_fusion.12), channel_id=1, source_target_pairs={{0,1},{1,0},{2,3},{3,2},{4,5},{5,4},{6,7},{7,6},{8,9},{9,8},{10,11... | collective-permute-start | bytes 786440 | tf_op jit(solution)/shard_map/ppermute | solution.py:173
  34.6 0.2 fusion.32
  34.8 0.4 fusion.28
  35.2 0.4 pad_maximum_fusion.11
  35.7 0.2 fusion.31
  35.9 0.2 fusion.27
  36.2 0.4 pad_maximum_fusion.10
  36.6 0.5 collective-permute-start.8
  37.1 0.3 fusion.25
  37.4 0.4 pad_maximum_fusion.9
  37.9 0.6 broadcast_select_fusion.1
  38.5 0.2 stack.190
  38.7 0.2 stack.189
  39.0 0.9 %copy.74 = bf16[2,2,2,2,4,2,8,256]{7,6,0,1,2,3,5,4:T(8,128)(2,1)} copy(bf16[2,2,2,2,4,2,8,256]{7,6,5,4,3,2,1,0:T(8,128)(2,1)S(1)} %pad_maximum_fusion.8) | data formatting | bytes 1048576 | tf_op jit(solution)/shard_map/stack | solution.py:175
  39.8 8.2 %shard_map.40 = f32[4,2,128]{2,1,0:T(2,128)} custom-call(f32[2,128,512]{2,1,0:T(8,128)} %pad_maximum_fusion.4.spec_ref, bf16[4,2,128,256]{3,2,1,0:T(8,128)(2,1)} %bitcast.178, bf16[512,256]{1,0:T(8,128)(2,1)} %get-tuple-element.20.fh_ref, bf16[512,256]{1,0:T(8,128)(2,1)} %get-tuple-element.19.fl_ref, f32[256,256]{1,0:T(8,128)} %copy-done.1, ...), custom_call_target="tpu_custom_call" | custom-call | flops 3221225472 | bytes 1052672 | tf_op jit(solution)/shard_map/pallas_call | solution.py:140
  48.1 0.7 copy.83
  48.8 0.6 broadcast_select_fusion.3
  49.4 0.2 stack.178
  49.5 0.2 stack.177
  49.8 0.9 %copy.73 = bf16[2,2,2,2,4,2,8,256]{7,6,0,1,2,3,5,4:T(8,128)(2,1)} copy(bf16[2,2,2,2,4,2,8,256]{7,6,5,4,3,2,1,0:T(8,128)(2,1)S(1)} %pad_maximum_fusion.7) | data formatting | bytes 1048576 | tf_op jit(solution)/shard_map/stack | solution.py:175
  50.7 8.2 %shard_map.39 = f32[4,2,128]{2,1,0:T(2,128)} custom-call(f32[2,128,512]{2,1,0:T(8,128)} %pad_maximum_fusion.4.spec_ref, bf16[4,2,128,256]{3,2,1,0:T(8,128)(2,1)} %bitcast.179, bf16[512,256]{1,0:T(8,128)(2,1)} %get-tuple-element.20.fh_ref, bf16[512,256]{1,0:T(8,128)(2,1)} %get-tuple-element.19.fl_ref, f32[256,256]{1,0:T(8,128)} %copy-done.1, ...), custom_call_target="tpu_custom_call" | custom-call | flops 3221225472 | bytes 1052672 | tf_op jit(solution)/shard_map/pallas_call | solution.py:140
  58.9 0.7 copy.84
  59.6 0.6 broadcast_select_fusion.5
  60.6 0.9 %copy.72 = bf16[2,2,2,2,4,2,8,256]{7,6,0,1,2,3,5,4:T(8,128)(2,1)} copy(bf16[2,2,2,2,4,2,8,256]{7,6,5,4,3,2,1,0:T(8,128)(2,1)S(1)} %pad_maximum_fusion.6) | data formatting | bytes 1048576 | tf_op jit(solution)/shard_map/stack | solution.py:175
  61.5 8.2 %shard_map.38 = f32[4,2,128]{2,1,0:T(2,128)} custom-call(f32[2,128,512]{2,1,0:T(8,128)} %pad_maximum_fusion.4.spec_ref, bf16[4,2,128,256]{3,2,1,0:T(8,128)(2,1)} %bitcast.180, bf16[512,256]{1,0:T(8,128)(2,1)} %get-tuple-element.20.fh_ref, bf16[512,256]{1,0:T(8,128)(2,1)} %get-tuple-element.19.fl_ref, f32[256,256]{1,0:T(8,128)} %copy-done.1, ...), custom_call_target="tpu_custom_call" | custom-call | flops 3221225472 | bytes 1052672 | tf_op jit(solution)/shard_map/pallas_call | solution.py:140
  69.7 0.7 copy.85
  70.4 0.6 broadcast_select_fusion.7
  71.4 0.9 %copy.71 = bf16[2,2,2,2,4,2,8,256]{7,6,0,1,2,3,5,4:T(8,128)(2,1)} copy(bf16[2,2,2,2,4,2,8,256]{7,6,5,4,3,2,1,0:T(8,128)(2,1)S(1)} %pad_maximum_fusion.5) | data formatting | bytes 1048576 | tf_op jit(solution)/shard_map/stack | solution.py:175
  72.3 8.2 %shard_map.37 = f32[4,2,128]{2,1,0:T(2,128)} custom-call(f32[2,128,512]{2,1,0:T(8,128)} %pad_maximum_fusion.4.spec_ref, bf16[4,2,128,256]{3,2,1,0:T(8,128)(2,1)} %bitcast.177, bf16[512,256]{1,0:T(8,128)(2,1)} %get-tuple-element.20.fh_ref, bf16[512,256]{1,0:T(8,128)(2,1)} %get-tuple-element.19.fl_ref, f32[256,256]{1,0:T(8,128)} %copy-done.1, ...), custom_call_target="tpu_custom_call" | custom-call | flops 3221225472 | bytes 1052672 | tf_op jit(solution)/shard_map/pallas_call | solution.py:140
  80.5 0.7 copy.86
  81.2 0.6 pad_maximum_fusion.21
  (51 shorter events, 2.9 us)
Async XLA Ops:
  1.1 4.7 %copy-start.2 = (bf16[16,2,2048]{2,1,0:T(2,128)(2,1)S(1)}, bf16[16,2,2048]{2,1,0:T(2,128)(2,1)}, u32[]{:S(2)}) copy-start(bf16[16,2,2048]{2,1,0:T(2,128)(2,1)} %param.5) | copy-start | bytes 393220
  1.1 26.5 %collective-permute-start = (f32[32768]{0:T(1024)S(1)}, f32[32768]{0:T(1024)S(1)}, u32[]{:S(2)}, u32[]{:S(2)}) collective-permute-start(f32[32768]{0:T(1024)S(1)} %get-tuple-element.25), channel_id=1, source_target_pairs={{0,1},{1,2},{2,3},{3,4},{4,5},{5,6},{6,7},{7,8},{8,9},{9,10},{10,1... | collective-permute-start | bytes 393224 | tf_op jit(solution)/shard_map/ppermute | solution.py:22
  5.9 11.0 %collective-permute-start.1 = (bf16[1,4,2,2048]{3,2,1,0:T(2,128)(2,1)S(1)}, bf16[1,4,2,2048]{3,2,1,0:T(2,128)(2,1)S(1)}, u32[]{:S(2)}, u32[]{:S(2)}) collective-permute-start(bf16[1,4,2,2048]{3,2,1,0:T(2,128)(2,1)S(1)} %get-tuple-element.43), channel_id=1, source_target_pairs={{0,8},{1,9},{2,10},{3,11},{4,12},{5,13},{6,14},{7,15},{8,0},{9,1},... | collective-permute-start | bytes 98312 | tf_op jit(solution)/shard_map/ppermute | solution.py:173
  8.3 8.7 %collective-permute-start.5 = (bf16[1,4,2,2048]{3,2,1,0:T(2,128)(2,1)S(1)}, bf16[1,4,2,2048]{3,2,1,0:T(2,128)(2,1)S(1)}, u32[]{:S(2)}, u32[]{:S(2)}) collective-permute-start(bf16[1,4,2,2048]{3,2,1,0:T(2,128)(2,1)S(1)} %get-tuple-element.44), channel_id=1, source_target_pairs={{0,8},{1,9},{2,10},{3,11},{4,12},{5,13},{6,14},{7,15},{8,0},{9,1},... | collective-permute-start | bytes 98312 | tf_op jit(solution)/shard_map/ppermute | solution.py:173
  8.3 8.6 %collective-permute-start.9 = (bf16[1,4,2,2048]{3,2,1,0:T(2,128)(2,1)S(1)}, bf16[1,4,2,2048]{3,2,1,0:T(2,128)(2,1)S(1)}, u32[]{:S(2)}, u32[]{:S(2)}) collective-permute-start(bf16[1,4,2,2048]{3,2,1,0:T(2,128)(2,1)S(1)} %get-tuple-element.46), channel_id=1, source_target_pairs={{0,8},{1,9},{2,10},{3,11},{4,12},{5,13},{6,14},{7,15},{8,0},{9,1},... | collective-permute-start | bytes 98312 | tf_op jit(solution)/shard_map/ppermute | solution.py:173
  10.6 6.3 %collective-permute-start.13 = (bf16[1,4,2,2048]{3,2,1,0:T(2,128)(2,1)S(1)}, bf16[1,4,2,2048]{3,2,1,0:T(2,128)(2,1)S(1)}, u32[]{:S(2)}, u32[]{:S(2)}) collective-permute-start(bf16[1,4,2,2048]{3,2,1,0:T(2,128)(2,1)S(1)} %get-tuple-element.45), channel_id=1, source_target_pairs={{0,8},{1,9},{2,10},{3,11},{4,12},{5,13},{6,14},{7,15},{8,0},{9,1},... | collective-permute-start | bytes 98312 | tf_op jit(solution)/shard_map/ppermute | solution.py:173
  12.8 15.5 %copy-start = (f32[256,256]{1,0:T(8,128)}, f32[256,256]{1,0:T(8,128)S(1)}, u32[]{:S(2)}) copy-start(f32[256,256]{1,0:T(8,128)S(1)} %get-tuple-element.51.ts_ref) | copy-start | bytes 786436
  12.8 15.5 %copy-start.1 = (f32[256,256]{1,0:T(8,128)}, f32[256,256]{1,0:T(8,128)S(1)}, u32[]{:S(2)}) copy-start(f32[256,256]{1,0:T(8,128)S(1)} %get-tuple-element.52.tc_ref) | copy-start | bytes 786436
  17.3 4.0 %collective-permute-start.2 = (bf16[2,1,4,2,2048]{4,3,2,0,1:T(2,128)(2,1)S(1)}, bf16[2,1,4,2,2048]{4,3,2,0,1:T(2,128)(2,1)S(1)}, u32[]{:S(2)}, u32[]{:S(2)}) collective-permute-start(bf16[2,1,4,2,2048]{4,3,2,0,1:T(2,128)(2,1)S(1)} %pad_maximum_fusion.17), channel_id=1, source_target_pairs={{0,4},{1,5},{2,6},{3,7},{4,0},{5,1},{6,2},{7,3},{8,12},{9,13},{10,... | collective-permute-start | bytes 196616 | tf_op jit(solution)/shard_map/ppermute | solution.py:173
  18.8 3.2 %collective-permute-start.14 = (bf16[2,1,4,2,2048]{4,3,2,0,1:T(2,128)(2,1)S(1)}, bf16[2,1,4,2,2048]{4,3,2,0,1:T(2,128)(2,1)S(1)}, u32[]{:S(2)}, u32[]{:S(2)}) collective-permute-start(bf16[2,1,4,2,2048]{4,3,2,0,1:T(2,128)(2,1)S(1)} %pad_maximum_fusion.20), channel_id=1, source_target_pairs={{0,4},{1,5},{2,6},{3,7},{4,0},{5,1},{6,2},{7,3},{8,12},{9,13},{10,... | collective-permute-start | bytes 196616 | tf_op jit(solution)/shard_map/ppermute | solution.py:173
  19.1 4.7 %collective-permute-start.10 = (bf16[2,1,4,2,2048]{4,3,2,0,1:T(2,128)(2,1)S(1)}, bf16[2,1,4,2,2048]{4,3,2,0,1:T(2,128)(2,1)S(1)}, u32[]{:S(2)}, u32[]{:S(2)}) collective-permute-start(bf16[2,1,4,2,2048]{4,3,2,0,1:T(2,128)(2,1)S(1)} %fusion.75), channel_id=1, source_target_pairs={{0,4},{1,5},{2,6},{3,7},{4,0},{5,1},{6,2},{7,3},{8,12},{9,13},{10,... | collective-permute-start | bytes 196616 | tf_op jit(solution)/shard_map/ppermute | solution.py:173
  20.5 4.8 %collective-permute-start.6 = (bf16[2,1,4,2,2048]{4,3,2,0,1:T(2,128)(2,1)S(1)}, bf16[2,1,4,2,2048]{4,3,2,0,1:T(2,128)(2,1)S(1)}, u32[]{:S(2)}, u32[]{:S(2)}) collective-permute-start(bf16[2,1,4,2,2048]{4,3,2,0,1:T(2,128)(2,1)S(1)} %fusion.76), channel_id=1, source_target_pairs={{0,4},{1,5},{2,6},{3,7},{4,0},{5,1},{6,2},{7,3},{8,12},{9,13},{10,... | collective-permute-start | bytes 196616 | tf_op jit(solution)/shard_map/ppermute | solution.py:173
  22.5 8.7 %collective-permute-start.15 = (bf16[2,2,1,4,2,2048]{5,4,3,1,0,2:T(2,128)(2,1)S(1)}, bf16[2,2,1,4,2,2048]{5,4,3,1,0,2:T(2,128)(2,1)S(1)}, u32[]{:S(2)}, u32[]{:S(2)}) collective-permute-start(bf16[2,2,1,4,2,2048]{5,4,3,1,0,2:T(2,128)(2,1)S(1)} %pad_maximum_fusion.16), channel_id=1, source_target_pairs={{0,2},{1,3},{2,0},{3,1},{4,6},{5,7},{6,4},{7,5},{8,10},{9,11},{10,... | collective-permute-start | bytes 393224 | tf_op jit(solution)/shard_map/ppermute | solution.py:173
  24.2 10.4 %collective-permute-start.11 = (bf16[2,2,1,4,2,2048]{5,4,3,1,0,2:T(2,128)(2,1)S(1)}, bf16[2,2,1,4,2,2048]{5,4,3,1,0,2:T(2,128)(2,1)S(1)}, u32[]{:S(2)}, u32[]{:S(2)}) collective-permute-start(bf16[2,2,1,4,2,2048]{5,4,3,1,0,2:T(2,128)(2,1)S(1)} %fusion.77), channel_id=1, source_target_pairs={{0,2},{1,3},{2,0},{3,1},{4,6},{5,7},{6,4},{7,5},{8,10},{9,11},{10,... | collective-permute-start | bytes 393224 | tf_op jit(solution)/shard_map/ppermute | solution.py:173
  25.8 9.9 %collective-permute-start.7 = (bf16[2,2,1,4,2,2048]{5,4,3,1,0,2:T(2,128)(2,1)S(1)}, bf16[2,2,1,4,2,2048]{5,4,3,1,0,2:T(2,128)(2,1)S(1)}, u32[]{:S(2)}, u32[]{:S(2)}) collective-permute-start(bf16[2,2,1,4,2,2048]{5,4,3,1,0,2:T(2,128)(2,1)S(1)} %fusion.78), channel_id=1, source_target_pairs={{0,2},{1,3},{2,0},{3,1},{4,6},{5,7},{6,4},{7,5},{8,10},{9,11},{10,... | collective-permute-start | bytes 393224 | tf_op jit(solution)/shard_map/ppermute | solution.py:173
  26.9 10.2 %collective-permute-start.3 = (bf16[2,2,1,4,2,2048]{5,4,3,1,0,2:T(2,128)(2,1)S(1)}, bf16[2,2,1,4,2,2048]{5,4,3,1,0,2:T(2,128)(2,1)S(1)}, u32[]{:S(2)}, u32[]{:S(2)}) collective-permute-start(bf16[2,2,1,4,2,2048]{5,4,3,1,0,2:T(2,128)(2,1)S(1)} %pad_maximum_fusion.13), channel_id=1, source_target_pairs={{0,2},{1,3},{2,0},{3,1},{4,6},{5,7},{6,4},{7,5},{8,10},{9,11},{10,... | collective-permute-start | bytes 393224 | tf_op jit(solution)/shard_map/ppermute | solution.py:173
  31.9 6.0 %collective-permute-start.16 = (bf16[2,2,2,1,4,2,2048]{6,5,4,2,1,3,0:T(2,128)(2,1)S(1)}, bf16[2,2,2,1,4,2,2048]{6,5,4,2,1,3,0:T(2,128)(2,1)S(1)}, u32[]{:S(2)}, u32[]{:S(2)}) collective-permute-start(bf16[2,2,2,1,4,2,2048]{6,5,4,2,1,3,0:T(2,128)(2,1)S(1)} %pad_maximum_fusion.12), channel_id=1, source_target_pairs={{0,1},{1,0},{2,3},{3,2},{4,5},{5,4},{6,7},{7,6},{8,9},{9,8},{10,11... | collective-permute-start | bytes 786440 | tf_op jit(solution)/shard_map/ppermute | solution.py:173
  35.6 13.1 %collective-permute-start.12 = (bf16[2,2,2,1,4,2,2048]{6,5,4,2,1,3,0:T(2,128)(2,1)S(1)}, bf16[2,2,2,1,4,2,2048]{6,5,4,2,1,3,0:T(2,128)(2,1)S(1)}, u32[]{:S(2)}, u32[]{:S(2)}) collective-permute-start(bf16[2,2,2,1,4,2,2048]{6,5,4,2,1,3,0:T(2,128)(2,1)S(1)} %pad_maximum_fusion.11), channel_id=1, source_target_pairs={{0,1},{1,0},{2,3},{3,2},{4,5},{5,4},{6,7},{7,6},{8,9},{9,8},{10,11... | collective-permute-start | bytes 786440 | tf_op jit(solution)/shard_map/ppermute | solution.py:173
  36.6 23.0 %collective-permute-start.8 = (bf16[2,2,2,1,4,2,2048]{6,5,4,2,1,3,0:T(2,128)(2,1)S(1)}, bf16[2,2,2,1,4,2,2048]{6,5,4,2,1,3,0:T(2,128)(2,1)S(1)}, u32[]{:S(2)}, u32[]{:S(2)}) collective-permute-start(bf16[2,2,2,1,4,2,2048]{6,5,4,2,1,3,0:T(2,128)(2,1)S(1)} %pad_maximum_fusion.10), channel_id=1, source_target_pairs={{0,1},{1,0},{2,3},{3,2},{4,5},{5,4},{6,7},{7,6},{8,9},{9,8},{10,11... | collective-permute-start | bytes 786440 | tf_op jit(solution)/shard_map/ppermute | solution.py:173
  37.8 32.6 %collective-permute-start.4 = (bf16[2,2,2,1,4,2,2048]{6,5,4,2,1,3,0:T(2,128)(2,1)S(1)}, bf16[2,2,2,1,4,2,2048]{6,5,4,2,1,3,0:T(2,128)(2,1)S(1)}, u32[]{:S(2)}, u32[]{:S(2)}) collective-permute-start(bf16[2,2,2,1,4,2,2048]{6,5,4,2,1,3,0:T(2,128)(2,1)S(1)} %pad_maximum_fusion.9), channel_id=1, source_target_pairs={{0,1},{1,0},{2,3},{3,2},{4,5},{5,4},{6,7},{7,6},{8,9},{9,8},{10,11... | collective-permute-start | bytes 786440 | tf_op jit(solution)/shard_map/ppermute | solution.py:173

commit v5 on v3

--- a/solution.py
+++ b/solution.py
@@ -10,6 +10,7 @@
 RADIX = 256
 BLOCK = 32768
 SUBBANK = 8
+STEP_TEMPLATES = 2
 
 
 PRECISE = lax.Precision.HIGH
@@ -99,51 +100,67 @@
 
 def peaks_kernel(spec_ref, bank_ref, fh_ref, fl_ref, tc_ref, ts_ref, sh_ref, sl_ref, out_ref):
     half_radix = RADIX // 2
-    wave_real = bank_ref[0, 0].astype(jnp.float32)
-    wave_imag = bank_ref[0, 1].astype(jnp.float32)
-    power_sum = jnp.sum(wave_real * wave_real + wave_imag * wave_imag, keepdims=True)
-    norm_scale = 1.0 / jnp.sqrt(BLOCK * power_sum + EPSILON)
-    for block in range(spec_ref.shape[0]):
-        spec_real = spec_ref[block, :, :RADIX]
-        spec_imag = spec_ref[block, :, RADIX:]
-        prod_real = spec_real * wave_real + spec_imag * wave_imag
-        prod_imag = spec_imag * wave_real - spec_real * wave_imag
-        stacked = jnp.concatenate([prod_real, prod_imag], axis=0)
-        stacked_high, stacked_low = split_pair(stacked)
-        first = triple_dot(fh_ref[...], fl_ref[...], stacked_high, stacked_low)
-        real_part = first[:RADIX]
-        imag_part = first[RADIX:]
-        cos_twist = tc_ref[...]
-        sin_twist = ts_ref[...]
-        turned = jnp.concatenate(
-            [
-                real_part * cos_twist - imag_part * sin_twist,
-                real_part * sin_twist + imag_part * cos_twist,
-            ],
-            axis=1,
+    block_total = spec_ref.shape[0]
+    step_templates = bank_ref.shape[0]
+    pair_total = step_templates * block_total
+    products = []
+    scales = []
+    for template in range(step_templates):
+        wave_real = bank_ref[template, 0].astype(jnp.float32)
+        wave_imag = bank_ref[template, 1].astype(jnp.float32)
+        power_sum = jnp.sum(wave_real * wave_real + wave_imag * wave_imag, keepdims=True)
+        norm_scale = 1.0 / jnp.sqrt(BLOCK * power_sum + EPSILON)
+        scales.append(norm_scale * norm_scale)
+        for block in range(block_total):
+            spec_real = spec_ref[block, :, :RADIX]
+            spec_imag = spec_ref[block, :, RADIX:]
+            prod_real = spec_real * wave_real + spec_imag * wave_imag
+            prod_imag = spec_imag * wave_real - spec_real * wave_imag
+            products.append(jnp.concatenate([prod_real, prod_imag], axis=0))
+    stacked = jnp.concatenate(products, axis=1)
+    stacked_high, stacked_low = split_pair(stacked)
+    first = triple_dot(fh_ref[...], fl_ref[...], stacked_high, stacked_low)
+    cos_twist = tc_ref[...]
+    sin_twist = ts_ref[...]
+    turned_rows = []
+    for pair in range(pair_total):
+        real_part = first[:RADIX, pair * RADIX : (pair + 1) * RADIX]
+        imag_part = first[RADIX:, pair * RADIX : (pair + 1) * RADIX]
+        turned_rows.append(
+            jnp.concatenate(
+                [
+                    real_part * cos_twist - imag_part * sin_twist,
+                    real_part * sin_twist + imag_part * cos_twist,
+                ],
+                axis=1,
+            )
         )
-        turned_high, turned_low = split_pair(turned)
-        series = triple_dot(turned_high, turned_low, sh_ref[...], sl_ref[...])
-        power_series = (
-            series[:, :half_radix] * series[:, :half_radix]
-            + series[:, half_radix:] * series[:, half_radix:]
-        )
-        peak = jnp.max(power_series, axis=0, keepdims=True)
-        out_ref[0, block : block + 1, :] = peak * (norm_scale * norm_scale)
+    turned = jnp.concatenate(turned_rows, axis=0)
+    turned_high, turned_low = split_pair(turned)
+    series = triple_dot(turned_high, turned_low, sh_ref[...], sl_ref[...])
+    power_series = (
+        series[:, :half_radix] * series[:, :half_radix]
+        + series[:, half_radix:] * series[:, half_radix:]
+    )
+    peaks = jnp.max(power_series.reshape(pair_total, RADIX, half_radix), axis=1)
+    for template in range(step_templates):
+        rows = peaks[template * block_total : (template + 1) * block_total]
+        out_ref[template] = rows * scales[template]
 
 
 def window_peaks(spectra, bank, tables):
     block_total, k_rows, _ = spectra.shape
     template_total = bank.shape[0]
+    step_templates = STEP_TEMPLATES if template_total % STEP_TEMPLATES == 0 else 1
     fixed = lambda k: (0, 0)
     pair_flops = 6 * (2 * RADIX) * (2 * k_rows) * RADIX + 6 * RADIX * (2 * RADIX) * RADIX
     return pl.pallas_call(
         peaks_kernel,
         out_shape=jax.ShapeDtypeStruct((template_total, block_total, RADIX // 2), jnp.float32),
-        grid=(template_total,),
+        grid=(template_total // step_templates,),
         in_specs=[
             pl.BlockSpec((block_total, k_rows, 2 * RADIX), lambda k: (0, 0, 0)),
-            pl.BlockSpec((1, 2, k_rows, RADIX), lambda k: (k, 0, 0, 0)),
+            pl.BlockSpec((step_templates, 2, k_rows, RADIX), lambda k: (k, 0, 0, 0)),
             pl.BlockSpec((2 * RADIX, 2 * k_rows), fixed),
             pl.BlockSpec((2 * RADIX, 2 * k_rows), fixed),
             pl.BlockSpec((RADIX, RADIX), fixed),
@@ -151,7 +168,7 @@
             pl.BlockSpec((2 * RADIX, RADIX), fixed),
             pl.BlockSpec((2 * RADIX, RADIX), fixed),
         ],
-        out_specs=pl.BlockSpec((1, block_total, RADIX // 2), lambda k: (k, 0, 0)),
+        out_specs=pl.BlockSpec((step_templates, block_total, RADIX // 2), lambda k: (k, 0, 0)),
         compiler_params=pltpu.CompilerParams(dimension_semantics=("arbitrary",)),
         cost_estimate=pl.CostEstimate(
             flops=pair_flops * template_total * block_total,

time: 74.5 us -> 66.3 us (0.89)
  Pallas kernels: 28.7 us -> 20.6 us
    pallas_call x2, Pallas kernels: 28.7 us -> 20.6 us  [window_peaks(): pl.pallas_call(peaks_kernel, out_shape=jax.ShapeDtypeStruct((template_tot...]
  transfers between devices with their start and end apart: 9 -> 9, of which waited for: 3 -> 3; matrix products, arithmetic and copies ran while one was open for 26% -> 29% of each run, Pallas kernels for 19% -> 16%
where the time goes in v5:
time: 66.3 us; the launch traced here: 66 us
  Pallas kernels  20.6 us (31%)
  starting transfers between devices  16.8 us (25%)
  other arithmetic  16.5 us (25%)
  local copies, waits for them, and re-layouts  5.59 us (8%)
  waiting for transfers between devices  3.85 us (6%)
  matrix products  2.4 us (4%)
    pallas_call x2, Pallas kernels, window_peaks(): pl.pallas_call(peaks_kernel, out_shape=jax.ShapeDtypeStruct((template_tot...  20.6 us
    ppermute x8, starting transfers between devices, gathered_bank(): arrived = lax.ppermute(held, 'seg', pairs)  12.2 us
    another operation x15, other arithmetic, gathered_bank(): jnp.stack([jnp.where(upper, arrived, held), jnp.where(upper, held, arrive...  5.46 us
    ppermute x1, starting transfers between devices, passed_along(): return lax.ppermute(value, axis, pairs)  4.67 us
    ppermute x8, waiting for transfers between devices, gathered_bank(): arrived = lax.ppermute(held, 'seg', pairs)  3.84 us
    another operation x6, local copies, waits for them, and re-layouts, gathered_bank(): jnp.stack([jnp.where(upper, arrived, held), jnp.where(upper, held, arrive...  3.62 us
    sin x3, other arithmetic, angle_table(): return (jnp.cos(angle_value), jnp.sin(angle_value))  2.54 us
    select_n x2, other arithmetic, gathered_bank(): jnp.where(upper, arrived, held)  2.46 us
  transfers between devices with their start and end apart: 9, of which 3 were waited for; matrix products, arithmetic and copies ran while one was open for 29% of the time, Pallas kernels for 16%

profile of v5, /device:TPU:1, one launch (start us, length us, event | category | flops | bytes accessed | tf_op | source)
XLA Modules:
  0.0 66.0 jit_solution(261356438286595062)
XLA Ops:
  0.0 1.1 %convert_multiply_fusion = f32[65536]{0:T(1024)S(1)} fusion(f32[65536]{0:T(1024)} %param.3, s32[65536]{0:T(1024)} %param.4), kind=kLoop, calls=%fused_computation.62 | loop fusion | flops 131072 | bytes 786432 | tf_op jit(solution)/shard_map/mul | solution.py:202
  1.1 0.0 copy-start.2
  1.1 4.7 %collective-permute-start = (f32[32768]{0:T(1024)S(1)}, f32[32768]{0:T(1024)S(1)}, u32[]{:S(2)}, u32[]{:S(2)}) collective-permute-start(f32[32768]{0:T(1024)S(1)} %get-tuple-element.21), channel_id=1, source_target_pairs={{0,1},{1,2},{2,3},{3,4},{4,5},{5,6},{6,7},{7,8},{8,9},{9,10},{10,1... | collective-permute-start | bytes 393224 | tf_op jit(solution)/shard_map/ppermute | solution.py:23
  5.8 0.1 slice_bitcast_fusion.1
  5.9 2.4 %collective-permute-start.1 = (bf16[1,8,2,2048]{3,2,1,0:T(2,128)(2,1)S(1)}, bf16[1,8,2,2048]{3,2,1,0:T(2,128)(2,1)S(1)}, u32[]{:S(2)}, u32[]{:S(2)}) collective-permute-start(bf16[1,8,2,2048]{3,2,1,0:T(2,128)(2,1)S(1)} %get-tuple-element.29), channel_id=1, source_target_pairs={{0,8},{1,9},{2,10},{3,11},{4,12},{5,13},{6,14},{7,15},{8,0},{9,1},... | collective-permute-start | bytes 196616 | tf_op jit(solution)/shard_map/ppermute | solution.py:190
  8.3 0.1 collective-permute-start.5
  8.3 0.1 concatenate.46
  8.4 1.0 %fusion.38 = (f32[256,256]{1,0:T(8,128)S(1)}, f32[256,256]{1,0:T(8,128)S(1)}) fusion(), kind=kLoop, calls=%fused_computation.85 | loop fusion | flops 983040 | bytes 524288 | tf_op jit(solution)/shard_map/cos | solution.py:31
  9.5 1.0 %fusion.35 = (f32[256,256]{1,0:T(8,128)S(1)}, f32[256,256]{1,0:T(8,128)S(1)}) fusion(), kind=kLoop, calls=%fused_computation.82 | loop fusion | flops 917504 | bytes 524288 | tf_op jit(solution)/shard_map/sin | solution.py:31
  10.5 0.5 fusion.47
  11.1 0.5 fusion.49
  11.6 1.0 %fusion.37 = f32[256,256]{1,0:T(8,128)S(1)} fusion(), kind=kLoop, calls=%fused_computation.84 | loop fusion | flops 917504 | bytes 262144 | tf_op jit(solution)/shard_map/sin | solution.py:31
  12.5 0.1 copy.22
  12.7 0.1 copy.21
  12.8 0.9 %fusion = (bf16[512,256]{1,0:T(8,128)(2,1)}, bf16[512,256]{1,0:T(8,128)(2,1)}) fusion(f32[256,128]{1,0:T(8,128)S(1)} %get-tuple-element.36, f32[256,128]{1,0:T(8,128)S(1)} %get-tuple-element.35, f32[256,128]{1,0:T(8,128)S(1)} %fusion.49), kind=kLoop, calls=%fused_computation.14 | loop fusion | flops 917504 | bytes 917504 | tf_op jit(solution)/shard_map/convert_element_type | solution.py:72
  13.7 0.9 %fusion.1 = (bf16[512,256]{1,0:T(8,128)(2,1)}, bf16[512,256]{1,0:T(8,128)(2,1)}) fusion(f32[256,256]{1,0:T(8,128)S(1)} %get-tuple-element.31, f32[256,256]{1,0:T(8,128)S(1)} %fusion.37, f32[256,256]{1,0:T(8,128)S(1)} %get-tuple-element.32), kind=kLoop, calls=%fused_computation.15 | loop fusion | flops 1310720 | bytes 1310720 | tf_op jit(solution)/shard_map/convert_element_type | solution.py:72
  14.6 0.0 collective-permute-done.1
  14.6 0.0 collective-permute-done.5
  14.6 0.2 fusion.43
  14.8 0.2 fusion.63
  15.0 1.4 %collective-permute-start.6 = (bf16[2,1,8,2,2048]{4,3,2,0,1:T(2,128)(2,1)S(1)}, bf16[2,1,8,2,2048]{4,3,2,0,1:T(2,128)(2,1)S(1)}, u32[]{:S(2)}, u32[]{:S(2)}) collective-permute-start(bf16[2,1,8,2,2048]{4,3,2,0,1:T(2,128)(2,1)S(1)} %fusion.63), channel_id=1, source_target_pairs={{0,4},{1,5},{2,6},{3,7},{4,0},{5,1},{6,2},{7,3},{8,12},{9,13},{10,... | collective-permute-start | bytes 393224 | tf_op jit(solution)/shard_map/ppermute | solution.py:190
  16.4 0.2 pad_maximum_fusion.11
  16.6 0.2 collective-permute-start.2
  16.8 0.0 collective-permute-done
  16.9 0.1 copy.20
  16.9 0.6 fusion.3
  17.6 0.1 multiply_add_fusion
  17.7 0.9 %convolution_bitcast_fusion = f32[2,128,512]{2,1,0:T(8,128)S(1)} fusion(f32[2,256,256]{2,1,0:T(8,128)S(1)} %get-tuple-element.6, f32[2,256,256]{2,1,0:T(8,128)S(1)} %get-tuple-element.5), kind=kOutput, calls=%fused_computation | convolution fusion | flops 202047488 | bytes 1572864 | tf_op jit(solution)/shard_map/bnf,nk->bkf/dot_general | solution.py:54
  18.6 0.9 %convolution_bitcast_fusion.1 = f32[2,128,512]{2,1,0:T(8,128)S(1)} fusion(f32[2,256,256]{2,1,0:T(8,128)S(1)} %get-tuple-element.6, f32[2,256,256]{2,1,0:T(8,128)S(1)} %get-tuple-element.5), kind=kOutput, calls=%fused_computation.1 | convolution fusion | flops 202047488 | bytes 1572864 | tf_op jit(solution)/shard_map/bnf,nk->bkf/dot_general | solution.py:53
  19.5 0.1 slice_add_fusion
  19.6 0.9 %pad_maximum_fusion.6.spec_ref = f32[2,128,512]{2,1,0:T(8,128)} fusion(f32[2,128,256]{2,1,0:T(8,128)S(1)} %get-tuple-element.12, f32[2,128,256]{2,1,0:T(8,128)S(1)} %get-tuple-element.11), kind=kLoop, calls=%fused_computation.29 | loop fusion | flops 131072 | bytes 1048576 | tf_op jit(solution)/shard_map/concatenate | solution.py:55
  20.5 0.2 fusion.32
  20.7 0.2 fusion.31
  20.9 0.4 fusion.64
  21.3 1.3 %collective-permute-start.7 = (bf16[2,2,1,8,2,2048]{5,4,3,1,0,2:T(2,128)(2,1)S(1)}, bf16[2,2,1,8,2,2048]{5,4,3,1,0,2:T(2,128)(2,1)S(1)}, u32[]{:S(2)}, u32[]{:S(2)}) collective-permute-start(bf16[2,2,1,8,2,2048]{5,4,3,1,0,2:T(2,128)(2,1)S(1)} %fusion.64), channel_id=1, source_target_pairs={{0,2},{1,3},{2,0},{3,1},{4,6},{5,7},{6,4},{7,5},{8,10},{9,11},{10,... | collective-permute-start | bytes 786440 | tf_op jit(solution)/shard_map/ppermute | solution.py:190
  22.6 0.3 collective-permute-done.2
  22.9 0.3 fusion.29
  23.3 0.4 pad_maximum_fusion.9
  23.6 1.3 %collective-permute-start.3 = (bf16[2,2,1,8,2,2048]{5,4,3,1,0,2:T(2,128)(2,1)S(1)}, bf16[2,2,1,8,2,2048]{5,4,3,1,0,2:T(2,128)(2,1)S(1)}, u32[]{:S(2)}, u32[]{:S(2)}) collective-permute-start(bf16[2,2,1,8,2,2048]{5,4,3,1,0,2:T(2,128)(2,1)S(1)} %pad_maximum_fusion.9), channel_id=1, source_target_pairs={{0,2},{1,3},{2,0},{3,1},{4,6},{5,7},{6,4},{7,5},{8,10},{9,11},{10,... | collective-permute-start | bytes 786440 | tf_op jit(solution)/shard_map/ppermute | solution.py:190
  24.9 3.2 %collective-permute-done.7 = bf16[2,2,1,8,2,2048]{5,4,3,1,0,2:T(2,128)(2,1)S(1)} collective-permute-done((bf16[2,2,1,8,2,2048]{5,4,3,1,0,2:T(2,128)(2,1)S(1)}, bf16[2,2,1,8,2,2048]{5,4,3,1,0,2:T(2,128)(2,1)S(1)}, u32[]{:S(2)}, u32[]{:S(2)}) %collective-permute-start.7) | collective-permute-done | bytes 262176 | tf_op jit(solution)/shard_map/ppermute | solution.py:190
  28.2 0.5 fusion.18
  28.6 0.5 fusion.17
  29.1 0.9 %pad_maximum_fusion.8 = bf16[2,2,2,1,8,2,2048]{6,5,4,2,1,3,0:T(2,128)(2,1)S(1)} fusion(bf16[1,2,2,1,8,2,2048]{6,5,4,2,1,3,0:T(2,128)(2,1)S(1)} %fusion.18, bf16[1,2,2,1,8,2,2048]{6,5,4,2,1,3,0:T(2,128)(2,1)S(1)} %fusion.17), kind=kLoop, calls=%fused_computation.32 | loop fusion | flops 262144 | bytes 1048576 | tf_op jit(solution)/shard_map/stack | solution.py:192
  30.0 3.5 %collective-permute-start.8 = (bf16[2,2,2,1,8,2,2048]{6,5,4,2,1,3,0:T(2,128)(2,1)S(1)}, bf16[2,2,2,1,8,2,2048]{6,5,4,2,1,3,0:T(2,128)(2,1)S(1)}, u32[]{:S(2)}, u32[]{:S(2)}) collective-permute-start(bf16[2,2,2,1,8,2,2048]{6,5,4,2,1,3,0:T(2,128)(2,1)S(1)} %pad_maximum_fusion.8), channel_id=1, source_target_pairs={{0,1},{1,0},{2,3},{3,2},{4,5},{5,4},{6,7},{7,6},{8,9},{9,8},{10,11... | collective-permute-start | bytes 1572872 | tf_op jit(solution)/shard_map/ppermute | solution.py:190
  33.5 0.3 collective-permute-done.3
  33.8 0.6 fusion.15
  34.4 0.7 %pad_maximum_fusion.7 = bf16[2,2,2,1,8,2,2048]{6,5,4,2,1,3,0:T(2,128)(2,1)S(1)} fusion(bf16[1,2,2,1,8,2,2048]{6,5,4,2,1,3,0:T(2,128)(2,1)S(1)} %get-tuple-element.16, bf16[1,2,2,1,8,2,2048]{6,5,4,2,1,3,0:T(2,128)(2,1)S(1)} %get-tuple-element.15), kind=kLoop, calls=%fused_computation.30 | loop fusion | flops 262144 | bytes 1048576 | tf_op jit(solution)/shard_map/stack | solution.py:192
  35.2 2.0 %collective-permute-start.4 = (bf16[2,2,2,1,8,2,2048]{6,5,4,2,1,3,0:T(2,128)(2,1)S(1)}, bf16[2,2,2,1,8,2,2048]{6,5,4,2,1,3,0:T(2,128)(2,1)S(1)}, u32[]{:S(2)}, u32[]{:S(2)}) collective-permute-start(bf16[2,2,2,1,8,2,2048]{6,5,4,2,1,3,0:T(2,128)(2,1)S(1)} %pad_maximum_fusion.7), channel_id=1, source_target_pairs={{0,1},{1,0},{2,3},{3,2},{4,5},{5,4},{6,7},{7,6},{8,9},{9,8},{10,11... | collective-permute-start | bytes 1572872 | tf_op jit(solution)/shard_map/ppermute | solution.py:190
  37.1 0.0 collective-permute-done.8
  37.1 1.2 %broadcast_select_fusion.1 = (bf16[2,2,2,1,8,2,2048]{6,5,4,2,1,3,0:T(2,128)(2,1)S(1)}, bf16[2,2,2,1,8,2,2048]{6,5,4,2,1,3,0:T(2,128)(2,1)S(1)}) fusion(bf16[2,2,2,1,8,2,2048]{6,5,4,2,1,3,0:T(2,128)(2,1)S(1)} %collective-permute-done.8, pred[]{:T(512)S(6)} %ne.97, bf16[1,2,2,1,8,2,2048]{6,5,4,2,1,3,0:T(2,128)(2,1)S(1)} %fusion.18, ...), kind=kLoop, calls=%fused_computation.7 | loop fusion | flops 786432 | bytes 2097153 | tf_op jit(solution)/shard_map/jit(_where)/select_n | solution.py:192
  38.4 0.3 stack.94
  38.7 0.3 stack.93
  39.1 0.1 pad_maximum_fusion.2
  39.2 1.1 %copy.44 = bf16[2,2,2,2,8,2,8,256]{7,6,0,1,2,3,5,4:T(8,128)(2,1)} copy(bf16[2,2,2,2,8,2,8,256]{7,6,5,4,3,2,1,0:T(8,128)(2,1)S(1)} %pad_maximum_fusion.2) | data formatting | bytes 2097152 | tf_op jit(solution)/shard_map/stack | solution.py:192
  40.3 10.3 %shard_map.38 = f32[8,2,128]{2,1,0:T(2,128)} custom-call(f32[2,128,512]{2,1,0:T(8,128)} %pad_maximum_fusion.6.spec_ref, bf16[8,2,128,256]{3,2,1,0:T(8,128)(2,1)} %bitcast.96, bf16[512,256]{1,0:T(8,128)(2,1)} %get-tuple-element.18.fh_ref, bf16[512,256]{1,0:T(8,128)(2,1)} %get-tuple-element.17.fl_ref, f32[256,256]{1,0:T(8,128)} %copy-done.1, ...), custom_call_target="tpu_custom_call" | custom-call | flops 6442450944 | bytes 1581056 | tf_op jit(solution)/shard_map/pallas_call | solution.py:157
  50.6 0.7 %copy.49 = f32[1,8,2,128]{3,1,2,0:T(8,128)S(1)} copy(f32[1,8,2,128]{3,2,1,0:T(2,128)} %bitcast.100) | data formatting | bytes 16384
  51.3 1.2 %broadcast_select_fusion.3 = (bf16[2,2,2,1,8,2,2048]{6,5,4,2,1,3,0:T(2,128)(2,1)S(1)}, bf16[2,2,2,1,8,2,2048]{6,5,4,2,1,3,0:T(2,128)(2,1)S(1)}) fusion(bf16[2,2,2,1,8,2,2048]{6,5,4,2,1,3,0:T(2,128)(2,1)S(1)} %collective-permute-done.4, pred[]{:T(512)S(6)} %ne.97, bf16[1,2,2,1,8,2,2048]{6,5,4,2,1,3,0:T(2,128)(2,1)S(1)} %get-tuple-element.16, ...), kind=kLoop, calls=%fused_computation.9 | loop fusion | flops 786432 | bytes 2097153 | tf_op jit(solution)/shard_map/jit(_where)/select_n | solution.py:192
  52.5 0.3 stack.82
  52.9 0.3 stack.81
  53.2 0.1 pad_maximum_fusion.1
  53.3 1.1 %copy.43 = bf16[2,2,2,2,8,2,8,256]{7,6,0,1,2,3,5,4:T(8,128)(2,1)} copy(bf16[2,2,2,2,8,2,8,256]{7,6,5,4,3,2,1,0:T(8,128)(2,1)S(1)} %pad_maximum_fusion.1) | data formatting | bytes 2097152 | tf_op jit(solution)/shard_map/stack | solution.py:192
  54.4 10.3 %shard_map.37 = f32[8,2,128]{2,1,0:T(2,128)} custom-call(f32[2,128,512]{2,1,0:T(8,128)} %pad_maximum_fusion.6.spec_ref, bf16[8,2,128,256]{3,2,1,0:T(8,128)(2,1)} %bitcast.95, bf16[512,256]{1,0:T(8,128)(2,1)} %get-tuple-element.18.fh_ref, bf16[512,256]{1,0:T(8,128)(2,1)} %get-tuple-element.17.fl_ref, f32[256,256]{1,0:T(8,128)} %copy-done.1, ...), custom_call_target="tpu_custom_call" | custom-call | flops 6442450944 | bytes 1581056 | tf_op jit(solution)/shard_map/pallas_call | solution.py:157
  64.7 0.7 %copy.50 = f32[1,8,2,128]{3,1,2,0:T(8,128)S(1)} copy(f32[1,8,2,128]{3,2,1,0:T(2,128)} %bitcast.99) | data formatting | bytes 16384
  65.4 0.6 pad_maximum_fusion.13
  (10 shorter events, 0.1 us)
Async XLA Ops:
  1.1 4.7 %copy-start.2 = (bf16[16,2,2048]{2,1,0:T(2,128)(2,1)S(1)}, bf16[16,2,2048]{2,1,0:T(2,128)(2,1)}, u32[]{:S(2)}) copy-start(bf16[16,2,2048]{2,1,0:T(2,128)(2,1)} %param.5) | copy-start | bytes 393220
  1.1 15.7 %collective-permute-start = (f32[32768]{0:T(1024)S(1)}, f32[32768]{0:T(1024)S(1)}, u32[]{:S(2)}, u32[]{:S(2)}) collective-permute-start(f32[32768]{0:T(1024)S(1)} %get-tuple-element.21), channel_id=1, source_target_pairs={{0,1},{1,2},{2,3},{3,4},{4,5},{5,6},{6,7},{7,8},{8,9},{9,10},{10,1... | collective-permute-start | bytes 393224 | tf_op jit(solution)/shard_map/ppermute | solution.py:23
  5.9 8.7 %collective-permute-start.1 = (bf16[1,8,2,2048]{3,2,1,0:T(2,128)(2,1)S(1)}, bf16[1,8,2,2048]{3,2,1,0:T(2,128)(2,1)S(1)}, u32[]{:S(2)}, u32[]{:S(2)}) collective-permute-start(bf16[1,8,2,2048]{3,2,1,0:T(2,128)(2,1)S(1)} %get-tuple-element.29), channel_id=1, source_target_pairs={{0,8},{1,9},{2,10},{3,11},{4,12},{5,13},{6,14},{7,15},{8,0},{9,1},... | collective-permute-start | bytes 196616 | tf_op jit(solution)/shard_map/ppermute | solution.py:190
  8.3 6.3 %collective-permute-start.5 = (bf16[1,8,2,2048]{3,2,1,0:T(2,128)(2,1)S(1)}, bf16[1,8,2,2048]{3,2,1,0:T(2,128)(2,1)S(1)}, u32[]{:S(2)}, u32[]{:S(2)}) collective-permute-start(bf16[1,8,2,2048]{3,2,1,0:T(2,128)(2,1)S(1)} %get-tuple-element.30), channel_id=1, source_target_pairs={{0,8},{1,9},{2,10},{3,11},{4,12},{5,13},{6,14},{7,15},{8,0},{9,1},... | collective-permute-start | bytes 196616 | tf_op jit(solution)/shard_map/ppermute | solution.py:190
  10.5 7.0 %copy-start = (f32[256,256]{1,0:T(8,128)}, f32[256,256]{1,0:T(8,128)S(1)}, u32[]{:S(2)}) copy-start(f32[256,256]{1,0:T(8,128)S(1)} %get-tuple-element.33.ts_ref) | copy-start | bytes 786436
  10.5 7.0 %copy-start.1 = (f32[256,256]{1,0:T(8,128)}, f32[256,256]{1,0:T(8,128)S(1)}, u32[]{:S(2)}) copy-start(f32[256,256]{1,0:T(8,128)S(1)} %get-tuple-element.34.tc_ref) | copy-start | bytes 786436
  15.0 5.4 %collective-permute-start.6 = (bf16[2,1,8,2,2048]{4,3,2,0,1:T(2,128)(2,1)S(1)}, bf16[2,1,8,2,2048]{4,3,2,0,1:T(2,128)(2,1)S(1)}, u32[]{:S(2)}, u32[]{:S(2)}) collective-permute-start(bf16[2,1,8,2,2048]{4,3,2,0,1:T(2,128)(2,1)S(1)} %fusion.63), channel_id=1, source_target_pairs={{0,4},{1,5},{2,6},{3,7},{4,0},{5,1},{6,2},{7,3},{8,12},{9,13},{10,... | collective-permute-start | bytes 393224 | tf_op jit(solution)/shard_map/ppermute | solution.py:190
  16.6 6.4 %collective-permute-start.2 = (bf16[2,1,8,2,2048]{4,3,2,0,1:T(2,128)(2,1)S(1)}, bf16[2,1,8,2,2048]{4,3,2,0,1:T(2,128)(2,1)S(1)}, u32[]{:S(2)}, u32[]{:S(2)}) collective-permute-start(bf16[2,1,8,2,2048]{4,3,2,0,1:T(2,128)(2,1)S(1)} %pad_maximum_fusion.11), channel_id=1, source_target_pairs={{0,4},{1,5},{2,6},{3,7},{4,0},{5,1},{6,2},{7,3},{8,12},{9,13},{10,... | collective-permute-start | bytes 393224 | tf_op jit(solution)/shard_map/ppermute | solution.py:190
  21.3 6.9 %collective-permute-start.7 = (bf16[2,2,1,8,2,2048]{5,4,3,1,0,2:T(2,128)(2,1)S(1)}, bf16[2,2,1,8,2,2048]{5,4,3,1,0,2:T(2,128)(2,1)S(1)}, u32[]{:S(2)}, u32[]{:S(2)}) collective-permute-start(bf16[2,2,1,8,2,2048]{5,4,3,1,0,2:T(2,128)(2,1)S(1)} %fusion.64), channel_id=1, source_target_pairs={{0,2},{1,3},{2,0},{3,1},{4,6},{5,7},{6,4},{7,5},{8,10},{9,11},{10,... | collective-permute-start | bytes 786440 | tf_op jit(solution)/shard_map/ppermute | solution.py:190
  23.6 10.2 %collective-permute-start.3 = (bf16[2,2,1,8,2,2048]{5,4,3,1,0,2:T(2,128)(2,1)S(1)}, bf16[2,2,1,8,2,2048]{5,4,3,1,0,2:T(2,128)(2,1)S(1)}, u32[]{:S(2)}, u32[]{:S(2)}) collective-permute-start(bf16[2,2,1,8,2,2048]{5,4,3,1,0,2:T(2,128)(2,1)S(1)} %pad_maximum_fusion.9), channel_id=1, source_target_pairs={{0,2},{1,3},{2,0},{3,1},{4,6},{5,7},{6,4},{7,5},{8,10},{9,11},{10,... | collective-permute-start | bytes 786440 | tf_op jit(solution)/shard_map/ppermute | solution.py:190
  30.0 7.1 %collective-permute-start.8 = (bf16[2,2,2,1,8,2,2048]{6,5,4,2,1,3,0:T(2,128)(2,1)S(1)}, bf16[2,2,2,1,8,2,2048]{6,5,4,2,1,3,0:T(2,128)(2,1)S(1)}, u32[]{:S(2)}, u32[]{:S(2)}) collective-permute-start(bf16[2,2,2,1,8,2,2048]{6,5,4,2,1,3,0:T(2,128)(2,1)S(1)} %pad_maximum_fusion.8), channel_id=1, source_target_pairs={{0,1},{1,0},{2,3},{3,2},{4,5},{5,4},{6,7},{7,6},{8,9},{9,8},{10,11... | collective-permute-start | bytes 1572872 | tf_op jit(solution)/shard_map/ppermute | solution.py:190
  35.2 16.1 %collective-permute-start.4 = (bf16[2,2,2,1,8,2,2048]{6,5,4,2,1,3,0:T(2,128)(2,1)S(1)}, bf16[2,2,2,1,8,2,2048]{6,5,4,2,1,3,0:T(2,128)(2,1)S(1)}, u32[]{:S(2)}, u32[]{:S(2)}) collective-permute-start(bf16[2,2,2,1,8,2,2048]{6,5,4,2,1,3,0:T(2,128)(2,1)S(1)} %pad_maximum_fusion.7), channel_id=1, source_target_pairs={{0,1},{1,0},{2,3},{3,2},{4,5},{5,4},{6,7},{7,6},{8,9},{9,8},{10,11... | collective-permute-start | bytes 1572872 | tf_op jit(solution)/shard_map/ppermute | solution.py:190

commit v6 on v5

--- a/solution.py
+++ b/solution.py
@@ -10,7 +10,7 @@
 RADIX = 256
 BLOCK = 32768
 SUBBANK = 8
-STEP_TEMPLATES = 2
+STEP_TEMPLATES = 4
 
 
 PRECISE = lax.Precision.HIGH

time: 66.3 us -> 66.6 us (level)
  no operation moved by 1% of the time
where the time goes in v6:
time: 66.6 us; the launch traced here: 66.3 us
  Pallas kernels  20.8 us (31%)
  starting transfers between devices  16.8 us (25%)
  other arithmetic  16.5 us (25%)
  local copies, waits for them, and re-layouts  5.59 us (8%)
  waiting for transfers between devices  3.85 us (6%)
  matrix products  2.4 us (4%)
    pallas_call x2, Pallas kernels, window_peaks(): pl.pallas_call(peaks_kernel, out_shape=jax.ShapeDtypeStruct((template_tot...  20.8 us
    ppermute x8, starting transfers between devices, gathered_bank(): arrived = lax.ppermute(held, 'seg', pairs)  12.2 us
    another operation x15, other arithmetic, gathered_bank(): jnp.stack([jnp.where(upper, arrived, held), jnp.where(upper, held, arrive...  5.46 us
    ppermute x1, starting transfers between devices, passed_along(): return lax.ppermute(value, axis, pairs)  4.67 us
    ppermute x8, waiting for transfers between devices, gathered_bank(): arrived = lax.ppermute(held, 'seg', pairs)  3.84 us
    another operation x6, local copies, waits for them, and re-layouts, gathered_bank(): jnp.stack([jnp.where(upper, arrived, held), jnp.where(upper, held, arrive...  3.62 us
    sin x3, other arithmetic, angle_table(): return (jnp.cos(angle_value), jnp.sin(angle_value))  2.54 us
    select_n x2, other arithmetic, gathered_bank(): jnp.where(upper, arrived, held)  2.46 us
  transfers between devices with their start and end apart: 9, of which 3 were waited for; matrix products, arithmetic and copies ran while one was open for 29% of the time, Pallas kernels for 16%

profile of v6, /device:TPU:1, one launch (start us, length us, event | category | flops | bytes accessed | tf_op | source)
XLA Modules:
  0.0 66.3 jit_solution(14012651457909450650)
XLA Ops:
  0.0 1.1 %convert_multiply_fusion = f32[65536]{0:T(1024)S(1)} fusion(f32[65536]{0:T(1024)} %param.3, s32[65536]{0:T(1024)} %param.4), kind=kLoop, calls=%fused_computation.62 | loop fusion | flops 131072 | bytes 786432 | tf_op jit(solution)/shard_map/mul | solution.py:202
  1.1 0.0 copy-start.2
  1.1 4.7 %collective-permute-start = (f32[32768]{0:T(1024)S(1)}, f32[32768]{0:T(1024)S(1)}, u32[]{:S(2)}, u32[]{:S(2)}) collective-permute-start(f32[32768]{0:T(1024)S(1)} %get-tuple-element.21), channel_id=1, source_target_pairs={{0,1},{1,2},{2,3},{3,4},{4,5},{5,6},{6,7},{7,8},{8,9},{9,10},{10,1... | collective-permute-start | bytes 393224 | tf_op jit(solution)/shard_map/ppermute | solution.py:23
  5.8 0.1 slice_bitcast_fusion.1
  5.9 2.4 %collective-permute-start.1 = (bf16[1,8,2,2048]{3,2,1,0:T(2,128)(2,1)S(1)}, bf16[1,8,2,2048]{3,2,1,0:T(2,128)(2,1)S(1)}, u32[]{:S(2)}, u32[]{:S(2)}) collective-permute-start(bf16[1,8,2,2048]{3,2,1,0:T(2,128)(2,1)S(1)} %get-tuple-element.29), channel_id=1, source_target_pairs={{0,8},{1,9},{2,10},{3,11},{4,12},{5,13},{6,14},{7,15},{8,0},{9,1},... | collective-permute-start | bytes 196616 | tf_op jit(solution)/shard_map/ppermute | solution.py:190
  8.3 0.1 collective-permute-start.5
  8.3 0.1 concatenate.46
  8.4 1.0 %fusion.38 = (f32[256,256]{1,0:T(8,128)S(1)}, f32[256,256]{1,0:T(8,128)S(1)}) fusion(), kind=kLoop, calls=%fused_computation.85 | loop fusion | flops 983040 | bytes 524288 | tf_op jit(solution)/shard_map/cos | solution.py:31
  9.5 1.0 %fusion.35 = (f32[256,256]{1,0:T(8,128)S(1)}, f32[256,256]{1,0:T(8,128)S(1)}) fusion(), kind=kLoop, calls=%fused_computation.82 | loop fusion | flops 917504 | bytes 524288 | tf_op jit(solution)/shard_map/sin | solution.py:31
  10.5 0.5 fusion.47
  11.1 0.5 fusion.49
  11.6 1.0 %fusion.37 = f32[256,256]{1,0:T(8,128)S(1)} fusion(), kind=kLoop, calls=%fused_computation.84 | loop fusion | flops 917504 | bytes 262144 | tf_op jit(solution)/shard_map/sin | solution.py:31
  12.5 0.1 copy.22
  12.7 0.1 copy.21
  12.8 0.9 %fusion = (bf16[512,256]{1,0:T(8,128)(2,1)}, bf16[512,256]{1,0:T(8,128)(2,1)}) fusion(f32[256,128]{1,0:T(8,128)S(1)} %get-tuple-element.36, f32[256,128]{1,0:T(8,128)S(1)} %get-tuple-element.35, f32[256,128]{1,0:T(8,128)S(1)} %fusion.49), kind=kLoop, calls=%fused_computation.14 | loop fusion | flops 917504 | bytes 917504 | tf_op jit(solution)/shard_map/convert_element_type | solution.py:72
  13.7 0.9 %fusion.1 = (bf16[512,256]{1,0:T(8,128)(2,1)}, bf16[512,256]{1,0:T(8,128)(2,1)}) fusion(f32[256,256]{1,0:T(8,128)S(1)} %get-tuple-element.31, f32[256,256]{1,0:T(8,128)S(1)} %fusion.37, f32[256,256]{1,0:T(8,128)S(1)} %get-tuple-element.32), kind=kLoop, calls=%fused_computation.15 | loop fusion | flops 1310720 | bytes 1310720 | tf_op jit(solution)/shard_map/convert_element_type | solution.py:72
  14.6 0.0 collective-permute-done.1
  14.6 0.0 collective-permute-done.5
  14.6 0.2 fusion.43
  14.8 0.2 fusion.63
  15.0 1.4 %collective-permute-start.6 = (bf16[2,1,8,2,2048]{4,3,2,0,1:T(2,128)(2,1)S(1)}, bf16[2,1,8,2,2048]{4,3,2,0,1:T(2,128)(2,1)S(1)}, u32[]{:S(2)}, u32[]{:S(2)}) collective-permute-start(bf16[2,1,8,2,2048]{4,3,2,0,1:T(2,128)(2,1)S(1)} %fusion.63), channel_id=1, source_target_pairs={{0,4},{1,5},{2,6},{3,7},{4,0},{5,1},{6,2},{7,3},{8,12},{9,13},{10,... | collective-permute-start | bytes 393224 | tf_op jit(solution)/shard_map/ppermute | solution.py:190
  16.4 0.2 pad_maximum_fusion.11
  16.6 0.2 collective-permute-start.2
  16.8 0.0 collective-permute-done
  16.9 0.1 copy.20
  16.9 0.6 fusion.3
  17.6 0.1 multiply_add_fusion
  17.7 0.9 %convolution_bitcast_fusion = f32[2,128,512]{2,1,0:T(8,128)S(1)} fusion(f32[2,256,256]{2,1,0:T(8,128)S(1)} %get-tuple-element.6, f32[2,256,256]{2,1,0:T(8,128)S(1)} %get-tuple-element.5), kind=kOutput, calls=%fused_computation | convolution fusion | flops 202047488 | bytes 1572864 | tf_op jit(solution)/shard_map/bnf,nk->bkf/dot_general | solution.py:54
  18.6 0.9 %convolution_bitcast_fusion.1 = f32[2,128,512]{2,1,0:T(8,128)S(1)} fusion(f32[2,256,256]{2,1,0:T(8,128)S(1)} %get-tuple-element.6, f32[2,256,256]{2,1,0:T(8,128)S(1)} %get-tuple-element.5), kind=kOutput, calls=%fused_computation.1 | convolution fusion | flops 202047488 | bytes 1572864 | tf_op jit(solution)/shard_map/bnf,nk->bkf/dot_general | solution.py:53
  19.5 0.1 slice_add_fusion
  19.6 0.9 %pad_maximum_fusion.6.spec_ref = f32[2,128,512]{2,1,0:T(8,128)} fusion(f32[2,128,256]{2,1,0:T(8,128)S(1)} %get-tuple-element.12, f32[2,128,256]{2,1,0:T(8,128)S(1)} %get-tuple-element.11), kind=kLoop, calls=%fused_computation.29 | loop fusion | flops 131072 | bytes 1048576 | tf_op jit(solution)/shard_map/concatenate | solution.py:55
  20.5 0.2 fusion.32
  20.7 0.2 fusion.31
  20.9 0.4 fusion.64
  21.3 1.3 %collective-permute-start.7 = (bf16[2,2,1,8,2,2048]{5,4,3,1,0,2:T(2,128)(2,1)S(1)}, bf16[2,2,1,8,2,2048]{5,4,3,1,0,2:T(2,128)(2,1)S(1)}, u32[]{:S(2)}, u32[]{:S(2)}) collective-permute-start(bf16[2,2,1,8,2,2048]{5,4,3,1,0,2:T(2,128)(2,1)S(1)} %fusion.64), channel_id=1, source_target_pairs={{0,2},{1,3},{2,0},{3,1},{4,6},{5,7},{6,4},{7,5},{8,10},{9,11},{10,... | collective-permute-start | bytes 786440 | tf_op jit(solution)/shard_map/ppermute | solution.py:190
  22.6 0.3 collective-permute-done.2
  22.9 0.3 fusion.29
  23.3 0.4 pad_maximum_fusion.9
  23.6 1.3 %collective-permute-start.3 = (bf16[2,2,1,8,2,2048]{5,4,3,1,0,2:T(2,128)(2,1)S(1)}, bf16[2,2,1,8,2,2048]{5,4,3,1,0,2:T(2,128)(2,1)S(1)}, u32[]{:S(2)}, u32[]{:S(2)}) collective-permute-start(bf16[2,2,1,8,2,2048]{5,4,3,1,0,2:T(2,128)(2,1)S(1)} %pad_maximum_fusion.9), channel_id=1, source_target_pairs={{0,2},{1,3},{2,0},{3,1},{4,6},{5,7},{6,4},{7,5},{8,10},{9,11},{10,... | collective-permute-start | bytes 786440 | tf_op jit(solution)/shard_map/ppermute | solution.py:190
  24.9 3.2 %collective-permute-done.7 = bf16[2,2,1,8,2,2048]{5,4,3,1,0,2:T(2,128)(2,1)S(1)} collective-permute-done((bf16[2,2,1,8,2,2048]{5,4,3,1,0,2:T(2,128)(2,1)S(1)}, bf16[2,2,1,8,2,2048]{5,4,3,1,0,2:T(2,128)(2,1)S(1)}, u32[]{:S(2)}, u32[]{:S(2)}) %collective-permute-start.7) | collective-permute-done | bytes 262176 | tf_op jit(solution)/shard_map/ppermute | solution.py:190
  28.2 0.5 fusion.18
  28.6 0.5 fusion.17
  29.1 0.9 %pad_maximum_fusion.8 = bf16[2,2,2,1,8,2,2048]{6,5,4,2,1,3,0:T(2,128)(2,1)S(1)} fusion(bf16[1,2,2,1,8,2,2048]{6,5,4,2,1,3,0:T(2,128)(2,1)S(1)} %fusion.18, bf16[1,2,2,1,8,2,2048]{6,5,4,2,1,3,0:T(2,128)(2,1)S(1)} %fusion.17), kind=kLoop, calls=%fused_computation.32 | loop fusion | flops 262144 | bytes 1048576 | tf_op jit(solution)/shard_map/stack | solution.py:192
  30.0 3.5 %collective-permute-start.8 = (bf16[2,2,2,1,8,2,2048]{6,5,4,2,1,3,0:T(2,128)(2,1)S(1)}, bf16[2,2,2,1,8,2,2048]{6,5,4,2,1,3,0:T(2,128)(2,1)S(1)}, u32[]{:S(2)}, u32[]{:S(2)}) collective-permute-start(bf16[2,2,2,1,8,2,2048]{6,5,4,2,1,3,0:T(2,128)(2,1)S(1)} %pad_maximum_fusion.8), channel_id=1, source_target_pairs={{0,1},{1,0},{2,3},{3,2},{4,5},{5,4},{6,7},{7,6},{8,9},{9,8},{10,11... | collective-permute-start | bytes 1572872 | tf_op jit(solution)/shard_map/ppermute | solution.py:190
  33.5 0.3 collective-permute-done.3
  33.8 0.6 fusion.15
  34.4 0.7 %pad_maximum_fusion.7 = bf16[2,2,2,1,8,2,2048]{6,5,4,2,1,3,0:T(2,128)(2,1)S(1)} fusion(bf16[1,2,2,1,8,2,2048]{6,5,4,2,1,3,0:T(2,128)(2,1)S(1)} %get-tuple-element.16, bf16[1,2,2,1,8,2,2048]{6,5,4,2,1,3,0:T(2,128)(2,1)S(1)} %get-tuple-element.15), kind=kLoop, calls=%fused_computation.30 | loop fusion | flops 262144 | bytes 1048576 | tf_op jit(solution)/shard_map/stack | solution.py:192
  35.2 2.0 %collective-permute-start.4 = (bf16[2,2,2,1,8,2,2048]{6,5,4,2,1,3,0:T(2,128)(2,1)S(1)}, bf16[2,2,2,1,8,2,2048]{6,5,4,2,1,3,0:T(2,128)(2,1)S(1)}, u32[]{:S(2)}, u32[]{:S(2)}) collective-permute-start(bf16[2,2,2,1,8,2,2048]{6,5,4,2,1,3,0:T(2,128)(2,1)S(1)} %pad_maximum_fusion.7), channel_id=1, source_target_pairs={{0,1},{1,0},{2,3},{3,2},{4,5},{5,4},{6,7},{7,6},{8,9},{9,8},{10,11... | collective-permute-start | bytes 1572872 | tf_op jit(solution)/shard_map/ppermute | solution.py:190
  37.1 0.0 collective-permute-done.8
  37.1 1.2 %broadcast_select_fusion.1 = (bf16[2,2,2,1,8,2,2048]{6,5,4,2,1,3,0:T(2,128)(2,1)S(1)}, bf16[2,2,2,1,8,2,2048]{6,5,4,2,1,3,0:T(2,128)(2,1)S(1)}) fusion(bf16[2,2,2,1,8,2,2048]{6,5,4,2,1,3,0:T(2,128)(2,1)S(1)} %collective-permute-done.8, pred[]{:T(512)S(6)} %ne.97, bf16[1,2,2,1,8,2,2048]{6,5,4,2,1,3,0:T(2,128)(2,1)S(1)} %fusion.18, ...), kind=kLoop, calls=%fused_computation.7 | loop fusion | flops 786432 | bytes 2097153 | tf_op jit(solution)/shard_map/jit(_where)/select_n | solution.py:192
  38.4 0.3 stack.94
  38.7 0.3 stack.93
  39.1 0.1 pad_maximum_fusion.2
  39.2 1.1 %copy.44 = bf16[2,2,2,2,8,2,8,256]{7,6,0,1,2,3,5,4:T(8,128)(2,1)} copy(bf16[2,2,2,2,8,2,8,256]{7,6,5,4,3,2,1,0:T(8,128)(2,1)S(1)} %pad_maximum_fusion.2) | data formatting | bytes 2097152 | tf_op jit(solution)/shard_map/stack | solution.py:192
  40.3 10.4 %shard_map.38 = f32[8,2,128]{2,1,0:T(2,128)} custom-call(f32[2,128,512]{2,1,0:T(8,128)} %pad_maximum_fusion.6.spec_ref, bf16[8,2,128,256]{3,2,1,0:T(8,128)(2,1)} %bitcast.96, bf16[512,256]{1,0:T(8,128)(2,1)} %get-tuple-element.18.fh_ref, bf16[512,256]{1,0:T(8,128)(2,1)} %get-tuple-element.17.fl_ref, f32[256,256]{1,0:T(8,128)} %copy-done.1, ...), custom_call_target="tpu_custom_call" | custom-call | flops 6442450944 | bytes 1581056 | tf_op jit(solution)/shard_map/pallas_call | solution.py:157
  50.7 0.7 %copy.49 = f32[1,8,2,128]{3,1,2,0:T(8,128)S(1)} copy(f32[1,8,2,128]{3,2,1,0:T(2,128)} %bitcast.100) | data formatting | bytes 16384
  51.4 1.2 %broadcast_select_fusion.3 = (bf16[2,2,2,1,8,2,2048]{6,5,4,2,1,3,0:T(2,128)(2,1)S(1)}, bf16[2,2,2,1,8,2,2048]{6,5,4,2,1,3,0:T(2,128)(2,1)S(1)}) fusion(bf16[2,2,2,1,8,2,2048]{6,5,4,2,1,3,0:T(2,128)(2,1)S(1)} %collective-permute-done.4, pred[]{:T(512)S(6)} %ne.97, bf16[1,2,2,1,8,2,2048]{6,5,4,2,1,3,0:T(2,128)(2,1)S(1)} %get-tuple-element.16, ...), kind=kLoop, calls=%fused_computation.9 | loop fusion | flops 786432 | bytes 2097153 | tf_op jit(solution)/shard_map/jit(_where)/select_n | solution.py:192
  52.7 0.3 stack.82
  53.0 0.3 stack.81
  53.3 0.1 pad_maximum_fusion.1
  53.4 1.1 %copy.43 = bf16[2,2,2,2,8,2,8,256]{7,6,0,1,2,3,5,4:T(8,128)(2,1)} copy(bf16[2,2,2,2,8,2,8,256]{7,6,5,4,3,2,1,0:T(8,128)(2,1)S(1)} %pad_maximum_fusion.1) | data formatting | bytes 2097152 | tf_op jit(solution)/shard_map/stack | solution.py:192
  54.6 10.4 %shard_map.37 = f32[8,2,128]{2,1,0:T(2,128)} custom-call(f32[2,128,512]{2,1,0:T(8,128)} %pad_maximum_fusion.6.spec_ref, bf16[8,2,128,256]{3,2,1,0:T(8,128)(2,1)} %bitcast.95, bf16[512,256]{1,0:T(8,128)(2,1)} %get-tuple-element.18.fh_ref, bf16[512,256]{1,0:T(8,128)(2,1)} %get-tuple-element.17.fl_ref, f32[256,256]{1,0:T(8,128)} %copy-done.1, ...), custom_call_target="tpu_custom_call" | custom-call | flops 6442450944 | bytes 1581056 | tf_op jit(solution)/shard_map/pallas_call | solution.py:157
  65.0 0.7 %copy.50 = f32[1,8,2,128]{3,1,2,0:T(8,128)S(1)} copy(f32[1,8,2,128]{3,2,1,0:T(2,128)} %bitcast.99) | data formatting | bytes 16384
  65.7 0.6 pad_maximum_fusion.13
  (10 shorter events, 0.1 us)
Async XLA Ops:
  1.1 4.7 %copy-start.2 = (bf16[16,2,2048]{2,1,0:T(2,128)(2,1)S(1)}, bf16[16,2,2048]{2,1,0:T(2,128)(2,1)}, u32[]{:S(2)}) copy-start(bf16[16,2,2048]{2,1,0:T(2,128)(2,1)} %param.5) | copy-start | bytes 393220
  1.1 15.7 %collective-permute-start = (f32[32768]{0:T(1024)S(1)}, f32[32768]{0:T(1024)S(1)}, u32[]{:S(2)}, u32[]{:S(2)}) collective-permute-start(f32[32768]{0:T(1024)S(1)} %get-tuple-element.21), channel_id=1, source_target_pairs={{0,1},{1,2},{2,3},{3,4},{4,5},{5,6},{6,7},{7,8},{8,9},{9,10},{10,1... | collective-permute-start | bytes 393224 | tf_op jit(solution)/shard_map/ppermute | solution.py:23
  5.9 8.7 %collective-permute-start.1 = (bf16[1,8,2,2048]{3,2,1,0:T(2,128)(2,1)S(1)}, bf16[1,8,2,2048]{3,2,1,0:T(2,128)(2,1)S(1)}, u32[]{:S(2)}, u32[]{:S(2)}) collective-permute-start(bf16[1,8,2,2048]{3,2,1,0:T(2,128)(2,1)S(1)} %get-tuple-element.29), channel_id=1, source_target_pairs={{0,8},{1,9},{2,10},{3,11},{4,12},{5,13},{6,14},{7,15},{8,0},{9,1},... | collective-permute-start | bytes 196616 | tf_op jit(solution)/shard_map/ppermute | solution.py:190
  8.3 6.3 %collective-permute-start.5 = (bf16[1,8,2,2048]{3,2,1,0:T(2,128)(2,1)S(1)}, bf16[1,8,2,2048]{3,2,1,0:T(2,128)(2,1)S(1)}, u32[]{:S(2)}, u32[]{:S(2)}) collective-permute-start(bf16[1,8,2,2048]{3,2,1,0:T(2,128)(2,1)S(1)} %get-tuple-element.30), channel_id=1, source_target_pairs={{0,8},{1,9},{2,10},{3,11},{4,12},{5,13},{6,14},{7,15},{8,0},{9,1},... | collective-permute-start | bytes 196616 | tf_op jit(solution)/shard_map/ppermute | solution.py:190
  10.5 7.0 %copy-start = (f32[256,256]{1,0:T(8,128)}, f32[256,256]{1,0:T(8,128)S(1)}, u32[]{:S(2)}) copy-start(f32[256,256]{1,0:T(8,128)S(1)} %get-tuple-element.33.ts_ref) | copy-start | bytes 786436
  10.5 7.0 %copy-start.1 = (f32[256,256]{1,0:T(8,128)}, f32[256,256]{1,0:T(8,128)S(1)}, u32[]{:S(2)}) copy-start(f32[256,256]{1,0:T(8,128)S(1)} %get-tuple-element.34.tc_ref) | copy-start | bytes 786436
  15.0 5.4 %collective-permute-start.6 = (bf16[2,1,8,2,2048]{4,3,2,0,1:T(2,128)(2,1)S(1)}, bf16[2,1,8,2,2048]{4,3,2,0,1:T(2,128)(2,1)S(1)}, u32[]{:S(2)}, u32[]{:S(2)}) collective-permute-start(bf16[2,1,8,2,2048]{4,3,2,0,1:T(2,128)(2,1)S(1)} %fusion.63), channel_id=1, source_target_pairs={{0,4},{1,5},{2,6},{3,7},{4,0},{5,1},{6,2},{7,3},{8,12},{9,13},{10,... | collective-permute-start | bytes 393224 | tf_op jit(solution)/shard_map/ppermute | solution.py:190
  16.6 6.4 %collective-permute-start.2 = (bf16[2,1,8,2,2048]{4,3,2,0,1:T(2,128)(2,1)S(1)}, bf16[2,1,8,2,2048]{4,3,2,0,1:T(2,128)(2,1)S(1)}, u32[]{:S(2)}, u32[]{:S(2)}) collective-permute-start(bf16[2,1,8,2,2048]{4,3,2,0,1:T(2,128)(2,1)S(1)} %pad_maximum_fusion.11), channel_id=1, source_target_pairs={{0,4},{1,5},{2,6},{3,7},{4,0},{5,1},{6,2},{7,3},{8,12},{9,13},{10,... | collective-permute-start | bytes 393224 | tf_op jit(solution)/shard_map/ppermute | solution.py:190
  21.3 6.9 %collective-permute-start.7 = (bf16[2,2,1,8,2,2048]{5,4,3,1,0,2:T(2,128)(2,1)S(1)}, bf16[2,2,1,8,2,2048]{5,4,3,1,0,2:T(2,128)(2,1)S(1)}, u32[]{:S(2)}, u32[]{:S(2)}) collective-permute-start(bf16[2,2,1,8,2,2048]{5,4,3,1,0,2:T(2,128)(2,1)S(1)} %fusion.64), channel_id=1, source_target_pairs={{0,2},{1,3},{2,0},{3,1},{4,6},{5,7},{6,4},{7,5},{8,10},{9,11},{10,... | collective-permute-start | bytes 786440 | tf_op jit(solution)/shard_map/ppermute | solution.py:190
  23.6 10.2 %collective-permute-start.3 = (bf16[2,2,1,8,2,2048]{5,4,3,1,0,2:T(2,128)(2,1)S(1)}, bf16[2,2,1,8,2,2048]{5,4,3,1,0,2:T(2,128)(2,1)S(1)}, u32[]{:S(2)}, u32[]{:S(2)}) collective-permute-start(bf16[2,2,1,8,2,2048]{5,4,3,1,0,2:T(2,128)(2,1)S(1)} %pad_maximum_fusion.9), channel_id=1, source_target_pairs={{0,2},{1,3},{2,0},{3,1},{4,6},{5,7},{6,4},{7,5},{8,10},{9,11},{10,... | collective-permute-start | bytes 786440 | tf_op jit(solution)/shard_map/ppermute | solution.py:190
  30.0 7.1 %collective-permute-start.8 = (bf16[2,2,2,1,8,2,2048]{6,5,4,2,1,3,0:T(2,128)(2,1)S(1)}, bf16[2,2,2,1,8,2,2048]{6,5,4,2,1,3,0:T(2,128)(2,1)S(1)}, u32[]{:S(2)}, u32[]{:S(2)}) collective-permute-start(bf16[2,2,2,1,8,2,2048]{6,5,4,2,1,3,0:T(2,128)(2,1)S(1)} %pad_maximum_fusion.8), channel_id=1, source_target_pairs={{0,1},{1,0},{2,3},{3,2},{4,5},{5,4},{6,7},{7,6},{8,9},{9,8},{10,11... | collective-permute-start | bytes 1572872 | tf_op jit(solution)/shard_map/ppermute | solution.py:190
  35.2 16.3 %collective-permute-start.4 = (bf16[2,2,2,1,8,2,2048]{6,5,4,2,1,3,0:T(2,128)(2,1)S(1)}, bf16[2,2,2,1,8,2,2048]{6,5,4,2,1,3,0:T(2,128)(2,1)S(1)}, u32[]{:S(2)}, u32[]{:S(2)}) collective-permute-start(bf16[2,2,2,1,8,2,2048]{6,5,4,2,1,3,0:T(2,128)(2,1)S(1)} %pad_maximum_fusion.7), channel_id=1, source_target_pairs={{0,1},{1,0},{2,3},{3,2},{4,5},{5,4},{6,7},{7,6},{8,9},{9,8},{10,11... | collective-permute-start | bytes 1572872 | tf_op jit(solution)/shard_map/ppermute | solution.py:190

commit v7 on v5

--- a/solution.py
+++ b/solution.py
@@ -1,6 +1,7 @@
 import math
 
 import jax
+import numpy as np
 import jax.numpy as jnp
 from jax import lax
 from jax.experimental import pallas as pl
@@ -78,9 +79,11 @@
     return total + jnp.dot(left_low, right_high, preferred_element_type=jnp.float32)
 
 
-def inverse_tables(k_rows):
+def inverse_tables(k_order):
     half_radix = RADIX // 2
-    cos_first, sin_first = angle_table(RADIX, k_rows, RADIX)
+    t_index = lax.broadcasted_iota(jnp.int32, (RADIX, k_order.shape[0]), 0)
+    first_angle = (t_index * k_order[None, :] % RADIX).astype(jnp.float32) * (2.0 * math.pi / RADIX)
+    cos_first, sin_first = jnp.cos(first_angle), jnp.sin(first_angle)
     first = jnp.concatenate(
         [
             jnp.concatenate([cos_first, -sin_first], axis=1),
@@ -101,13 +104,13 @@
 def peaks_kernel(spec_ref, bank_ref, fh_ref, fl_ref, tc_ref, ts_ref, sh_ref, sl_ref, out_ref):
     half_radix = RADIX // 2
     block_total = spec_ref.shape[0]
-    step_templates = bank_ref.shape[0]
+    step_templates = bank_ref.shape[1]
     pair_total = step_templates * block_total
     products = []
     scales = []
     for template in range(step_templates):
-        wave_real = bank_ref[template, 0].astype(jnp.float32)
-        wave_imag = bank_ref[template, 1].astype(jnp.float32)
+        wave_real = bank_ref[:, template, 0].astype(jnp.float32).reshape(-1, RADIX)
+        wave_imag = bank_ref[:, template, 1].astype(jnp.float32).reshape(-1, RADIX)
         power_sum = jnp.sum(wave_real * wave_real + wave_imag * wave_imag, keepdims=True)
         norm_scale = 1.0 / jnp.sqrt(BLOCK * power_sum + EPSILON)
         scales.append(norm_scale * norm_scale)
@@ -150,8 +153,10 @@
 
 def window_peaks(spectra, bank, tables):
     block_total, k_rows, _ = spectra.shape
-    template_total = bank.shape[0]
-    step_templates = STEP_TEMPLATES if template_total % STEP_TEMPLATES == 0 else 1
+    template_total = bank.shape[1]
+    bank_block = (bank.shape[0], STEP_TEMPLATES) + bank.shape[2:]
+    bank_map = lambda k: (0, k) + (0,) * (bank.ndim - 2)
+    step_templates = STEP_TEMPLATES
     fixed = lambda k: (0, 0)
     pair_flops = 6 * (2 * RADIX) * (2 * k_rows) * RADIX + 6 * RADIX * (2 * RADIX) * RADIX
     return pl.pallas_call(
@@ -160,7 +165,7 @@
         grid=(template_total // step_templates,),
         in_specs=[
             pl.BlockSpec((block_total, k_rows, 2 * RADIX), lambda k: (0, 0, 0)),
-            pl.BlockSpec((step_templates, 2, k_rows, RADIX), lambda k: (k, 0, 0, 0)),
+            pl.BlockSpec(bank_block, bank_map),
             pl.BlockSpec((2 * RADIX, 2 * k_rows), fixed),
             pl.BlockSpec((2 * RADIX, 2 * k_rows), fixed),
             pl.BlockSpec((RADIX, RADIX), fixed),
@@ -178,24 +183,45 @@
     )(spectra, bank, *tables)
 
 
+def chain_groups(seg_total):
+    distances = []
+    distance = seg_total // 2
+    while distance >= 1:
+        distances.append(distance)
+        distance //= 2
+    inter = distances[:-1]
+    return [tuple(inter[i : i + 2]) for i in range(0, len(inter), 2)] + [tuple(distances[-1:])]
+
+
+def group_offsets(group):
+    offsets = []
+    for position in range(2 ** len(group)):
+        bits = [(position >> (len(group) - 1 - j)) & 1 for j in range(len(group))]
+        offsets.append(sum(bit * distance for bit, distance in zip(bits, group)))
+    return offsets
+
+
+def piece_offsets(seg_total):
+    offsets = np.zeros((1,), np.int32)
+    for group in chain_groups(seg_total):
+        offsets = (np.array(group_offsets(group), np.int32)[:, None] ^ offsets[None, :]).reshape(-1)
+    return offsets
+
+
 def gathered_bank(bank_rows):
     seg_total = lax.axis_size("seg")
-    me = lax.axis_index("seg")
     rows, parts, local_bins = bank_rows.shape
-    held = bank_rows[None]
-    distance = seg_total // 2
-    steps = 0
-    while distance >= 1:
-        pairs = [(i, i ^ distance) for i in range(seg_total)]
-        arrived = lax.ppermute(held, "seg", pairs)
-        upper = (me & distance) != 0
-        held = jnp.stack([jnp.where(upper, arrived, held), jnp.where(upper, held, arrived)], axis=0)
-        distance //= 2
-        steps += 1
-    held = held.reshape((2,) * steps + (rows, parts, local_bins // RADIX, RADIX))
-    order = tuple(reversed(range(steps)))
-    held = jnp.transpose(held, (steps, steps + 1) + order + (steps + 2, steps + 3))
-    return held.reshape(rows, parts, seg_total * local_bins // RADIX, RADIX)
+    held = bank_rows
+    for group in chain_groups(seg_total):
+        arrived = [held]
+        for offset in group_offsets(group)[1:]:
+            pairs = [(i, i ^ offset) for i in range(seg_total)]
+            arrived.append(lax.ppermute(held, "seg", pairs))
+        held = jnp.stack(arrived, axis=0)
+    piece_rows = local_bins // RADIX
+    if piece_rows == 1:
+        return held.reshape(seg_total, rows, parts, RADIX)
+    return held.reshape(seg_total, rows, parts, piece_rows, RADIX)
 
 
 def local(strain, gate_mask, template_bank):
@@ -206,13 +232,18 @@
     before = jnp.concatenate([earlier[None], local_blocks[:-1]], axis=0)
     windows = jnp.concatenate([before, local_blocks], axis=1)
     spectra = forward(windows)
-    tables = inverse_tables(spectra.shape[1])
+    seg_total = lax.axis_size("seg")
+    source = lax.axis_index("seg") ^ jnp.asarray(piece_offsets(seg_total))
+    piece_rows = spectra.shape[1] // seg_total
+    k_order = (source[:, None] * piece_rows + jnp.arange(piece_rows, dtype=jnp.int32)[None, :]).reshape(-1)
+    spectra = jnp.take(spectra, k_order, axis=1)
+    tables = inverse_tables(k_order)
     template_total = template_bank.shape[0]
     results = []
     for start in range(0, template_total, SUBBANK):
         bank = gathered_bank(template_bank[start : start + SUBBANK])
         peaks = window_peaks(spectra, bank, tables)
-        results.append(peaks.reshape(bank.shape[0], block_total * (RADIX // 2)))
+        results.append(peaks.reshape(bank.shape[1], block_total * (RADIX // 2)))
     return jnp.concatenate(results, axis=0)
 
 

time: 66.3 us -> 67.2 us (1.014); the launches traced: 66 us -> 66.2 us
  local copies, waits for them, and re-layouts: 5.59 us -> 8.55 us
  other arithmetic: 16.5 us -> 15.1 us
  waiting for transfers between devices: 3.85 us -> 2.64 us
    reshape x0 -> x2, local copies, waits for them, and re-layouts: none -> 3.24 us  [gathered_bank(): return held.reshape(seg_total, rows, parts, piece_rows, RADIX)]
    another operation x6 -> x1, local copies, waits for them, and re-layouts: 3.62 us -> 1.02 us  [gathered_bank(): held = jnp.stack(arrived, axis=0)]
    another operation x15 -> x10, other arithmetic: 5.46 us -> 7.8 us  [gathered_bank(): held = jnp.stack(arrived, axis=0)]
    select_n x2, other arithmetic: 2.46 us -> 0.98 us  [local(): spectra = jnp.take(spectra, k_order, axis=1)]
    ppermute x8 -> x10, waiting for transfers between devices: 3.84 us -> 2.64 us  [gathered_bank(): arrived.append(lax.ppermute(held, 'seg', pairs))]
    gather x0 -> x1, local copies, waits for them, and re-layouts: none -> 1.13 us  [local(): spectra = jnp.take(spectra, k_order, axis=1)]
    ppermute x8 -> x10, starting transfers between devices: 12.2 us -> 11.1 us  [gathered_bank(): arrived.append(lax.ppermute(held, 'seg', pairs))]
    mul x1, other arithmetic: 1.06 us -> 0.03 us  [local(): gated = strain * gate_mask.astype(jnp.float32)]
  transfers between devices with their start and end apart: 9 -> 11, of which waited for: 3 -> 2; matrix products, arithmetic and copies ran while one was open for 29% -> 30% of each run, Pallas kernels for 16% -> 16%
where the time goes in v7:
time: 67.2 us; the launch traced here: 66.2 us
  Pallas kernels  20.6 us (31%)
  starting transfers between devices  16.5 us (25%)
  other arithmetic  15.1 us (22%)
  local copies, waits for them, and re-layouts  8.55 us (13%)
  waiting for transfers between devices  2.64 us (4%)
  matrix products  2.41 us (4%)
    pallas_call x2, Pallas kernels, window_peaks(): pl.pallas_call(peaks_kernel, out_shape=jax.ShapeDtypeStruct((template_tot...  20.6 us
    ppermute x10, starting transfers between devices, gathered_bank(): arrived.append(lax.ppermute(held, 'seg', pairs))  11.1 us
    another operation x10, other arithmetic, gathered_bank(): held = jnp.stack(arrived, axis=0)  7.8 us
    ppermute x1, starting transfers between devices, passed_along(): return lax.ppermute(value, axis, pairs)  5.42 us
    reshape x2, local copies, waits for them, and re-layouts, gathered_bank(): return held.reshape(seg_total, rows, parts, piece_rows, RADIX)  3.24 us
    ppermute x10, waiting for transfers between devices, gathered_bank(): arrived.append(lax.ppermute(held, 'seg', pairs))  2.64 us
    unnamed x12, local copies, waits for them, and re-layouts  2.1 us
    sin x2, other arithmetic, angle_table(): return (jnp.cos(angle_value), jnp.sin(angle_value))  2 us
  transfers between devices with their start and end apart: 11, of which 2 were waited for; matrix products, arithmetic and copies ran while one was open for 30% of the time, Pallas kernels for 16%

profile of v7, /device:TPU:1, one launch (start us, length us, event | category | flops | bytes accessed | tf_op | source)
XLA Modules:
  0.0 66.2 jit_solution(5251707849299759738)
XLA Ops:
  0.0 1.0 %slice_bitcast_fusion.1 = (bf16[1,8,2,2048]{3,2,1,0:T(2,128)(2,1)S(1)}, bf16[1,8,2,2048]{3,2,1,0:T(2,128)(2,1)S(1)}, bf16[8,2,2048]{2,1,0:T(2,128)(2,1)S(1)}, bf16[8,2,2048]{2,1,0:T(2,128)(2,1)S(1)}) fusion(bf16[16,2,2048]{2,1,0:T(2,128)(2,1)} %param.6), kind=kLoop, calls=%fused_computation.107 | loop fusion | bytes 393216 | tf_op jit(solution)/shard_map/stack | solution.py:220
  1.0 4.2 %collective-permute-start.3 = (bf16[8,2,2048]{2,1,0:T(2,128)(2,1)S(1)}, bf16[8,2,2048]{2,1,0:T(2,128)(2,1)S(1)}, u32[]{:S(2)}, u32[]{:S(2)}) collective-permute-start(bf16[8,2,2048]{2,1,0:T(2,128)(2,1)S(1)} %get-tuple-element.18), channel_id=1, source_target_pairs={{0,12},{1,13},{2,14},{3,15},{4,8},{5,9},{6,10},{7,11},{8,4},{9,5},... | collective-permute-start | bytes 196616 | tf_op jit(solution)/shard_map/ppermute | solution.py:219
  5.2 0.0 collective-permute-start.1
  5.2 0.4 collective-permute-start.2
  5.6 1.1 %collective-permute-start.6 = (bf16[8,2,2048]{2,1,0:T(2,128)(2,1)S(1)}, bf16[8,2,2048]{2,1,0:T(2,128)(2,1)S(1)}, u32[]{:S(2)}, u32[]{:S(2)}) collective-permute-start(bf16[8,2,2048]{2,1,0:T(2,128)(2,1)S(1)} %get-tuple-element.17), channel_id=1, source_target_pairs={{0,4},{1,5},{2,6},{3,7},{4,0},{5,1},{6,2},{7,3},{8,12},{9,13},{10,... | collective-permute-start | bytes 196616 | tf_op jit(solution)/shard_map/ppermute | solution.py:219
  6.7 2.4 %collective-permute-start.7 = (bf16[8,2,2048]{2,1,0:T(2,128)(2,1)S(1)}, bf16[8,2,2048]{2,1,0:T(2,128)(2,1)S(1)}, u32[]{:S(2)}, u32[]{:S(2)}) collective-permute-start(bf16[8,2,2048]{2,1,0:T(2,128)(2,1)S(1)} %get-tuple-element.17), channel_id=1, source_target_pairs={{0,8},{1,9},{2,10},{3,11},{4,12},{5,13},{6,14},{7,15},{8,0},{9,1},... | collective-permute-start | bytes 196616 | tf_op jit(solution)/shard_map/ppermute | solution.py:219
  9.1 1.0 %fusion.37 = (f32[256,256]{1,0:T(8,128)S(1)}, f32[256,256]{1,0:T(8,128)S(1)}) fusion(), kind=kLoop, calls=%fused_computation.75 | loop fusion | flops 983040 | bytes 524288 | tf_op jit(solution)/shard_map/cos | solution.py:32
  10.2 0.1 concatenate.44
  10.3 1.0 %fusion.34 = (f32[256,256]{1,0:T(8,128)S(1)}, f32[256,256]{1,0:T(8,128)S(1)}) fusion(), kind=kLoop, calls=%fused_computation.72 | loop fusion | flops 917504 | bytes 524288 | tf_op jit(solution)/shard_map/sin | solution.py:32
  11.4 0.0 copy-start.4
  11.4 0.7 %copy-done.4 = s32[16]{0:T(128)S(1)} copy-done((s32[16]{0:T(128)S(1)}, s32[16]{0:T(128)}, u32[]{:S(2)}) %copy-start.4) | copy-done | bytes 88
  12.1 0.1 iota_add_fusion
  12.1 0.1 add.128
  12.2 0.1 add.120
  12.3 0.5 fusion.48
  12.9 1.0 %fusion.36 = f32[256,256]{1,0:T(8,128)S(1)} fusion(), kind=kLoop, calls=%fused_computation.74 | loop fusion | flops 917504 | bytes 262144 | tf_op jit(solution)/shard_map/sin | solution.py:32
  13.9 0.1 copy.8
  14.0 0.1 copy.9
  14.1 0.9 %fusion = (bf16[512,256]{1,0:T(8,128)(2,1)}, bf16[512,256]{1,0:T(8,128)(2,1)}) fusion(f32[256,128]{1,0:T(8,128)S(1)} %get-tuple-element.20, f32[256,128]{1,0:T(8,128)S(1)} %get-tuple-element.21, f32[256,128]{1,0:T(8,128)S(1)} %get-tuple-element.19), kind=kLoop, calls=%fused_computation.10 | loop fusion | flops 917504 | bytes 917504 | tf_op jit(solution)/shard_map/convert_element_type | solution.py:73
  15.0 0.9 %fusion.1 = (bf16[512,256]{1,0:T(8,128)(2,1)}, bf16[512,256]{1,0:T(8,128)(2,1)}) fusion(f32[256,256]{1,0:T(8,128)S(1)} %get-tuple-element.22, f32[256,256]{1,0:T(8,128)S(1)} %fusion.36, f32[256,256]{1,0:T(8,128)S(1)} %get-tuple-element.23), kind=kLoop, calls=%fused_computation.11 | loop fusion | flops 1310720 | bytes 1310720 | tf_op jit(solution)/shard_map/convert_element_type | solution.py:73
  15.9 0.0 collective-permute-done.3
  15.9 0.1 collective-permute-start.8
  16.1 0.0 collective-permute-done.1
  16.1 5.4 %collective-permute-start = (f32[32768]{0:T(1024)S(1)}, f32[32768]{0:T(1024)S(1)}, u32[]{:S(2)}, u32[]{:S(2)}) collective-permute-start(f32[32768]{0:T(1024)S(1)} %get-tuple-element.13), channel_id=1, source_target_pairs={{0,1},{1,2},{2,3},{3,4},{4,5},{5,6},{6,7},{7,8},{8,9},{9,10},{10,1... | collective-permute-start | bytes 393224 | tf_op jit(solution)/shard_map/ppermute | solution.py:24
  21.5 0.0 collective-permute-done.2
  21.5 0.5 pad_maximum_fusion.9
  22.0 0.5 fusion.63
  22.5 0.1 collective-permute-start.4
  22.5 0.0 collective-permute-done.6
  22.5 0.0 collective-permute-done.7
  22.6 0.0 collective-permute-done.8
  22.6 0.5 pad_maximum_fusion.10
  23.0 1.5 %collective-permute-start.9 = (bf16[4,8,2,2048]{3,2,1,0:T(2,128)(2,1)S(1)}, bf16[4,8,2,2048]{3,2,1,0:T(2,128)(2,1)S(1)}, u32[]{:S(2)}, u32[]{:S(2)}) collective-permute-start(bf16[4,8,2,2048]{3,2,1,0:T(2,128)(2,1)S(1)} %pad_maximum_fusion.10), channel_id=1, source_target_pairs={{0,2},{1,3},{2,0},{3,1},{4,6},{5,7},{6,4},{7,5},{8,10},{9,11},{10,... | collective-permute-start | bytes 786440 | tf_op jit(solution)/shard_map/ppermute | solution.py:219
  24.5 0.5 fusion.65
  25.0 0.0 collective-permute-done
  25.1 0.1 copy.7
  25.2 0.6 fusion.3
  25.8 0.1 multiply_add_fusion
  25.9 0.9 %convolution_bitcast_fusion.1 = f32[2,128,512]{2,1,0:T(8,128)S(1)} fusion(f32[2,256,256]{2,1,0:T(8,128)S(1)} %get-tuple-element.6, f32[2,256,256]{2,1,0:T(8,128)S(1)} %get-tuple-element.5), kind=kOutput, calls=%fused_computation.2 | convolution fusion | flops 202047488 | bytes 1572864 | tf_op jit(solution)/shard_map/bnf,nk->bkf/dot_general | solution.py:54
  26.8 0.9 %convolution_bitcast_fusion = f32[2,128,512]{2,1,0:T(8,128)S(1)} fusion(f32[2,256,256]{2,1,0:T(8,128)S(1)} %get-tuple-element.6, f32[2,256,256]{2,1,0:T(8,128)S(1)} %get-tuple-element.5), kind=kOutput, calls=%fused_computation.1 | convolution fusion | flops 202047488 | bytes 1572864 | tf_op jit(solution)/shard_map/bnf,nk->bkf/dot_general | solution.py:55
  27.7 0.1 slice_add_fusion
  27.8 0.1 pad_maximum_fusion.6
  27.9 0.4 copy.12
  28.3 1.1 %gather_fusion = f32[128,2,512]{2,1,0:T(2,128)S(1)} fusion(f32[2,128,512]{2,0,1:T(2,128)S(1)} %copy.12, s32[1024]{0:T(1024)S(1)} %pad_clamp_fusion), kind=kCustom, calls=%fused_computation | custom fusion | bytes 1049088 | tf_op jit(solution)/shard_map/jit(_take)/gather | solution.py:239
  29.4 1.0 %fusion.11.spec_ref = f32[2,128,512]{2,1,0:T(8,128)} fusion(f32[128,2,512]{2,1,0:T(2,128)S(1)} %gather_fusion, pred[128]{0:T(512)(128)(4,1)S(1)} %compare_and_fusion), kind=kLoop, calls=%fused_computation.30 | loop fusion | flops 131072 | bytes 1048704 | tf_op jit(solution)/shard_map/jit(_take)/select_n | solution.py:239
  30.4 0.5 collective-permute-done.4
  30.9 0.7 %pad_maximum_fusion.7 = bf16[2,4,8,2,2048]{4,3,2,1,0:T(2,128)(2,1)S(1)} fusion(bf16[1,4,8,2,2048]{4,3,2,1,0:T(2,128)(2,1)S(1)} %bitcast.47, bf16[1,4,8,2,2048]{4,3,2,1,0:T(2,128)(2,1)S(1)} %fusion.63), kind=kLoop, calls=%fused_computation.26 | loop fusion | flops 262144 | bytes 1048576 | tf_op jit(solution)/shard_map/stack | solution.py:220
  31.6 1.2 %collective-permute-start.5 = (bf16[2,4,8,2,2048]{4,3,2,1,0:T(2,128)(2,1)S(1)}, bf16[2,4,8,2,2048]{4,3,2,1,0:T(2,128)(2,1)S(1)}, u32[]{:S(2)}, u32[]{:S(2)}) collective-permute-start(bf16[2,4,8,2,2048]{4,3,2,1,0:T(2,128)(2,1)S(1)} %pad_maximum_fusion.7), channel_id=1, source_target_pairs={{0,1},{1,0},{2,3},{3,2},{4,5},{5,4},{6,7},{7,6},{8,9},{9,8},{10,11... | collective-permute-start | bytes 1572872 | tf_op jit(solution)/shard_map/ppermute | solution.py:219
  32.8 2.2 %collective-permute-done.9 = bf16[4,8,2,2048]{3,2,1,0:T(2,128)(2,1)S(1)} collective-permute-done((bf16[4,8,2,2048]{3,2,1,0:T(2,128)(2,1)S(1)}, bf16[4,8,2,2048]{3,2,1,0:T(2,128)(2,1)S(1)}, u32[]{:S(2)}, u32[]{:S(2)}) %collective-permute-start.9) | collective-permute-done | bytes 262176 | tf_op jit(solution)/shard_map/ppermute | solution.py:219
  35.0 0.7 %pad_maximum_fusion.8 = bf16[2,4,8,2,2048]{4,3,2,1,0:T(2,128)(2,1)S(1)} fusion(bf16[1,4,8,2,2048]{4,3,2,1,0:T(2,128)(2,1)S(1)} %bitcast.49, bf16[1,4,8,2,2048]{4,3,2,1,0:T(2,128)(2,1)S(1)} %fusion.65), kind=kLoop, calls=%fused_computation.28 | loop fusion | flops 262144 | bytes 1048576 | tf_op jit(solution)/shard_map/stack | solution.py:220
  35.8 0.1 collective-permute-start.10
  35.8 0.7 %fusion.62 = bf16[1,2,4,8,2,2048]{5,4,3,2,1,0:T(2,128)(2,1)S(1)} fusion(bf16[1,4,8,2,2048]{4,3,2,1,0:T(2,128)(2,1)S(1)} %bitcast.48, bf16[1,4,8,2,2048]{4,3,2,1,0:T(2,128)(2,1)S(1)} %fusion.63), kind=kLoop, calls=%fused_computation.109 | loop fusion | flops 262144 | bytes 1048576 | tf_op jit(solution)/shard_map/stack | solution.py:220
  36.6 0.7 %fusion.64 = bf16[1,2,4,8,2,2048]{5,4,3,2,1,0:T(2,128)(2,1)S(1)} fusion(bf16[1,4,8,2,2048]{4,3,2,1,0:T(2,128)(2,1)S(1)} %bitcast.50, bf16[1,4,8,2,2048]{4,3,2,1,0:T(2,128)(2,1)S(1)} %fusion.65), kind=kLoop, calls=%fused_computation.111 | loop fusion | flops 262144 | bytes 1048576 | tf_op jit(solution)/shard_map/stack | solution.py:220
  37.3 0.0 collective-permute-done.5
  37.3 1.5 %pad_maximum_fusion.1 = bf16[2,2,4,8,2,2048]{5,4,3,2,1,0:T(2,128)(2,1)S(1)} fusion(bf16[1,2,4,8,2,2048]{5,4,3,2,1,0:T(2,128)(2,1)S(1)} %bitcast.52, bf16[1,2,4,8,2,2048]{5,4,3,2,1,0:T(2,128)(2,1)S(1)} %fusion.62), kind=kLoop, calls=%fused_computation.4 | loop fusion | flops 524288 | bytes 2097152 | tf_op jit(solution)/shard_map/stack | solution.py:220
  38.8 1.7 %reshape.110.bank_ref = bf16[16,8,2,8,256]{4,3,2,1,0:T(8,128)(2,1)} reshape(bf16[2,2,4,8,2,2048]{5,4,3,2,1,0:T(2,128)(2,1)S(1)} %pad_maximum_fusion.1) | data formatting | bytes 2097152 | tf_op jit(solution)/shard_map/reshape | solution.py:224
  40.6 10.3 %shard_map.46 = f32[8,2,128]{2,1,0:T(2,128)} custom-call(f32[2,128,512]{2,1,0:T(8,128)} %fusion.11.spec_ref, bf16[16,8,2,8,256]{4,3,2,1,0:T(8,128)(2,1)} %reshape.110.bank_ref, bf16[512,256]{1,0:T(8,128)(2,1)} %get-tuple-element.12.fh_ref, bf16[512,256]{1,0:T(8,128)(2,1)} %get-tuple-element.11.fl_ref, f32[256,256]{1,0:T(8,128)} %copy-done.1, ...), custom_call_target="tpu_custom_call" | custom-call | flops 6442450944 | bytes 1581056 | tf_op jit(solution)/shard_map/pallas_call | solution.py:162
  50.9 0.7 %copy.26 = f32[1,8,2,128]{3,1,2,0:T(8,128)S(1)} copy(f32[1,8,2,128]{3,2,1,0:T(2,128)} %bitcast.68) | data formatting | bytes 16384
  51.6 0.0 collective-permute-done.10
  51.6 1.5 %pad_maximum_fusion.2 = bf16[2,2,4,8,2,2048]{5,4,3,2,1,0:T(2,128)(2,1)S(1)} fusion(bf16[1,2,4,8,2,2048]{5,4,3,2,1,0:T(2,128)(2,1)S(1)} %bitcast.51, bf16[1,2,4,8,2,2048]{5,4,3,2,1,0:T(2,128)(2,1)S(1)} %fusion.64), kind=kLoop, calls=%fused_computation.5 | loop fusion | flops 524288 | bytes 2097152 | tf_op jit(solution)/shard_map/stack | solution.py:220
  53.0 1.5 %reshape.112.bank_ref = bf16[16,8,2,8,256]{4,3,2,1,0:T(8,128)(2,1)} reshape(bf16[2,2,4,8,2,2048]{5,4,3,2,1,0:T(2,128)(2,1)S(1)} %pad_maximum_fusion.2) | data formatting | bytes 2097152 | tf_op jit(solution)/shard_map/reshape | solution.py:224
  54.6 10.3 %shard_map.47 = f32[8,2,128]{2,1,0:T(2,128)} custom-call(f32[2,128,512]{2,1,0:T(8,128)} %fusion.11.spec_ref, bf16[16,8,2,8,256]{4,3,2,1,0:T(8,128)(2,1)} %reshape.112.bank_ref, bf16[512,256]{1,0:T(8,128)(2,1)} %get-tuple-element.12.fh_ref, bf16[512,256]{1,0:T(8,128)(2,1)} %get-tuple-element.11.fl_ref, f32[256,256]{1,0:T(8,128)} %copy-done.1, ...), custom_call_target="tpu_custom_call" | custom-call | flops 6442450944 | bytes 1581056 | tf_op jit(solution)/shard_map/pallas_call | solution.py:162
  64.9 0.7 %copy.25 = f32[1,8,2,128]{3,1,2,0:T(8,128)S(1)} copy(f32[1,8,2,128]{3,2,1,0:T(2,128)} %bitcast.67) | data formatting | bytes 16384
  65.6 0.6 pad_maximum_fusion.11
  (16 shorter events, 0.2 us)
Async XLA Ops:
  1.0 14.9 %collective-permute-start.3 = (bf16[8,2,2048]{2,1,0:T(2,128)(2,1)S(1)}, bf16[8,2,2048]{2,1,0:T(2,128)(2,1)S(1)}, u32[]{:S(2)}, u32[]{:S(2)}) collective-permute-start(bf16[8,2,2048]{2,1,0:T(2,128)(2,1)S(1)} %get-tuple-element.18), channel_id=1, source_target_pairs={{0,12},{1,13},{2,14},{3,15},{4,8},{5,9},{6,10},{7,11},{8,4},{9,5},... | collective-permute-start | bytes 196616 | tf_op jit(solution)/shard_map/ppermute | solution.py:219
  5.2 10.8 %collective-permute-start.1 = (bf16[8,2,2048]{2,1,0:T(2,128)(2,1)S(1)}, bf16[8,2,2048]{2,1,0:T(2,128)(2,1)S(1)}, u32[]{:S(2)}, u32[]{:S(2)}) collective-permute-start(bf16[8,2,2048]{2,1,0:T(2,128)(2,1)S(1)} %get-tuple-element.18), channel_id=1, source_target_pairs={{0,4},{1,5},{2,6},{3,7},{4,0},{5,1},{6,2},{7,3},{8,12},{9,13},{10,... | collective-permute-start | bytes 196616 | tf_op jit(solution)/shard_map/ppermute | solution.py:219
  5.2 16.2 %collective-permute-start.2 = (bf16[8,2,2048]{2,1,0:T(2,128)(2,1)S(1)}, bf16[8,2,2048]{2,1,0:T(2,128)(2,1)S(1)}, u32[]{:S(2)}, u32[]{:S(2)}) collective-permute-start(bf16[8,2,2048]{2,1,0:T(2,128)(2,1)S(1)} %get-tuple-element.18), channel_id=1, source_target_pairs={{0,8},{1,9},{2,10},{3,11},{4,12},{5,13},{6,14},{7,15},{8,0},{9,1},... | collective-permute-start | bytes 196616 | tf_op jit(solution)/shard_map/ppermute | solution.py:219
  5.6 4.5 %copy-start.2 = (f32[65536]{0:T(1024)S(1)}, f32[65536]{0:T(1024)}, u32[]{:S(2)}) copy-start(f32[65536]{0:T(1024)} %param.4) | copy-start | bytes 786436
  5.6 4.5 %copy-start.3 = (s32[65536]{0:T(1024)S(1)}, s32[65536]{0:T(1024)}, u32[]{:S(2)}) copy-start(s32[65536]{0:T(1024)} %param.5) | copy-start | bytes 786436
  5.6 16.9 %collective-permute-start.6 = (bf16[8,2,2048]{2,1,0:T(2,128)(2,1)S(1)}, bf16[8,2,2048]{2,1,0:T(2,128)(2,1)S(1)}, u32[]{:S(2)}, u32[]{:S(2)}) collective-permute-start(bf16[8,2,2048]{2,1,0:T(2,128)(2,1)S(1)} %get-tuple-element.17), channel_id=1, source_target_pairs={{0,4},{1,5},{2,6},{3,7},{4,0},{5,1},{6,2},{7,3},{8,12},{9,13},{10,... | collective-permute-start | bytes 196616 | tf_op jit(solution)/shard_map/ppermute | solution.py:219
  6.7 15.8 %collective-permute-start.7 = (bf16[8,2,2048]{2,1,0:T(2,128)(2,1)S(1)}, bf16[8,2,2048]{2,1,0:T(2,128)(2,1)S(1)}, u32[]{:S(2)}, u32[]{:S(2)}) collective-permute-start(bf16[8,2,2048]{2,1,0:T(2,128)(2,1)S(1)} %get-tuple-element.17), channel_id=1, source_target_pairs={{0,8},{1,9},{2,10},{3,11},{4,12},{5,13},{6,14},{7,15},{8,0},{9,1},... | collective-permute-start | bytes 196616 | tf_op jit(solution)/shard_map/ppermute | solution.py:219
  11.3 14.4 %copy-start = (f32[256,256]{1,0:T(8,128)}, f32[256,256]{1,0:T(8,128)S(1)}, u32[]{:S(2)}) copy-start(f32[256,256]{1,0:T(8,128)S(1)} %get-tuple-element.24.ts_ref) | copy-start | bytes 786436
  11.3 14.4 %copy-start.1 = (f32[256,256]{1,0:T(8,128)}, f32[256,256]{1,0:T(8,128)S(1)}, u32[]{:S(2)}) copy-start(f32[256,256]{1,0:T(8,128)S(1)} %get-tuple-element.25.tc_ref) | copy-start | bytes 786436
  11.4 0.7 %copy-start.4 = (s32[16]{0:T(128)S(1)}, s32[16]{0:T(128)}, u32[]{:S(2)}) copy-start(s32[16]{0:T(128)} %constant.75.clone) | copy-start | bytes 196
  15.9 6.6 %collective-permute-start.8 = (bf16[8,2,2048]{2,1,0:T(2,128)(2,1)S(1)}, bf16[8,2,2048]{2,1,0:T(2,128)(2,1)S(1)}, u32[]{:S(2)}, u32[]{:S(2)}) collective-permute-start(bf16[8,2,2048]{2,1,0:T(2,128)(2,1)S(1)} %get-tuple-element.17), channel_id=1, source_target_pairs={{0,12},{1,13},{2,14},{3,15},{4,8},{5,9},{6,10},{7,11},{8,4},{9,5},... | collective-permute-start | bytes 196616 | tf_op jit(solution)/shard_map/ppermute | solution.py:219
  16.1 9.0 %collective-permute-start = (f32[32768]{0:T(1024)S(1)}, f32[32768]{0:T(1024)S(1)}, u32[]{:S(2)}, u32[]{:S(2)}) collective-permute-start(f32[32768]{0:T(1024)S(1)} %get-tuple-element.13), channel_id=1, source_target_pairs={{0,1},{1,2},{2,3},{3,4},{4,5},{5,6},{6,7},{7,8},{8,9},{9,10},{10,1... | collective-permute-start | bytes 393224 | tf_op jit(solution)/shard_map/ppermute | solution.py:24
  22.5 8.4 %collective-permute-start.4 = (bf16[4,8,2,2048]{3,2,1,0:T(2,128)(2,1)S(1)}, bf16[4,8,2,2048]{3,2,1,0:T(2,128)(2,1)S(1)}, u32[]{:S(2)}, u32[]{:S(2)}) collective-permute-start(bf16[4,8,2,2048]{3,2,1,0:T(2,128)(2,1)S(1)} %pad_maximum_fusion.9), channel_id=1, source_target_pairs={{0,2},{1,3},{2,0},{3,1},{4,6},{5,7},{6,4},{7,5},{8,10},{9,11},{10,... | collective-permute-start | bytes 786440 | tf_op jit(solution)/shard_map/ppermute | solution.py:219
  23.0 12.0 %collective-permute-start.9 = (bf16[4,8,2,2048]{3,2,1,0:T(2,128)(2,1)S(1)}, bf16[4,8,2,2048]{3,2,1,0:T(2,128)(2,1)S(1)}, u32[]{:S(2)}, u32[]{:S(2)}) collective-permute-start(bf16[4,8,2,2048]{3,2,1,0:T(2,128)(2,1)S(1)} %pad_maximum_fusion.10), channel_id=1, source_target_pairs={{0,2},{1,3},{2,0},{3,1},{4,6},{5,7},{6,4},{7,5},{8,10},{9,11},{10,... | collective-permute-start | bytes 786440 | tf_op jit(solution)/shard_map/ppermute | solution.py:219
  31.6 5.7 %collective-permute-start.5 = (bf16[2,4,8,2,2048]{4,3,2,1,0:T(2,128)(2,1)S(1)}, bf16[2,4,8,2,2048]{4,3,2,1,0:T(2,128)(2,1)S(1)}, u32[]{:S(2)}, u32[]{:S(2)}) collective-permute-start(bf16[2,4,8,2,2048]{4,3,2,1,0:T(2,128)(2,1)S(1)} %pad_maximum_fusion.7), channel_id=1, source_target_pairs={{0,1},{1,0},{2,3},{3,2},{4,5},{5,4},{6,7},{7,6},{8,9},{9,8},{10,11... | collective-permute-start | bytes 1572872 | tf_op jit(solution)/shard_map/ppermute | solution.py:219
  35.8 15.8 %collective-permute-start.10 = (bf16[2,4,8,2,2048]{4,3,2,1,0:T(2,128)(2,1)S(1)}, bf16[2,4,8,2,2048]{4,3,2,1,0:T(2,128)(2,1)S(1)}, u32[]{:S(2)}, u32[]{:S(2)}) collective-permute-start(bf16[2,4,8,2,2048]{4,3,2,1,0:T(2,128)(2,1)S(1)} %pad_maximum_fusion.8), channel_id=1, source_target_pairs={{0,1},{1,0},{2,3},{3,2},{4,5},{5,4},{6,7},{7,6},{8,9},{9,8},{10,11... | collective-permute-start | bytes 1572872 | tf_op jit(solution)/shard_map/ppermute | solution.py:219

commit v8 on v5

--- a/solution.py
+++ b/solution.py
@@ -198,6 +198,16 @@
     return held.reshape(rows, parts, seg_total * local_bins // RADIX, RADIX)
 
 
+def offloaded_bank(bank_rows):
+    seg_total = lax.axis_size("seg")
+    rows, parts, local_bins = bank_rows.shape
+    flat = bank_rows.reshape(1, rows * parts * local_bins)
+    every = lax.all_gather(flat, "seg", axis=0, tiled=True)
+    every = every.reshape(seg_total, rows, parts, local_bins // RADIX, RADIX)
+    every = jnp.transpose(every, (1, 2, 0, 3, 4))
+    return every.reshape(rows, parts, seg_total * local_bins // RADIX, RADIX)
+
+
 def local(strain, gate_mask, template_bank):
     gated = strain * gate_mask.astype(jnp.float32)
     local_blocks = gated.reshape(-1, BLOCK)
@@ -210,7 +220,8 @@
     template_total = template_bank.shape[0]
     results = []
     for start in range(0, template_total, SUBBANK):
-        bank = gathered_bank(template_bank[start : start + SUBBANK])
+        rows = template_bank[start : start + SUBBANK]
+        bank = offloaded_bank(rows) if start == 0 else gathered_bank(rows)
         peaks = window_peaks(spectra, bank, tables)
         results.append(peaks.reshape(bank.shape[0], block_total * (RADIX // 2)))
     return jnp.concatenate(results, axis=0)

time: 66.3 us -> 85.5 us (1.29)
  between operations: 0.33 us -> 13.7 us
  waiting for transfers between devices: 3.85 us -> 10.5 us
  starting transfers between devices: 16.8 us -> 10.8 us
  other arithmetic: 16.5 us -> 20.6 us
  local copies, waits for them, and re-layouts: 5.59 us -> 6.65 us
    all_gather x0 -> x1, other arithmetic: none -> 7.73 us  [offloaded_bank(): every = lax.all_gather(flat, 'seg', axis=0, tiled=True)]
    ppermute x8 -> x4, waiting for transfers between devices: 3.84 us -> 10.5 us  [gathered_bank(): arrived = lax.ppermute(held, 'seg', pairs)]
    ppermute x8 -> x4, starting transfers between devices: 12.2 us -> 6.26 us  [gathered_bank(): arrived = lax.ppermute(held, 'seg', pairs)]
    another operation x15 -> x9, other arithmetic: 5.46 us -> 2.85 us  [gathered_bank(): jnp.stack([jnp.where(upper, arrived, held), jnp.where(upper, held, arrive...]
    another operation x6 -> x3, local copies, waits for them, and re-layouts: 3.62 us -> 1.78 us  [gathered_bank(): jnp.stack([jnp.where(upper, arrived, held), jnp.where(upper, held, arrive...]
    transpose x0 -> x1, local copies, waits for them, and re-layouts: none -> 1.09 us  [offloaded_bank(): every = jnp.transpose(every, (1, 2, 0, 3, 4))]
    select_n x2 -> x1, other arithmetic: 2.46 us -> 1.44 us  [gathered_bank(): jnp.where(upper, arrived, held)]
    slice x0 -> x1, local copies, waits for them, and re-layouts: none -> 0.97 us  [local(): rows = template_bank[start:start + SUBBANK]]
  transfers between devices with their start and end apart: 9 -> 6, of which waited for: 3 -> 2; matrix products, arithmetic and copies ran while one was open for 29% -> 21% of each run, Pallas kernels for 16% -> 12%
where the time goes in v8:
time: 85.5 us; the launch traced here: 85.1 us
  other arithmetic  20.6 us (24%)
  Pallas kernels  20.6 us (24%)
  between operations  13.7 us (16%)
  starting transfers between devices  10.8 us (13%)
  waiting for transfers between devices  10.5 us (12%)
  local copies, waits for them, and re-layouts  6.65 us (8%)
  matrix products  2.41 us (3%)
    pallas_call x2, Pallas kernels, window_peaks(): pl.pallas_call(peaks_kernel, out_shape=jax.ShapeDtypeStruct((template_tot...  20.6 us
    ppermute x4, waiting for transfers between devices, gathered_bank(): arrived = lax.ppermute(held, 'seg', pairs)  10.5 us
    all_gather x1, other arithmetic, offloaded_bank(): every = lax.all_gather(flat, 'seg', axis=0, tiled=True)  7.73 us
    ppermute x4, starting transfers between devices, gathered_bank(): arrived = lax.ppermute(held, 'seg', pairs)  6.26 us
    ppermute x1, starting transfers between devices, passed_along(): return lax.ppermute(value, axis, pairs)  4.54 us
    another operation x9, other arithmetic, gathered_bank(): jnp.stack([jnp.where(upper, arrived, held), jnp.where(upper, held, arrive...  2.85 us
    sin x3, other arithmetic, angle_table(): return (jnp.cos(angle_value), jnp.sin(angle_value))  2.54 us
    unnamed x10, local copies, waits for them, and re-layouts  2.35 us
  transfers between devices with their start and end apart: 6, of which 2 were waited for; matrix products, arithmetic and copies ran while one was open for 21% of the time, Pallas kernels for 12%

profile of v8, /device:TPU:1, one launch (start us, length us, event | category | flops | bytes accessed | tf_op | source)
XLA Modules:
  0.0 85.1 jit_solution(10910791215649670246)
XLA Ops:
  6.5 0.0 all-gather.3.cloned.1.call-start
  6.5 1.1 %convert_multiply_fusion = f32[65536]{0:T(1024)S(1)} fusion(f32[65536]{0:T(1024)} %param.3, s32[65536]{0:T(1024)} %param.4), kind=kLoop, calls=%fused_computation.54 | loop fusion | flops 131072 | bytes 786432 | tf_op jit(solution)/shard_map/mul | solution.py:212
  7.6 4.5 %collective-permute-start = (f32[32768]{0:T(1024)S(1)}, f32[32768]{0:T(1024)S(1)}, u32[]{:S(2)}, u32[]{:S(2)}) collective-permute-start(f32[32768]{0:T(1024)S(1)} %get-tuple-element.15), channel_id=1, source_target_pairs={{0,1},{1,2},{2,3},{3,4},{4,5},{5,6},{6,7},{7,8},{8,9},{9,10},{10,1... | collective-permute-start | bytes 393224 | tf_op jit(solution)/shard_map/ppermute | solution.py:23
  12.2 1.0 %fusion.60 = (bf16[8,2,2048]{2,1,0:T(2,128)(2,1)S(1)}, bf16[1,8,2,2048]{3,2,1,0:T(2,128)(2,1)S(1)}) fusion(bf16[16,2,2048]{2,1,0:T(2,128)(2,1)} %param.5), kind=kLoop, calls=%fused_computation.102 | loop fusion | bytes 262144 | tf_op jit(solution)/shard_map/slice | solution.py:223
  13.1 2.4 %collective-permute-start.1 = (bf16[1,8,2,2048]{3,2,1,0:T(2,128)(2,1)S(1)}, bf16[1,8,2,2048]{3,2,1,0:T(2,128)(2,1)S(1)}, u32[]{:S(2)}, u32[]{:S(2)}) collective-permute-start(bf16[1,8,2,2048]{3,2,1,0:T(2,128)(2,1)S(1)} %get-tuple-element.20), channel_id=1, source_target_pairs={{0,8},{1,9},{2,10},{3,11},{4,12},{5,13},{6,14},{7,15},{8,0},{9,1},... | collective-permute-start | bytes 196616 | tf_op jit(solution)/shard_map/ppermute | solution.py:190
  15.5 0.7 reshape.73
  16.2 0.0 all-gather.3.cloned.1.call-update
  16.3 0.1 concatenate.45
  16.3 1.0 %fusion.34 = (f32[256,256]{1,0:T(8,128)S(1)}, f32[256,256]{1,0:T(8,128)S(1)}) fusion(), kind=kLoop, calls=%fused_computation.72 | loop fusion | flops 983040 | bytes 524288 | tf_op jit(solution)/shard_map/cos | solution.py:31
  17.4 1.0 %fusion.31 = (f32[256,256]{1,0:T(8,128)S(1)}, f32[256,256]{1,0:T(8,128)S(1)}) fusion(), kind=kLoop, calls=%fused_computation.69 | loop fusion | flops 917504 | bytes 524288 | tf_op jit(solution)/shard_map/sin | solution.py:31
  18.4 0.0 copy-start
  18.4 0.0 copy-start.1
  18.4 0.0 copy-start.2
  18.5 0.5 fusion.41
  19.0 0.5 fusion.43
  19.5 1.0 %fusion.33 = f32[256,256]{1,0:T(8,128)S(1)} fusion(), kind=kLoop, calls=%fused_computation.71 | loop fusion | flops 917504 | bytes 262144 | tf_op jit(solution)/shard_map/sin | solution.py:31
  20.5 0.1 copy.35
  20.7 0.1 copy.34
  20.8 0.9 %fusion = (bf16[512,256]{1,0:T(8,128)(2,1)}, bf16[512,256]{1,0:T(8,128)(2,1)}) fusion(f32[256,128]{1,0:T(8,128)S(1)} %get-tuple-element.26, f32[256,128]{1,0:T(8,128)S(1)} %get-tuple-element.25, f32[256,128]{1,0:T(8,128)S(1)} %fusion.43), kind=kLoop, calls=%fused_computation.12 | loop fusion | flops 917504 | bytes 917504 | tf_op jit(solution)/shard_map/convert_element_type | solution.py:72
  21.6 0.9 %fusion.1 = (bf16[512,256]{1,0:T(8,128)(2,1)}, bf16[512,256]{1,0:T(8,128)(2,1)}) fusion(f32[256,256]{1,0:T(8,128)S(1)} %get-tuple-element.21, f32[256,256]{1,0:T(8,128)S(1)} %fusion.33, f32[256,256]{1,0:T(8,128)S(1)} %get-tuple-element.22), kind=kLoop, calls=%fused_computation.13 | loop fusion | flops 1310720 | bytes 1310720 | tf_op jit(solution)/shard_map/convert_element_type | solution.py:72
  22.5 0.0 collective-permute-done.1
  22.5 0.0 copy-done.2
  22.5 0.1 fusion.39
  22.6 0.2 fusion.57
  22.8 1.4 %collective-permute-start.2 = (bf16[2,1,8,2,2048]{4,3,2,0,1:T(2,128)(2,1)S(1)}, bf16[2,1,8,2,2048]{4,3,2,0,1:T(2,128)(2,1)S(1)}, u32[]{:S(2)}, u32[]{:S(2)}) collective-permute-start(bf16[2,1,8,2,2048]{4,3,2,0,1:T(2,128)(2,1)S(1)} %fusion.57), channel_id=1, source_target_pairs={{0,4},{1,5},{2,6},{3,7},{4,0},{5,1},{6,2},{7,3},{8,12},{9,13},{10,... | collective-permute-start | bytes 393224 | tf_op jit(solution)/shard_map/ppermute | solution.py:190
  24.2 0.0 collective-permute-done
  24.2 0.1 copy.33
  24.3 0.6 fusion.3
  24.9 4.3 %collective-permute-done.2 = bf16[2,1,8,2,2048]{4,3,2,0,1:T(2,128)(2,1)S(1)} collective-permute-done((bf16[2,1,8,2,2048]{4,3,2,0,1:T(2,128)(2,1)S(1)}, bf16[2,1,8,2,2048]{4,3,2,0,1:T(2,128)(2,1)S(1)}, u32[]{:S(2)}, u32[]{:S(2)}) %collective-permute-start.2) | collective-permute-done | bytes 131104 | tf_op jit(solution)/shard_map/ppermute | solution.py:190
  29.2 0.2 fusion.28
  29.4 0.2 fusion.27
  29.7 0.4 fusion.58
  30.0 1.3 %collective-permute-start.3 = (bf16[2,2,1,8,2,2048]{5,4,3,1,0,2:T(2,128)(2,1)S(1)}, bf16[2,2,1,8,2,2048]{5,4,3,1,0,2:T(2,128)(2,1)S(1)}, u32[]{:S(2)}, u32[]{:S(2)}) collective-permute-start(bf16[2,2,1,8,2,2048]{5,4,3,1,0,2:T(2,128)(2,1)S(1)} %fusion.58), channel_id=1, source_target_pairs={{0,2},{1,3},{2,0},{3,1},{4,6},{5,7},{6,4},{7,5},{8,10},{9,11},{10,... | collective-permute-start | bytes 786440 | tf_op jit(solution)/shard_map/ppermute | solution.py:190
  31.3 0.0 copy-done
  31.3 0.0 copy-done.1
  31.3 0.1 multiply_add_fusion
  31.4 6.2 %collective-permute-done.3 = bf16[2,2,1,8,2,2048]{5,4,3,1,0,2:T(2,128)(2,1)S(1)} collective-permute-done((bf16[2,2,1,8,2,2048]{5,4,3,1,0,2:T(2,128)(2,1)S(1)}, bf16[2,2,1,8,2,2048]{5,4,3,1,0,2:T(2,128)(2,1)S(1)}, u32[]{:S(2)}, u32[]{:S(2)}) %collective-permute-start.3) | collective-permute-done | bytes 262176 | tf_op jit(solution)/shard_map/ppermute | solution.py:190
  37.6 0.5 fusion.16
  38.1 0.5 fusion.15
  38.5 0.7 pad_maximum_fusion.6
  39.3 1.3 %collective-permute-start.4 = (bf16[2,2,2,1,8,2,2048]{6,5,4,2,1,3,0:T(2,128)(2,1)S(1)}, bf16[2,2,2,1,8,2,2048]{6,5,4,2,1,3,0:T(2,128)(2,1)S(1)}, u32[]{:S(2)}, u32[]{:S(2)}) collective-permute-start(bf16[2,2,2,1,8,2,2048]{6,5,4,2,1,3,0:T(2,128)(2,1)S(1)} %pad_maximum_fusion.6), channel_id=1, source_target_pairs={{0,1},{1,0},{2,3},{3,2},{4,5},{5,4},{6,7},{7,6},{8,9},{9,8},{10,11... | collective-permute-start | bytes 1572872 | tf_op jit(solution)/shard_map/ppermute | solution.py:190
  40.5 0.9 %convolution_bitcast_fusion = f32[2,128,512]{2,1,0:T(8,128)S(1)} fusion(f32[2,256,256]{2,1,0:T(8,128)S(1)} %get-tuple-element.6, f32[2,256,256]{2,1,0:T(8,128)S(1)} %get-tuple-element.5), kind=kOutput, calls=%fused_computation | convolution fusion | flops 202047488 | bytes 1572864 | tf_op jit(solution)/shard_map/bnf,nk->bkf/dot_general | solution.py:54
  41.5 0.9 %convolution_bitcast_fusion.1 = f32[2,128,512]{2,1,0:T(8,128)S(1)} fusion(f32[2,256,256]{2,1,0:T(8,128)S(1)} %get-tuple-element.6, f32[2,256,256]{2,1,0:T(8,128)S(1)} %get-tuple-element.5), kind=kOutput, calls=%fused_computation.1 | convolution fusion | flops 202047488 | bytes 1572864 | tf_op jit(solution)/shard_map/bnf,nk->bkf/dot_general | solution.py:53
  42.4 0.1 slice_add_fusion
  42.4 0.9 %pad_maximum_fusion.5.spec_ref = f32[2,128,512]{2,1,0:T(8,128)} fusion(f32[2,128,256]{2,1,0:T(8,128)S(1)} %get-tuple-element.10, f32[2,128,256]{2,1,0:T(8,128)S(1)} %get-tuple-element.9), kind=kLoop, calls=%fused_computation.27 | loop fusion | flops 131072 | bytes 1048576 | tf_op jit(solution)/shard_map/concatenate | solution.py:55
  43.3 0.0 collective-permute-done.4
  43.3 1.4 %broadcast_select_fusion.1 = (bf16[2,2,2,1,8,2,2048]{6,5,4,2,1,3,0:T(2,128)(2,1)S(1)}, bf16[2,2,2,1,8,2,2048]{6,5,4,2,1,3,0:T(2,128)(2,1)S(1)}) fusion(bf16[2,2,2,1,8,2,2048]{6,5,4,2,1,3,0:T(2,128)(2,1)S(1)} %collective-permute-done.4, pred[]{:T(512)S(6)} %ne.93, bf16[1,2,2,1,8,2,2048]{6,5,4,2,1,3,0:T(2,128)(2,1)S(1)} %fusion.16, ...), kind=kLoop, calls=%fused_computation.7 | loop fusion | flops 786432 | bytes 2097153 | tf_op jit(solution)/shard_map/jit(_where)/select_n | solution.py:192
  44.7 0.3 stack.46
  45.1 0.3 stack.45
  45.4 0.1 pad_maximum_fusion.1
  45.5 1.1 %copy.53 = bf16[2,2,2,2,8,2,8,256]{7,6,0,1,2,3,5,4:T(8,128)(2,1)} copy(bf16[2,2,2,2,8,2,8,256]{7,6,5,4,3,2,1,0:T(8,128)(2,1)S(1)} %pad_maximum_fusion.1) | data formatting | bytes 2097152 | tf_op jit(solution)/shard_map/stack | solution.py:192
  46.6 10.3 %shard_map.38 = f32[8,2,128]{2,1,0:T(2,128)} custom-call(f32[2,128,512]{2,1,0:T(8,128)} %pad_maximum_fusion.5.spec_ref, bf16[8,2,128,256]{3,2,1,0:T(8,128)(2,1)} %bitcast.77, bf16[512,256]{1,0:T(8,128)(2,1)} %get-tuple-element.14.fh_ref, bf16[512,256]{1,0:T(8,128)(2,1)} %get-tuple-element.13.fl_ref, f32[256,256]{1,0:T(8,128)} %copy-done.1, ...), custom_call_target="tpu_custom_call" | custom-call | flops 6442450944 | bytes 1581056 | tf_op jit(solution)/shard_map/pallas_call | solution.py:157
  56.9 0.7 copy.61
  57.6 0.0 all-gather.3.cloned.1.call-done
  57.6 7.7 %reduce = bf16[16,32768]{1,0:T(8,128)(2,1)S(1)} reduce(bf16[16,1,32768]{2,1,0:T(2,128)(2,1)} %all-gather.3.cloned.1.call-done, bf16[]{:T(256)} %constant.63), dimensions={1}, to_apply=%all-gather.reduce_sub_computation | reduce | bytes 2097154 | tf_op jit(solution)/shard_map/all_gather | solution.py:205
  65.4 0.2 copy.54
  65.6 1.1 %copy.60 = bf16[8,2,16,8,256]{4,3,2,1,0:T(8,128)(2,1)} copy(bf16[8,2,16,8,256]{4,3,1,0,2:T(8,128)(2,1)S(1)} %bitcast.75) | data formatting | bytes 2097152 | tf_op jit(solution)/shard_map/transpose | solution.py:207
  66.7 10.3 %shard_map.37 = f32[8,2,128]{2,1,0:T(2,128)} custom-call(f32[2,128,512]{2,1,0:T(8,128)} %pad_maximum_fusion.5.spec_ref, bf16[8,2,128,256]{3,2,1,0:T(8,128)(2,1)} %bitcast.76, bf16[512,256]{1,0:T(8,128)(2,1)} %get-tuple-element.14.fh_ref, bf16[512,256]{1,0:T(8,128)(2,1)} %get-tuple-element.13.fl_ref, f32[256,256]{1,0:T(8,128)} %copy-done.1, ...), custom_call_target="tpu_custom_call" | custom-call | flops 6442450944 | bytes 1581056 | tf_op jit(solution)/shard_map/pallas_call | solution.py:157
  77.0 0.7 copy.62
  77.7 0.6 pad_maximum_fusion.9
  (3 shorter events, 0.1 us)
Async XLA Ops:
  6.5 51.1 %all-gather.3.cloned.1.call-start = ((), (), s32[]{:S(2)}) async-start(), calls=%async_computation | async-start | bytes 2228224 | tf_op jit(solution)/shard_map/all_gather | solution.py:205
  7.6 16.6 %collective-permute-start = (f32[32768]{0:T(1024)S(1)}, f32[32768]{0:T(1024)S(1)}, u32[]{:S(2)}, u32[]{:S(2)}) collective-permute-start(f32[32768]{0:T(1024)S(1)} %get-tuple-element.15), channel_id=1, source_target_pairs={{0,1},{1,2},{2,3},{3,4},{4,5},{5,6},{6,7},{7,8},{8,9},{9,10},{10,1... | collective-permute-start | bytes 393224 | tf_op jit(solution)/shard_map/ppermute | solution.py:23
  13.1 9.4 %collective-permute-start.1 = (bf16[1,8,2,2048]{3,2,1,0:T(2,128)(2,1)S(1)}, bf16[1,8,2,2048]{3,2,1,0:T(2,128)(2,1)S(1)}, u32[]{:S(2)}, u32[]{:S(2)}) collective-permute-start(bf16[1,8,2,2048]{3,2,1,0:T(2,128)(2,1)S(1)} %get-tuple-element.20), channel_id=1, source_target_pairs={{0,8},{1,9},{2,10},{3,11},{4,12},{5,13},{6,14},{7,15},{8,0},{9,1},... | collective-permute-start | bytes 196616 | tf_op jit(solution)/shard_map/ppermute | solution.py:190
  18.4 12.9 %copy-start = (f32[256,256]{1,0:T(8,128)}, f32[256,256]{1,0:T(8,128)S(1)}, u32[]{:S(2)}) copy-start(f32[256,256]{1,0:T(8,128)S(1)} %get-tuple-element.23.ts_ref) | copy-start | bytes 786436
  18.4 12.9 %copy-start.1 = (f32[256,256]{1,0:T(8,128)}, f32[256,256]{1,0:T(8,128)S(1)}, u32[]{:S(2)}) copy-start(f32[256,256]{1,0:T(8,128)S(1)} %get-tuple-element.24.tc_ref) | copy-start | bytes 786436
  18.4 4.1 %copy-start.2 = (bf16[16,2,2048]{2,1,0:T(2,128)(2,1)S(1)}, bf16[16,2,2048]{2,1,0:T(2,128)(2,1)}, u32[]{:S(2)}) copy-start(bf16[16,2,2048]{2,1,0:T(2,128)(2,1)} %param.5) | copy-start | bytes 393220
  22.8 6.4 %collective-permute-start.2 = (bf16[2,1,8,2,2048]{4,3,2,0,1:T(2,128)(2,1)S(1)}, bf16[2,1,8,2,2048]{4,3,2,0,1:T(2,128)(2,1)S(1)}, u32[]{:S(2)}, u32[]{:S(2)}) collective-permute-start(bf16[2,1,8,2,2048]{4,3,2,0,1:T(2,128)(2,1)S(1)} %fusion.57), channel_id=1, source_target_pairs={{0,4},{1,5},{2,6},{3,7},{4,0},{5,1},{6,2},{7,3},{8,12},{9,13},{10,... | collective-permute-start | bytes 393224 | tf_op jit(solution)/shard_map/ppermute | solution.py:190
  30.0 7.6 %collective-permute-start.3 = (bf16[2,2,1,8,2,2048]{5,4,3,1,0,2:T(2,128)(2,1)S(1)}, bf16[2,2,1,8,2,2048]{5,4,3,1,0,2:T(2,128)(2,1)S(1)}, u32[]{:S(2)}, u32[]{:S(2)}) collective-permute-start(bf16[2,2,1,8,2,2048]{5,4,3,1,0,2:T(2,128)(2,1)S(1)} %fusion.58), channel_id=1, source_target_pairs={{0,2},{1,3},{2,0},{3,1},{4,6},{5,7},{6,4},{7,5},{8,10},{9,11},{10,... | collective-permute-start | bytes 786440 | tf_op jit(solution)/shard_map/ppermute | solution.py:190
  39.3 4.0 %collective-permute-start.4 = (bf16[2,2,2,1,8,2,2048]{6,5,4,2,1,3,0:T(2,128)(2,1)S(1)}, bf16[2,2,2,1,8,2,2048]{6,5,4,2,1,3,0:T(2,128)(2,1)S(1)}, u32[]{:S(2)}, u32[]{:S(2)}) collective-permute-start(bf16[2,2,2,1,8,2,2048]{6,5,4,2,1,3,0:T(2,128)(2,1)S(1)} %pad_maximum_fusion.6), channel_id=1, source_target_pairs={{0,1},{1,0},{2,3},{3,2},{4,5},{5,4},{6,7},{7,6},{8,9},{9,8},{10,11... | collective-permute-start | bytes 1572872 | tf_op jit(solution)/shard_map/ppermute | solution.py:190
Sparse Core Ops, SparseCore 0:
  16.4 40.7 all-gather.2

commit v9 on v7

--- a/solution.py
+++ b/solution.py
@@ -104,13 +104,13 @@
 def peaks_kernel(spec_ref, bank_ref, fh_ref, fl_ref, tc_ref, ts_ref, sh_ref, sl_ref, out_ref):
     half_radix = RADIX // 2
     block_total = spec_ref.shape[0]
-    step_templates = bank_ref.shape[1]
+    step_templates = bank_ref.shape[0]
     pair_total = step_templates * block_total
     products = []
     scales = []
     for template in range(step_templates):
-        wave_real = bank_ref[:, template, 0].astype(jnp.float32).reshape(-1, RADIX)
-        wave_imag = bank_ref[:, template, 1].astype(jnp.float32).reshape(-1, RADIX)
+        wave_real = bank_ref[template, 0].astype(jnp.float32)
+        wave_imag = bank_ref[template, 1].astype(jnp.float32)
         power_sum = jnp.sum(wave_real * wave_real + wave_imag * wave_imag, keepdims=True)
         norm_scale = 1.0 / jnp.sqrt(BLOCK * power_sum + EPSILON)
         scales.append(norm_scale * norm_scale)
@@ -153,9 +153,9 @@
 
 def window_peaks(spectra, bank, tables):
     block_total, k_rows, _ = spectra.shape
-    template_total = bank.shape[1]
-    bank_block = (bank.shape[0], STEP_TEMPLATES) + bank.shape[2:]
-    bank_map = lambda k: (0, k) + (0,) * (bank.ndim - 2)
+    template_total = bank.shape[0]
+    bank_block = (STEP_TEMPLATES, 2, k_rows, RADIX)
+    bank_map = lambda k: (k, 0, 0, 0)
     step_templates = STEP_TEMPLATES
     fixed = lambda k: (0, 0)
     pair_flops = 6 * (2 * RADIX) * (2 * k_rows) * RADIX + 6 * RADIX * (2 * RADIX) * RADIX
@@ -189,8 +189,7 @@
     while distance >= 1:
         distances.append(distance)
         distance //= 2
-    inter = distances[:-1]
-    return [tuple(inter[i : i + 2]) for i in range(0, len(inter), 2)] + [tuple(distances[-1:])]
+    return [(distance,) for distance in distances]
 
 
 def group_offsets(group):
@@ -218,10 +217,8 @@
             pairs = [(i, i ^ offset) for i in range(seg_total)]
             arrived.append(lax.ppermute(held, "seg", pairs))
         held = jnp.stack(arrived, axis=0)
-    piece_rows = local_bins // RADIX
-    if piece_rows == 1:
-        return held.reshape(seg_total, rows, parts, RADIX)
-    return held.reshape(seg_total, rows, parts, piece_rows, RADIX)
+    held = held.reshape(seg_total, rows, parts, local_bins)
+    return jnp.transpose(held, (1, 2, 0, 3)).reshape(rows, parts, seg_total * local_bins // RADIX, RADIX)
 
 
 def local(strain, gate_mask, template_bank):
@@ -243,7 +240,7 @@
     for start in range(0, template_total, SUBBANK):
         bank = gathered_bank(template_bank[start : start + SUBBANK])
         peaks = window_peaks(spectra, bank, tables)
-        results.append(peaks.reshape(bank.shape[1], block_total * (RADIX // 2)))
+        results.append(peaks.reshape(bank.shape[0], block_total * (RADIX // 2)))
     return jnp.concatenate(results, axis=0)
 
 

time: 67.2 us -> 69.6 us (1.036); the launches traced: 66.2 us -> 69.3 us
  waiting for transfers between devices: 2.64 us -> 9.34 us
  starting transfers between devices: 16.5 us -> 11.8 us
  other arithmetic: 15.1 us -> 16.6 us
    ppermute x10 -> x8, waiting for transfers between devices: 2.64 us -> 9.34 us  [gathered_bank(): arrived.append(lax.ppermute(held, 'seg', pairs))]
    ppermute x10 -> x8, starting transfers between devices: 11.1 us -> 7.14 us  [gathered_bank(): arrived.append(lax.ppermute(held, 'seg', pairs))]
    mul x1, other arithmetic: 0.03 us -> 1.06 us  [local(): gated = strain * gate_mask.astype(jnp.float32)]
    another operation x1, local copies, waits for them, and re-layouts: 1.02 us -> 0.15 us  [gathered_bank(): held = jnp.stack(arrived, axis=0)]
    ppermute x1, starting transfers between devices: 5.42 us -> 4.67 us  [passed_along(): return lax.ppermute(value, axis, pairs)]
    reshape x2 -> x4, local copies, waits for them, and re-layouts: 3.24 us -> 3.76 us  [the longest x2 2.61 us: gathered_bank(): jnp.transpose(held, (1, 2, 0, 3))]
    another operation x10 -> x14, other arithmetic: 7.8 us -> 8.31 us  [gathered_bank(): held = jnp.stack(arrived, axis=0)]
    unnamed x12 -> x10, local copies, waits for them, and re-layouts: 2.1 us -> 2.1 us
  transfers between devices with their start and end apart: 11 -> 9, of which waited for: 2 -> 2; matrix products, arithmetic and copies ran while one was open for 30% -> 30% of each run, Pallas kernels for 16% -> 15%
where the time goes in v9:
time: 69.6 us; the launch traced here: 69.3 us
  Pallas kernels  20.5 us (29%)
  other arithmetic  16.6 us (24%)
  starting transfers between devices  11.8 us (17%)
  waiting for transfers between devices  9.34 us (13%)
  local copies, waits for them, and re-layouts  8.21 us (12%)
  matrix products  2.41 us (3%)
    pallas_call x2, Pallas kernels, window_peaks(): pl.pallas_call(peaks_kernel, out_shape=jax.ShapeDtypeStruct((template_tot...  20.5 us
    ppermute x8, waiting for transfers between devices, gathered_bank(): arrived.append(lax.ppermute(held, 'seg', pairs))  9.34 us
    another operation x14, other arithmetic, gathered_bank(): held = jnp.stack(arrived, axis=0)  8.31 us
    ppermute x8, starting transfers between devices, gathered_bank(): arrived.append(lax.ppermute(held, 'seg', pairs))  7.14 us
    ppermute x1, starting transfers between devices, passed_along(): return lax.ppermute(value, axis, pairs)  4.67 us
    reshape x2, local copies, waits for them, and re-layouts, gathered_bank(): jnp.transpose(held, (1, 2, 0, 3))  2.61 us
    unnamed x10, local copies, waits for them, and re-layouts  2.1 us
    sin x2, other arithmetic, angle_table(): return (jnp.cos(angle_value), jnp.sin(angle_value))  2 us
  transfers between devices with their start and end apart: 9, of which 2 were waited for; matrix products, arithmetic and copies ran while one was open for 30% of the time, Pallas kernels for 15%

profile of v9, /device:TPU:1, one launch (start us, length us, event | category | flops | bytes accessed | tf_op | source)
XLA Modules:
  0.0 69.3 jit_solution(11243111388938940410)
XLA Ops:
  0.0 1.1 %convert_multiply_fusion = f32[65536]{0:T(1024)S(1)} fusion(f32[65536]{0:T(1024)} %param.4, s32[65536]{0:T(1024)} %param.5), kind=kLoop, calls=%fused_computation.54 | loop fusion | flops 131072 | bytes 786432 | tf_op jit(solution)/shard_map/mul | solution.py:225
  1.1 0.0 copy-start.2
  1.1 4.7 %collective-permute-start = (f32[32768]{0:T(1024)S(1)}, f32[32768]{0:T(1024)S(1)}, u32[]{:S(2)}, u32[]{:S(2)}) collective-permute-start(f32[32768]{0:T(1024)S(1)} %get-tuple-element.13), channel_id=1, source_target_pairs={{0,1},{1,2},{2,3},{3,4},{4,5},{5,6},{6,7},{7,8},{8,9},{9,10},{10,1... | collective-permute-start | bytes 393224 | tf_op jit(solution)/shard_map/ppermute | solution.py:24
  5.8 0.2 slice_bitcast_fusion.1
  5.9 2.4 %collective-permute-start.1 = (bf16[8,2,2048]{2,1,0:T(2,128)(2,1)S(1)}, bf16[8,2,2048]{2,1,0:T(2,128)(2,1)S(1)}, u32[]{:S(2)}, u32[]{:S(2)}) collective-permute-start(bf16[8,2,2048]{2,1,0:T(2,128)(2,1)S(1)} %get-tuple-element.18), channel_id=1, source_target_pairs={{0,8},{1,9},{2,10},{3,11},{4,12},{5,13},{6,14},{7,15},{8,0},{9,1},... | collective-permute-start | bytes 196616 | tf_op jit(solution)/shard_map/ppermute | solution.py:218
  8.3 0.1 collective-permute-start.5
  8.4 1.0 %fusion.37 = (f32[256,256]{1,0:T(8,128)S(1)}, f32[256,256]{1,0:T(8,128)S(1)}) fusion(), kind=kLoop, calls=%fused_computation.79 | loop fusion | flops 983040 | bytes 524288 | tf_op jit(solution)/shard_map/cos | solution.py:32
  9.4 0.1 concatenate.44
  9.5 1.0 %fusion.34 = (f32[256,256]{1,0:T(8,128)S(1)}, f32[256,256]{1,0:T(8,128)S(1)}) fusion(), kind=kLoop, calls=%fused_computation.76 | loop fusion | flops 917504 | bytes 524288 | tf_op jit(solution)/shard_map/sin | solution.py:32
  10.6 0.0 copy-start.3
  10.6 0.7 copy-done.3
  11.3 0.1 iota_add_fusion
  11.4 0.1 add.128
  11.5 0.1 add.120
  11.6 0.5 fusion.48
  12.1 1.0 %fusion.36 = f32[256,256]{1,0:T(8,128)S(1)} fusion(), kind=kLoop, calls=%fused_computation.78 | loop fusion | flops 917504 | bytes 262144 | tf_op jit(solution)/shard_map/sin | solution.py:32
  13.1 0.1 copy.10
  13.2 0.1 copy.11
  13.4 0.9 %fusion = (bf16[512,256]{1,0:T(8,128)(2,1)}, bf16[512,256]{1,0:T(8,128)(2,1)}) fusion(f32[256,128]{1,0:T(8,128)S(1)} %get-tuple-element.20, f32[256,128]{1,0:T(8,128)S(1)} %get-tuple-element.21, f32[256,128]{1,0:T(8,128)S(1)} %get-tuple-element.19), kind=kLoop, calls=%fused_computation.12 | loop fusion | flops 917504 | bytes 917504 | tf_op jit(solution)/shard_map/convert_element_type | solution.py:73
  14.3 0.9 %fusion.1 = (bf16[512,256]{1,0:T(8,128)(2,1)}, bf16[512,256]{1,0:T(8,128)(2,1)}) fusion(f32[256,256]{1,0:T(8,128)S(1)} %get-tuple-element.22, f32[256,256]{1,0:T(8,128)S(1)} %fusion.36, f32[256,256]{1,0:T(8,128)S(1)} %get-tuple-element.23), kind=kLoop, calls=%fused_computation.13 | loop fusion | flops 1310720 | bytes 1310720 | tf_op jit(solution)/shard_map/convert_element_type | solution.py:73
  15.1 0.2 pad_maximum_fusion.11
  15.3 0.2 fusion.64
  15.5 1.4 %collective-permute-start.2 = (bf16[2,8,2,2048]{3,2,1,0:T(2,128)(2,1)S(1)}, bf16[2,8,2,2048]{3,2,1,0:T(2,128)(2,1)S(1)}, u32[]{:S(2)}, u32[]{:S(2)}) collective-permute-start(bf16[2,8,2,2048]{3,2,1,0:T(2,128)(2,1)S(1)} %pad_maximum_fusion.11), channel_id=1, source_target_pairs={{0,4},{1,5},{2,6},{3,7},{4,0},{5,1},{6,2},{7,3},{8,12},{9,13},{10,... | collective-permute-start | bytes 393224 | tf_op jit(solution)/shard_map/ppermute | solution.py:218
  16.9 0.0 collective-permute-done.5
  16.9 0.2 pad_maximum_fusion.12
  17.1 0.2 collective-permute-start.6
  17.3 0.2 fusion.67
  17.6 0.1 copy.9
  17.7 0.6 fusion.3
  18.3 0.1 multiply_add_fusion
  18.4 0.9 %convolution_bitcast_fusion.1 = f32[2,128,512]{2,1,0:T(8,128)S(1)} fusion(f32[2,256,256]{2,1,0:T(8,128)S(1)} %get-tuple-element.6, f32[2,256,256]{2,1,0:T(8,128)S(1)} %get-tuple-element.5), kind=kOutput, calls=%fused_computation.2 | convolution fusion | flops 202047488 | bytes 1572864 | tf_op jit(solution)/shard_map/bnf,nk->bkf/dot_general | solution.py:54
  19.3 0.9 %convolution_bitcast_fusion = f32[2,128,512]{2,1,0:T(8,128)S(1)} fusion(f32[2,256,256]{2,1,0:T(8,128)S(1)} %get-tuple-element.6, f32[2,256,256]{2,1,0:T(8,128)S(1)} %get-tuple-element.5), kind=kOutput, calls=%fused_computation.1 | convolution fusion | flops 202047488 | bytes 1572864 | tf_op jit(solution)/shard_map/bnf,nk->bkf/dot_general | solution.py:55
  20.2 0.1 slice_add_fusion
  20.3 0.1 pad_maximum_fusion.6
  20.4 0.4 copy.14
  20.8 1.1 %gather_fusion = f32[128,2,512]{2,1,0:T(2,128)S(1)} fusion(f32[2,128,512]{2,0,1:T(2,128)S(1)} %copy.14, s32[1024]{0:T(1024)S(1)} %pad_clamp_fusion), kind=kCustom, calls=%fused_computation | custom fusion | bytes 1049088 | tf_op jit(solution)/shard_map/jit(_take)/gather | solution.py:236
  21.9 1.0 %fusion.11.spec_ref = f32[2,128,512]{2,1,0:T(8,128)} fusion(f32[128,2,512]{2,1,0:T(2,128)S(1)} %gather_fusion, pred[128]{0:T(512)(128)(4,1)S(1)} %compare_and_fusion), kind=kLoop, calls=%fused_computation.32 | loop fusion | flops 131072 | bytes 1048704 | tf_op jit(solution)/shard_map/jit(_take)/select_n | solution.py:236
  22.9 0.0 collective-permute-done.2
  22.9 0.4 pad_maximum_fusion.9
  23.3 1.3 %collective-permute-start.3 = (bf16[2,2,8,2,2048]{4,3,2,1,0:T(2,128)(2,1)S(1)}, bf16[2,2,8,2,2048]{4,3,2,1,0:T(2,128)(2,1)S(1)}, u32[]{:S(2)}, u32[]{:S(2)}) collective-permute-start(bf16[2,2,8,2,2048]{4,3,2,1,0:T(2,128)(2,1)S(1)} %pad_maximum_fusion.9), channel_id=1, source_target_pairs={{0,2},{1,3},{2,0},{3,1},{4,6},{5,7},{6,4},{7,5},{8,10},{9,11},{10,... | collective-permute-start | bytes 786440 | tf_op jit(solution)/shard_map/ppermute | solution.py:218
  24.6 0.4 fusion.63
  25.0 0.4 pad_maximum_fusion.10
  25.3 0.3 collective-permute-start.7
  25.6 0.4 fusion.66
  26.0 5.5 %collective-permute-done.3 = bf16[2,2,8,2,2048]{4,3,2,1,0:T(2,128)(2,1)S(1)} collective-permute-done((bf16[2,2,8,2,2048]{4,3,2,1,0:T(2,128)(2,1)S(1)}, bf16[2,2,8,2,2048]{4,3,2,1,0:T(2,128)(2,1)S(1)}, u32[]{:S(2)}, u32[]{:S(2)}) %collective-permute-start.3) | collective-permute-done | bytes 262176 | tf_op jit(solution)/shard_map/ppermute | solution.py:218
  31.5 0.9 %pad_maximum_fusion.7 = bf16[2,2,2,8,2,2048]{5,4,3,2,1,0:T(2,128)(2,1)S(1)} fusion(bf16[1,2,2,8,2,2048]{5,4,3,2,1,0:T(2,128)(2,1)S(1)} %bitcast.65, bf16[1,2,2,8,2,2048]{5,4,3,2,1,0:T(2,128)(2,1)S(1)} %fusion.63), kind=kLoop, calls=%fused_computation.28 | loop fusion | flops 262144 | bytes 1048576 | tf_op jit(solution)/shard_map/stack | solution.py:219
  32.4 0.8 %collective-permute-start.4 = (bf16[2,2,2,8,2,2048]{5,4,3,2,1,0:T(2,128)(2,1)S(1)}, bf16[2,2,2,8,2,2048]{5,4,3,2,1,0:T(2,128)(2,1)S(1)}, u32[]{:S(2)}, u32[]{:S(2)}) collective-permute-start(bf16[2,2,2,8,2,2048]{5,4,3,2,1,0:T(2,128)(2,1)S(1)} %pad_maximum_fusion.7), channel_id=1, source_target_pairs={{0,1},{1,0},{2,3},{3,2},{4,5},{5,4},{6,7},{7,6},{8,9},{9,8},{10,11... | collective-permute-start | bytes 1572872 | tf_op jit(solution)/shard_map/ppermute | solution.py:218
  33.2 3.9 %collective-permute-done.7 = bf16[2,2,8,2,2048]{4,3,2,1,0:T(2,128)(2,1)S(1)} collective-permute-done((bf16[2,2,8,2,2048]{4,3,2,1,0:T(2,128)(2,1)S(1)}, bf16[2,2,8,2,2048]{4,3,2,1,0:T(2,128)(2,1)S(1)}, u32[]{:S(2)}, u32[]{:S(2)}) %collective-permute-start.7) | collective-permute-done | bytes 262176 | tf_op jit(solution)/shard_map/ppermute | solution.py:218
  37.1 0.7 %pad_maximum_fusion.8 = bf16[2,2,2,8,2,2048]{5,4,3,2,1,0:T(2,128)(2,1)S(1)} fusion(bf16[1,2,2,8,2,2048]{5,4,3,2,1,0:T(2,128)(2,1)S(1)} %bitcast.67, bf16[1,2,2,8,2,2048]{5,4,3,2,1,0:T(2,128)(2,1)S(1)} %fusion.66), kind=kLoop, calls=%fused_computation.30 | loop fusion | flops 262144 | bytes 1048576 | tf_op jit(solution)/shard_map/stack | solution.py:219
  37.8 0.7 collective-permute-start.8
  38.5 0.7 %fusion.62 = bf16[1,2,2,2,8,2,2048]{6,5,4,3,2,1,0:T(2,128)(2,1)S(1)} fusion(bf16[1,2,2,8,2,2048]{5,4,3,2,1,0:T(2,128)(2,1)S(1)} %bitcast.66, bf16[1,2,2,8,2,2048]{5,4,3,2,1,0:T(2,128)(2,1)S(1)} %fusion.63), kind=kLoop, calls=%fused_computation.113 | loop fusion | flops 262144 | bytes 1048576 | tf_op jit(solution)/shard_map/stack | solution.py:219
  39.2 0.7 %fusion.65 = bf16[1,2,2,2,8,2,2048]{6,5,4,3,2,1,0:T(2,128)(2,1)S(1)} fusion(bf16[1,2,2,8,2,2048]{5,4,3,2,1,0:T(2,128)(2,1)S(1)} %bitcast.68, bf16[1,2,2,8,2,2048]{5,4,3,2,1,0:T(2,128)(2,1)S(1)} %fusion.66), kind=kLoop, calls=%fused_computation.116 | loop fusion | flops 262144 | bytes 1048576 | tf_op jit(solution)/shard_map/stack | solution.py:219
  40.0 1.5 %pad_maximum_fusion.1 = bf16[2,2,2,2,8,2,2048]{6,5,4,3,2,1,0:T(2,128)(2,1)S(1)} fusion(bf16[1,2,2,2,8,2,2048]{6,5,4,3,2,1,0:T(2,128)(2,1)S(1)} %bitcast.70, bf16[1,2,2,2,8,2,2048]{6,5,4,3,2,1,0:T(2,128)(2,1)S(1)} %fusion.62), kind=kLoop, calls=%fused_computation.4 | loop fusion | flops 524288 | bytes 2097152 | tf_op jit(solution)/shard_map/stack | solution.py:219
  41.5 0.6 copy.32
  42.1 1.3 %reshape.117.bank_ref = bf16[8,2,128,256]{3,2,1,0:T(8,128)(2,1)} reshape(bf16[8,2,16,2048]{3,2,1,0:T(8,128)(2,1)S(1)} %bitcast.63) | data formatting | bytes 2097152 | tf_op jit(solution)/shard_map/reshape | solution.py:221
  43.4 10.3 %shard_map.46 = f32[8,2,128]{2,1,0:T(2,128)} custom-call(f32[2,128,512]{2,1,0:T(8,128)} %fusion.11.spec_ref, bf16[8,2,128,256]{3,2,1,0:T(8,128)(2,1)} %reshape.117.bank_ref, bf16[512,256]{1,0:T(8,128)(2,1)} %get-tuple-element.12.fh_ref, bf16[512,256]{1,0:T(8,128)(2,1)} %get-tuple-element.11.fl_ref, f32[256,256]{1,0:T(8,128)} %copy-done.1, ...), custom_call_target="tpu_custom_call" | custom-call | flops 6442450944 | bytes 1581056 | tf_op jit(solution)/shard_map/pallas_call | solution.py:162
  53.6 0.7 %copy.34 = f32[1,8,2,128]{3,1,2,0:T(8,128)S(1)} copy(f32[1,8,2,128]{3,2,1,0:T(2,128)} %bitcast.82) | data formatting | bytes 16384
  54.3 0.0 collective-permute-done.8
  54.3 1.5 %pad_maximum_fusion.2 = bf16[2,2,2,2,8,2,2048]{6,5,4,3,2,1,0:T(2,128)(2,1)S(1)} fusion(bf16[1,2,2,2,8,2,2048]{6,5,4,3,2,1,0:T(2,128)(2,1)S(1)} %bitcast.69, bf16[1,2,2,2,8,2,2048]{6,5,4,3,2,1,0:T(2,128)(2,1)S(1)} %fusion.65), kind=kLoop, calls=%fused_computation.5 | loop fusion | flops 524288 | bytes 2097152 | tf_op jit(solution)/shard_map/stack | solution.py:219
  55.8 0.6 copy.31
  56.4 1.3 %reshape.120.bank_ref = bf16[8,2,128,256]{3,2,1,0:T(8,128)(2,1)} reshape(bf16[8,2,16,2048]{3,2,1,0:T(8,128)(2,1)S(1)} %bitcast.64) | data formatting | bytes 2097152 | tf_op jit(solution)/shard_map/reshape | solution.py:221
  57.7 10.3 %shard_map.47 = f32[8,2,128]{2,1,0:T(2,128)} custom-call(f32[2,128,512]{2,1,0:T(8,128)} %fusion.11.spec_ref, bf16[8,2,128,256]{3,2,1,0:T(8,128)(2,1)} %reshape.120.bank_ref, bf16[512,256]{1,0:T(8,128)(2,1)} %get-tuple-element.12.fh_ref, bf16[512,256]{1,0:T(8,128)(2,1)} %get-tuple-element.11.fl_ref, f32[256,256]{1,0:T(8,128)} %copy-done.1, ...), custom_call_target="tpu_custom_call" | custom-call | flops 6442450944 | bytes 1581056 | tf_op jit(solution)/shard_map/pallas_call | solution.py:162
  68.0 0.7 %copy.33 = f32[1,8,2,128]{3,1,2,0:T(8,128)S(1)} copy(f32[1,8,2,128]{3,2,1,0:T(2,128)} %bitcast.81) | data formatting | bytes 16384
  68.7 0.6 pad_maximum_fusion.13
  (16 shorter events, 0.1 us)
Async XLA Ops:
  1.1 4.7 %copy-start.2 = (bf16[16,2,2048]{2,1,0:T(2,128)(2,1)S(1)}, bf16[16,2,2048]{2,1,0:T(2,128)(2,1)}, u32[]{:S(2)}) copy-start(bf16[16,2,2048]{2,1,0:T(2,128)(2,1)} %param.6) | copy-start | bytes 393220
  1.1 16.4 %collective-permute-start = (f32[32768]{0:T(1024)S(1)}, f32[32768]{0:T(1024)S(1)}, u32[]{:S(2)}, u32[]{:S(2)}) collective-permute-start(f32[32768]{0:T(1024)S(1)} %get-tuple-element.13), channel_id=1, source_target_pairs={{0,1},{1,2},{2,3},{3,4},{4,5},{5,6},{6,7},{7,8},{8,9},{9,10},{10,1... | collective-permute-start | bytes 393224 | tf_op jit(solution)/shard_map/ppermute | solution.py:24
  5.9 9.2 %collective-permute-start.1 = (bf16[8,2,2048]{2,1,0:T(2,128)(2,1)S(1)}, bf16[8,2,2048]{2,1,0:T(2,128)(2,1)S(1)}, u32[]{:S(2)}, u32[]{:S(2)}) collective-permute-start(bf16[8,2,2048]{2,1,0:T(2,128)(2,1)S(1)} %get-tuple-element.18), channel_id=1, source_target_pairs={{0,8},{1,9},{2,10},{3,11},{4,12},{5,13},{6,14},{7,15},{8,0},{9,1},... | collective-permute-start | bytes 196616 | tf_op jit(solution)/shard_map/ppermute | solution.py:218
  8.3 8.6 %collective-permute-start.5 = (bf16[8,2,2048]{2,1,0:T(2,128)(2,1)S(1)}, bf16[8,2,2048]{2,1,0:T(2,128)(2,1)S(1)}, u32[]{:S(2)}, u32[]{:S(2)}) collective-permute-start(bf16[8,2,2048]{2,1,0:T(2,128)(2,1)S(1)} %get-tuple-element.17), channel_id=1, source_target_pairs={{0,8},{1,9},{2,10},{3,11},{4,12},{5,13},{6,14},{7,15},{8,0},{9,1},... | collective-permute-start | bytes 196616 | tf_op jit(solution)/shard_map/ppermute | solution.py:218
  10.6 7.7 %copy-start = (f32[256,256]{1,0:T(8,128)}, f32[256,256]{1,0:T(8,128)S(1)}, u32[]{:S(2)}) copy-start(f32[256,256]{1,0:T(8,128)S(1)} %get-tuple-element.24.ts_ref) | copy-start | bytes 786436
  10.6 7.7 %copy-start.1 = (f32[256,256]{1,0:T(8,128)}, f32[256,256]{1,0:T(8,128)S(1)}, u32[]{:S(2)}) copy-start(f32[256,256]{1,0:T(8,128)S(1)} %get-tuple-element.25.tc_ref) | copy-start | bytes 786436
  10.6 0.7 %copy-start.3 = (s32[16]{0:T(128)S(1)}, s32[16]{0:T(128)}, u32[]{:S(2)}) copy-start(s32[16]{0:T(128)} %constant.75.clone) | copy-start | bytes 196
  15.5 7.4 %collective-permute-start.2 = (bf16[2,8,2,2048]{3,2,1,0:T(2,128)(2,1)S(1)}, bf16[2,8,2,2048]{3,2,1,0:T(2,128)(2,1)S(1)}, u32[]{:S(2)}, u32[]{:S(2)}) collective-permute-start(bf16[2,8,2,2048]{3,2,1,0:T(2,128)(2,1)S(1)} %pad_maximum_fusion.11), channel_id=1, source_target_pairs={{0,4},{1,5},{2,6},{3,7},{4,0},{5,1},{6,2},{7,3},{8,12},{9,13},{10,... | collective-permute-start | bytes 393224 | tf_op jit(solution)/shard_map/ppermute | solution.py:218
  17.1 7.9 %collective-permute-start.6 = (bf16[2,8,2,2048]{3,2,1,0:T(2,128)(2,1)S(1)}, bf16[2,8,2,2048]{3,2,1,0:T(2,128)(2,1)S(1)}, u32[]{:S(2)}, u32[]{:S(2)}) collective-permute-start(bf16[2,8,2,2048]{3,2,1,0:T(2,128)(2,1)S(1)} %pad_maximum_fusion.12), channel_id=1, source_target_pairs={{0,4},{1,5},{2,6},{3,7},{4,0},{5,1},{6,2},{7,3},{8,12},{9,13},{10,... | collective-permute-start | bytes 393224 | tf_op jit(solution)/shard_map/ppermute | solution.py:218
  23.3 8.2 %collective-permute-start.3 = (bf16[2,2,8,2,2048]{4,3,2,1,0:T(2,128)(2,1)S(1)}, bf16[2,2,8,2,2048]{4,3,2,1,0:T(2,128)(2,1)S(1)}, u32[]{:S(2)}, u32[]{:S(2)}) collective-permute-start(bf16[2,2,8,2,2048]{4,3,2,1,0:T(2,128)(2,1)S(1)} %pad_maximum_fusion.9), channel_id=1, source_target_pairs={{0,2},{1,3},{2,0},{3,1},{4,6},{5,7},{6,4},{7,5},{8,10},{9,11},{10,... | collective-permute-start | bytes 786440 | tf_op jit(solution)/shard_map/ppermute | solution.py:218
  25.3 11.7 %collective-permute-start.7 = (bf16[2,2,8,2,2048]{4,3,2,1,0:T(2,128)(2,1)S(1)}, bf16[2,2,8,2,2048]{4,3,2,1,0:T(2,128)(2,1)S(1)}, u32[]{:S(2)}, u32[]{:S(2)}) collective-permute-start(bf16[2,2,8,2,2048]{4,3,2,1,0:T(2,128)(2,1)S(1)} %pad_maximum_fusion.10), channel_id=1, source_target_pairs={{0,2},{1,3},{2,0},{3,1},{4,6},{5,7},{6,4},{7,5},{8,10},{9,11},{10,... | collective-permute-start | bytes 786440 | tf_op jit(solution)/shard_map/ppermute | solution.py:218
  32.4 7.6 %collective-permute-start.4 = (bf16[2,2,2,8,2,2048]{5,4,3,2,1,0:T(2,128)(2,1)S(1)}, bf16[2,2,2,8,2,2048]{5,4,3,2,1,0:T(2,128)(2,1)S(1)}, u32[]{:S(2)}, u32[]{:S(2)}) collective-permute-start(bf16[2,2,2,8,2,2048]{5,4,3,2,1,0:T(2,128)(2,1)S(1)} %pad_maximum_fusion.7), channel_id=1, source_target_pairs={{0,1},{1,0},{2,3},{3,2},{4,5},{5,4},{6,7},{7,6},{8,9},{9,8},{10,11... | collective-permute-start | bytes 1572872 | tf_op jit(solution)/shard_map/ppermute | solution.py:218
  37.8 16.5 %collective-permute-start.8 = (bf16[2,2,2,8,2,2048]{5,4,3,2,1,0:T(2,128)(2,1)S(1)}, bf16[2,2,2,8,2,2048]{5,4,3,2,1,0:T(2,128)(2,1)S(1)}, u32[]{:S(2)}, u32[]{:S(2)}) collective-permute-start(bf16[2,2,2,8,2,2048]{5,4,3,2,1,0:T(2,128)(2,1)S(1)} %pad_maximum_fusion.8), channel_id=1, source_target_pairs={{0,1},{1,0},{2,3},{3,2},{4,5},{5,4},{6,7},{7,6},{8,9},{9,8},{10,11... | collective-permute-start | bytes 1572872 | tf_op jit(solution)/shard_map/ppermute | solution.py:218

commit v10 on v5

--- a/solution.py
+++ b/solution.py
@@ -178,23 +178,33 @@
     )(spectra, bank, *tables)
 
 
-def gathered_bank(bank_rows):
+def chain_order(seg_total, chunk):
+    distances = []
+    distance = seg_total // 2
+    while distance >= 1:
+        distances.append(distance)
+        distance //= 2
+    if chunk % 2 == 1 and len(distances) > 2:
+        distances = distances[-2:-1] + distances[:-2] + distances[-1:]
+    return distances
+
+
+def gathered_bank(bank_rows, chunk):
     seg_total = lax.axis_size("seg")
     me = lax.axis_index("seg")
     rows, parts, local_bins = bank_rows.shape
     held = bank_rows[None]
-    distance = seg_total // 2
-    steps = 0
-    while distance >= 1:
+    order = chain_order(seg_total, chunk)
+    for distance in order:
         pairs = [(i, i ^ distance) for i in range(seg_total)]
         arrived = lax.ppermute(held, "seg", pairs)
         upper = (me & distance) != 0
         held = jnp.stack([jnp.where(upper, arrived, held), jnp.where(upper, held, arrived)], axis=0)
-        distance //= 2
-        steps += 1
+    steps = len(order)
     held = held.reshape((2,) * steps + (rows, parts, local_bins // RADIX, RADIX))
-    order = tuple(reversed(range(steps)))
-    held = jnp.transpose(held, (steps, steps + 1) + order + (steps + 2, steps + 3))
+    axis_distance = list(reversed(order))
+    bit_axes = tuple(sorted(range(steps), key=lambda axis: -axis_distance[axis]))
+    held = jnp.transpose(held, (steps, steps + 1) + bit_axes + (steps + 2, steps + 3))
     return held.reshape(rows, parts, seg_total * local_bins // RADIX, RADIX)
 
 
@@ -210,7 +220,7 @@
     template_total = template_bank.shape[0]
     results = []
     for start in range(0, template_total, SUBBANK):
-        bank = gathered_bank(template_bank[start : start + SUBBANK])
+        bank = gathered_bank(template_bank[start : start + SUBBANK], start // SUBBANK)
         peaks = window_peaks(spectra, bank, tables)
         results.append(peaks.reshape(bank.shape[0], block_total * (RADIX // 2)))
     return jnp.concatenate(results, axis=0)

time: 66.3 us -> 67.8 us (1.023)
  waiting for transfers between devices: 3.85 us -> 10.2 us
  starting transfers between devices: 16.8 us -> 11.6 us
    ppermute x8, waiting for transfers between devices: 3.84 us -> 10.2 us  [gathered_bank(): arrived = lax.ppermute(held, 'seg', pairs)]
    ppermute x8, starting transfers between devices: 12.2 us -> 6.93 us  [gathered_bank(): arrived = lax.ppermute(held, 'seg', pairs)]
  transfers between devices with their start and end apart: 9 -> 9, of which waited for: 3 -> 3; matrix products, arithmetic and copies ran while one was open for 29% -> 28% of each run, Pallas kernels for 16% -> 15%
where the time goes in v10:
time: 67.8 us; the launch traced here: 67.2 us
  Pallas kernels  20.5 us (30%)
  other arithmetic  16.5 us (24%)
  starting transfers between devices  11.6 us (17%)
  waiting for transfers between devices  10.2 us (15%)
  local copies, waits for them, and re-layouts  5.59 us (8%)
  matrix products  2.4 us (4%)
    pallas_call x2, Pallas kernels, window_peaks(): pl.pallas_call(peaks_kernel, out_shape=jax.ShapeDtypeStruct((template_tot...  20.5 us
    ppermute x8, waiting for transfers between devices, gathered_bank(): arrived = lax.ppermute(held, 'seg', pairs)  10.2 us
    ppermute x8, starting transfers between devices, gathered_bank(): arrived = lax.ppermute(held, 'seg', pairs)  6.93 us
    another operation x15, other arithmetic, gathered_bank(): jnp.stack([jnp.where(upper, arrived, held), jnp.where(upper, held, arrive...  5.46 us
    ppermute x1, starting transfers between devices, passed_along(): return lax.ppermute(value, axis, pairs)  4.67 us
    another operation x6, local copies, waits for them, and re-layouts, gathered_bank(): jnp.stack([jnp.where(upper, arrived, held), jnp.where(upper, held, arrive...  3.62 us
    sin x3, other arithmetic, angle_table(): return (jnp.cos(angle_value), jnp.sin(angle_value))  2.54 us
    select_n x2, other arithmetic, gathered_bank(): jnp.where(upper, arrived, held)  2.46 us
  transfers between devices with their start and end apart: 9, of which 3 were waited for; matrix products, arithmetic and copies ran while one was open for 28% of the time, Pallas kernels for 15%

profile of v10, /device:TPU:1, one launch (start us, length us, event | category | flops | bytes accessed | tf_op | source)
XLA Modules:
  0.0 67.2 jit_solution(12190634106976787830)
XLA Ops:
  0.0 1.1 %convert_multiply_fusion = f32[65536]{0:T(1024)S(1)} fusion(f32[65536]{0:T(1024)} %param.3, s32[65536]{0:T(1024)} %param.4), kind=kLoop, calls=%fused_computation.62 | loop fusion | flops 131072 | bytes 786432 | tf_op jit(solution)/shard_map/mul | solution.py:212
  1.1 0.0 copy-start.2
  1.1 4.7 %collective-permute-start = (f32[32768]{0:T(1024)S(1)}, f32[32768]{0:T(1024)S(1)}, u32[]{:S(2)}, u32[]{:S(2)}) collective-permute-start(f32[32768]{0:T(1024)S(1)} %get-tuple-element.21), channel_id=1, source_target_pairs={{0,1},{1,2},{2,3},{3,4},{4,5},{5,6},{6,7},{7,8},{8,9},{9,10},{10,1... | collective-permute-start | bytes 393224 | tf_op jit(solution)/shard_map/ppermute | solution.py:23
  5.8 0.1 slice_bitcast_fusion.1
  5.9 2.4 %collective-permute-start.1 = (bf16[1,8,2,2048]{3,2,1,0:T(2,128)(2,1)S(1)}, bf16[1,8,2,2048]{3,2,1,0:T(2,128)(2,1)S(1)}, u32[]{:S(2)}, u32[]{:S(2)}) collective-permute-start(bf16[1,8,2,2048]{3,2,1,0:T(2,128)(2,1)S(1)} %get-tuple-element.29), channel_id=1, source_target_pairs={{0,8},{1,9},{2,10},{3,11},{4,12},{5,13},{6,14},{7,15},{8,0},{9,1},... | collective-permute-start | bytes 196616 | tf_op jit(solution)/shard_map/ppermute | solution.py:200
  8.3 1.2 %collective-permute-start.5 = (bf16[1,8,2,2048]{3,2,1,0:T(2,128)(2,1)S(1)}, bf16[1,8,2,2048]{3,2,1,0:T(2,128)(2,1)S(1)}, u32[]{:S(2)}, u32[]{:S(2)}) collective-permute-start(bf16[1,8,2,2048]{3,2,1,0:T(2,128)(2,1)S(1)} %get-tuple-element.30), channel_id=1, source_target_pairs={{0,2},{1,3},{2,0},{3,1},{4,6},{5,7},{6,4},{7,5},{8,10},{9,11},{10,... | collective-permute-start | bytes 196616 | tf_op jit(solution)/shard_map/ppermute | solution.py:200
  9.5 0.1 concatenate.46
  9.6 1.0 %fusion.38 = (f32[256,256]{1,0:T(8,128)S(1)}, f32[256,256]{1,0:T(8,128)S(1)}) fusion(), kind=kLoop, calls=%fused_computation.85 | loop fusion | flops 983040 | bytes 524288 | tf_op jit(solution)/shard_map/cos | solution.py:31
  10.6 1.0 %fusion.35 = (f32[256,256]{1,0:T(8,128)S(1)}, f32[256,256]{1,0:T(8,128)S(1)}) fusion(), kind=kLoop, calls=%fused_computation.82 | loop fusion | flops 917504 | bytes 524288 | tf_op jit(solution)/shard_map/sin | solution.py:31
  11.7 0.5 fusion.47
  12.2 0.5 fusion.49
  12.7 1.0 %fusion.37 = f32[256,256]{1,0:T(8,128)S(1)} fusion(), kind=kLoop, calls=%fused_computation.84 | loop fusion | flops 917504 | bytes 262144 | tf_op jit(solution)/shard_map/sin | solution.py:31
  13.7 0.1 copy.22
  13.9 0.1 copy.21
  14.0 0.9 %fusion = (bf16[512,256]{1,0:T(8,128)(2,1)}, bf16[512,256]{1,0:T(8,128)(2,1)}) fusion(f32[256,128]{1,0:T(8,128)S(1)} %get-tuple-element.36, f32[256,128]{1,0:T(8,128)S(1)} %get-tuple-element.35, f32[256,128]{1,0:T(8,128)S(1)} %fusion.49), kind=kLoop, calls=%fused_computation.14 | loop fusion | flops 917504 | bytes 917504 | tf_op jit(solution)/shard_map/convert_element_type | solution.py:72
  14.9 0.9 %fusion.1 = (bf16[512,256]{1,0:T(8,128)(2,1)}, bf16[512,256]{1,0:T(8,128)(2,1)}) fusion(f32[256,256]{1,0:T(8,128)S(1)} %get-tuple-element.31, f32[256,256]{1,0:T(8,128)S(1)} %fusion.37, f32[256,256]{1,0:T(8,128)S(1)} %get-tuple-element.32), kind=kLoop, calls=%fused_computation.15 | loop fusion | flops 1310720 | bytes 1310720 | tf_op jit(solution)/shard_map/convert_element_type | solution.py:72
  15.8 0.0 collective-permute-done.1
  15.8 0.0 collective-permute-done.5
  15.8 0.2 fusion.43
  16.0 0.2 fusion.63
  16.2 0.1 collective-permute-start.6
  16.3 0.2 pad_maximum_fusion.11
  16.5 1.3 %collective-permute-start.2 = (bf16[2,1,8,2,2048]{4,3,2,0,1:T(2,128)(2,1)S(1)}, bf16[2,1,8,2,2048]{4,3,2,0,1:T(2,128)(2,1)S(1)}, u32[]{:S(2)}, u32[]{:S(2)}) collective-permute-start(bf16[2,1,8,2,2048]{4,3,2,0,1:T(2,128)(2,1)S(1)} %pad_maximum_fusion.11), channel_id=1, source_target_pairs={{0,4},{1,5},{2,6},{3,7},{4,0},{5,1},{6,2},{7,3},{8,12},{9,13},{10,... | collective-permute-start | bytes 393224 | tf_op jit(solution)/shard_map/ppermute | solution.py:200
  17.9 0.0 collective-permute-done
  17.9 0.1 copy.20
  18.0 0.6 fusion.3
  18.6 0.1 multiply_add_fusion
  18.7 0.9 %convolution_bitcast_fusion = f32[2,128,512]{2,1,0:T(8,128)S(1)} fusion(f32[2,256,256]{2,1,0:T(8,128)S(1)} %get-tuple-element.6, f32[2,256,256]{2,1,0:T(8,128)S(1)} %get-tuple-element.5), kind=kOutput, calls=%fused_computation | convolution fusion | flops 202047488 | bytes 1572864 | tf_op jit(solution)/shard_map/bnf,nk->bkf/dot_general | solution.py:54
  19.7 0.9 %convolution_bitcast_fusion.1 = f32[2,128,512]{2,1,0:T(8,128)S(1)} fusion(f32[2,256,256]{2,1,0:T(8,128)S(1)} %get-tuple-element.6, f32[2,256,256]{2,1,0:T(8,128)S(1)} %get-tuple-element.5), kind=kOutput, calls=%fused_computation.1 | convolution fusion | flops 202047488 | bytes 1572864 | tf_op jit(solution)/shard_map/bnf,nk->bkf/dot_general | solution.py:53
  20.6 0.1 slice_add_fusion
  20.6 0.9 %pad_maximum_fusion.6.spec_ref = f32[2,128,512]{2,1,0:T(8,128)} fusion(f32[2,128,256]{2,1,0:T(8,128)S(1)} %get-tuple-element.12, f32[2,128,256]{2,1,0:T(8,128)S(1)} %get-tuple-element.11), kind=kLoop, calls=%fused_computation.29 | loop fusion | flops 131072 | bytes 1048576 | tf_op jit(solution)/shard_map/concatenate | solution.py:55
  21.5 3.7 %collective-permute-done.6 = bf16[2,1,8,2,2048]{4,3,2,0,1:T(2,128)(2,1)S(1)} collective-permute-done((bf16[2,1,8,2,2048]{4,3,2,0,1:T(2,128)(2,1)S(1)}, bf16[2,1,8,2,2048]{4,3,2,0,1:T(2,128)(2,1)S(1)}, u32[]{:S(2)}, u32[]{:S(2)}) %collective-permute-start.6) | collective-permute-done | bytes 131104 | tf_op jit(solution)/shard_map/ppermute | solution.py:200
  25.2 0.2 fusion.32
  25.5 0.2 fusion.31
  25.7 0.4 fusion.64
  26.1 0.1 collective-permute-start.7
  26.2 0.3 fusion.29
  26.5 0.4 pad_maximum_fusion.9
  26.9 0.4 collective-permute-start.3
  27.2 6.4 %collective-permute-done.7 = bf16[2,2,1,8,2,2048]{5,4,3,1,0,2:T(2,128)(2,1)S(1)} collective-permute-done((bf16[2,2,1,8,2,2048]{5,4,3,1,0,2:T(2,128)(2,1)S(1)}, bf16[2,2,1,8,2,2048]{5,4,3,1,0,2:T(2,128)(2,1)S(1)}, u32[]{:S(2)}, u32[]{:S(2)}) %collective-permute-start.7) | collective-permute-done | bytes 262176 | tf_op jit(solution)/shard_map/ppermute | solution.py:200
  33.6 0.5 fusion.18
  34.1 0.5 fusion.17
  34.5 0.9 %pad_maximum_fusion.8 = bf16[2,2,2,1,8,2,2048]{6,5,4,2,1,3,0:T(2,128)(2,1)S(1)} fusion(bf16[1,2,2,1,8,2,2048]{6,5,4,2,1,3,0:T(2,128)(2,1)S(1)} %fusion.18, bf16[1,2,2,1,8,2,2048]{6,5,4,2,1,3,0:T(2,128)(2,1)S(1)} %fusion.17), kind=kLoop, calls=%fused_computation.32 | loop fusion | flops 262144 | bytes 1048576 | tf_op jit(solution)/shard_map/stack | solution.py:202
  35.5 1.3 %collective-permute-start.8 = (bf16[2,2,2,1,8,2,2048]{6,5,4,2,1,3,0:T(2,128)(2,1)S(1)}, bf16[2,2,2,1,8,2,2048]{6,5,4,2,1,3,0:T(2,128)(2,1)S(1)}, u32[]{:S(2)}, u32[]{:S(2)}) collective-permute-start(bf16[2,2,2,1,8,2,2048]{6,5,4,2,1,3,0:T(2,128)(2,1)S(1)} %pad_maximum_fusion.8), channel_id=1, source_target_pairs={{0,1},{1,0},{2,3},{3,2},{4,5},{5,4},{6,7},{7,6},{8,9},{9,8},{10,11... | collective-permute-start | bytes 1572872 | tf_op jit(solution)/shard_map/ppermute | solution.py:200
  36.8 0.0 collective-permute-done.3
  36.8 0.6 fusion.15
  37.4 0.7 %pad_maximum_fusion.7 = bf16[2,2,2,1,8,2,2048]{6,5,4,2,1,3,0:T(2,128)(2,1)S(1)} fusion(bf16[1,2,2,1,8,2,2048]{6,5,4,2,1,3,0:T(2,128)(2,1)S(1)} %get-tuple-element.16, bf16[1,2,2,1,8,2,2048]{6,5,4,2,1,3,0:T(2,128)(2,1)S(1)} %get-tuple-element.15), kind=kLoop, calls=%fused_computation.30 | loop fusion | flops 262144 | bytes 1048576 | tf_op jit(solution)/shard_map/stack | solution.py:202
  38.1 0.1 collective-permute-start.4
  38.2 0.1 collective-permute-done.8
  38.3 1.2 %broadcast_select_fusion.1 = (bf16[2,2,2,1,8,2,2048]{6,5,4,2,1,3,0:T(2,128)(2,1)S(1)}, bf16[2,2,2,1,8,2,2048]{6,5,4,2,1,3,0:T(2,128)(2,1)S(1)}) fusion(bf16[2,2,2,1,8,2,2048]{6,5,4,2,1,3,0:T(2,128)(2,1)S(1)} %collective-permute-done.8, pred[]{:T(512)S(6)} %ne.97, bf16[1,2,2,1,8,2,2048]{6,5,4,2,1,3,0:T(2,128)(2,1)S(1)} %fusion.18, ...), kind=kLoop, calls=%fused_computation.7 | loop fusion | flops 786432 | bytes 2097153 | tf_op jit(solution)/shard_map/jit(_where)/select_n | solution.py:202
  39.5 0.3 stack.94
  39.9 0.3 stack.93
  40.2 0.1 pad_maximum_fusion.2
  40.3 1.1 %copy.44 = bf16[2,2,2,2,8,2,8,256]{7,6,0,3,1,2,5,4:T(8,128)(2,1)} copy(bf16[2,2,2,2,8,2,8,256]{7,6,5,4,3,2,1,0:T(8,128)(2,1)S(1)} %pad_maximum_fusion.2) | data formatting | bytes 2097152 | tf_op jit(solution)/shard_map/stack | solution.py:202
  41.5 10.3 %shard_map.38 = f32[8,2,128]{2,1,0:T(2,128)} custom-call(f32[2,128,512]{2,1,0:T(8,128)} %pad_maximum_fusion.6.spec_ref, bf16[8,2,128,256]{3,2,1,0:T(8,128)(2,1)} %bitcast.96, bf16[512,256]{1,0:T(8,128)(2,1)} %get-tuple-element.18.fh_ref, bf16[512,256]{1,0:T(8,128)(2,1)} %get-tuple-element.17.fl_ref, f32[256,256]{1,0:T(8,128)} %copy-done.1, ...), custom_call_target="tpu_custom_call" | custom-call | flops 6442450944 | bytes 1581056 | tf_op jit(solution)/shard_map/pallas_call | solution.py:157
  51.8 0.7 %copy.49 = f32[1,8,2,128]{3,1,2,0:T(8,128)S(1)} copy(f32[1,8,2,128]{3,2,1,0:T(2,128)} %bitcast.100) | data formatting | bytes 16384
  52.5 1.2 %broadcast_select_fusion.3 = (bf16[2,2,2,1,8,2,2048]{6,5,4,2,1,3,0:T(2,128)(2,1)S(1)}, bf16[2,2,2,1,8,2,2048]{6,5,4,2,1,3,0:T(2,128)(2,1)S(1)}) fusion(bf16[2,2,2,1,8,2,2048]{6,5,4,2,1,3,0:T(2,128)(2,1)S(1)} %collective-permute-done.4, pred[]{:T(512)S(6)} %ne.97, bf16[1,2,2,1,8,2,2048]{6,5,4,2,1,3,0:T(2,128)(2,1)S(1)} %get-tuple-element.16, ...), kind=kLoop, calls=%fused_computation.9 | loop fusion | flops 786432 | bytes 2097153 | tf_op jit(solution)/shard_map/jit(_where)/select_n | solution.py:202
  53.7 0.3 stack.82
  54.0 0.3 stack.81
  54.4 0.1 pad_maximum_fusion.1
  54.5 1.1 %copy.43 = bf16[2,2,2,2,8,2,8,256]{7,6,0,1,2,3,5,4:T(8,128)(2,1)} copy(bf16[2,2,2,2,8,2,8,256]{7,6,5,4,3,2,1,0:T(8,128)(2,1)S(1)} %pad_maximum_fusion.1) | data formatting | bytes 2097152 | tf_op jit(solution)/shard_map/stack | solution.py:202
  55.6 10.3 %shard_map.37 = f32[8,2,128]{2,1,0:T(2,128)} custom-call(f32[2,128,512]{2,1,0:T(8,128)} %pad_maximum_fusion.6.spec_ref, bf16[8,2,128,256]{3,2,1,0:T(8,128)(2,1)} %bitcast.95, bf16[512,256]{1,0:T(8,128)(2,1)} %get-tuple-element.18.fh_ref, bf16[512,256]{1,0:T(8,128)(2,1)} %get-tuple-element.17.fl_ref, f32[256,256]{1,0:T(8,128)} %copy-done.1, ...), custom_call_target="tpu_custom_call" | custom-call | flops 6442450944 | bytes 1581056 | tf_op jit(solution)/shard_map/pallas_call | solution.py:157
  65.9 0.7 %copy.50 = f32[1,8,2,128]{3,1,2,0:T(8,128)S(1)} copy(f32[1,8,2,128]{3,2,1,0:T(2,128)} %bitcast.99) | data formatting | bytes 16384
  66.6 0.6 pad_maximum_fusion.13
  (10 shorter events, 0.1 us)
Async XLA Ops:
  1.1 4.7 %copy-start.2 = (bf16[16,2,2048]{2,1,0:T(2,128)(2,1)S(1)}, bf16[16,2,2048]{2,1,0:T(2,128)(2,1)}, u32[]{:S(2)}) copy-start(bf16[16,2,2048]{2,1,0:T(2,128)(2,1)} %param.5) | copy-start | bytes 393220
  1.1 16.8 %collective-permute-start = (f32[32768]{0:T(1024)S(1)}, f32[32768]{0:T(1024)S(1)}, u32[]{:S(2)}, u32[]{:S(2)}) collective-permute-start(f32[32768]{0:T(1024)S(1)} %get-tuple-element.21), channel_id=1, source_target_pairs={{0,1},{1,2},{2,3},{3,4},{4,5},{5,6},{6,7},{7,8},{8,9},{9,10},{10,1... | collective-permute-start | bytes 393224 | tf_op jit(solution)/shard_map/ppermute | solution.py:23
  5.9 9.9 %collective-permute-start.1 = (bf16[1,8,2,2048]{3,2,1,0:T(2,128)(2,1)S(1)}, bf16[1,8,2,2048]{3,2,1,0:T(2,128)(2,1)S(1)}, u32[]{:S(2)}, u32[]{:S(2)}) collective-permute-start(bf16[1,8,2,2048]{3,2,1,0:T(2,128)(2,1)S(1)} %get-tuple-element.29), channel_id=1, source_target_pairs={{0,8},{1,9},{2,10},{3,11},{4,12},{5,13},{6,14},{7,15},{8,0},{9,1},... | collective-permute-start | bytes 196616 | tf_op jit(solution)/shard_map/ppermute | solution.py:200
  8.3 7.5 %collective-permute-start.5 = (bf16[1,8,2,2048]{3,2,1,0:T(2,128)(2,1)S(1)}, bf16[1,8,2,2048]{3,2,1,0:T(2,128)(2,1)S(1)}, u32[]{:S(2)}, u32[]{:S(2)}) collective-permute-start(bf16[1,8,2,2048]{3,2,1,0:T(2,128)(2,1)S(1)} %get-tuple-element.30), channel_id=1, source_target_pairs={{0,2},{1,3},{2,0},{3,1},{4,6},{5,7},{6,4},{7,5},{8,10},{9,11},{10,... | collective-permute-start | bytes 196616 | tf_op jit(solution)/shard_map/ppermute | solution.py:200
  11.7 6.9 %copy-start = (f32[256,256]{1,0:T(8,128)}, f32[256,256]{1,0:T(8,128)S(1)}, u32[]{:S(2)}) copy-start(f32[256,256]{1,0:T(8,128)S(1)} %get-tuple-element.33.ts_ref) | copy-start | bytes 786436
  11.7 6.9 %copy-start.1 = (f32[256,256]{1,0:T(8,128)}, f32[256,256]{1,0:T(8,128)S(1)}, u32[]{:S(2)}) copy-start(f32[256,256]{1,0:T(8,128)S(1)} %get-tuple-element.34.tc_ref) | copy-start | bytes 786436
  16.2 9.1 %collective-permute-start.6 = (bf16[2,1,8,2,2048]{4,3,2,0,1:T(2,128)(2,1)S(1)}, bf16[2,1,8,2,2048]{4,3,2,0,1:T(2,128)(2,1)S(1)}, u32[]{:S(2)}, u32[]{:S(2)}) collective-permute-start(bf16[2,1,8,2,2048]{4,3,2,0,1:T(2,128)(2,1)S(1)} %fusion.63), channel_id=1, source_target_pairs={{0,8},{1,9},{2,10},{3,11},{4,12},{5,13},{6,14},{7,15},{8,0},{9,1},... | collective-permute-start | bytes 393224 | tf_op jit(solution)/shard_map/ppermute | solution.py:200
  16.5 9.6 %collective-permute-start.2 = (bf16[2,1,8,2,2048]{4,3,2,0,1:T(2,128)(2,1)S(1)}, bf16[2,1,8,2,2048]{4,3,2,0,1:T(2,128)(2,1)S(1)}, u32[]{:S(2)}, u32[]{:S(2)}) collective-permute-start(bf16[2,1,8,2,2048]{4,3,2,0,1:T(2,128)(2,1)S(1)} %pad_maximum_fusion.11), channel_id=1, source_target_pairs={{0,4},{1,5},{2,6},{3,7},{4,0},{5,1},{6,2},{7,3},{8,12},{9,13},{10,... | collective-permute-start | bytes 393224 | tf_op jit(solution)/shard_map/ppermute | solution.py:200
  26.1 7.6 %collective-permute-start.7 = (bf16[2,2,1,8,2,2048]{5,4,3,1,0,2:T(2,128)(2,1)S(1)}, bf16[2,2,1,8,2,2048]{5,4,3,1,0,2:T(2,128)(2,1)S(1)}, u32[]{:S(2)}, u32[]{:S(2)}) collective-permute-start(bf16[2,2,1,8,2,2048]{5,4,3,1,0,2:T(2,128)(2,1)S(1)} %fusion.64), channel_id=1, source_target_pairs={{0,4},{1,5},{2,6},{3,7},{4,0},{5,1},{6,2},{7,3},{8,12},{9,13},{10,... | collective-permute-start | bytes 786440 | tf_op jit(solution)/shard_map/ppermute | solution.py:200
  26.9 9.9 %collective-permute-start.3 = (bf16[2,2,1,8,2,2048]{5,4,3,1,0,2:T(2,128)(2,1)S(1)}, bf16[2,2,1,8,2,2048]{5,4,3,1,0,2:T(2,128)(2,1)S(1)}, u32[]{:S(2)}, u32[]{:S(2)}) collective-permute-start(bf16[2,2,1,8,2,2048]{5,4,3,1,0,2:T(2,128)(2,1)S(1)} %pad_maximum_fusion.9), channel_id=1, source_target_pairs={{0,2},{1,3},{2,0},{3,1},{4,6},{5,7},{6,4},{7,5},{8,10},{9,11},{10,... | collective-permute-start | bytes 786440 | tf_op jit(solution)/shard_map/ppermute | solution.py:200
  35.5 2.8 %collective-permute-start.8 = (bf16[2,2,2,1,8,2,2048]{6,5,4,2,1,3,0:T(2,128)(2,1)S(1)}, bf16[2,2,2,1,8,2,2048]{6,5,4,2,1,3,0:T(2,128)(2,1)S(1)}, u32[]{:S(2)}, u32[]{:S(2)}) collective-permute-start(bf16[2,2,2,1,8,2,2048]{6,5,4,2,1,3,0:T(2,128)(2,1)S(1)} %pad_maximum_fusion.8), channel_id=1, source_target_pairs={{0,1},{1,0},{2,3},{3,2},{4,5},{5,4},{6,7},{7,6},{8,9},{9,8},{10,11... | collective-permute-start | bytes 1572872 | tf_op jit(solution)/shard_map/ppermute | solution.py:200
  38.1 14.3 %collective-permute-start.4 = (bf16[2,2,2,1,8,2,2048]{6,5,4,2,1,3,0:T(2,128)(2,1)S(1)}, bf16[2,2,2,1,8,2,2048]{6,5,4,2,1,3,0:T(2,128)(2,1)S(1)}, u32[]{:S(2)}, u32[]{:S(2)}) collective-permute-start(bf16[2,2,2,1,8,2,2048]{6,5,4,2,1,3,0:T(2,128)(2,1)S(1)} %pad_maximum_fusion.7), channel_id=1, source_target_pairs={{0,1},{1,0},{2,3},{3,2},{4,5},{5,4},{6,7},{7,6},{8,9},{9,8},{10,11... | collective-permute-start | bytes 1572872 | tf_op jit(solution)/shard_map/ppermute | solution.py:200

commit v11 on v5

--- a/solution.py
+++ b/solution.py
@@ -185,9 +185,12 @@
     held = bank_rows[None]
     distance = seg_total // 2
     steps = 0
+    first_arrived = None
     while distance >= 1:
         pairs = [(i, i ^ distance) for i in range(seg_total)]
         arrived = lax.ppermute(held, "seg", pairs)
+        if first_arrived is None:
+            first_arrived = arrived
         upper = (me & distance) != 0
         held = jnp.stack([jnp.where(upper, arrived, held), jnp.where(upper, held, arrived)], axis=0)
         distance //= 2
@@ -195,22 +198,28 @@
     held = held.reshape((2,) * steps + (rows, parts, local_bins // RADIX, RADIX))
     order = tuple(reversed(range(steps)))
     held = jnp.transpose(held, (steps, steps + 1) + order + (steps + 2, steps + 3))
-    return held.reshape(rows, parts, seg_total * local_bins // RADIX, RADIX)
+    return held.reshape(rows, parts, seg_total * local_bins // RADIX, RADIX), first_arrived
 
 
 def local(strain, gate_mask, template_bank):
+    template_total = template_bank.shape[0]
+    banks = []
+    first_pieces = []
+    for start in range(0, template_total, SUBBANK):
+        bank, first_arrived = gathered_bank(template_bank[start : start + SUBBANK])
+        banks.append(bank)
+        first_pieces.append(first_arrived)
     gated = strain * gate_mask.astype(jnp.float32)
     local_blocks = gated.reshape(-1, BLOCK)
     block_total = local_blocks.shape[0]
-    earlier = passed_along(local_blocks[block_total - 1], "seg", 1)
+    last_block, _ = lax.optimization_barrier((local_blocks[block_total - 1], first_pieces))
+    earlier = passed_along(last_block, "seg", 1)
     before = jnp.concatenate([earlier[None], local_blocks[:-1]], axis=0)
     windows = jnp.concatenate([before, local_blocks], axis=1)
     spectra = forward(windows)
     tables = inverse_tables(spectra.shape[1])
-    template_total = template_bank.shape[0]
     results = []
-    for start in range(0, template_total, SUBBANK):
-        bank = gathered_bank(template_bank[start : start + SUBBANK])
+    for bank in banks:
         peaks = window_peaks(spectra, bank, tables)
         results.append(peaks.reshape(bank.shape[0], block_total * (RADIX // 2)))
     return jnp.concatenate(results, axis=0)

time: 66.3 us -> 66.9 us (level)
  starting transfers between devices: 16.8 us -> 11.7 us
  waiting for transfers between devices: 3.85 us -> 8.7 us
  local copies, waits for them, and re-layouts: 5.59 us -> 6.54 us
    ppermute x8, waiting for transfers between devices: 3.84 us -> 8.69 us  [gathered_bank(): arrived = lax.ppermute(held, 'seg', pairs)]
    ppermute x8, starting transfers between devices: 12.2 us -> 7.32 us  [gathered_bank(): arrived = lax.ppermute(held, 'seg', pairs)]
    broadcast_in_dim x1, local copies, waits for them, and re-layouts: 0.09 us -> 1.01 us  [gathered_bank(): held = bank_rows[None]]
    unnamed x8 -> x10, local copies, waits for them, and re-layouts: 1.41 us -> 1.41 us
  transfers between devices with their start and end apart: 9 -> 9, of which waited for: 3 -> 3; matrix products, arithmetic and copies ran while one was open for 29% -> 30% of each run, Pallas kernels for 16% -> 15%
where the time goes in v11:
time: 66.9 us; the launch traced here: 66.5 us
  Pallas kernels  20.5 us (31%)
  other arithmetic  16.2 us (24%)
  starting transfers between devices  11.7 us (17%)
  waiting for transfers between devices  8.7 us (13%)
  local copies, waits for them, and re-layouts  6.54 us (10%)
  matrix products  2.4 us (4%)
    pallas_call x2, Pallas kernels, window_peaks(): pl.pallas_call(peaks_kernel, out_shape=jax.ShapeDtypeStruct((template_tot...  20.5 us
    ppermute x8, waiting for transfers between devices, gathered_bank(): arrived = lax.ppermute(held, 'seg', pairs)  8.69 us
    ppermute x8, starting transfers between devices, gathered_bank(): arrived = lax.ppermute(held, 'seg', pairs)  7.32 us
    another operation x15, other arithmetic, gathered_bank(): jnp.stack([jnp.where(upper, arrived, held), jnp.where(upper, held, arrive...  5.29 us
    ppermute x1, starting transfers between devices, passed_along(): return lax.ppermute(value, axis, pairs)  4.42 us
    another operation x6, local copies, waits for them, and re-layouts, gathered_bank(): jnp.stack([jnp.where(upper, arrived, held), jnp.where(upper, held, arrive...  3.65 us
    sin x3, other arithmetic, angle_table(): return (jnp.cos(angle_value), jnp.sin(angle_value))  2.54 us
    select_n x2, other arithmetic, gathered_bank(): jnp.where(upper, arrived, held)  2.46 us
  transfers between devices with their start and end apart: 9, of which 3 were waited for; matrix products, arithmetic and copies ran while one was open for 30% of the time, Pallas kernels for 15%

profile of v11, /device:TPU:1, one launch (start us, length us, event | category | flops | bytes accessed | tf_op | source)
XLA Modules:
  0.0 66.5 jit_solution(10354823886874859803)
XLA Ops:
  0.0 1.0 %slice_bitcast_fusion = (bf16[1,8,2,2048]{3,2,1,0:T(2,128)(2,1)S(1)}, bf16[1,8,2,2048]{3,2,1,0:T(2,128)(2,1)S(1)}) fusion(bf16[16,2,2048]{2,1,0:T(2,128)(2,1)} %param.5), kind=kLoop, calls=%fused_computation.98 | loop fusion | bytes 262144 | tf_op jit(solution)/shard_map/broadcast_in_dim | solution.py:185
  1.0 3.2 %collective-permute-start = (bf16[1,8,2,2048]{3,2,1,0:T(2,128)(2,1)S(1)}, bf16[1,8,2,2048]{3,2,1,0:T(2,128)(2,1)S(1)}, u32[]{:S(2)}, u32[]{:S(2)}) collective-permute-start(bf16[1,8,2,2048]{3,2,1,0:T(2,128)(2,1)S(1)} %get-tuple-element.32), channel_id=1, source_target_pairs={{0,8},{1,9},{2,10},{3,11},{4,12},{5,13},{6,14},{7,15},{8,0},{9,1},... | collective-permute-start | bytes 196616 | tf_op jit(solution)/shard_map/ppermute | solution.py:191
  4.2 0.1 collective-permute-start.1
  4.3 1.0 %convert_multiply_fusion = f32[65536]{0:T(1024)S(1)} fusion(f32[65536]{0:T(1024)S(1)} %copy-done.3, s32[65536]{0:T(1024)} %param.4), kind=kLoop, calls=%fused_computation.62 | loop fusion | flops 131072 | bytes 786432 | tf_op jit(solution)/shard_map/mul | solution.py:212
  5.3 0.1 concatenate.46
  5.4 1.0 %fusion.38 = (f32[256,256]{1,0:T(8,128)S(1)}, f32[256,256]{1,0:T(8,128)S(1)}) fusion(), kind=kLoop, calls=%fused_computation.85 | loop fusion | flops 983040 | bytes 524288 | tf_op jit(solution)/shard_map/cos | solution.py:31
  6.4 1.0 %fusion.35 = (f32[256,256]{1,0:T(8,128)S(1)}, f32[256,256]{1,0:T(8,128)S(1)}) fusion(), kind=kLoop, calls=%fused_computation.82 | loop fusion | flops 917504 | bytes 524288 | tf_op jit(solution)/shard_map/sin | solution.py:31
  7.5 0.5 fusion.47
  8.0 0.5 fusion.49
  8.6 1.0 %fusion.37 = f32[256,256]{1,0:T(8,128)S(1)} fusion(), kind=kLoop, calls=%fused_computation.84 | loop fusion | flops 917504 | bytes 262144 | tf_op jit(solution)/shard_map/sin | solution.py:31
  9.5 0.1 copy.22
  9.7 0.1 copy.21
  9.8 0.9 %fusion = (bf16[512,256]{1,0:T(8,128)(2,1)}, bf16[512,256]{1,0:T(8,128)(2,1)}) fusion(f32[256,128]{1,0:T(8,128)S(1)} %get-tuple-element.38, f32[256,128]{1,0:T(8,128)S(1)} %get-tuple-element.37, f32[256,128]{1,0:T(8,128)S(1)} %fusion.49), kind=kLoop, calls=%fused_computation.14 | loop fusion | flops 917504 | bytes 917504 | tf_op jit(solution)/shard_map/convert_element_type | solution.py:72
  10.7 0.9 %fusion.1 = (bf16[512,256]{1,0:T(8,128)(2,1)}, bf16[512,256]{1,0:T(8,128)(2,1)}) fusion(f32[256,256]{1,0:T(8,128)S(1)} %get-tuple-element.33, f32[256,256]{1,0:T(8,128)S(1)} %fusion.37, f32[256,256]{1,0:T(8,128)S(1)} %get-tuple-element.34), kind=kLoop, calls=%fused_computation.15 | loop fusion | flops 1310720 | bytes 1310720 | tf_op jit(solution)/shard_map/convert_element_type | solution.py:72
  11.6 0.0 collective-permute-done
  11.6 4.4 %collective-permute-start.2 = (f32[32768]{0:T(1024)S(1)}, f32[32768]{0:T(1024)S(1)}, u32[]{:S(2)}, u32[]{:S(2)}) collective-permute-start(f32[32768]{0:T(1024)S(1)} %get-tuple-element.6), channel_id=1, source_target_pairs={{0,1},{1,2},{2,3},{3,4},{4,5},{5,6},{6,7},{7,8},{8,9},{9,10},{10,1... | collective-permute-start | bytes 393224 | tf_op jit(solution)/shard_map/ppermute | solution.py:23
  16.0 0.2 fusion.43
  16.2 0.2 fusion.63
  16.4 1.4 %collective-permute-start.6 = (bf16[2,1,8,2,2048]{4,3,2,0,1:T(2,128)(2,1)S(1)}, bf16[2,1,8,2,2048]{4,3,2,0,1:T(2,128)(2,1)S(1)}, u32[]{:S(2)}, u32[]{:S(2)}) collective-permute-start(bf16[2,1,8,2,2048]{4,3,2,0,1:T(2,128)(2,1)S(1)} %fusion.63), channel_id=1, source_target_pairs={{0,4},{1,5},{2,6},{3,7},{4,0},{5,1},{6,2},{7,3},{8,12},{9,13},{10,... | collective-permute-start | bytes 393224 | tf_op jit(solution)/shard_map/ppermute | solution.py:191
  17.8 0.2 pad_maximum_fusion.11
  18.0 0.2 collective-permute-start.3
  18.2 0.0 collective-permute-done.2
  18.3 0.1 copy.20
  18.4 3.1 %collective-permute-done.6 = bf16[2,1,8,2,2048]{4,3,2,0,1:T(2,128)(2,1)S(1)} collective-permute-done((bf16[2,1,8,2,2048]{4,3,2,0,1:T(2,128)(2,1)S(1)}, bf16[2,1,8,2,2048]{4,3,2,0,1:T(2,128)(2,1)S(1)}, u32[]{:S(2)}, u32[]{:S(2)}) %collective-permute-start.6) | collective-permute-done | bytes 131104 | tf_op jit(solution)/shard_map/ppermute | solution.py:191
  21.4 0.2 fusion.32
  21.7 0.2 fusion.31
  21.9 0.4 fusion.64
  22.3 1.8 %collective-permute-start.7 = (bf16[2,2,1,8,2,2048]{5,4,3,1,0,2:T(2,128)(2,1)S(1)}, bf16[2,2,1,8,2,2048]{5,4,3,1,0,2:T(2,128)(2,1)S(1)}, u32[]{:S(2)}, u32[]{:S(2)}) collective-permute-start(bf16[2,2,1,8,2,2048]{5,4,3,1,0,2:T(2,128)(2,1)S(1)} %fusion.64), channel_id=1, source_target_pairs={{0,2},{1,3},{2,0},{3,1},{4,6},{5,7},{6,4},{7,5},{8,10},{9,11},{10,... | collective-permute-start | bytes 786440 | tf_op jit(solution)/shard_map/ppermute | solution.py:191
  24.1 0.6 fusion.3
  24.7 0.1 multiply_add_fusion
  24.8 0.9 %convolution_bitcast_fusion = f32[2,128,512]{2,1,0:T(8,128)S(1)} fusion(f32[2,256,256]{2,1,0:T(8,128)S(1)} %get-tuple-element.8, f32[2,256,256]{2,1,0:T(8,128)S(1)} %get-tuple-element.7), kind=kOutput, calls=%fused_computation | convolution fusion | flops 202047488 | bytes 1572864 | tf_op jit(solution)/shard_map/bnf,nk->bkf/dot_general | solution.py:54
  25.8 0.9 %convolution_bitcast_fusion.1 = f32[2,128,512]{2,1,0:T(8,128)S(1)} fusion(f32[2,256,256]{2,1,0:T(8,128)S(1)} %get-tuple-element.8, f32[2,256,256]{2,1,0:T(8,128)S(1)} %get-tuple-element.7), kind=kOutput, calls=%fused_computation.1 | convolution fusion | flops 202047488 | bytes 1572864 | tf_op jit(solution)/shard_map/bnf,nk->bkf/dot_general | solution.py:53
  26.7 0.0 collective-permute-done.3
  26.7 0.3 fusion.29
  27.0 0.4 pad_maximum_fusion.9
  27.4 0.1 collective-permute-start.4
  27.5 0.1 slice_add_fusion
  27.5 0.9 %pad_maximum_fusion.6.spec_ref = f32[2,128,512]{2,1,0:T(8,128)} fusion(f32[2,128,256]{2,1,0:T(8,128)S(1)} %get-tuple-element.14, f32[2,128,256]{2,1,0:T(8,128)S(1)} %get-tuple-element.13), kind=kLoop, calls=%fused_computation.29 | loop fusion | flops 131072 | bytes 1048576 | tf_op jit(solution)/shard_map/concatenate | solution.py:55
  28.4 2.1 %collective-permute-done.7 = bf16[2,2,1,8,2,2048]{5,4,3,1,0,2:T(2,128)(2,1)S(1)} collective-permute-done((bf16[2,2,1,8,2,2048]{5,4,3,1,0,2:T(2,128)(2,1)S(1)}, bf16[2,2,1,8,2,2048]{5,4,3,1,0,2:T(2,128)(2,1)S(1)}, u32[]{:S(2)}, u32[]{:S(2)}) %collective-permute-start.7) | collective-permute-done | bytes 262176 | tf_op jit(solution)/shard_map/ppermute | solution.py:191
  30.5 0.5 fusion.18
  31.0 0.5 fusion.17
  31.5 0.7 %pad_maximum_fusion.8 = bf16[2,2,2,1,8,2,2048]{6,5,4,2,1,3,0:T(2,128)(2,1)S(1)} fusion(bf16[1,2,2,1,8,2,2048]{6,5,4,2,1,3,0:T(2,128)(2,1)S(1)} %fusion.18, bf16[1,2,2,1,8,2,2048]{6,5,4,2,1,3,0:T(2,128)(2,1)S(1)} %fusion.17), kind=kLoop, calls=%fused_computation.32 | loop fusion | flops 262144 | bytes 1048576 | tf_op jit(solution)/shard_map/stack | solution.py:195
  32.2 0.1 collective-permute-start.8
  32.3 3.5 %collective-permute-done.4 = bf16[2,2,1,8,2,2048]{5,4,3,1,0,2:T(2,128)(2,1)S(1)} collective-permute-done((bf16[2,2,1,8,2,2048]{5,4,3,1,0,2:T(2,128)(2,1)S(1)}, bf16[2,2,1,8,2,2048]{5,4,3,1,0,2:T(2,128)(2,1)S(1)}, u32[]{:S(2)}, u32[]{:S(2)}) %collective-permute-start.4) | collective-permute-done | bytes 262176 | tf_op jit(solution)/shard_map/ppermute | solution.py:191
  35.8 0.6 fusion.15
  36.4 0.7 %pad_maximum_fusion.7 = bf16[2,2,2,1,8,2,2048]{6,5,4,2,1,3,0:T(2,128)(2,1)S(1)} fusion(bf16[1,2,2,1,8,2,2048]{6,5,4,2,1,3,0:T(2,128)(2,1)S(1)} %get-tuple-element.18, bf16[1,2,2,1,8,2,2048]{6,5,4,2,1,3,0:T(2,128)(2,1)S(1)} %get-tuple-element.17), kind=kLoop, calls=%fused_computation.30 | loop fusion | flops 262144 | bytes 1048576 | tf_op jit(solution)/shard_map/stack | solution.py:195
  37.1 0.5 collective-permute-start.5
  37.6 0.0 collective-permute-done.8
  37.6 1.2 %broadcast_select_fusion.1 = (bf16[2,2,2,1,8,2,2048]{6,5,4,2,1,3,0:T(2,128)(2,1)S(1)}, bf16[2,2,2,1,8,2,2048]{6,5,4,2,1,3,0:T(2,128)(2,1)S(1)}) fusion(bf16[2,2,2,1,8,2,2048]{6,5,4,2,1,3,0:T(2,128)(2,1)S(1)} %collective-permute-done.8, pred[]{:T(512)S(6)} %ne.97, bf16[1,2,2,1,8,2,2048]{6,5,4,2,1,3,0:T(2,128)(2,1)S(1)} %fusion.18, ...), kind=kLoop, calls=%fused_computation.7 | loop fusion | flops 786432 | bytes 2097153 | tf_op jit(solution)/shard_map/jit(_where)/select_n | solution.py:195
  38.8 0.3 stack.94
  39.2 0.3 stack.93
  39.5 0.1 pad_maximum_fusion.2
  39.6 1.2 %copy.44 = bf16[2,2,2,2,8,2,8,256]{7,6,0,1,2,3,5,4:T(8,128)(2,1)} copy(bf16[2,2,2,2,8,2,8,256]{7,6,5,4,3,2,1,0:T(8,128)(2,1)S(1)} %pad_maximum_fusion.2) | data formatting | bytes 2097152 | tf_op jit(solution)/shard_map/stack | solution.py:195
  40.8 10.3 %shard_map.38 = f32[8,2,128]{2,1,0:T(2,128)} custom-call(f32[2,128,512]{2,1,0:T(8,128)} %pad_maximum_fusion.6.spec_ref, bf16[8,2,128,256]{3,2,1,0:T(8,128)(2,1)} %bitcast.96, bf16[512,256]{1,0:T(8,128)(2,1)} %get-tuple-element.20.fh_ref, bf16[512,256]{1,0:T(8,128)(2,1)} %get-tuple-element.19.fl_ref, f32[256,256]{1,0:T(8,128)} %copy-done.1, ...), custom_call_target="tpu_custom_call" | custom-call | flops 6442450944 | bytes 1581056 | tf_op jit(solution)/shard_map/pallas_call | solution.py:157
  51.0 0.7 %copy.49 = f32[1,8,2,128]{3,1,2,0:T(8,128)S(1)} copy(f32[1,8,2,128]{3,2,1,0:T(2,128)} %bitcast.100) | data formatting | bytes 16384
  51.7 0.0 collective-permute-done.5
  51.7 1.2 %broadcast_select_fusion.3 = (bf16[2,2,2,1,8,2,2048]{6,5,4,2,1,3,0:T(2,128)(2,1)S(1)}, bf16[2,2,2,1,8,2,2048]{6,5,4,2,1,3,0:T(2,128)(2,1)S(1)}) fusion(bf16[2,2,2,1,8,2,2048]{6,5,4,2,1,3,0:T(2,128)(2,1)S(1)} %collective-permute-done.5, pred[]{:T(512)S(6)} %ne.97, bf16[1,2,2,1,8,2,2048]{6,5,4,2,1,3,0:T(2,128)(2,1)S(1)} %get-tuple-element.18, ...), kind=kLoop, calls=%fused_computation.9 | loop fusion | flops 786432 | bytes 2097153 | tf_op jit(solution)/shard_map/jit(_where)/select_n | solution.py:195
  53.0 0.3 stack.82
  53.3 0.3 stack.81
  53.7 0.1 pad_maximum_fusion.1
  53.8 1.2 %copy.43 = bf16[2,2,2,2,8,2,8,256]{7,6,0,1,2,3,5,4:T(8,128)(2,1)} copy(bf16[2,2,2,2,8,2,8,256]{7,6,5,4,3,2,1,0:T(8,128)(2,1)S(1)} %pad_maximum_fusion.1) | data formatting | bytes 2097152 | tf_op jit(solution)/shard_map/stack | solution.py:195
  54.9 10.3 %shard_map.37 = f32[8,2,128]{2,1,0:T(2,128)} custom-call(f32[2,128,512]{2,1,0:T(8,128)} %pad_maximum_fusion.6.spec_ref, bf16[8,2,128,256]{3,2,1,0:T(8,128)(2,1)} %bitcast.95, bf16[512,256]{1,0:T(8,128)(2,1)} %get-tuple-element.20.fh_ref, bf16[512,256]{1,0:T(8,128)(2,1)} %get-tuple-element.19.fl_ref, f32[256,256]{1,0:T(8,128)} %copy-done.1, ...), custom_call_target="tpu_custom_call" | custom-call | flops 6442450944 | bytes 1581056 | tf_op jit(solution)/shard_map/pallas_call | solution.py:157
  65.2 0.7 %copy.50 = f32[1,8,2,128]{3,1,2,0:T(8,128)S(1)} copy(f32[1,8,2,128]{3,2,1,0:T(2,128)} %bitcast.99) | data formatting | bytes 16384
  65.9 0.6 pad_maximum_fusion.13
  (12 shorter events, 0.1 us)
Async XLA Ops:
  0.0 4.3 %copy-start.3 = (f32[65536]{0:T(1024)S(1)}, f32[65536]{0:T(1024)}, u32[]{:S(2)}) copy-start(f32[65536]{0:T(1024)} %param.3) | copy-start | bytes 786436
  1.0 10.5 %collective-permute-start = (bf16[1,8,2,2048]{3,2,1,0:T(2,128)(2,1)S(1)}, bf16[1,8,2,2048]{3,2,1,0:T(2,128)(2,1)S(1)}, u32[]{:S(2)}, u32[]{:S(2)}) collective-permute-start(bf16[1,8,2,2048]{3,2,1,0:T(2,128)(2,1)S(1)} %get-tuple-element.32), channel_id=1, source_target_pairs={{0,8},{1,9},{2,10},{3,11},{4,12},{5,13},{6,14},{7,15},{8,0},{9,1},... | collective-permute-start | bytes 196616 | tf_op jit(solution)/shard_map/ppermute | solution.py:191
  4.2 7.3 %collective-permute-start.1 = (bf16[1,8,2,2048]{3,2,1,0:T(2,128)(2,1)S(1)}, bf16[1,8,2,2048]{3,2,1,0:T(2,128)(2,1)S(1)}, u32[]{:S(2)}, u32[]{:S(2)}) collective-permute-start(bf16[1,8,2,2048]{3,2,1,0:T(2,128)(2,1)S(1)} %get-tuple-element.31), channel_id=1, source_target_pairs={{0,8},{1,9},{2,10},{3,11},{4,12},{5,13},{6,14},{7,15},{8,0},{9,1},... | collective-permute-start | bytes 196616 | tf_op jit(solution)/shard_map/ppermute | solution.py:191
  7.5 17.2 %copy-start = (f32[256,256]{1,0:T(8,128)}, f32[256,256]{1,0:T(8,128)S(1)}, u32[]{:S(2)}) copy-start(f32[256,256]{1,0:T(8,128)S(1)} %get-tuple-element.35.ts_ref) | copy-start | bytes 786436
  7.5 17.2 %copy-start.1 = (f32[256,256]{1,0:T(8,128)}, f32[256,256]{1,0:T(8,128)S(1)}, u32[]{:S(2)}) copy-start(f32[256,256]{1,0:T(8,128)S(1)} %get-tuple-element.36.tc_ref) | copy-start | bytes 786436
  10.7 5.3 %copy-start.2 = (bf16[16,2,2048]{2,1,0:T(2,128)(2,1)S(1)}, bf16[16,2,2048]{2,1,0:T(2,128)(2,1)}, u32[]{:S(2)}) copy-start(bf16[16,2,2048]{2,1,0:T(2,128)(2,1)} %param.5) | copy-start | bytes 393220
  11.6 6.7 %collective-permute-start.2 = (f32[32768]{0:T(1024)S(1)}, f32[32768]{0:T(1024)S(1)}, u32[]{:S(2)}, u32[]{:S(2)}) collective-permute-start(f32[32768]{0:T(1024)S(1)} %get-tuple-element.6), channel_id=1, source_target_pairs={{0,1},{1,2},{2,3},{3,4},{4,5},{5,6},{6,7},{7,8},{8,9},{9,10},{10,1... | collective-permute-start | bytes 393224 | tf_op jit(solution)/shard_map/ppermute | solution.py:23
  16.4 5.0 %collective-permute-start.6 = (bf16[2,1,8,2,2048]{4,3,2,0,1:T(2,128)(2,1)S(1)}, bf16[2,1,8,2,2048]{4,3,2,0,1:T(2,128)(2,1)S(1)}, u32[]{:S(2)}, u32[]{:S(2)}) collective-permute-start(bf16[2,1,8,2,2048]{4,3,2,0,1:T(2,128)(2,1)S(1)} %fusion.63), channel_id=1, source_target_pairs={{0,4},{1,5},{2,6},{3,7},{4,0},{5,1},{6,2},{7,3},{8,12},{9,13},{10,... | collective-permute-start | bytes 393224 | tf_op jit(solution)/shard_map/ppermute | solution.py:191
  18.0 8.7 %collective-permute-start.3 = (bf16[2,1,8,2,2048]{4,3,2,0,1:T(2,128)(2,1)S(1)}, bf16[2,1,8,2,2048]{4,3,2,0,1:T(2,128)(2,1)S(1)}, u32[]{:S(2)}, u32[]{:S(2)}) collective-permute-start(bf16[2,1,8,2,2048]{4,3,2,0,1:T(2,128)(2,1)S(1)} %pad_maximum_fusion.11), channel_id=1, source_target_pairs={{0,4},{1,5},{2,6},{3,7},{4,0},{5,1},{6,2},{7,3},{8,12},{9,13},{10,... | collective-permute-start | bytes 393224 | tf_op jit(solution)/shard_map/ppermute | solution.py:191
  22.3 8.3 %collective-permute-start.7 = (bf16[2,2,1,8,2,2048]{5,4,3,1,0,2:T(2,128)(2,1)S(1)}, bf16[2,2,1,8,2,2048]{5,4,3,1,0,2:T(2,128)(2,1)S(1)}, u32[]{:S(2)}, u32[]{:S(2)}) collective-permute-start(bf16[2,2,1,8,2,2048]{5,4,3,1,0,2:T(2,128)(2,1)S(1)} %fusion.64), channel_id=1, source_target_pairs={{0,2},{1,3},{2,0},{3,1},{4,6},{5,7},{6,4},{7,5},{8,10},{9,11},{10,... | collective-permute-start | bytes 786440 | tf_op jit(solution)/shard_map/ppermute | solution.py:191
  27.4 8.4 %collective-permute-start.4 = (bf16[2,2,1,8,2,2048]{5,4,3,1,0,2:T(2,128)(2,1)S(1)}, bf16[2,2,1,8,2,2048]{5,4,3,1,0,2:T(2,128)(2,1)S(1)}, u32[]{:S(2)}, u32[]{:S(2)}) collective-permute-start(bf16[2,2,1,8,2,2048]{5,4,3,1,0,2:T(2,128)(2,1)S(1)} %pad_maximum_fusion.9), channel_id=1, source_target_pairs={{0,2},{1,3},{2,0},{3,1},{4,6},{5,7},{6,4},{7,5},{8,10},{9,11},{10,... | collective-permute-start | bytes 786440 | tf_op jit(solution)/shard_map/ppermute | solution.py:191
  32.2 5.4 %collective-permute-start.8 = (bf16[2,2,2,1,8,2,2048]{6,5,4,2,1,3,0:T(2,128)(2,1)S(1)}, bf16[2,2,2,1,8,2,2048]{6,5,4,2,1,3,0:T(2,128)(2,1)S(1)}, u32[]{:S(2)}, u32[]{:S(2)}) collective-permute-start(bf16[2,2,2,1,8,2,2048]{6,5,4,2,1,3,0:T(2,128)(2,1)S(1)} %pad_maximum_fusion.8), channel_id=1, source_target_pairs={{0,1},{1,0},{2,3},{3,2},{4,5},{5,4},{6,7},{7,6},{8,9},{9,8},{10,11... | collective-permute-start | bytes 1572872 | tf_op jit(solution)/shard_map/ppermute | solution.py:191
  37.1 14.6 %collective-permute-start.5 = (bf16[2,2,2,1,8,2,2048]{6,5,4,2,1,3,0:T(2,128)(2,1)S(1)}, bf16[2,2,2,1,8,2,2048]{6,5,4,2,1,3,0:T(2,128)(2,1)S(1)}, u32[]{:S(2)}, u32[]{:S(2)}) collective-permute-start(bf16[2,2,2,1,8,2,2048]{6,5,4,2,1,3,0:T(2,128)(2,1)S(1)} %pad_maximum_fusion.7), channel_id=1, source_target_pairs={{0,1},{1,0},{2,3},{3,2},{4,5},{5,4},{6,7},{7,6},{8,9},{9,8},{10,11... | collective-permute-start | bytes 1572872 | tf_op jit(solution)/shard_map/ppermute | solution.py:191

commit v12 on v5

--- a/solution.py
+++ b/solution.py
@@ -182,20 +182,27 @@
     seg_total = lax.axis_size("seg")
     me = lax.axis_index("seg")
     rows, parts, local_bins = bank_rows.shape
+    piece_rows = local_bins // RADIX
     held = bank_rows[None]
     distance = seg_total // 2
     steps = 0
-    while distance >= 1:
+    while distance > 1:
         pairs = [(i, i ^ distance) for i in range(seg_total)]
         arrived = lax.ppermute(held, "seg", pairs)
-        upper = (me & distance) != 0
-        held = jnp.stack([jnp.where(upper, arrived, held), jnp.where(upper, held, arrived)], axis=0)
+        slot = lax.broadcasted_iota(jnp.int32, (2,) + (1,) * held.ndim, 0)
+        held = jnp.where(slot == (me // distance) % 2, held[None], arrived[None])
         distance //= 2
         steps += 1
-    held = held.reshape((2,) * steps + (rows, parts, local_bins // RADIX, RADIX))
-    order = tuple(reversed(range(steps)))
-    held = jnp.transpose(held, (steps, steps + 1) + order + (steps + 2, steps + 3))
-    return held.reshape(rows, parts, seg_total * local_bins // RADIX, RADIX)
+    arrived = lax.ppermute(held, "seg", [(i, i ^ 1) for i in range(seg_total)])
+
+    def by_template(value):
+        value = value.reshape((2,) * steps + (rows, parts, piece_rows, RADIX))
+        value = jnp.transpose(value, (steps, steps + 1) + tuple(reversed(range(steps))) + (steps + 2, steps + 3))
+        return value.reshape(rows, parts, seg_total // 2, 1, piece_rows, RADIX)
+
+    slot = lax.broadcasted_iota(jnp.int32, (1, 1, 1, 2, 1, 1), 3)
+    every = jnp.where(slot == me % 2, by_template(held), by_template(arrived))
+    return every.reshape(rows, parts, seg_total * piece_rows, RADIX)
 
 
 def local(strain, gate_mask, template_bank):

time: 66.3 us -> 70.4 us (1.062)
  waiting for transfers between devices: 3.85 us -> 13.5 us
  starting transfers between devices: 16.8 us -> 11.7 us
  other arithmetic: 16.5 us -> 14.2 us
  local copies, waits for them, and re-layouts: 5.59 us -> 6.83 us
    ppermute x8 -> x6, waiting for transfers between devices: 3.84 us -> 12.8 us  [gathered_bank(): arrived = lax.ppermute(held, 'seg', pairs)]
    ppermute x8 -> x6, starting transfers between devices: 12.2 us -> 6.65 us  [gathered_bank(): arrived = lax.ppermute(held, 'seg', pairs)]
    another operation x15 -> x0, other arithmetic: 5.46 us -> none  [gathered_bank(): jnp.stack([jnp.where(upper, arrived, held), jnp.where(upper, held, arrive...]
    another operation x6 -> x0, local copies, waits for them, and re-layouts: 3.62 us -> none  [gathered_bank(): jnp.stack([jnp.where(upper, arrived, held), jnp.where(upper, held, arrive...]
    select_n x2 -> x9, other arithmetic: 2.46 us -> 5.69 us  [the longest x8 4.17 us: gathered_bank(): held = jnp.where(slot == me // distance % 2, held[None], arrived[None])]
    reshape x0 -> x2, local copies, waits for them, and re-layouts: none -> 2.75 us  [by_template(): value = value.reshape((2,) * steps + (rows, parts, piece_rows, RADIX))]
    slice x0 -> x1, local copies, waits for them, and re-layouts: none -> 1.06 us  [local(): bank = gathered_bank(template_bank[start:start + SUBBANK])]
    broadcast_in_dim x1 -> x16, local copies, waits for them, and re-layouts: 0.09 us -> 1.14 us  [the longest x14 0.97 us: gathered_bank(): held = jnp.where(slot == me // distance % 2, held[None], arrived[None])]
  transfers between devices with their start and end apart: 9 -> 9, of which waited for: 3 -> 4; matrix products, arithmetic and copies ran while one was open for 29% -> 22% of each run, Pallas kernels for 16% -> 0%
where the time goes in v12:
time: 70.4 us; the launch traced here: 69.6 us
  Pallas kernels  20.5 us (29%)
  other arithmetic  14.2 us (20%)
  waiting for transfers between devices  13.5 us (19%)
  starting transfers between devices  11.7 us (17%)
  local copies, waits for them, and re-layouts  6.83 us (10%)
  matrix products  2.41 us (3%)
    pallas_call x2, Pallas kernels, window_peaks(): pl.pallas_call(peaks_kernel, out_shape=jax.ShapeDtypeStruct((template_tot...  20.5 us
    ppermute x6, waiting for transfers between devices, gathered_bank(): arrived = lax.ppermute(held, 'seg', pairs)  12.8 us
    ppermute x6, starting transfers between devices, gathered_bank(): arrived = lax.ppermute(held, 'seg', pairs)  6.65 us
    ppermute x1, starting transfers between devices, passed_along(): return lax.ppermute(value, axis, pairs)  4.25 us
    select_n x8, other arithmetic, gathered_bank(): held = jnp.where(slot == me // distance % 2, held[None], arrived[None])  4.17 us
    reshape x2, local copies, waits for them, and re-layouts, by_template(): value = value.reshape((2,) * steps + (rows, parts, piece_rows, RADIX))  2.75 us
    sin x3, other arithmetic, angle_table(): return (jnp.cos(angle_value), jnp.sin(angle_value))  2.54 us
    convert_element_type x2, other arithmetic, table_pair(): return (high.astype(jnp.bfloat16), (value - high).astype(jnp.bfloat16))  1.72 us
  transfers between devices with their start and end apart: 9, of which 4 were waited for; matrix products, arithmetic and copies ran while one was open for 22% of the time, Pallas kernels for 0%

profile of v12, /device:TPU:1, one launch (start us, length us, event | category | flops | bytes accessed | tf_op | source)
XLA Modules:
  0.0 69.6 jit_solution(17666341791225907041)
XLA Ops:
  0.0 1.1 %fusion.52 = (bf16[8,2,2048]{2,1,0:T(2,128)(2,1)S(1)}, bf16[1,8,2,2048]{3,2,1,0:T(2,128)(2,1)S(1)}, bf16[1,8,2,2048]{3,2,1,0:T(2,128)(2,1)S(1)}, bf16[8,2,2048]{2,1,0:T(2,128)(2,1)S(1)}) fusion(bf16[16,2,2048]{2,1,0:T(2,128)(2,1)} %param.5), kind=kLoop, calls=%fused_computation.104 | loop fusion | bytes 393216 | tf_op jit(solution)/shard_map/slice | solution.py:220
  1.1 3.2 %collective-permute-start.5 = (bf16[1,8,2,2048]{3,2,1,0:T(2,128)(2,1)S(1)}, bf16[1,8,2,2048]{3,2,1,0:T(2,128)(2,1)S(1)}, u32[]{:S(2)}, u32[]{:S(2)}) collective-permute-start(bf16[1,8,2,2048]{3,2,1,0:T(2,128)(2,1)S(1)} %get-tuple-element.17), channel_id=1, source_target_pairs={{0,8},{1,9},{2,10},{3,11},{4,12},{5,13},{6,14},{7,15},{8,0},{9,1},... | collective-permute-start | bytes 196616 | tf_op jit(solution)/shard_map/ppermute | solution.py:191
  4.3 0.1 collective-permute-start.1
  4.4 0.0 copy-done.2
  4.4 1.0 %convert_multiply_fusion = f32[65536]{0:T(1024)S(1)} fusion(f32[65536]{0:T(1024)S(1)} %copy-done.2, s32[65536]{0:T(1024)} %param.4), kind=kLoop, calls=%fused_computation.53 | loop fusion | flops 131072 | bytes 786432 | tf_op jit(solution)/shard_map/mul | solution.py:209
  5.4 4.2 %collective-permute-start = (f32[32768]{0:T(1024)S(1)}, f32[32768]{0:T(1024)S(1)}, u32[]{:S(2)}, u32[]{:S(2)}) collective-permute-start(f32[32768]{0:T(1024)S(1)} %get-tuple-element.13), channel_id=1, source_target_pairs={{0,1},{1,2},{2,3},{3,4},{4,5},{5,6},{6,7},{7,8},{8,9},{9,10},{10,1... | collective-permute-start | bytes 393224 | tf_op jit(solution)/shard_map/ppermute | solution.py:23
  9.7 1.0 %fusion.30 = (f32[256,256]{1,0:T(8,128)S(1)}, f32[256,256]{1,0:T(8,128)S(1)}) fusion(), kind=kLoop, calls=%fused_computation.73 | loop fusion | flops 983040 | bytes 524288 | tf_op jit(solution)/shard_map/cos | solution.py:31
  10.7 0.1 concatenate.44
  10.8 1.0 %fusion.27 = (f32[256,256]{1,0:T(8,128)S(1)}, f32[256,256]{1,0:T(8,128)S(1)}) fusion(), kind=kLoop, calls=%fused_computation.70 | loop fusion | flops 917504 | bytes 524288 | tf_op jit(solution)/shard_map/sin | solution.py:31
  11.9 0.0 copy-start
  11.9 1.0 %fusion.29 = f32[256,256]{1,0:T(8,128)S(1)} fusion(), kind=kLoop, calls=%fused_computation.72 | loop fusion | flops 917504 | bytes 262144 | tf_op jit(solution)/shard_map/sin | solution.py:31
  12.9 0.5 fusion.35
  13.4 0.5 fusion.37
  14.1 0.1 broadcast_in_dim.287
  14.2 0.1 broadcast_in_dim.283
  14.2 0.1 broadcast_in_dim.284
  14.4 0.1 copy.7
  14.5 0.1 copy.8
  14.6 0.9 %fusion.1 = (bf16[512,256]{1,0:T(8,128)(2,1)}, bf16[512,256]{1,0:T(8,128)(2,1)}) fusion(f32[256,256]{1,0:T(8,128)S(1)} %get-tuple-element.37, f32[256,256]{1,0:T(8,128)S(1)} %fusion.29, f32[256,256]{1,0:T(8,128)S(1)} %get-tuple-element.38), kind=kLoop, calls=%fused_computation.12 | loop fusion | flops 1310720 | bytes 1310720 | tf_op jit(solution)/shard_map/convert_element_type | solution.py:72
  15.5 0.9 %fusion = (bf16[512,256]{1,0:T(8,128)(2,1)}, bf16[512,256]{1,0:T(8,128)(2,1)}) fusion(f32[256,128]{1,0:T(8,128)S(1)} %get-tuple-element.42, f32[256,128]{1,0:T(8,128)S(1)} %get-tuple-element.41, f32[256,128]{1,0:T(8,128)S(1)} %fusion.37), kind=kLoop, calls=%fused_computation.11 | loop fusion | flops 917504 | bytes 917504 | tf_op jit(solution)/shard_map/convert_element_type | solution.py:72
  16.3 0.0 collective-permute-done.5
  16.3 0.0 collective-permute-done.1
  16.4 0.4 broadcast_select_fusion.13
  16.7 0.4 broadcast_select_fusion.11
  17.1 1.4 %collective-permute-start.6 = (bf16[2,1,8,2,2048]{4,0,3,2,1:T(2,128)(2,1)S(1)}, bf16[2,1,8,2,2048]{4,0,3,2,1:T(2,128)(2,1)S(1)}, u32[]{:S(2)}, u32[]{:S(2)}) collective-permute-start(bf16[2,1,8,2,2048]{4,0,3,2,1:T(2,128)(2,1)S(1)} %get-tuple-element.36), channel_id=1, source_target_pairs={{0,4},{1,5},{2,6},{3,7},{4,0},{5,1},{6,2},{7,3},{8,12},{9,13},{10,... | collective-permute-start | bytes 393224 | tf_op jit(solution)/shard_map/ppermute | solution.py:191
  18.5 0.2 collective-permute-start.2
  18.8 0.1 broadcast_select_fusion.15
  18.9 0.0 collective-permute-done
  18.9 0.1 copy.6
  19.0 0.6 fusion.3
  19.6 0.0 copy-done
  19.6 0.0 copy-done.1
  19.6 0.1 multiply_add_fusion
  19.8 0.9 %convolution_bitcast_fusion.1 = f32[2,128,512]{2,1,0:T(8,128)S(1)} fusion(f32[2,256,256]{2,1,0:T(8,128)S(1)} %get-tuple-element.6, f32[2,256,256]{2,1,0:T(8,128)S(1)} %get-tuple-element.5), kind=kOutput, calls=%fused_computation.1 | convolution fusion | flops 202047488 | bytes 1572864 | tf_op jit(solution)/shard_map/bnf,nk->bkf/dot_general | solution.py:53
  20.7 0.9 %convolution_bitcast_fusion = f32[2,128,512]{2,1,0:T(8,128)S(1)} fusion(f32[2,256,256]{2,1,0:T(8,128)S(1)} %get-tuple-element.6, f32[2,256,256]{2,1,0:T(8,128)S(1)} %get-tuple-element.5), kind=kOutput, calls=%fused_computation | convolution fusion | flops 202047488 | bytes 1572864 | tf_op jit(solution)/shard_map/bnf,nk->bkf/dot_general | solution.py:54
  21.6 0.1 slice_add_fusion
  21.7 0.9 %pad_maximum_fusion.4.spec_ref = f32[2,128,512]{2,1,0:T(8,128)} fusion(f32[2,128,256]{2,1,0:T(8,128)S(1)} %get-tuple-element.8, f32[2,128,256]{2,1,0:T(8,128)S(1)} %get-tuple-element.7), kind=kLoop, calls=%fused_computation.26 | loop fusion | flops 131072 | bytes 1048576 | tf_op jit(solution)/shard_map/concatenate | solution.py:55
  22.6 0.0 collective-permute-done.6
  22.6 1.6 %collective-permute-done.2 = bf16[2,1,8,2,2048]{4,0,3,2,1:T(2,128)(2,1)S(1)} collective-permute-done((bf16[2,1,8,2,2048]{4,0,3,2,1:T(2,128)(2,1)S(1)}, bf16[2,1,8,2,2048]{4,0,3,2,1:T(2,128)(2,1)S(1)}, u32[]{:S(2)}, u32[]{:S(2)}) %collective-permute-start.2) | collective-permute-done | bytes 131104 | tf_op jit(solution)/shard_map/ppermute | solution.py:191
  24.1 0.8 %broadcast_select_fusion.7 = (bf16[2,2,1,8,2,2048]{5,0,1,4,3,2:T(2,128)(2,1)S(1)}, bf16[2,2,1,8,2,2048]{5,0,1,4,3,2:T(2,128)(2,1)S(1)}) fusion(pred[2]{0:T(512)(128)(4,1)S(1)} %iota_compare_fusion.2, bf16[2,8,2,2048]{3,0,2,1:T(2,128)(2,1)S(1)} %bitcast.73, bf16[2,8,2,2048]{3,0,2,1:T(2,128)(2,1)S(1)} %get-tuple-element.33, ...), kind=kLoop, calls=%fused_computation.35 | loop fusion | flops 262144 | bytes 1048578 | tf_op jit(solution)/shard_map/jit(_where)/select_n | solution.py:193
  24.9 1.8 %collective-permute-start.3 = (bf16[2,2,1,8,2,2048]{5,0,1,4,3,2:T(2,128)(2,1)S(1)}, bf16[2,2,1,8,2,2048]{5,0,1,4,3,2:T(2,128)(2,1)S(1)}, u32[]{:S(2)}, u32[]{:S(2)}) collective-permute-start(bf16[2,2,1,8,2,2048]{5,0,1,4,3,2:T(2,128)(2,1)S(1)} %get-tuple-element.31), channel_id=1, source_target_pairs={{0,2},{1,3},{2,0},{3,1},{4,6},{5,7},{6,4},{7,5},{8,10},{9,11},{10,... | collective-permute-start | bytes 786440 | tf_op jit(solution)/shard_map/ppermute | solution.py:191
  26.7 0.1 collective-permute-start.7
  26.7 0.1 broadcast_in_dim.338
  26.8 0.1 broadcast_in_dim.301
  26.9 0.8 %broadcast_select_fusion.5 = (bf16[2,2,8,2,2048]{4,0,1,3,2:T(2,128)(2,1)S(1)}, bf16[2,2,8,2,2048]{4,0,1,3,2:T(2,128)(2,1)S(1)}) fusion(pred[2]{0:T(512)(128)(4,1)S(1)} %iota_compare_fusion.2, bf16[2,8,2,2048]{3,0,2,1:T(2,128)(2,1)S(1)} %bitcast.74, bf16[2,8,2,2048]{3,0,2,1:T(2,128)(2,1)S(1)} %get-tuple-element.33, bf16[2,8,2,2048]{3,0,2,1:T(2,128)(2,1)S(1)} %bitcast.72, ...), kind=kLoop, calls=%fused_computation.33 | loop fusion | flops 262144 | bytes 1048578 | tf_op jit(solution)/shard_map/jit(_where)/select_n | solution.py:193
  27.7 5.6 %collective-permute-done.3 = bf16[2,2,1,8,2,2048]{5,0,1,4,3,2:T(2,128)(2,1)S(1)} collective-permute-done((bf16[2,2,1,8,2,2048]{5,0,1,4,3,2:T(2,128)(2,1)S(1)}, bf16[2,2,1,8,2,2048]{5,0,1,4,3,2:T(2,128)(2,1)S(1)}, u32[]{:S(2)}, u32[]{:S(2)}) %collective-permute-start.3) | collective-permute-done | bytes 262176 | tf_op jit(solution)/shard_map/ppermute | solution.py:191
  33.2 5.6 %collective-permute-done.7 = bf16[2,2,1,8,2,2048]{5,0,1,4,3,2:T(2,128)(2,1)S(1)} collective-permute-done((bf16[2,2,1,8,2,2048]{5,0,1,4,3,2:T(2,128)(2,1)S(1)}, bf16[2,2,1,8,2,2048]{5,0,1,4,3,2:T(2,128)(2,1)S(1)}, u32[]{:S(2)}, u32[]{:S(2)}) %collective-permute-start.7) | collective-permute-done | bytes 262176 | tf_op jit(solution)/shard_map/ppermute | solution.py:191
  38.9 1.5 %broadcast_select_fusion.1 = (bf16[2,2,2,1,8,2,2048]{6,0,1,2,5,4,3:T(2,128)(2,1)S(1)}, bf16[2,2,2,1,8,2,2048]{6,0,1,2,5,4,3:T(2,128)(2,1)S(1)}) fusion(pred[2]{0:T(512)(128)(4,1)S(1)} %iota_compare_fusion.3, bf16[2,2,8,2,2048]{4,0,1,3,2:T(2,128)(2,1)S(1)} %bitcast.75, bf16[2,2,8,2,2048]{4,0,1,3,2:T(2,128)(2,1)S(1)} %get-tuple-element.29, ...), kind=kLoop, calls=%fused_computation.6 | loop fusion | flops 524288 | bytes 2097154 | tf_op jit(solution)/shard_map/jit(_where)/select_n | solution.py:193
  40.4 0.7 %collective-permute-start.4 = (bf16[2,2,2,1,8,2,2048]{6,0,1,2,5,4,3:T(2,128)(2,1)S(1)}, bf16[2,2,2,1,8,2,2048]{6,0,1,2,5,4,3:T(2,128)(2,1)}, u32[]{:S(2)}, u32[]{:S(2)}) collective-permute-start(bf16[2,2,2,1,8,2,2048]{6,0,1,2,5,4,3:T(2,128)(2,1)S(1)} %get-tuple-element.27), channel_id=1, source_target_pairs={{0,1},{1,0},{2,3},{3,2},{4,5},{5,4},{6,7},{7,6},{8,9},{9,8},{10,11... | collective-permute-start | bytes 1572872 | tf_op jit(solution)/shard_map/ppermute | solution.py:196
  41.1 0.1 collective-permute-start.8
  41.2 0.1 broadcast_select_fusion.9
  41.3 0.2 broadcast_in_dim.313
  41.5 0.2 broadcast_in_dim.348
  41.9 0.2 broadcast_select_fusion.3
  42.0 0.8 %collective-permute-done.4 = bf16[2,2,2,1,8,2,2048]{6,0,1,2,5,4,3:T(2,128)(2,1)} collective-permute-done((bf16[2,2,2,1,8,2,2048]{6,0,1,2,5,4,3:T(2,128)(2,1)S(1)}, bf16[2,2,2,1,8,2,2048]{6,0,1,2,5,4,3:T(2,128)(2,1)}, u32[]{:S(2)}, u32[]{:S(2)}) %collective-permute-start.4) | collective-permute-done | bytes 524320 | tf_op jit(solution)/shard_map/ppermute | solution.py:196
  42.8 1.4 %reshape.186 = bf16[2,2,2,8,2,8,256]{6,5,0,1,2,4,3:T(8,128)(2,1)S(1)} reshape(bf16[2,2,2,1,8,2,2048]{6,0,1,2,5,4,3:T(2,128)(2,1)} %collective-permute-done.4) | data formatting | bytes 1048576 | tf_op jit(solution)/shard_map/reshape | solution.py:199
  44.2 0.0 collective-permute-done.8
  44.2 1.4 %reshape.188 = bf16[2,2,2,8,2,8,256]{6,5,0,1,2,4,3:T(8,128)(2,1)S(1)} reshape(bf16[2,2,2,1,8,2,2048]{6,0,1,2,5,4,3:T(2,128)(2,1)} %collective-permute-done.8) | data formatting | bytes 1048576 | tf_op jit(solution)/shard_map/reshape | solution.py:199
  45.6 1.5 %bitcast_select_fusion.1 = (bf16[8,2,128,256]{3,2,1,0:T(8,128)(2,1)}, bf16[8,2,128,256]{3,2,1,0:T(8,128)(2,1)}) fusion(pred[128]{0:T(512)(128)(4,1)S(1)} %broadcast_in_dim.284, bf16[8,2,8,8,256]{4,3,2,1,0:T(8,128)(2,1)S(1)} %bitcast.65, bf16[8,2,8,8,256]{4,3,2,1,0:T(8,128)(2,1)S(1)} %get-tuple-element.21, bf16[8,2,8,8,256]{4,3,2,1,0:T(8,128)(2,1)S(1)} %bitcast.66, ...), kind=kLoop, calls=%fused_computation.4 | loop fusion | flops 1048576 | bytes 4194432 | tf_op jit(solution)/shard_map/jit(_where)/select_n | solution.py:204
  47.1 10.3 %shard_map.37 = f32[8,2,128]{2,1,0:T(2,128)} custom-call(f32[2,128,512]{2,1,0:T(8,128)} %pad_maximum_fusion.4.spec_ref, bf16[8,2,128,256]{3,2,1,0:T(8,128)(2,1)} %get-tuple-element.19.bank_ref, bf16[512,256]{1,0:T(8,128)(2,1)} %get-tuple-element.12.fh_ref, bf16[512,256]{1,0:T(8,128)(2,1)} %get-tuple-element.11.fl_ref, f32[256,256]{1,0:T(8,128)} %copy-done.1, ...), custom_call_target="tpu_custom_call" | custom-call | flops 6442450944 | bytes 1581056 | tf_op jit(solution)/shard_map/pallas_call | solution.py:157
  57.4 0.7 %copy.20 = f32[1,8,2,128]{3,1,2,0:T(8,128)S(1)} copy(f32[1,8,2,128]{3,2,1,0:T(2,128)} %bitcast.88) | data formatting | bytes 16384
  58.0 10.3 %shard_map.38 = f32[8,2,128]{2,1,0:T(2,128)} custom-call(f32[2,128,512]{2,1,0:T(8,128)} %pad_maximum_fusion.4.spec_ref, bf16[8,2,128,256]{3,2,1,0:T(8,128)(2,1)} %get-tuple-element.20.bank_ref, bf16[512,256]{1,0:T(8,128)(2,1)} %get-tuple-element.12.fh_ref, bf16[512,256]{1,0:T(8,128)(2,1)} %get-tuple-element.11.fl_ref, f32[256,256]{1,0:T(8,128)} %copy-done.1, ...), custom_call_target="tpu_custom_call" | custom-call | flops 6442450944 | bytes 1581056 | tf_op jit(solution)/shard_map/pallas_call | solution.py:157
  68.3 0.7 %copy.19 = f32[1,8,2,128]{3,1,2,0:T(8,128)S(1)} copy(f32[1,8,2,128]{3,2,1,0:T(2,128)} %bitcast.87) | data formatting | bytes 16384
  69.0 0.6 pad_maximum_fusion.5
  (18 shorter events, 0.5 us)
Async XLA Ops:
  0.0 4.4 %copy-start.2 = (f32[65536]{0:T(1024)S(1)}, f32[65536]{0:T(1024)}, u32[]{:S(2)}) copy-start(f32[65536]{0:T(1024)} %param.3) | copy-start | bytes 786436
  1.1 15.3 %collective-permute-start.5 = (bf16[1,8,2,2048]{3,2,1,0:T(2,128)(2,1)S(1)}, bf16[1,8,2,2048]{3,2,1,0:T(2,128)(2,1)S(1)}, u32[]{:S(2)}, u32[]{:S(2)}) collective-permute-start(bf16[1,8,2,2048]{3,2,1,0:T(2,128)(2,1)S(1)} %get-tuple-element.17), channel_id=1, source_target_pairs={{0,8},{1,9},{2,10},{3,11},{4,12},{5,13},{6,14},{7,15},{8,0},{9,1},... | collective-permute-start | bytes 196616 | tf_op jit(solution)/shard_map/ppermute | solution.py:191
  4.3 12.1 %collective-permute-start.1 = (bf16[1,8,2,2048]{3,2,1,0:T(2,128)(2,1)S(1)}, bf16[1,8,2,2048]{3,2,1,0:T(2,128)(2,1)S(1)}, u32[]{:S(2)}, u32[]{:S(2)}) collective-permute-start(bf16[1,8,2,2048]{3,2,1,0:T(2,128)(2,1)S(1)} %get-tuple-element.16), channel_id=1, source_target_pairs={{0,8},{1,9},{2,10},{3,11},{4,12},{5,13},{6,14},{7,15},{8,0},{9,1},... | collective-permute-start | bytes 196616 | tf_op jit(solution)/shard_map/ppermute | solution.py:191
  5.4 13.5 %collective-permute-start = (f32[32768]{0:T(1024)S(1)}, f32[32768]{0:T(1024)S(1)}, u32[]{:S(2)}, u32[]{:S(2)}) collective-permute-start(f32[32768]{0:T(1024)S(1)} %get-tuple-element.13), channel_id=1, source_target_pairs={{0,1},{1,2},{2,3},{3,4},{4,5},{5,6},{6,7},{7,8},{8,9},{9,10},{10,1... | collective-permute-start | bytes 393224 | tf_op jit(solution)/shard_map/ppermute | solution.py:23
  11.9 7.8 %copy-start = (f32[256,256]{1,0:T(8,128)}, f32[256,256]{1,0:T(8,128)S(1)}, u32[]{:S(2)}) copy-start(f32[256,256]{1,0:T(8,128)S(1)} %get-tuple-element.39.ts_ref) | copy-start | bytes 786436
  11.9 7.8 %copy-start.1 = (f32[256,256]{1,0:T(8,128)}, f32[256,256]{1,0:T(8,128)S(1)}, u32[]{:S(2)}) copy-start(f32[256,256]{1,0:T(8,128)S(1)} %get-tuple-element.40.tc_ref) | copy-start | bytes 786436
  17.1 5.4 %collective-permute-start.6 = (bf16[2,1,8,2,2048]{4,0,3,2,1:T(2,128)(2,1)S(1)}, bf16[2,1,8,2,2048]{4,0,3,2,1:T(2,128)(2,1)S(1)}, u32[]{:S(2)}, u32[]{:S(2)}) collective-permute-start(bf16[2,1,8,2,2048]{4,0,3,2,1:T(2,128)(2,1)S(1)} %get-tuple-element.36), channel_id=1, source_target_pairs={{0,4},{1,5},{2,6},{3,7},{4,0},{5,1},{6,2},{7,3},{8,12},{9,13},{10,... | collective-permute-start | bytes 393224 | tf_op jit(solution)/shard_map/ppermute | solution.py:191
  18.5 5.6 %collective-permute-start.2 = (bf16[2,1,8,2,2048]{4,0,3,2,1:T(2,128)(2,1)S(1)}, bf16[2,1,8,2,2048]{4,0,3,2,1:T(2,128)(2,1)S(1)}, u32[]{:S(2)}, u32[]{:S(2)}) collective-permute-start(bf16[2,1,8,2,2048]{4,0,3,2,1:T(2,128)(2,1)S(1)} %get-tuple-element.35), channel_id=1, source_target_pairs={{0,4},{1,5},{2,6},{3,7},{4,0},{5,1},{6,2},{7,3},{8,12},{9,13},{10,... | collective-permute-start | bytes 393224 | tf_op jit(solution)/shard_map/ppermute | solution.py:191
  24.9 8.3 %collective-permute-start.3 = (bf16[2,2,1,8,2,2048]{5,0,1,4,3,2:T(2,128)(2,1)S(1)}, bf16[2,2,1,8,2,2048]{5,0,1,4,3,2:T(2,128)(2,1)S(1)}, u32[]{:S(2)}, u32[]{:S(2)}) collective-permute-start(bf16[2,2,1,8,2,2048]{5,0,1,4,3,2:T(2,128)(2,1)S(1)} %get-tuple-element.31), channel_id=1, source_target_pairs={{0,2},{1,3},{2,0},{3,1},{4,6},{5,7},{6,4},{7,5},{8,10},{9,11},{10,... | collective-permute-start | bytes 786440 | tf_op jit(solution)/shard_map/ppermute | solution.py:191
  26.7 12.2 %collective-permute-start.7 = (bf16[2,2,1,8,2,2048]{5,0,1,4,3,2:T(2,128)(2,1)S(1)}, bf16[2,2,1,8,2,2048]{5,0,1,4,3,2:T(2,128)(2,1)S(1)}, u32[]{:S(2)}, u32[]{:S(2)}) collective-permute-start(bf16[2,2,1,8,2,2048]{5,0,1,4,3,2:T(2,128)(2,1)S(1)} %get-tuple-element.32), channel_id=1, source_target_pairs={{0,2},{1,3},{2,0},{3,1},{4,6},{5,7},{6,4},{7,5},{8,10},{9,11},{10,... | collective-permute-start | bytes 786440 | tf_op jit(solution)/shard_map/ppermute | solution.py:191
  40.4 2.4 %collective-permute-start.4 = (bf16[2,2,2,1,8,2,2048]{6,0,1,2,5,4,3:T(2,128)(2,1)S(1)}, bf16[2,2,2,1,8,2,2048]{6,0,1,2,5,4,3:T(2,128)(2,1)}, u32[]{:S(2)}, u32[]{:S(2)}) collective-permute-start(bf16[2,2,2,1,8,2,2048]{6,0,1,2,5,4,3:T(2,128)(2,1)S(1)} %get-tuple-element.27), channel_id=1, source_target_pairs={{0,1},{1,0},{2,3},{3,2},{4,5},{5,4},{6,7},{7,6},{8,9},{9,8},{10,11... | collective-permute-start | bytes 1572872 | tf_op jit(solution)/shard_map/ppermute | solution.py:196
  41.1 3.0 %collective-permute-start.8 = (bf16[2,2,2,1,8,2,2048]{6,0,1,2,5,4,3:T(2,128)(2,1)S(1)}, bf16[2,2,2,1,8,2,2048]{6,0,1,2,5,4,3:T(2,128)(2,1)}, u32[]{:S(2)}, u32[]{:S(2)}) collective-permute-start(bf16[2,2,2,1,8,2,2048]{6,0,1,2,5,4,3:T(2,128)(2,1)S(1)} %get-tuple-element.28), channel_id=1, source_target_pairs={{0,1},{1,0},{2,3},{3,2},{4,5},{5,4},{6,7},{7,6},{8,9},{9,8},{10,11... | collective-permute-start | bytes 1572872 | tf_op jit(solution)/shard_map/ppermute | solution.py:196

commit v13 on v5

--- a/solution.py
+++ b/solution.py
@@ -178,42 +178,63 @@
     )(spectra, bank, *tables)
 
 
-def gathered_bank(bank_rows):
+def gathered_half(template_bank):
     seg_total = lax.axis_size("seg")
     me = lax.axis_index("seg")
-    rows, parts, local_bins = bank_rows.shape
-    held = bank_rows[None]
+    core = me % 2
+    template_total, parts, local_bins = template_bank.shape
+    half = template_total // 2
+    mine = lax.dynamic_slice_in_dim(template_bank, core * half, half, axis=0)
+    theirs = lax.dynamic_slice_in_dim(template_bank, (1 - core) * half, half, axis=0)
+    arrived = lax.ppermute(theirs[None], "seg", [(i, i ^ 1) for i in range(seg_total)])
+    upper = core != 0
+    held = jnp.stack([jnp.where(upper, arrived, mine[None]), jnp.where(upper, mine[None], arrived)], axis=0)
+    order = [1]
     distance = seg_total // 2
-    steps = 0
-    while distance >= 1:
+    while distance > 1:
         pairs = [(i, i ^ distance) for i in range(seg_total)]
         arrived = lax.ppermute(held, "seg", pairs)
         upper = (me & distance) != 0
         held = jnp.stack([jnp.where(upper, arrived, held), jnp.where(upper, held, arrived)], axis=0)
+        order.append(distance)
         distance //= 2
-        steps += 1
-    held = held.reshape((2,) * steps + (rows, parts, local_bins // RADIX, RADIX))
-    order = tuple(reversed(range(steps)))
-    held = jnp.transpose(held, (steps, steps + 1) + order + (steps + 2, steps + 3))
-    return held.reshape(rows, parts, seg_total * local_bins // RADIX, RADIX)
+    steps = len(order)
+    held = held.reshape((2,) * steps + (half, parts, local_bins // RADIX, RADIX))
+    axis_distance = list(reversed(order))
+    bit_axes = tuple(sorted(range(steps), key=lambda axis: -axis_distance[axis]))
+    held = jnp.transpose(held, (steps, steps + 1) + bit_axes + (steps + 2, steps + 3))
+    return held.reshape(half, parts, seg_total * local_bins // RADIX, RADIX)
 
 
 def local(strain, gate_mask, template_bank):
+    seg_total = lax.axis_size("seg")
+    core = lax.axis_index("seg") % 2
+    bank = gathered_half(template_bank)
     gated = strain * gate_mask.astype(jnp.float32)
     local_blocks = gated.reshape(-1, BLOCK)
     block_total = local_blocks.shape[0]
     earlier = passed_along(local_blocks[block_total - 1], "seg", 1)
-    before = jnp.concatenate([earlier[None], local_blocks[:-1]], axis=0)
-    windows = jnp.concatenate([before, local_blocks], axis=1)
+    mine = jnp.concatenate([earlier[None], local_blocks], axis=0)
+    other = lax.ppermute(mine, "seg", [(i, i ^ 1) for i in range(seg_total)])
+    chip_blocks = jnp.where(
+        core == 0,
+        jnp.concatenate([mine, other[1:]], axis=0),
+        jnp.concatenate([other, mine[1:]], axis=0),
+    )
+    windows = jnp.concatenate([chip_blocks[:-1], chip_blocks[1:]], axis=1)
     spectra = forward(windows)
     tables = inverse_tables(spectra.shape[1])
-    template_total = template_bank.shape[0]
-    results = []
-    for start in range(0, template_total, SUBBANK):
-        bank = gathered_bank(template_bank[start : start + SUBBANK])
-        peaks = window_peaks(spectra, bank, tables)
-        results.append(peaks.reshape(bank.shape[0], block_total * (RADIX // 2)))
-    return jnp.concatenate(results, axis=0)
+    partner_spectra = lax.dynamic_slice_in_dim(spectra, (1 - core) * block_total, block_total, axis=0)
+    own_spectra = lax.dynamic_slice_in_dim(spectra, core * block_total, block_total, axis=0)
+    half = bank.shape[0]
+    partner_peaks = window_peaks(partner_spectra, bank, tables).reshape(half, block_total * (RADIX // 2))
+    returned = lax.ppermute(partner_peaks, "seg", [(i, i ^ 1) for i in range(seg_total)])
+    own_peaks = window_peaks(own_spectra, bank, tables).reshape(half, block_total * (RADIX // 2))
+    return jnp.where(
+        core == 0,
+        jnp.concatenate([own_peaks, returned], axis=0),
+        jnp.concatenate([returned, own_peaks], axis=0),
+    )
 
 
 def solution(mesh):

time: 66.3 us -> 65.5 us (0.988)
  the two profiles are of different devices: /device:TPU:1 before, /device:TPU:19 now
where the time goes in v13:
time: 65.5 us; the launch traced here: 65.2 us
  Pallas kernels  20.5 us (31%)
  waiting for transfers between devices  14.6 us (22%)
  starting transfers between devices  11.6 us (18%)
  other arithmetic  11.3 us (17%)
  matrix products  3.71 us (6%)
  local copies, waits for them, and re-layouts  3.13 us (5%)
    pallas_call x2, Pallas kernels, window_peaks(): pl.pallas_call(peaks_kernel, out_shape=jax.ShapeDtypeStruct((template_tot...  20.5 us
    ppermute x3, waiting for transfers between devices, gathered_half(): arrived = lax.ppermute(held, 'seg', pairs)  14.6 us
    ppermute x3, starting transfers between devices, gathered_half(): arrived = lax.ppermute(held, 'seg', pairs)  5.07 us
    ppermute x1, starting transfers between devices, passed_along(): return lax.ppermute(value, axis, pairs)  3.71 us
    sin x3, other arithmetic, angle_table(): return (jnp.cos(angle_value), jnp.sin(angle_value))  2.54 us
    ppermute x1, starting transfers between devices, local(): lax.ppermute(partner_peaks, 'seg', [(i, i ^ 1) for i in range(seg_total)])  1.93 us
    convert_element_type x2, other arithmetic, table_pair(): return (high.astype(jnp.bfloat16), (value - high).astype(jnp.bfloat16))  1.73 us
    unnamed x6, local copies, waits for them, and re-layouts  1.4 us
  transfers between devices with their start and end apart: 7, of which 3 were waited for; matrix products, arithmetic and copies ran while one was open for 22% of the time, Pallas kernels for 16%

profile of v13, /device:TPU:19, one launch (start us, length us, event | category | flops | bytes accessed | tf_op | source)
XLA Modules:
  0.0 65.2 jit_solution(146360683095534230)
XLA Ops:
  0.0 1.1 %convert_multiply_fusion = f32[65536]{0:T(1024)S(1)} fusion(f32[65536]{0:T(1024)} %param.3, s32[65536]{0:T(1024)} %param.4), kind=kLoop, calls=%fused_computation.57 | loop fusion | flops 131072 | bytes 786432 | tf_op jit(solution)/shard_map/mul | solution.py:213
  1.1 3.7 %collective-permute-start = (f32[32768]{0:T(1024)S(1)}, f32[32768]{0:T(1024)S(1)}, u32[]{:S(2)}, u32[]{:S(2)}) collective-permute-start(f32[32768]{0:T(1024)S(1)} %slice.49), channel_id=1, source_target_pairs={{0,1},{1,2},{2,3},{3,4},{4,5},{5,6},{6,7},{7,8},{8,9},{9,10},{10,1... | collective-permute-start | bytes 393224 | tf_op jit(solution)/shard_map/ppermute | solution.py:23
  4.8 1.0 %constant_dynamic-slice_fusion = (bf16[8,2,2048]{2,1,0:T(2,128)(2,1)S(1)}, bf16[8,2,2048]{2,1,0:T(2,128)(2,1)S(1)}) fusion(bf16[16,2,2048]{2,1,0:T(2,128)(2,1)} %param.5, s32[]{:T(128)S(6)} %select_n.161, s32[]{:T(128)S(6)} %select_n.160), kind=kLoop, calls=%fused_computation.92 | loop fusion | bytes 262152 | tf_op jit(solution)/shard_map/dynamic_slice | solution.py:187
  5.8 0.1 collective-permute-start.2
  5.9 1.0 %fusion.33 = (f32[256,256]{1,0:T(8,128)S(1)}, f32[256,256]{1,0:T(8,128)S(1)}) fusion(), kind=kLoop, calls=%fused_computation.74 | loop fusion | flops 983040 | bytes 524288 | tf_op jit(solution)/shard_map/cos | solution.py:31
  6.9 1.0 %fusion.30 = (f32[256,256]{1,0:T(8,128)S(1)}, f32[256,256]{1,0:T(8,128)S(1)}) fusion(), kind=kLoop, calls=%fused_computation.71 | loop fusion | flops 917504 | bytes 524288 | tf_op jit(solution)/shard_map/sin | solution.py:31
  8.0 0.0 copy-start
  8.0 0.0 copy-start.1
  8.0 0.5 fusion.40
  8.5 0.5 fusion.42
  9.1 0.9 %fusion.7 = (bf16[512,256]{1,0:T(8,128)(2,1)}, bf16[512,256]{1,0:T(8,128)(2,1)}) fusion(f32[256,128]{1,0:T(8,128)S(1)} %get-tuple-element.32, f32[256,128]{1,0:T(8,128)S(1)} %get-tuple-element.31, f32[256,128]{1,0:T(8,128)S(1)} %fusion.42), kind=kLoop, calls=%fused_computation.21 | loop fusion | flops 917504 | bytes 917504 | tf_op jit(solution)/shard_map/convert_element_type | solution.py:72
  9.9 0.0 collective-permute-done.2
  10.0 0.1 collective-permute-start.3
  10.1 1.0 %fusion.32 = f32[256,256]{1,0:T(8,128)S(1)} fusion(), kind=kLoop, calls=%fused_computation.73 | loop fusion | flops 917504 | bytes 262144 | tf_op jit(solution)/shard_map/sin | solution.py:31
  11.1 0.2 reshape.48
  11.3 0.9 %fusion.8 = (bf16[512,256]{1,0:T(8,128)(2,1)}, bf16[512,256]{1,0:T(8,128)(2,1)}) fusion(f32[256,256]{1,0:T(8,128)S(1)} %get-tuple-element.27, f32[256,256]{1,0:T(8,128)S(1)} %fusion.32, f32[256,256]{1,0:T(8,128)S(1)} %get-tuple-element.28), kind=kLoop, calls=%fused_computation.22 | loop fusion | flops 1310720 | bytes 1310720 | tf_op jit(solution)/shard_map/convert_element_type | solution.py:72
  12.1 3.4 %collective-permute-done.3 = bf16[2,1,8,2,2048]{4,2,3,0,1:T(8,128)(2,1)S(1)} collective-permute-done((bf16[2,1,8,2,2048]{4,2,3,0,1:T(8,128)(2,1)S(1)}, bf16[2,1,8,2,2048]{4,2,3,0,1:T(8,128)(2,1)S(1)}, u32[]{:S(2)}, u32[]{:S(2)}) %collective-permute-start.3) | collective-permute-done | bytes 131104 | tf_op jit(solution)/shard_map/ppermute | solution.py:196
  15.6 4.9 %collective-permute-start.4 = (bf16[2,2,1,8,2,2048]{5,3,4,1,0,2:T(8,128)(2,1)S(1)}, bf16[2,2,1,8,2,2048]{5,3,4,1,0,2:T(8,128)(2,1)S(1)}, u32[]{:S(2)}, u32[]{:S(2)}) collective-permute-start(bf16[2,2,1,8,2,2048]{5,3,4,1,0,2:T(8,128)(2,1)S(1)} %pad_maximum_fusion.12), channel_id=1, source_target_pairs={{0,4},{1,5},{2,6},{3,7},{4,0},{5,1},{6,2},{7,3},{8,12},{9,13},{10,... | collective-permute-start | bytes 786440 | tf_op jit(solution)/shard_map/ppermute | solution.py:196
  20.5 0.0 collective-permute-done
  20.5 0.2 pad_maximum_fusion.10
  20.7 0.8 %collective-permute-start.1 = (f32[3,32768]{1,0:T(4,128)S(1)}, f32[3,32768]{1,0:T(4,128)S(1)}, u32[]{:S(2)}, u32[]{:S(2)}) collective-permute-start(f32[3,32768]{1,0:T(4,128)S(1)} %pad_maximum_fusion.10), channel_id=1, source_target_pairs={{0,1},{1,0},{2,3},{3,2},{4,5},{5,4},{6,7},{7,6},{8,9},{9,8},{10,11... | collective-permute-start | bytes 1179656 | tf_op jit(solution)/shard_map/ppermute | solution.py:218
  21.6 5.2 %collective-permute-done.4 = bf16[2,2,1,8,2,2048]{5,3,4,1,0,2:T(8,128)(2,1)S(1)} collective-permute-done((bf16[2,2,1,8,2,2048]{5,3,4,1,0,2:T(8,128)(2,1)S(1)}, bf16[2,2,1,8,2,2048]{5,3,4,1,0,2:T(8,128)(2,1)S(1)}, u32[]{:S(2)}, u32[]{:S(2)}) %collective-permute-start.4) | collective-permute-done | bytes 262176 | tf_op jit(solution)/shard_map/ppermute | solution.py:196
  26.8 0.1 pad_maximum_fusion.11
  26.8 0.1 collective-permute-start.5
  26.9 0.0 collective-permute-done.1
  26.9 0.1 slice.50
  27.1 0.5 maximum_select_fusion
  27.5 0.2 fusion.56
  27.8 0.2 pad_maximum_fusion.7
  28.0 1.1 %fusion.4 = f32[4,256,512]{2,1,0:T(8,128)S(1)} fusion(f32[1,4,256,256]{3,1,2,0:T(4,128)S(1)} %bitcast.57, f32[256,256]{1,0:T(8,128)S(1)} %get-tuple-element.28, f32[256,256]{1,0:T(8,128)S(1)} %get-tuple-element.27), kind=kOutput, calls=%fused_computation.9 | convolution fusion | flops 805437440 | bytes 3670016 | tf_op jit(solution)/shard_map/bnm,nf->bmf/dot_general | solution.py:41
  29.1 0.0 copy-done
  29.1 0.0 copy-done.1
  29.1 0.3 multiply_add_fusion
  29.4 1.3 %fusion.3 = f32[4,128,512]{2,1,0:T(8,128)S(1)} fusion(f32[4,256,256]{2,1,0:T(8,128)S(1)} %get-tuple-element.6, f32[4,256,256]{2,1,0:T(8,128)S(1)} %get-tuple-element.5), kind=kOutput, calls=%fused_computation.4 | convolution fusion | flops 403636224 | bytes 3145728 | tf_op jit(solution)/shard_map/bnf,nk->bkf/dot_general | solution.py:54
  30.7 1.3 %fusion.2 = f32[4,128,512]{2,1,0:T(8,128)S(1)} fusion(f32[4,256,256]{2,1,0:T(8,128)S(1)} %get-tuple-element.6, f32[4,256,256]{2,1,0:T(8,128)S(1)} %get-tuple-element.5), kind=kOutput, calls=%fused_computation.3 | convolution fusion | flops 403636224 | bytes 3145728 | tf_op jit(solution)/shard_map/bnf,nk->bkf/dot_general | solution.py:53
  32.0 0.1 slice_subtract_fusion
  32.2 1.1 %fusion.10 = (f32[2,128,512]{2,1,0:T(8,128)}, f32[2,128,512]{2,1,0:T(8,128)}) fusion(s32[]{:T(128)S(6)} %select_n.155, f32[4,128,256]{2,1,0:T(8,128)S(1)} %get-tuple-element.8, f32[4,128,256]{2,1,0:T(8,128)S(1)} %get-tuple-element.7, s32[]{:T(128)S(6)} %select_n.170), kind=kLoop, calls=%fused_computation.24 | loop fusion | flops 262144 | bytes 2097160 | tf_op jit(solution)/shard_map/concatenate | solution.py:55
  33.3 6.0 %collective-permute-done.5 = bf16[2,2,2,1,8,2,2048]{6,4,5,3,2,1,0:T(8,128)(2,1)S(1)} collective-permute-done((bf16[2,2,2,1,8,2,2048]{6,4,5,3,2,1,0:T(8,128)(2,1)S(1)}, bf16[2,2,2,1,8,2,2048]{6,4,5,3,2,1,0:T(8,128)(2,1)S(1)}, u32[]{:S(2)}, u32[]{:S(2)}) %collective-permute-start.5) | collective-permute-done | bytes 524320 | tf_op jit(solution)/shard_map/ppermute | solution.py:196
  39.3 0.1 broadcast_select_fusion.1
  39.4 0.1 copy.21
  39.5 0.1 copy.20
  39.6 1.1 %pad_maximum_fusion.8 = bf16[2,2,2,2,8,2,8,256]{7,6,3,0,1,2,5,4:T(8,128)(2,1)} fusion(bf16[1,2,2,2,8,2,8,256]{7,6,3,0,1,2,5,4:T(8,128)(2,1)S(1)} %copy.21, bf16[1,2,2,2,8,2,8,256]{7,6,3,0,1,2,5,4:T(8,128)(2,1)S(1)} %copy.20), kind=kLoop, calls=%fused_computation.14 | loop fusion | flops 524288 | bytes 2097152 | tf_op jit(solution)/shard_map/stack | solution.py:198
  40.7 10.3 %shard_map.38 = f32[8,2,128]{2,1,0:T(2,128)} custom-call(f32[2,128,512]{2,1,0:T(8,128)} %get-tuple-element.10.spec_ref, bf16[8,2,128,256]{3,2,1,0:T(8,128)(2,1)} %bitcast.60, bf16[512,256]{1,0:T(8,128)(2,1)} %get-tuple-element.20.fh_ref, bf16[512,256]{1,0:T(8,128)(2,1)} %get-tuple-element.19.fl_ref, f32[256,256]{1,0:T(8,128)} %copy-done.1, ...), custom_call_target="tpu_custom_call" | custom-call | flops 6442450944 | bytes 1581056 | tf_op jit(solution)/shard_map/pallas_call | solution.py:157
  51.0 0.7 %copy.40 = f32[1,8,2,128]{3,1,2,0:T(8,128)S(1)} copy(f32[1,8,2,128]{3,2,1,0:T(2,128)} %bitcast.68) | data formatting | bytes 16384
  51.7 1.9 %collective-permute-start.6 = (f32[8,256]{1,0:T(8,128)S(1)}, f32[8,256]{1,0:T(8,128)S(1)}, u32[]{:S(2)}, u32[]{:S(2)}) collective-permute-start(f32[8,256]{1,0:T(8,128)S(1)} %bitcast.66), channel_id=1, source_target_pairs={{0,1},{1,0},{2,3},{3,2},{4,5},{5,4},{6,7},{7,6},{8,9},{9,8},{10,11... | collective-permute-start | bytes 24584 | tf_op jit(solution)/shard_map/ppermute | solution.py:231
  53.6 10.3 %shard_map.37 = f32[8,2,128]{2,1,0:T(2,128)} custom-call(f32[2,128,512]{2,1,0:T(8,128)} %get-tuple-element.9.spec_ref, bf16[8,2,128,256]{3,2,1,0:T(8,128)(2,1)} %bitcast.61, bf16[512,256]{1,0:T(8,128)(2,1)} %get-tuple-element.20.fh_ref, bf16[512,256]{1,0:T(8,128)(2,1)} %get-tuple-element.19.fl_ref, f32[256,256]{1,0:T(8,128)} %copy-done.1, ...), custom_call_target="tpu_custom_call" | custom-call | flops 6442450944 | bytes 1581056 | tf_op jit(solution)/shard_map/pallas_call | solution.py:157
  63.9 0.7 %copy.41 = f32[1,8,2,128]{3,1,2,0:T(8,128)S(1)} copy(f32[1,8,2,128]{3,2,1,0:T(2,128)} %bitcast.67) | data formatting | bytes 16384
  64.6 0.0 collective-permute-done.6
  64.6 0.6 maximum_select_fusion.1
  (7 shorter events, 0.2 us)
Async XLA Ops:
  1.1 19.4 %collective-permute-start = (f32[32768]{0:T(1024)S(1)}, f32[32768]{0:T(1024)S(1)}, u32[]{:S(2)}, u32[]{:S(2)}) collective-permute-start(f32[32768]{0:T(1024)S(1)} %slice.49), channel_id=1, source_target_pairs={{0,1},{1,2},{2,3},{3,4},{4,5},{5,6},{6,7},{7,8},{8,9},{9,10},{10,1... | collective-permute-start | bytes 393224 | tf_op jit(solution)/shard_map/ppermute | solution.py:23
  5.8 4.1 %collective-permute-start.2 = (bf16[1,8,2,2048]{3,1,2,0:T(8,128)(2,1)S(1)}, bf16[1,8,2,2048]{3,1,2,0:T(8,128)(2,1)S(1)}, u32[]{:S(2)}, u32[]{:S(2)}) collective-permute-start(bf16[1,8,2,2048]{3,1,2,0:T(8,128)(2,1)S(1)} %bitcast.64), channel_id=1, source_target_pairs={{0,1},{1,0},{2,3},{3,2},{4,5},{5,4},{6,7},{7,6},{8,9},{9,8},{10,11... | collective-permute-start | bytes 196616 | tf_op jit(solution)/shard_map/ppermute | solution.py:189
  8.0 21.1 %copy-start = (f32[256,256]{1,0:T(8,128)}, f32[256,256]{1,0:T(8,128)S(1)}, u32[]{:S(2)}) copy-start(f32[256,256]{1,0:T(8,128)S(1)} %get-tuple-element.29.ts_ref) | copy-start | bytes 786436
  8.0 21.1 %copy-start.1 = (f32[256,256]{1,0:T(8,128)}, f32[256,256]{1,0:T(8,128)S(1)}, u32[]{:S(2)}) copy-start(f32[256,256]{1,0:T(8,128)S(1)} %get-tuple-element.30.tc_ref) | copy-start | bytes 786436
  10.0 5.6 %collective-permute-start.3 = (bf16[2,1,8,2,2048]{4,2,3,0,1:T(8,128)(2,1)S(1)}, bf16[2,1,8,2,2048]{4,2,3,0,1:T(8,128)(2,1)S(1)}, u32[]{:S(2)}, u32[]{:S(2)}) collective-permute-start(bf16[2,1,8,2,2048]{4,2,3,0,1:T(8,128)(2,1)S(1)} %pad_maximum_fusion.13), channel_id=1, source_target_pairs={{0,8},{1,9},{2,10},{3,11},{4,12},{5,13},{6,14},{7,15},{8,0},{9,1},... | collective-permute-start | bytes 393224 | tf_op jit(solution)/shard_map/ppermute | solution.py:196
  15.6 11.1 %collective-permute-start.4 = (bf16[2,2,1,8,2,2048]{5,3,4,1,0,2:T(8,128)(2,1)S(1)}, bf16[2,2,1,8,2,2048]{5,3,4,1,0,2:T(8,128)(2,1)S(1)}, u32[]{:S(2)}, u32[]{:S(2)}) collective-permute-start(bf16[2,2,1,8,2,2048]{5,3,4,1,0,2:T(8,128)(2,1)S(1)} %pad_maximum_fusion.12), channel_id=1, source_target_pairs={{0,4},{1,5},{2,6},{3,7},{4,0},{5,1},{6,2},{7,3},{8,12},{9,13},{10,... | collective-permute-start | bytes 786440 | tf_op jit(solution)/shard_map/ppermute | solution.py:196
  20.7 6.2 %collective-permute-start.1 = (f32[3,32768]{1,0:T(4,128)S(1)}, f32[3,32768]{1,0:T(4,128)S(1)}, u32[]{:S(2)}, u32[]{:S(2)}) collective-permute-start(f32[3,32768]{1,0:T(4,128)S(1)} %pad_maximum_fusion.10), channel_id=1, source_target_pairs={{0,1},{1,0},{2,3},{3,2},{4,5},{5,4},{6,7},{7,6},{8,9},{9,8},{10,11... | collective-permute-start | bytes 1179656 | tf_op jit(solution)/shard_map/ppermute | solution.py:218
  26.8 12.5 %collective-permute-start.5 = (bf16[2,2,2,1,8,2,2048]{6,4,5,3,2,1,0:T(8,128)(2,1)S(1)}, bf16[2,2,2,1,8,2,2048]{6,4,5,3,2,1,0:T(8,128)(2,1)S(1)}, u32[]{:S(2)}, u32[]{:S(2)}) collective-permute-start(bf16[2,2,2,1,8,2,2048]{6,4,5,3,2,1,0:T(8,128)(2,1)S(1)} %pad_maximum_fusion.11), channel_id=1, source_target_pairs={{0,2},{1,3},{2,0},{3,1},{4,6},{5,7},{6,4},{7,5},{8,10},{9,11},{10,... | collective-permute-start | bytes 1572872 | tf_op jit(solution)/shard_map/ppermute | solution.py:196
  51.7 12.9 %collective-permute-start.6 = (f32[8,256]{1,0:T(8,128)S(1)}, f32[8,256]{1,0:T(8,128)S(1)}, u32[]{:S(2)}, u32[]{:S(2)}) collective-permute-start(f32[8,256]{1,0:T(8,128)S(1)} %bitcast.66), channel_id=1, source_target_pairs={{0,1},{1,0},{2,3},{3,2},{4,5},{5,4},{6,7},{7,6},{8,9},{9,8},{10,11... | collective-permute-start | bytes 24584 | tf_op jit(solution)/shard_map/ppermute | solution.py:231

commit v14 on v13

--- a/solution.py
+++ b/solution.py
@@ -10,6 +10,7 @@
 RADIX = 256
 BLOCK = 32768
 SUBBANK = 8
+SUBHALF = 4
 STEP_TEMPLATES = 2
 
 
@@ -178,14 +179,14 @@
     )(spectra, bank, *tables)
 
 
-def gathered_half(template_bank):
+def gathered_half(template_bank, start, count):
     seg_total = lax.axis_size("seg")
     me = lax.axis_index("seg")
     core = me % 2
     template_total, parts, local_bins = template_bank.shape
     half = template_total // 2
-    mine = lax.dynamic_slice_in_dim(template_bank, core * half, half, axis=0)
-    theirs = lax.dynamic_slice_in_dim(template_bank, (1 - core) * half, half, axis=0)
+    mine = lax.dynamic_slice_in_dim(template_bank, core * half + start, count, axis=0)
+    theirs = lax.dynamic_slice_in_dim(template_bank, (1 - core) * half + start, count, axis=0)
     arrived = lax.ppermute(theirs[None], "seg", [(i, i ^ 1) for i in range(seg_total)])
     upper = core != 0
     held = jnp.stack([jnp.where(upper, arrived, mine[None]), jnp.where(upper, mine[None], arrived)], axis=0)
@@ -199,17 +200,18 @@
         order.append(distance)
         distance //= 2
     steps = len(order)
-    held = held.reshape((2,) * steps + (half, parts, local_bins // RADIX, RADIX))
+    held = held.reshape((2,) * steps + (count, parts, local_bins // RADIX, RADIX))
     axis_distance = list(reversed(order))
     bit_axes = tuple(sorted(range(steps), key=lambda axis: -axis_distance[axis]))
     held = jnp.transpose(held, (steps, steps + 1) + bit_axes + (steps + 2, steps + 3))
-    return held.reshape(half, parts, seg_total * local_bins // RADIX, RADIX)
+    return held.reshape(count, parts, seg_total * local_bins // RADIX, RADIX)
 
 
 def local(strain, gate_mask, template_bank):
     seg_total = lax.axis_size("seg")
     core = lax.axis_index("seg") % 2
-    bank = gathered_half(template_bank)
+    half = template_bank.shape[0] // 2
+    banks = [gathered_half(template_bank, start, SUBHALF) for start in range(0, half, SUBHALF)]
     gated = strain * gate_mask.astype(jnp.float32)
     local_blocks = gated.reshape(-1, BLOCK)
     block_total = local_blocks.shape[0]
@@ -226,10 +228,14 @@
     tables = inverse_tables(spectra.shape[1])
     partner_spectra = lax.dynamic_slice_in_dim(spectra, (1 - core) * block_total, block_total, axis=0)
     own_spectra = lax.dynamic_slice_in_dim(spectra, core * block_total, block_total, axis=0)
-    half = bank.shape[0]
-    partner_peaks = window_peaks(partner_spectra, bank, tables).reshape(half, block_total * (RADIX // 2))
-    returned = lax.ppermute(partner_peaks, "seg", [(i, i ^ 1) for i in range(seg_total)])
-    own_peaks = window_peaks(own_spectra, bank, tables).reshape(half, block_total * (RADIX // 2))
+    own_parts = []
+    returned_parts = []
+    for bank in banks:
+        partner_peaks = window_peaks(partner_spectra, bank, tables).reshape(SUBHALF, block_total * (RADIX // 2))
+        returned_parts.append(lax.ppermute(partner_peaks, "seg", [(i, i ^ 1) for i in range(seg_total)]))
+        own_parts.append(window_peaks(own_spectra, bank, tables).reshape(SUBHALF, block_total * (RADIX // 2)))
+    own_peaks = jnp.concatenate(own_parts, axis=0)
+    returned = jnp.concatenate(returned_parts, axis=0)
     return jnp.where(
         core == 0,
         jnp.concatenate([own_peaks, returned], axis=0),

time: 65.5 us -> 78.9 us (1.20)
  the two profiles are of different devices: /device:TPU:19 before, /device:TPU:1 now
where the time goes in v14:
time: 78.9 us; the launch traced here: 78 us
  Pallas kernels  24.8 us (31%)
  starting transfers between devices  18.4 us (23%)
  other arithmetic  15.4 us (20%)
  waiting for transfers between devices  9.26 us (12%)
  local copies, waits for them, and re-layouts  5.84 us (7%)
  matrix products  3.9 us (5%)
    pallas_call x4, Pallas kernels, window_peaks(): pl.pallas_call(peaks_kernel, out_shape=jax.ShapeDtypeStruct((template_tot...  24.8 us
    ppermute x6, starting transfers between devices, gathered_half(): arrived = lax.ppermute(held, 'seg', pairs)  9.67 us
    ppermute x6, waiting for transfers between devices, gathered_half(): arrived = lax.ppermute(held, 'seg', pairs)  9.24 us
    ppermute x1, starting transfers between devices, passed_along(): return lax.ppermute(value, axis, pairs)  4.54 us
    another operation x11, other arithmetic, gathered_half(): jnp.stack([jnp.where(upper, arrived, held), jnp.where(upper, held, arrive...  2.93 us
    ppermute x2, starting transfers between devices, local(): lax.ppermute(partner_peaks, 'seg', [(i, i ^ 1) for i in range(seg_total)])  2.77 us
    sin x3, other arithmetic, angle_table(): return (jnp.cos(angle_value), jnp.sin(angle_value))  2.54 us
    another operation x6, local copies, waits for them, and re-layouts, gathered_half(): jnp.stack([jnp.where(upper, arrived, held), jnp.where(upper, held, arrive...  2.43 us
  transfers between devices with their start and end apart: 12, of which 6 were waited for; matrix products, arithmetic and copies ran while one was open for 21% of the time, Pallas kernels for 24%

profile of v14, /device:TPU:1, one launch (start us, length us, event | category | flops | bytes accessed | tf_op | source)
XLA Modules:
  0.0 78.0 jit_solution(18346663991957912883)
XLA Ops:
  0.0 1.1 %convert_multiply_fusion = f32[65536]{0:T(1024)S(1)} fusion(f32[65536]{0:T(1024)} %param.3, s32[65536]{0:T(1024)} %param.4), kind=kLoop, calls=%fused_computation.60 | loop fusion | flops 131072 | bytes 786432 | tf_op jit(solution)/shard_map/mul | solution.py:215
  1.1 4.5 %collective-permute-start = (f32[32768]{0:T(1024)S(1)}, f32[32768]{0:T(1024)S(1)}, u32[]{:S(2)}, u32[]{:S(2)}) collective-permute-start(f32[32768]{0:T(1024)S(1)} %slice.49), channel_id=1, source_target_pairs={{0,1},{1,2},{2,3},{3,4},{4,5},{5,6},{6,7},{7,8},{8,9},{9,10},{10,1... | collective-permute-start | bytes 393224 | tf_op jit(solution)/shard_map/ppermute | solution.py:24
  5.6 0.8 %dynamic-slice_bitcast_fusion.1 = (bf16[1,4,2,2048]{3,2,1,0:T(2,128)(2,1)S(1)}, bf16[1,4,2,2048]{3,2,1,0:T(2,128)(2,1)S(1)}) fusion(bf16[16,2,2048]{2,1,0:T(2,128)(2,1)} %param.5, s32[]{:T(128)S(6)} %select_n.208, s32[]{:T(128)S(6)} %select_n.218), kind=kLoop, calls=%fused_computation.109 | loop fusion | bytes 131080 | tf_op jit(solution)/shard_map/broadcast_in_dim | solution.py:190
  6.6 0.5 collective-permute-start.6
  7.1 1.0 %fusion.37 = (f32[256,256]{1,0:T(8,128)S(1)}, f32[256,256]{1,0:T(8,128)S(1)}) fusion(), kind=kLoop, calls=%fused_computation.83 | loop fusion | flops 983040 | bytes 524288 | tf_op jit(solution)/shard_map/cos | solution.py:32
  8.1 1.0 %fusion.34 = (f32[256,256]{1,0:T(8,128)S(1)}, f32[256,256]{1,0:T(8,128)S(1)}) fusion(), kind=kLoop, calls=%fused_computation.80 | loop fusion | flops 917504 | bytes 524288 | tf_op jit(solution)/shard_map/sin | solution.py:32
  9.2 0.5 fusion.46
  9.7 0.5 fusion.48
  10.2 1.0 %fusion.36 = f32[256,256]{1,0:T(8,128)S(1)} fusion(), kind=kLoop, calls=%fused_computation.82 | loop fusion | flops 917504 | bytes 262144 | tf_op jit(solution)/shard_map/sin | solution.py:32
  11.2 0.9 %fusion.7 = (bf16[512,256]{1,0:T(8,128)(2,1)}, bf16[512,256]{1,0:T(8,128)(2,1)}) fusion(f32[256,128]{1,0:T(8,128)S(1)} %get-tuple-element.40, f32[256,128]{1,0:T(8,128)S(1)} %get-tuple-element.39, f32[256,128]{1,0:T(8,128)S(1)} %fusion.48), kind=kLoop, calls=%fused_computation.22 | loop fusion | flops 917504 | bytes 917504 | tf_op jit(solution)/shard_map/convert_element_type | solution.py:73
  12.1 0.9 %fusion.8 = (bf16[512,256]{1,0:T(8,128)(2,1)}, bf16[512,256]{1,0:T(8,128)(2,1)}) fusion(f32[256,256]{1,0:T(8,128)S(1)} %get-tuple-element.35, f32[256,256]{1,0:T(8,128)S(1)} %fusion.36, f32[256,256]{1,0:T(8,128)S(1)} %get-tuple-element.36), kind=kLoop, calls=%fused_computation.23 | loop fusion | flops 1310720 | bytes 1310720 | tf_op jit(solution)/shard_map/convert_element_type | solution.py:73
  13.0 0.2 reshape.62
  13.2 0.1 fusion.51
  13.3 0.1 pad_maximum_fusion.17
  13.4 2.4 %collective-permute-start.7 = (bf16[2,1,4,2,2048]{4,3,2,0,1:T(2,128)(2,1)S(1)}, bf16[2,1,4,2,2048]{4,3,2,0,1:T(2,128)(2,1)S(1)}, u32[]{:S(2)}, u32[]{:S(2)}) collective-permute-start(bf16[2,1,4,2,2048]{4,3,2,0,1:T(2,128)(2,1)S(1)} %pad_maximum_fusion.17), channel_id=1, source_target_pairs={{0,8},{1,9},{2,10},{3,11},{4,12},{5,13},{6,14},{7,15},{8,0},{9,1},... | collective-permute-start | bytes 196616 | tf_op jit(solution)/shard_map/ppermute | solution.py:197
  15.9 0.1 collective-permute-start.3
  16.0 2.0 %collective-permute-done.7 = bf16[2,1,4,2,2048]{4,3,2,0,1:T(2,128)(2,1)S(1)} collective-permute-done((bf16[2,1,4,2,2048]{4,3,2,0,1:T(2,128)(2,1)S(1)}, bf16[2,1,4,2,2048]{4,3,2,0,1:T(2,128)(2,1)S(1)}, u32[]{:S(2)}, u32[]{:S(2)}) %collective-permute-start.7) | collective-permute-done | bytes 65568 | tf_op jit(solution)/shard_map/ppermute | solution.py:197
  18.0 0.2 fusion.43
  18.2 0.2 pad_maximum_fusion.15
  18.4 3.7 %collective-permute-start.8 = (bf16[2,2,1,4,2,2048]{5,4,3,1,0,2:T(2,128)(2,1)S(1)}, bf16[2,2,1,4,2,2048]{5,4,3,1,0,2:T(2,128)(2,1)S(1)}, u32[]{:S(2)}, u32[]{:S(2)}) collective-permute-start(bf16[2,2,1,4,2,2048]{5,4,3,1,0,2:T(2,128)(2,1)S(1)} %pad_maximum_fusion.15), channel_id=1, source_target_pairs={{0,4},{1,5},{2,6},{3,7},{4,0},{5,1},{6,2},{7,3},{8,12},{9,13},{10,... | collective-permute-start | bytes 393224 | tf_op jit(solution)/shard_map/ppermute | solution.py:197
  22.1 0.2 collective-permute-done.3
  22.3 0.1 fusion.45
  22.4 0.1 fusion.42
  22.5 0.2 pad_maximum_fusion.14
  22.7 0.8 %collective-permute-start.4 = (bf16[2,2,1,4,2,2048]{5,4,3,1,2,0:T(2,128)(2,1)S(1)}, bf16[2,2,1,4,2,2048]{5,4,3,1,2,0:T(2,128)(2,1)S(1)}, u32[]{:S(2)}, u32[]{:S(2)}) collective-permute-start(bf16[2,2,1,4,2,2048]{5,4,3,1,2,0:T(2,128)(2,1)S(1)} %pad_maximum_fusion.14), channel_id=1, source_target_pairs={{0,4},{1,5},{2,6},{3,7},{4,0},{5,1},{6,2},{7,3},{8,12},{9,13},{10,... | collective-permute-start | bytes 393224 | tf_op jit(solution)/shard_map/ppermute | solution.py:197
  23.6 0.2 pad_maximum_fusion.9
  23.8 0.8 %collective-permute-start.1 = (f32[3,32768]{1,0:T(4,128)S(1)}, f32[3,32768]{1,0:T(4,128)S(1)}, u32[]{:S(2)}, u32[]{:S(2)}) collective-permute-start(f32[3,32768]{1,0:T(4,128)S(1)} %pad_maximum_fusion.9), channel_id=1, source_target_pairs={{0,1},{1,0},{2,3},{3,2},{4,5},{5,4},{6,7},{7,6},{8,9},{9,8},{10,11... | collective-permute-start | bytes 1179656 | tf_op jit(solution)/shard_map/ppermute | solution.py:220
  24.6 0.8 collective-permute-done.8
  25.4 0.3 fusion.30
  25.7 0.4 pad_maximum_fusion.13
  26.1 1.2 %collective-permute-start.9 = (bf16[2,2,2,1,4,2,2048]{6,5,4,2,1,3,0:T(2,128)(2,1)S(1)}, bf16[2,2,2,1,4,2,2048]{6,5,4,2,1,3,0:T(2,128)(2,1)S(1)}, u32[]{:S(2)}, u32[]{:S(2)}) collective-permute-start(bf16[2,2,2,1,4,2,2048]{6,5,4,2,1,3,0:T(2,128)(2,1)S(1)} %pad_maximum_fusion.13), channel_id=1, source_target_pairs={{0,2},{1,3},{2,0},{3,1},{4,6},{5,7},{6,4},{7,5},{8,10},{9,11},{10,... | collective-permute-start | bytes 786440 | tf_op jit(solution)/shard_map/ppermute | solution.py:197
  27.2 1.0 %collective-permute-done.4 = bf16[2,2,1,4,2,2048]{5,4,3,1,2,0:T(2,128)(2,1)S(1)} collective-permute-done((bf16[2,2,1,4,2,2048]{5,4,3,1,2,0:T(2,128)(2,1)S(1)}, bf16[2,2,1,4,2,2048]{5,4,3,1,2,0:T(2,128)(2,1)S(1)}, u32[]{:S(2)}, u32[]{:S(2)}) %collective-permute-start.4) | collective-permute-done | bytes 131104 | tf_op jit(solution)/shard_map/ppermute | solution.py:197
  28.3 0.3 fusion.28
  28.6 1.1 %pad_maximum_fusion.12 = bf16[2,2,2,1,4,2,2048]{6,5,4,2,1,3,0:T(2,128)(2,1)} fusion(bf16[1,2,2,1,4,2,2048]{6,5,4,2,1,3,0:T(2,128)(2,1)S(1)} %get-tuple-element.22, bf16[1,2,2,1,4,2,2048]{6,5,4,2,1,3,0:T(2,128)(2,1)S(1)} %get-tuple-element.21), kind=kLoop, calls=%fused_computation.52 | loop fusion | flops 131072 | bytes 524288 | tf_op jit(solution)/shard_map/stack | solution.py:199
  29.7 1.5 %collective-permute-start.5 = (bf16[2,2,2,1,4,2,2048]{6,5,4,2,1,3,0:T(2,128)(2,1)}, bf16[2,2,2,1,4,2,2048]{6,5,4,2,1,3,0:T(2,128)(2,1)}, u32[]{:S(2)}, u32[]{:S(2)}) collective-permute-start(bf16[2,2,2,1,4,2,2048]{6,5,4,2,1,3,0:T(2,128)(2,1)} %pad_maximum_fusion.12), channel_id=1, source_target_pairs={{0,2},{1,3},{2,0},{3,1},{4,6},{5,7},{6,4},{7,5},{8,10},{9,11},{10,... | collective-permute-start | bytes 786440 | tf_op jit(solution)/shard_map/ppermute | solution.py:197
  31.1 0.2 collective-permute-done.9
  31.3 0.6 broadcast_select_fusion.1
  32.0 0.2 stack.94
  32.1 0.2 stack.93
  32.4 0.9 %copy.42 = bf16[2,2,2,2,4,2,8,256]{7,6,3,0,1,2,5,4:T(8,128)(2,1)} copy(bf16[2,2,2,2,4,2,8,256]{7,6,5,4,3,2,1,0:T(8,128)(2,1)S(1)} %pad_maximum_fusion.11) | data formatting | bytes 1048576 | tf_op jit(solution)/shard_map/stack | solution.py:199
  33.2 5.0 %collective-permute-done.5 = bf16[2,2,2,1,4,2,2048]{6,5,4,2,1,3,0:T(2,128)(2,1)} collective-permute-done((bf16[2,2,2,1,4,2,2048]{6,5,4,2,1,3,0:T(2,128)(2,1)}, bf16[2,2,2,1,4,2,2048]{6,5,4,2,1,3,0:T(2,128)(2,1)}, u32[]{:S(2)}, u32[]{:S(2)}) %collective-permute-start.5) | collective-permute-done | bytes 262176 | tf_op jit(solution)/shard_map/ppermute | solution.py:197
  38.3 1.6 %broadcast_select_fusion.3 = (bf16[2,2,2,1,4,2,2048]{6,5,4,2,1,3,0:T(2,128)(2,1)S(1)}, bf16[2,2,2,1,4,2,2048]{6,5,4,2,1,3,0:T(2,128)(2,1)S(1)}) fusion(bf16[2,2,2,1,4,2,2048]{6,5,4,2,1,3,0:T(2,128)(2,1)} %collective-permute-done.5, pred[]{:T(512)S(6)} %ne.116, bf16[1,2,2,1,4,2,2048]{6,5,4,2,1,3,0:T(2,128)(2,1)S(1)} %get-tuple-element.22, ...), kind=kLoop, calls=%fused_computation.42 | loop fusion | flops 393216 | bytes 1048577 | tf_op jit(solution)/shard_map/jit(_where)/select_n | solution.py:199
  39.8 0.2 stack.82
  40.0 0.2 stack.81
  40.2 0.9 %copy.41 = bf16[2,2,2,2,4,2,8,256]{7,6,3,0,1,2,5,4:T(8,128)(2,1)} copy(bf16[2,2,2,2,4,2,8,256]{7,6,5,4,3,2,1,0:T(8,128)(2,1)S(1)} %pad_maximum_fusion.10) | data formatting | bytes 1048576 | tf_op jit(solution)/shard_map/stack | solution.py:199
  41.1 0.1 slice.50
  41.3 0.5 maximum_select_fusion
  41.7 0.2 fusion.67
  42.0 0.2 pad_maximum_fusion.7
  42.2 1.3 %fusion.4 = f32[4,256,512]{2,1,0:T(8,128)S(1)} fusion(f32[1,4,256,256]{3,1,2,0:T(4,128)S(1)} %bitcast.104, f32[256,256]{1,0:T(8,128)S(1)} %get-tuple-element.36, f32[256,256]{1,0:T(8,128)S(1)} %get-tuple-element.35), kind=kOutput, calls=%fused_computation.9 | convolution fusion | flops 805437440 | bytes 3670016 | tf_op jit(solution)/shard_map/bnm,nf->bmf/dot_general | solution.py:42
  43.5 0.3 multiply_add_fusion
  43.8 1.3 %fusion.3 = f32[4,128,512]{2,1,0:T(8,128)S(1)} fusion(f32[4,256,256]{2,1,0:T(8,128)S(1)} %get-tuple-element.6, f32[4,256,256]{2,1,0:T(8,128)S(1)} %get-tuple-element.5), kind=kOutput, calls=%fused_computation.4 | convolution fusion | flops 403636224 | bytes 3145728 | tf_op jit(solution)/shard_map/bnf,nk->bkf/dot_general | solution.py:55
  45.1 1.3 %fusion.2 = f32[4,128,512]{2,1,0:T(8,128)S(1)} fusion(f32[4,256,256]{2,1,0:T(8,128)S(1)} %get-tuple-element.6, f32[4,256,256]{2,1,0:T(8,128)S(1)} %get-tuple-element.5), kind=kOutput, calls=%fused_computation.3 | convolution fusion | flops 403636224 | bytes 3145728 | tf_op jit(solution)/shard_map/bnf,nk->bkf/dot_general | solution.py:54
  46.4 0.1 slice_subtract_fusion
  46.6 1.1 %fusion.10 = (f32[2,128,512]{2,1,0:T(8,128)}, f32[2,128,512]{2,1,0:T(8,128)}) fusion(s32[]{:T(128)S(6)} %select_n.203, f32[4,128,256]{2,1,0:T(8,128)S(1)} %get-tuple-element.8, f32[4,128,256]{2,1,0:T(8,128)S(1)} %get-tuple-element.7, s32[]{:T(128)S(6)} %select_n.228), kind=kLoop, calls=%fused_computation.25 | loop fusion | flops 262144 | bytes 2097160 | tf_op jit(solution)/shard_map/concatenate | solution.py:56
  47.7 6.2 %shard_map.40 = f32[4,2,128]{2,1,0:T(2,128)} custom-call(f32[2,128,512]{2,1,0:T(8,128)} %get-tuple-element.10.spec_ref, bf16[4,2,128,256]{3,2,1,0:T(8,128)(2,1)} %bitcast.107, bf16[512,256]{1,0:T(8,128)(2,1)} %get-tuple-element.20.fh_ref, bf16[512,256]{1,0:T(8,128)(2,1)} %get-tuple-element.19.fl_ref, f32[256,256]{1,0:T(8,128)} %copy-done.1, ...), custom_call_target="tpu_custom_call" | custom-call | flops 3221225472 | bytes 1052672 | tf_op jit(solution)/shard_map/pallas_call | solution.py:158
  53.9 0.7 copy.56
  54.6 2.7 %collective-permute-start.11 = (f32[4,256]{1,0:T(4,128)S(1)}, f32[4,256]{1,0:T(4,128)S(1)}, u32[]{:S(2)}, u32[]{:S(2)}) collective-permute-start(f32[4,256]{1,0:T(4,128)S(1)} %bitcast.113), channel_id=1, source_target_pairs={{0,1},{1,0},{2,3},{3,2},{4,5},{5,4},{6,7},{7,6},{8,9},{9,8},{10,11... | collective-permute-start | bytes 12296 | tf_op jit(solution)/shard_map/ppermute | solution.py:235
  57.3 6.2 %shard_map.39 = f32[4,2,128]{2,1,0:T(2,128)} custom-call(f32[2,128,512]{2,1,0:T(8,128)} %get-tuple-element.10.spec_ref, bf16[4,2,128,256]{3,2,1,0:T(8,128)(2,1)} %bitcast.109, bf16[512,256]{1,0:T(8,128)(2,1)} %get-tuple-element.20.fh_ref, bf16[512,256]{1,0:T(8,128)(2,1)} %get-tuple-element.19.fl_ref, f32[256,256]{1,0:T(8,128)} %copy-done.1, ...), custom_call_target="tpu_custom_call" | custom-call | flops 3221225472 | bytes 1052672 | tf_op jit(solution)/shard_map/pallas_call | solution.py:158
  63.5 0.7 copy.57
  64.2 6.2 %shard_map.38 = f32[4,2,128]{2,1,0:T(2,128)} custom-call(f32[2,128,512]{2,1,0:T(8,128)} %get-tuple-element.9.spec_ref, bf16[4,2,128,256]{3,2,1,0:T(8,128)(2,1)} %bitcast.108, bf16[512,256]{1,0:T(8,128)(2,1)} %get-tuple-element.20.fh_ref, bf16[512,256]{1,0:T(8,128)(2,1)} %get-tuple-element.19.fl_ref, f32[256,256]{1,0:T(8,128)} %copy-done.1, ...), custom_call_target="tpu_custom_call" | custom-call | flops 3221225472 | bytes 1052672 | tf_op jit(solution)/shard_map/pallas_call | solution.py:158
  70.5 6.2 %shard_map.37 = f32[4,2,128]{2,1,0:T(2,128)} custom-call(f32[2,128,512]{2,1,0:T(8,128)} %get-tuple-element.9.spec_ref, bf16[4,2,128,256]{3,2,1,0:T(8,128)(2,1)} %bitcast.110, bf16[512,256]{1,0:T(8,128)(2,1)} %get-tuple-element.20.fh_ref, bf16[512,256]{1,0:T(8,128)(2,1)} %get-tuple-element.19.fl_ref, f32[256,256]{1,0:T(8,128)} %copy-done.1, ...), custom_call_target="tpu_custom_call" | custom-call | flops 3221225472 | bytes 1052672 | tf_op jit(solution)/shard_map/pallas_call | solution.py:158
  76.7 0.7 copy.59
  77.4 0.6 maximum_select_fusion.1
  (21 shorter events, 0.3 us)
Async XLA Ops:
  1.1 22.5 %collective-permute-start = (f32[32768]{0:T(1024)S(1)}, f32[32768]{0:T(1024)S(1)}, u32[]{:S(2)}, u32[]{:S(2)}) collective-permute-start(f32[32768]{0:T(1024)S(1)} %slice.49), channel_id=1, source_target_pairs={{0,1},{1,2},{2,3},{3,4},{4,5},{5,6},{6,7},{7,8},{8,9},{9,10},{10,1... | collective-permute-start | bytes 393224 | tf_op jit(solution)/shard_map/ppermute | solution.py:24
  6.5 6.7 %collective-permute-start.2 = (bf16[1,4,2,2048]{3,2,1,0:T(2,128)(2,1)S(1)}, bf16[1,4,2,2048]{3,2,1,0:T(2,128)(2,1)S(1)}, u32[]{:S(2)}, u32[]{:S(2)}) collective-permute-start(bf16[1,4,2,2048]{3,2,1,0:T(2,128)(2,1)S(1)} %get-tuple-element.31), channel_id=1, source_target_pairs={{0,1},{1,0},{2,3},{3,2},{4,5},{5,4},{6,7},{7,6},{8,9},{9,8},{10,11... | collective-permute-start | bytes 98312 | tf_op jit(solution)/shard_map/ppermute | solution.py:190
  6.6 6.6 %collective-permute-start.6 = (bf16[1,4,2,2048]{3,2,1,0:T(2,128)(2,1)S(1)}, bf16[1,4,2,2048]{3,2,1,0:T(2,128)(2,1)S(1)}, u32[]{:S(2)}, u32[]{:S(2)}) collective-permute-start(bf16[1,4,2,2048]{3,2,1,0:T(2,128)(2,1)S(1)} %get-tuple-element.32), channel_id=1, source_target_pairs={{0,1},{1,0},{2,3},{3,2},{4,5},{5,4},{6,7},{7,6},{8,9},{9,8},{10,11... | collective-permute-start | bytes 98312 | tf_op jit(solution)/shard_map/ppermute | solution.py:190
  8.1 5.1 %copy-start.2 = (bf16[16,2,2048]{2,1,0:T(2,128)(2,1)S(1)}, bf16[16,2,2048]{2,1,0:T(2,128)(2,1)}, u32[]{:S(2)}) copy-start(bf16[16,2,2048]{2,1,0:T(2,128)(2,1)} %param.5) | copy-start | bytes 393220
  9.2 34.3 %copy-start = (f32[256,256]{1,0:T(8,128)}, f32[256,256]{1,0:T(8,128)S(1)}, u32[]{:S(2)}) copy-start(f32[256,256]{1,0:T(8,128)S(1)} %get-tuple-element.37.ts_ref) | copy-start | bytes 786436
  9.2 34.3 %copy-start.1 = (f32[256,256]{1,0:T(8,128)}, f32[256,256]{1,0:T(8,128)S(1)}, u32[]{:S(2)}) copy-start(f32[256,256]{1,0:T(8,128)S(1)} %get-tuple-element.38.tc_ref) | copy-start | bytes 786436
  13.4 4.6 %collective-permute-start.7 = (bf16[2,1,4,2,2048]{4,3,2,0,1:T(2,128)(2,1)S(1)}, bf16[2,1,4,2,2048]{4,3,2,0,1:T(2,128)(2,1)S(1)}, u32[]{:S(2)}, u32[]{:S(2)}) collective-permute-start(bf16[2,1,4,2,2048]{4,3,2,0,1:T(2,128)(2,1)S(1)} %pad_maximum_fusion.17), channel_id=1, source_target_pairs={{0,8},{1,9},{2,10},{3,11},{4,12},{5,13},{6,14},{7,15},{8,0},{9,1},... | collective-permute-start | bytes 196616 | tf_op jit(solution)/shard_map/ppermute | solution.py:197
  15.9 6.4 %collective-permute-start.3 = (bf16[2,1,4,2,2048]{4,3,2,0,1:T(2,128)(2,1)S(1)}, bf16[2,1,4,2,2048]{4,3,2,0,1:T(2,128)(2,1)S(1)}, u32[]{:S(2)}, u32[]{:S(2)}) collective-permute-start(bf16[2,1,4,2,2048]{4,3,2,0,1:T(2,128)(2,1)S(1)} %fusion.66), channel_id=1, source_target_pairs={{0,8},{1,9},{2,10},{3,11},{4,12},{5,13},{6,14},{7,15},{8,0},{9,1},... | collective-permute-start | bytes 196616 | tf_op jit(solution)/shard_map/ppermute | solution.py:197
  18.4 7.0 %collective-permute-start.8 = (bf16[2,2,1,4,2,2048]{5,4,3,1,0,2:T(2,128)(2,1)S(1)}, bf16[2,2,1,4,2,2048]{5,4,3,1,0,2:T(2,128)(2,1)S(1)}, u32[]{:S(2)}, u32[]{:S(2)}) collective-permute-start(bf16[2,2,1,4,2,2048]{5,4,3,1,0,2:T(2,128)(2,1)S(1)} %pad_maximum_fusion.15), channel_id=1, source_target_pairs={{0,4},{1,5},{2,6},{3,7},{4,0},{5,1},{6,2},{7,3},{8,12},{9,13},{10,... | collective-permute-start | bytes 393224 | tf_op jit(solution)/shard_map/ppermute | solution.py:197
  22.7 5.5 %collective-permute-start.4 = (bf16[2,2,1,4,2,2048]{5,4,3,1,2,0:T(2,128)(2,1)S(1)}, bf16[2,2,1,4,2,2048]{5,4,3,1,2,0:T(2,128)(2,1)S(1)}, u32[]{:S(2)}, u32[]{:S(2)}) collective-permute-start(bf16[2,2,1,4,2,2048]{5,4,3,1,2,0:T(2,128)(2,1)S(1)} %pad_maximum_fusion.14), channel_id=1, source_target_pairs={{0,4},{1,5},{2,6},{3,7},{4,0},{5,1},{6,2},{7,3},{8,12},{9,13},{10,... | collective-permute-start | bytes 393224 | tf_op jit(solution)/shard_map/ppermute | solution.py:197
  23.8 17.3 %collective-permute-start.1 = (f32[3,32768]{1,0:T(4,128)S(1)}, f32[3,32768]{1,0:T(4,128)S(1)}, u32[]{:S(2)}, u32[]{:S(2)}) collective-permute-start(f32[3,32768]{1,0:T(4,128)S(1)} %pad_maximum_fusion.9), channel_id=1, source_target_pairs={{0,1},{1,0},{2,3},{3,2},{4,5},{5,4},{6,7},{7,6},{8,9},{9,8},{10,11... | collective-permute-start | bytes 1179656 | tf_op jit(solution)/shard_map/ppermute | solution.py:220
  26.1 5.3 %collective-permute-start.9 = (bf16[2,2,2,1,4,2,2048]{6,5,4,2,1,3,0:T(2,128)(2,1)S(1)}, bf16[2,2,2,1,4,2,2048]{6,5,4,2,1,3,0:T(2,128)(2,1)S(1)}, u32[]{:S(2)}, u32[]{:S(2)}) collective-permute-start(bf16[2,2,2,1,4,2,2048]{6,5,4,2,1,3,0:T(2,128)(2,1)S(1)} %pad_maximum_fusion.13), channel_id=1, source_target_pairs={{0,2},{1,3},{2,0},{3,1},{4,6},{5,7},{6,4},{7,5},{8,10},{9,11},{10,... | collective-permute-start | bytes 786440 | tf_op jit(solution)/shard_map/ppermute | solution.py:197
  29.7 8.6 %collective-permute-start.5 = (bf16[2,2,2,1,4,2,2048]{6,5,4,2,1,3,0:T(2,128)(2,1)}, bf16[2,2,2,1,4,2,2048]{6,5,4,2,1,3,0:T(2,128)(2,1)}, u32[]{:S(2)}, u32[]{:S(2)}) collective-permute-start(bf16[2,2,2,1,4,2,2048]{6,5,4,2,1,3,0:T(2,128)(2,1)} %pad_maximum_fusion.12), channel_id=1, source_target_pairs={{0,2},{1,3},{2,0},{3,1},{4,6},{5,7},{6,4},{7,5},{8,10},{9,11},{10,... | collective-permute-start | bytes 786440 | tf_op jit(solution)/shard_map/ppermute | solution.py:197
  54.6 22.8 %collective-permute-start.11 = (f32[4,256]{1,0:T(4,128)S(1)}, f32[4,256]{1,0:T(4,128)S(1)}, u32[]{:S(2)}, u32[]{:S(2)}) collective-permute-start(f32[4,256]{1,0:T(4,128)S(1)} %bitcast.113), channel_id=1, source_target_pairs={{0,1},{1,0},{2,3},{3,2},{4,5},{5,4},{6,7},{7,6},{8,9},{9,8},{10,11... | collective-permute-start | bytes 12296 | tf_op jit(solution)/shard_map/ppermute | solution.py:235
  64.2 13.2 %collective-permute-start.10 = (f32[4,256]{1,0:T(4,128)S(1)}, f32[4,256]{1,0:T(4,128)S(1)}, u32[]{:S(2)}, u32[]{:S(2)}) collective-permute-start(f32[4,256]{1,0:T(4,128)S(1)} %bitcast.114), channel_id=1, source_target_pairs={{0,1},{1,0},{2,3},{3,2},{4,5},{5,4},{6,7},{7,6},{8,9},{9,8},{10,11... | collective-permute-start | bytes 12296 | tf_op jit(solution)/shard_map/ppermute | solution.py:235
  70.4 6.2 %copy-start.3 = (f32[4,2,128]{2,1,0:T(2,128)S(1)}, f32[4,2,128]{2,1,0:T(2,128)}, u32[]{:S(2)}) copy-start(f32[4,2,128]{2,1,0:T(2,128)} %shard_map.38) | copy-start | bytes 12292

commit v15 on v13

--- a/solution.py
+++ b/solution.py
@@ -189,20 +189,26 @@
     arrived = lax.ppermute(theirs[None], "seg", [(i, i ^ 1) for i in range(seg_total)])
     upper = core != 0
     held = jnp.stack([jnp.where(upper, arrived, mine[None]), jnp.where(upper, mine[None], arrived)], axis=0)
-    order = [1]
+    odd_order = []
     distance = seg_total // 2
     while distance > 1:
-        pairs = [(i, i ^ distance) for i in range(seg_total)]
+        odd_order.append(distance)
+        distance //= 2
+    even_order = odd_order[:-2] + odd_order[-2:][::-1]
+    for even_distance, odd_distance in zip(even_order, odd_order):
+        pairs = [(i, i ^ (even_distance if i % 2 == 0 else odd_distance)) for i in range(seg_total)]
         arrived = lax.ppermute(held, "seg", pairs)
-        upper = (me & distance) != 0
+        upper = (me & jnp.where(core == 0, even_distance, odd_distance)) != 0
         held = jnp.stack([jnp.where(upper, arrived, held), jnp.where(upper, held, arrived)], axis=0)
-        order.append(distance)
-        distance //= 2
-    steps = len(order)
+    steps = len(odd_order) + 1
     held = held.reshape((2,) * steps + (half, parts, local_bins // RADIX, RADIX))
-    axis_distance = list(reversed(order))
-    bit_axes = tuple(sorted(range(steps), key=lambda axis: -axis_distance[axis]))
-    held = jnp.transpose(held, (steps, steps + 1) + bit_axes + (steps + 2, steps + 3))
+
+    def in_bin_order(order):
+        axis_distance = list(reversed([1] + order))
+        bit_axes = tuple(sorted(range(steps), key=lambda axis: -axis_distance[axis]))
+        return jnp.transpose(held, (steps, steps + 1) + bit_axes + (steps + 2, steps + 3))
+
+    held = jnp.where(core == 0, in_bin_order(even_order), in_bin_order(odd_order))
     return held.reshape(half, parts, seg_total * local_bins // RADIX, RADIX)
 
 

time: 65.5 us -> 60.9 us (0.930)
  the two profiles are of different devices: /device:TPU:19 before, /device:TPU:1 now
where the time goes in v15:
time: 60.9 us; the launch traced here: 60.5 us
  Pallas kernels  20.5 us (34%)
  starting transfers between devices  14.3 us (23%)
  other arithmetic  11.5 us (19%)
  waiting for transfers between devices  7 us (11%)
  matrix products  3.7 us (6%)
  local copies, waits for them, and re-layouts  3.13 us (5%)
    pallas_call x2, Pallas kernels, window_peaks(): pl.pallas_call(peaks_kernel, out_shape=jax.ShapeDtypeStruct((template_tot...  20.5 us
    ppermute x3, waiting for transfers between devices, gathered_half(): arrived = lax.ppermute(held, 'seg', pairs)  6.99 us
    ppermute x3, starting transfers between devices, gathered_half(): arrived = lax.ppermute(held, 'seg', pairs)  4.99 us
    ppermute x1, starting transfers between devices, passed_along(): return lax.ppermute(value, axis, pairs)  4.54 us
    ppermute x1, starting transfers between devices, local(): lax.ppermute(partner_peaks, 'seg', [(i, i ^ 1) for i in range(seg_total)])  3.05 us
    sin x3, other arithmetic, angle_table(): return (jnp.cos(angle_value), jnp.sin(angle_value))  2.54 us
    convert_element_type x2, other arithmetic, table_pair(): return (high.astype(jnp.bfloat16), (value - high).astype(jnp.bfloat16))  1.73 us
    ppermute x1, starting transfers between devices, local(): other = lax.ppermute(mine, 'seg', [(i, i ^ 1) for i in range(seg_total)])  1.68 us
  transfers between devices with their start and end apart: 7, of which 3 were waited for; matrix products, arithmetic and copies ran while one was open for 24% of the time, Pallas kernels for 17%

profile of v15, /device:TPU:1, one launch (start us, length us, event | category | flops | bytes accessed | tf_op | source)
XLA Modules:
  0.0 60.5 jit_solution(8385377293002566352)
XLA Ops:
  0.0 1.1 %convert_multiply_fusion = f32[65536]{0:T(1024)S(1)} fusion(f32[65536]{0:T(1024)} %param.3, s32[65536]{0:T(1024)} %param.4), kind=kLoop, calls=%fused_computation.59 | loop fusion | flops 131072 | bytes 786432 | tf_op jit(solution)/shard_map/mul | solution.py:219
  1.1 4.5 %collective-permute-start = (f32[32768]{0:T(1024)S(1)}, f32[32768]{0:T(1024)S(1)}, u32[]{:S(2)}, u32[]{:S(2)}) collective-permute-start(f32[32768]{0:T(1024)S(1)} %slice.49), channel_id=1, source_target_pairs={{0,1},{1,2},{2,3},{3,4},{4,5},{5,6},{6,7},{7,8},{8,9},{9,10},{10,1... | collective-permute-start | bytes 393224 | tf_op jit(solution)/shard_map/ppermute | solution.py:23
  5.6 1.0 %constant_dynamic-slice_fusion = (bf16[8,2,2048]{2,1,0:T(2,128)(2,1)S(1)}, bf16[8,2,2048]{2,1,0:T(2,128)(2,1)S(1)}) fusion(bf16[16,2,2048]{2,1,0:T(2,128)(2,1)} %param.5, s32[]{:T(128)S(6)} %select_n.180, s32[]{:T(128)S(6)} %select_n.179), kind=kLoop, calls=%fused_computation.94 | loop fusion | bytes 262152 | tf_op jit(solution)/shard_map/dynamic_slice | solution.py:187
  6.7 0.1 collective-permute-start.2
  6.7 1.0 %fusion.33 = (f32[256,256]{1,0:T(8,128)S(1)}, f32[256,256]{1,0:T(8,128)S(1)}) fusion(), kind=kLoop, calls=%fused_computation.76 | loop fusion | flops 983040 | bytes 524288 | tf_op jit(solution)/shard_map/cos | solution.py:31
  7.8 1.0 %fusion.30 = (f32[256,256]{1,0:T(8,128)S(1)}, f32[256,256]{1,0:T(8,128)S(1)}) fusion(), kind=kLoop, calls=%fused_computation.73 | loop fusion | flops 917504 | bytes 524288 | tf_op jit(solution)/shard_map/sin | solution.py:31
  8.8 0.0 copy-start
  8.8 0.0 copy-start.1
  8.8 0.5 fusion.40
  9.4 0.5 fusion.42
  9.9 0.9 %fusion.7 = (bf16[512,256]{1,0:T(8,128)(2,1)}, bf16[512,256]{1,0:T(8,128)(2,1)}) fusion(f32[256,128]{1,0:T(8,128)S(1)} %get-tuple-element.32, f32[256,128]{1,0:T(8,128)S(1)} %get-tuple-element.31, f32[256,128]{1,0:T(8,128)S(1)} %fusion.42), kind=kLoop, calls=%fused_computation.21 | loop fusion | flops 917504 | bytes 917504 | tf_op jit(solution)/shard_map/convert_element_type | solution.py:72
  10.7 0.0 collective-permute-done.2
  10.8 2.4 %collective-permute-start.3 = (bf16[2,1,8,2,2048]{4,2,3,0,1:T(8,128)(2,1)S(1)}, bf16[2,1,8,2,2048]{4,2,3,0,1:T(8,128)(2,1)S(1)}, u32[]{:S(2)}, u32[]{:S(2)}) collective-permute-start(bf16[2,1,8,2,2048]{4,2,3,0,1:T(8,128)(2,1)S(1)} %pad_maximum_fusion.12), channel_id=1, source_target_pairs={{0,8},{1,9},{2,10},{3,11},{4,12},{5,13},{6,14},{7,15},{8,0},{9,1},... | collective-permute-start | bytes 393224 | tf_op jit(solution)/shard_map/ppermute | solution.py:200
  13.2 1.0 %fusion.32 = f32[256,256]{1,0:T(8,128)S(1)} fusion(), kind=kLoop, calls=%fused_computation.75 | loop fusion | flops 917504 | bytes 262144 | tf_op jit(solution)/shard_map/sin | solution.py:31
  14.2 0.2 reshape.48
  14.3 0.9 %fusion.8 = (bf16[512,256]{1,0:T(8,128)(2,1)}, bf16[512,256]{1,0:T(8,128)(2,1)}) fusion(f32[256,256]{1,0:T(8,128)S(1)} %get-tuple-element.27, f32[256,256]{1,0:T(8,128)S(1)} %fusion.32, f32[256,256]{1,0:T(8,128)S(1)} %get-tuple-element.28), kind=kLoop, calls=%fused_computation.22 | loop fusion | flops 1310720 | bytes 1310720 | tf_op jit(solution)/shard_map/convert_element_type | solution.py:72
  15.2 3.9 %collective-permute-done.3 = bf16[2,1,8,2,2048]{4,2,3,0,1:T(8,128)(2,1)S(1)} collective-permute-done((bf16[2,1,8,2,2048]{4,2,3,0,1:T(8,128)(2,1)S(1)}, bf16[2,1,8,2,2048]{4,2,3,0,1:T(8,128)(2,1)S(1)}, u32[]{:S(2)}, u32[]{:S(2)}) %collective-permute-start.3) | collective-permute-done | bytes 131104 | tf_op jit(solution)/shard_map/ppermute | solution.py:200
  19.2 1.3 %collective-permute-start.4 = (bf16[2,2,1,8,2,2048]{5,3,4,1,0,2:T(8,128)(2,1)S(1)}, bf16[2,2,1,8,2,2048]{5,3,4,1,0,2:T(8,128)(2,1)S(1)}, u32[]{:S(2)}, u32[]{:S(2)}) collective-permute-start(bf16[2,2,1,8,2,2048]{5,3,4,1,0,2:T(8,128)(2,1)S(1)} %pad_maximum_fusion.11), channel_id=1, source_target_pairs={{0,2},{1,5},{2,0},{3,7},{4,6},{5,1},{6,4},{7,3},{8,10},{9,13},{10,... | collective-permute-start | bytes 786440 | tf_op jit(solution)/shard_map/ppermute | solution.py:200
  20.5 0.0 collective-permute-done
  20.5 0.2 pad_maximum_fusion.9
  20.8 1.7 %collective-permute-start.1 = (f32[3,32768]{1,0:T(4,128)S(1)}, f32[3,32768]{1,0:T(4,128)S(1)}, u32[]{:S(2)}, u32[]{:S(2)}) collective-permute-start(f32[3,32768]{1,0:T(4,128)S(1)} %pad_maximum_fusion.9), channel_id=1, source_target_pairs={{0,1},{1,0},{2,3},{3,2},{4,5},{5,4},{6,7},{7,6},{8,9},{9,8},{10,11... | collective-permute-start | bytes 1179656 | tf_op jit(solution)/shard_map/ppermute | solution.py:224
  22.4 2.3 %collective-permute-done.4 = bf16[2,2,1,8,2,2048]{5,3,4,1,0,2:T(8,128)(2,1)S(1)} collective-permute-done((bf16[2,2,1,8,2,2048]{5,3,4,1,0,2:T(8,128)(2,1)S(1)}, bf16[2,2,1,8,2,2048]{5,3,4,1,0,2:T(8,128)(2,1)S(1)}, u32[]{:S(2)}, u32[]{:S(2)}) %collective-permute-start.4) | collective-permute-done | bytes 262176 | tf_op jit(solution)/shard_map/ppermute | solution.py:200
  24.8 0.1 pad_maximum_fusion.10
  24.9 1.3 %collective-permute-start.5 = (bf16[2,2,2,1,8,2,2048]{6,4,5,3,2,1,0:T(8,128)(2,1)S(1)}, bf16[2,2,2,1,8,2,2048]{6,4,5,3,2,1,0:T(8,128)(2,1)S(1)}, u32[]{:S(2)}, u32[]{:S(2)}) collective-permute-start(bf16[2,2,2,1,8,2,2048]{6,4,5,3,2,1,0:T(8,128)(2,1)S(1)} %pad_maximum_fusion.10), channel_id=1, source_target_pairs={{0,4},{1,3},{2,6},{3,1},{4,0},{5,7},{6,2},{7,5},{8,12},{9,11},{10,... | collective-permute-start | bytes 1572872 | tf_op jit(solution)/shard_map/ppermute | solution.py:200
  26.2 0.0 collective-permute-done.1
  26.2 0.1 slice.50
  26.3 0.5 maximum_select_fusion
  26.8 0.2 fusion.56
  27.0 0.2 pad_maximum_fusion.7
  27.3 1.1 %fusion.4 = f32[4,256,512]{2,1,0:T(8,128)S(1)} fusion(f32[1,4,256,256]{3,1,2,0:T(4,128)S(1)} %bitcast.60, f32[256,256]{1,0:T(8,128)S(1)} %get-tuple-element.28, f32[256,256]{1,0:T(8,128)S(1)} %get-tuple-element.27), kind=kOutput, calls=%fused_computation.9 | convolution fusion | flops 805437440 | bytes 3670016 | tf_op jit(solution)/shard_map/bnm,nf->bmf/dot_general | solution.py:41
  28.4 0.0 copy-done
  28.4 0.0 copy-done.1
  28.4 0.3 multiply_add_fusion
  28.7 1.3 %fusion.3 = f32[4,128,512]{2,1,0:T(8,128)S(1)} fusion(f32[4,256,256]{2,1,0:T(8,128)S(1)} %get-tuple-element.6, f32[4,256,256]{2,1,0:T(8,128)S(1)} %get-tuple-element.5), kind=kOutput, calls=%fused_computation.4 | convolution fusion | flops 403636224 | bytes 3145728 | tf_op jit(solution)/shard_map/bnf,nk->bkf/dot_general | solution.py:54
  30.0 1.3 %fusion.2 = f32[4,128,512]{2,1,0:T(8,128)S(1)} fusion(f32[4,256,256]{2,1,0:T(8,128)S(1)} %get-tuple-element.6, f32[4,256,256]{2,1,0:T(8,128)S(1)} %get-tuple-element.5), kind=kOutput, calls=%fused_computation.3 | convolution fusion | flops 403636224 | bytes 3145728 | tf_op jit(solution)/shard_map/bnf,nk->bkf/dot_general | solution.py:53
  31.3 0.1 slice_subtract_fusion
  31.4 1.1 %fusion.10 = (f32[2,128,512]{2,1,0:T(8,128)}, f32[2,128,512]{2,1,0:T(8,128)}) fusion(s32[]{:T(128)S(6)} %select_n.171, f32[4,128,256]{2,1,0:T(8,128)S(1)} %get-tuple-element.8, f32[4,128,256]{2,1,0:T(8,128)S(1)} %get-tuple-element.7, s32[]{:T(128)S(6)} %select_n.190), kind=kLoop, calls=%fused_computation.24 | loop fusion | flops 262144 | bytes 2097160 | tf_op jit(solution)/shard_map/concatenate | solution.py:55
  32.6 0.7 %collective-permute-done.5 = bf16[2,2,2,1,8,2,2048]{6,4,5,3,2,1,0:T(8,128)(2,1)S(1)} collective-permute-done((bf16[2,2,2,1,8,2,2048]{6,4,5,3,2,1,0:T(8,128)(2,1)S(1)}, bf16[2,2,2,1,8,2,2048]{6,4,5,3,2,1,0:T(8,128)(2,1)S(1)}, u32[]{:S(2)}, u32[]{:S(2)}) %collective-permute-start.5) | collective-permute-done | bytes 524320 | tf_op jit(solution)/shard_map/ppermute | solution.py:200
  33.3 0.1 broadcast_select_fusion
  33.4 0.1 copy_dynamic-update-slice_fusion.1
  33.5 0.1 copy_dynamic-update-slice_fusion
  33.6 1.3 %bitcast_select_fusion = bf16[8,2,2,2,2,2,8,256]{7,6,5,4,3,2,1,0:T(8,128)(2,1)} fusion(bf16[2,2,2,2,8,2,8,256]{7,6,3,0,1,2,5,4:T(8,128)(2,1)S(1)} %copy_dynamic-update-slice_fusion, pred[]{:T(512)S(6)} %eq.19), kind=kLoop, calls=%fused_computation.14 | loop fusion | flops 524288 | bytes 2097153 | tf_op jit(solution)/shard_map/jit(_where)/select_n | solution.py:211
  34.9 10.3 %shard_map.38 = f32[8,2,128]{2,1,0:T(2,128)} custom-call(f32[2,128,512]{2,1,0:T(8,128)} %get-tuple-element.10.spec_ref, bf16[8,2,128,256]{3,2,1,0:T(8,128)(2,1)} %bitcast.63, bf16[512,256]{1,0:T(8,128)(2,1)} %get-tuple-element.20.fh_ref, bf16[512,256]{1,0:T(8,128)(2,1)} %get-tuple-element.19.fl_ref, f32[256,256]{1,0:T(8,128)} %copy-done.1, ...), custom_call_target="tpu_custom_call" | custom-call | flops 6442450944 | bytes 1581056 | tf_op jit(solution)/shard_map/pallas_call | solution.py:157
  45.2 0.7 %copy.45 = f32[1,8,2,128]{3,1,2,0:T(8,128)S(1)} copy(f32[1,8,2,128]{3,2,1,0:T(2,128)} %bitcast.71) | data formatting | bytes 16384
  45.9 3.0 %collective-permute-start.6 = (f32[8,256]{1,0:T(8,128)S(1)}, f32[8,256]{1,0:T(8,128)S(1)}, u32[]{:S(2)}, u32[]{:S(2)}) collective-permute-start(f32[8,256]{1,0:T(8,128)S(1)} %bitcast.69), channel_id=1, source_target_pairs={{0,1},{1,0},{2,3},{3,2},{4,5},{5,4},{6,7},{7,6},{8,9},{9,8},{10,11... | collective-permute-start | bytes 24584 | tf_op jit(solution)/shard_map/ppermute | solution.py:237
  48.9 10.3 %shard_map.37 = f32[8,2,128]{2,1,0:T(2,128)} custom-call(f32[2,128,512]{2,1,0:T(8,128)} %get-tuple-element.9.spec_ref, bf16[8,2,128,256]{3,2,1,0:T(8,128)(2,1)} %bitcast.64, bf16[512,256]{1,0:T(8,128)(2,1)} %get-tuple-element.20.fh_ref, bf16[512,256]{1,0:T(8,128)(2,1)} %get-tuple-element.19.fl_ref, f32[256,256]{1,0:T(8,128)} %copy-done.1, ...), custom_call_target="tpu_custom_call" | custom-call | flops 6442450944 | bytes 1581056 | tf_op jit(solution)/shard_map/pallas_call | solution.py:157
  59.2 0.7 %copy.46 = f32[1,8,2,128]{3,1,2,0:T(8,128)S(1)} copy(f32[1,8,2,128]{3,2,1,0:T(2,128)} %bitcast.70) | data formatting | bytes 16384
  59.9 0.0 collective-permute-done.6
  59.9 0.6 %maximum_select_fusion.1 = f32[16,256]{1,0:T(8,128)} fusion(f32[8,256]{1,0:T(8,128)S(1)} %collective-permute-done.6, f32[8,256]{1,0:T(8,128)S(1)} %bitcast.68, pred[]{:T(512)S(6)} %eq.19), kind=kLoop, calls=%fused_computation.89 | loop fusion | flops 12288 | bytes 32769 | tf_op jit(solution)/shard_map/jit(_where)/select_n | solution.py:239
  (7 shorter events, 0.2 us)
Async XLA Ops:
  1.1 19.4 %collective-permute-start = (f32[32768]{0:T(1024)S(1)}, f32[32768]{0:T(1024)S(1)}, u32[]{:S(2)}, u32[]{:S(2)}) collective-permute-start(f32[32768]{0:T(1024)S(1)} %slice.49), channel_id=1, source_target_pairs={{0,1},{1,2},{2,3},{3,4},{4,5},{5,6},{6,7},{7,8},{8,9},{9,10},{10,1... | collective-permute-start | bytes 393224 | tf_op jit(solution)/shard_map/ppermute | solution.py:23
  6.7 4.1 %collective-permute-start.2 = (bf16[1,8,2,2048]{3,1,2,0:T(8,128)(2,1)S(1)}, bf16[1,8,2,2048]{3,1,2,0:T(8,128)(2,1)S(1)}, u32[]{:S(2)}, u32[]{:S(2)}) collective-permute-start(bf16[1,8,2,2048]{3,1,2,0:T(8,128)(2,1)S(1)} %bitcast.67), channel_id=1, source_target_pairs={{0,1},{1,0},{2,3},{3,2},{4,5},{5,4},{6,7},{7,6},{8,9},{9,8},{10,11... | collective-permute-start | bytes 196616 | tf_op jit(solution)/shard_map/ppermute | solution.py:189
  8.8 19.5 %copy-start = (f32[256,256]{1,0:T(8,128)}, f32[256,256]{1,0:T(8,128)S(1)}, u32[]{:S(2)}) copy-start(f32[256,256]{1,0:T(8,128)S(1)} %get-tuple-element.29.ts_ref) | copy-start | bytes 786436
  8.8 19.5 %copy-start.1 = (f32[256,256]{1,0:T(8,128)}, f32[256,256]{1,0:T(8,128)S(1)}, u32[]{:S(2)}) copy-start(f32[256,256]{1,0:T(8,128)S(1)} %get-tuple-element.30.tc_ref) | copy-start | bytes 786436
  10.8 8.3 %collective-permute-start.3 = (bf16[2,1,8,2,2048]{4,2,3,0,1:T(8,128)(2,1)S(1)}, bf16[2,1,8,2,2048]{4,2,3,0,1:T(8,128)(2,1)S(1)}, u32[]{:S(2)}, u32[]{:S(2)}) collective-permute-start(bf16[2,1,8,2,2048]{4,2,3,0,1:T(8,128)(2,1)S(1)} %pad_maximum_fusion.12), channel_id=1, source_target_pairs={{0,8},{1,9},{2,10},{3,11},{4,12},{5,13},{6,14},{7,15},{8,0},{9,1},... | collective-permute-start | bytes 393224 | tf_op jit(solution)/shard_map/ppermute | solution.py:200
  19.2 5.6 %collective-permute-start.4 = (bf16[2,2,1,8,2,2048]{5,3,4,1,0,2:T(8,128)(2,1)S(1)}, bf16[2,2,1,8,2,2048]{5,3,4,1,0,2:T(8,128)(2,1)S(1)}, u32[]{:S(2)}, u32[]{:S(2)}) collective-permute-start(bf16[2,2,1,8,2,2048]{5,3,4,1,0,2:T(8,128)(2,1)S(1)} %pad_maximum_fusion.11), channel_id=1, source_target_pairs={{0,2},{1,5},{2,0},{3,7},{4,6},{5,1},{6,4},{7,3},{8,10},{9,13},{10,... | collective-permute-start | bytes 786440 | tf_op jit(solution)/shard_map/ppermute | solution.py:200
  20.8 5.4 %collective-permute-start.1 = (f32[3,32768]{1,0:T(4,128)S(1)}, f32[3,32768]{1,0:T(4,128)S(1)}, u32[]{:S(2)}, u32[]{:S(2)}) collective-permute-start(f32[3,32768]{1,0:T(4,128)S(1)} %pad_maximum_fusion.9), channel_id=1, source_target_pairs={{0,1},{1,0},{2,3},{3,2},{4,5},{5,4},{6,7},{7,6},{8,9},{9,8},{10,11... | collective-permute-start | bytes 1179656 | tf_op jit(solution)/shard_map/ppermute | solution.py:224
  24.9 8.4 %collective-permute-start.5 = (bf16[2,2,2,1,8,2,2048]{6,4,5,3,2,1,0:T(8,128)(2,1)S(1)}, bf16[2,2,2,1,8,2,2048]{6,4,5,3,2,1,0:T(8,128)(2,1)S(1)}, u32[]{:S(2)}, u32[]{:S(2)}) collective-permute-start(bf16[2,2,2,1,8,2,2048]{6,4,5,3,2,1,0:T(8,128)(2,1)S(1)} %pad_maximum_fusion.10), channel_id=1, source_target_pairs={{0,4},{1,3},{2,6},{3,1},{4,0},{5,7},{6,2},{7,5},{8,12},{9,11},{10,... | collective-permute-start | bytes 1572872 | tf_op jit(solution)/shard_map/ppermute | solution.py:200
  45.9 14.0 %collective-permute-start.6 = (f32[8,256]{1,0:T(8,128)S(1)}, f32[8,256]{1,0:T(8,128)S(1)}, u32[]{:S(2)}, u32[]{:S(2)}) collective-permute-start(f32[8,256]{1,0:T(8,128)S(1)} %bitcast.69), channel_id=1, source_target_pairs={{0,1},{1,0},{2,3},{3,2},{4,5},{5,4},{6,7},{7,6},{8,9},{9,8},{10,11... | collective-permute-start | bytes 24584 | tf_op jit(solution)/shard_map/ppermute | solution.py:237

commit v16 on v15

--- a/solution.py
+++ b/solution.py
@@ -184,11 +184,7 @@
     core = me % 2
     template_total, parts, local_bins = template_bank.shape
     half = template_total // 2
-    mine = lax.dynamic_slice_in_dim(template_bank, core * half, half, axis=0)
-    theirs = lax.dynamic_slice_in_dim(template_bank, (1 - core) * half, half, axis=0)
-    arrived = lax.ppermute(theirs[None], "seg", [(i, i ^ 1) for i in range(seg_total)])
-    upper = core != 0
-    held = jnp.stack([jnp.where(upper, arrived, mine[None]), jnp.where(upper, mine[None], arrived)], axis=0)
+    held = template_bank[None]
     odd_order = []
     distance = seg_total // 2
     while distance > 1:
@@ -200,11 +196,18 @@
         arrived = lax.ppermute(held, "seg", pairs)
         upper = (me & jnp.where(core == 0, even_distance, odd_distance)) != 0
         held = jnp.stack([jnp.where(upper, arrived, held), jnp.where(upper, held, arrived)], axis=0)
+    template_axis = len(odd_order) + 1
+    mine = lax.dynamic_slice_in_dim(held, core * half, half, axis=template_axis)
+    theirs = lax.dynamic_slice_in_dim(held, (1 - core) * half, half, axis=template_axis)
+    arrived = lax.ppermute(theirs, "seg", [(i, i ^ 1) for i in range(seg_total)])
+    arrived = jnp.swapaxes(arrived, 0, 1)
+    upper = core != 0
+    held = jnp.stack([jnp.where(upper, arrived, mine), jnp.where(upper, mine, arrived)], axis=0)
     steps = len(odd_order) + 1
     held = held.reshape((2,) * steps + (half, parts, local_bins // RADIX, RADIX))
 
     def in_bin_order(order):
-        axis_distance = list(reversed([1] + order))
+        axis_distance = list(reversed(order + [1]))
         bit_axes = tuple(sorted(range(steps), key=lambda axis: -axis_distance[axis]))
         return jnp.transpose(held, (steps, steps + 1) + bit_axes + (steps + 2, steps + 3))
 

time: 60.9 us -> 64.7 us (1.062)
  other arithmetic: 11.5 us -> 18 us
  starting transfers between devices: 14.3 us -> 11.6 us
    another operation x4 -> x8, other arithmetic: 0.14 us -> 5.1 us  [gathered_half(): jnp.stack([jnp.where(upper, arrived, held), jnp.where(upper, held, arrive...]
    ppermute x1, starting transfers between devices: 3.05 us -> 0.01 us  [local(): lax.ppermute(partner_peaks, 'seg', [(i, i ^ 1) for i in range(seg_total)])]
    select_n x1 -> x2, other arithmetic: 0.07 us -> 1.72 us  [the longest x1 1.17 us: gathered_half(): jnp.where(upper, mine, arrived)]
    ppermute x1, starting transfers between devices: 0.07 us -> 1.44 us  [gathered_half(): lax.ppermute(theirs, 'seg', [(i, i ^ 1) for i in range(seg_total)])]
    ppermute x1, starting transfers between devices: 1.68 us -> 0.46 us  [local(): other = lax.ppermute(mine, 'seg', [(i, i ^ 1) for i in range(seg_total)])]
    dynamic_slice x2 -> x0, local copies, waits for them, and re-layouts: 0.99 us -> none  [the longest x1 0.97 us: gathered_half(): mine = lax.dynamic_slice_in_dim(template_bank, core * half, half, axis=0)]
    unnamed x7 -> x10, local copies, waits for them, and re-layouts: 1.52 us -> 1.82 us
  transfers between devices with their start and end apart: 7 -> 7, of which waited for: 3 -> 2; matrix products, arithmetic and copies ran while one was open for 24% -> 24% of each run, Pallas kernels for 17% -> 16%
where the time goes in v16:
time: 64.7 us; the launch traced here: 64 us
  Pallas kernels  20.6 us (32%)
  other arithmetic  18 us (28%)
  starting transfers between devices  11.6 us (18%)
  waiting for transfers between devices  6.74 us (10%)
  matrix products  3.7 us (6%)
  local copies, waits for them, and re-layouts  3.03 us (5%)
    pallas_call x2, Pallas kernels, window_peaks(): pl.pallas_call(peaks_kernel, out_shape=jax.ShapeDtypeStruct((template_tot...  20.6 us
    ppermute x3, waiting for transfers between devices, gathered_half(): arrived = lax.ppermute(held, 'seg', pairs)  6.73 us
    ppermute x3, starting transfers between devices, gathered_half(): arrived = lax.ppermute(held, 'seg', pairs)  5.12 us
    another operation x8, other arithmetic, gathered_half(): jnp.stack([jnp.where(upper, arrived, held), jnp.where(upper, held, arrive...  5.1 us
    ppermute x1, starting transfers between devices, passed_along(): return lax.ppermute(value, axis, pairs)  4.54 us
    sin x3, other arithmetic, angle_table(): return (jnp.cos(angle_value), jnp.sin(angle_value))  2.54 us
    unnamed x10, local copies, waits for them, and re-layouts  1.82 us
    convert_element_type x2, other arithmetic, table_pair(): return (high.astype(jnp.bfloat16), (value - high).astype(jnp.bfloat16))  1.74 us
  transfers between devices with their start and end apart: 7, of which 2 were waited for; matrix products, arithmetic and copies ran while one was open for 24% of the time, Pallas kernels for 16%

profile of v16, /device:TPU:1, one launch (start us, length us, event | category | flops | bytes accessed | tf_op | source)
XLA Modules:
  0.0 64.0 jit_solution(10256547245176340336)
XLA Ops:
  0.0 1.1 %convert_multiply_fusion = f32[65536]{0:T(1024)S(1)} fusion(f32[65536]{0:T(1024)} %param.3, s32[65536]{0:T(1024)} %param.4), kind=kLoop, calls=%fused_computation.69 | loop fusion | flops 131072 | bytes 786432 | tf_op jit(solution)/shard_map/mul | solution.py:222
  1.1 4.5 %collective-permute-start = (f32[32768]{0:T(1024)S(1)}, f32[32768]{0:T(1024)S(1)}, u32[]{:S(2)}, u32[]{:S(2)}) collective-permute-start(f32[32768]{0:T(1024)S(1)} %slice.49), channel_id=1, source_target_pairs={{0,1},{1,2},{2,3},{3,4},{4,5},{5,6},{6,7},{7,8},{8,9},{9,10},{10,1... | collective-permute-start | bytes 393224 | tf_op jit(solution)/shard_map/ppermute | solution.py:23
  5.6 2.4 %collective-permute-start.2 = (bf16[1,16,2,2048]{3,2,1,0:T(2,128)(2,1)}, bf16[1,16,2,2048]{3,2,1,0:T(2,128)(2,1)S(1)}, u32[]{:S(2)}, u32[]{:S(2)}) collective-permute-start(bf16[1,16,2,2048]{3,2,1,0:T(2,128)(2,1)} %bitcast.80), channel_id=1, source_target_pairs={{0,8},{1,9},{2,10},{3,11},{4,12},{5,13},{6,14},{7,15},{8,0},{9,1},... | collective-permute-start | bytes 393224 | tf_op jit(solution)/shard_map/ppermute | solution.py:196
  8.0 1.0 %fusion.41 = (f32[256,256]{1,0:T(8,128)S(1)}, f32[256,256]{1,0:T(8,128)S(1)}) fusion(), kind=kLoop, calls=%fused_computation.87 | loop fusion | flops 983040 | bytes 524288 | tf_op jit(solution)/shard_map/cos | solution.py:31
  9.0 0.0 copy-start.2
  9.1 1.0 %fusion.38 = (f32[256,256]{1,0:T(8,128)S(1)}, f32[256,256]{1,0:T(8,128)S(1)}) fusion(), kind=kLoop, calls=%fused_computation.84 | loop fusion | flops 917504 | bytes 524288 | tf_op jit(solution)/shard_map/sin | solution.py:31
  10.1 0.0 copy-start
  10.1 0.0 copy-start.1
  10.1 0.5 fusion.46
  10.7 0.5 fusion.48
  11.2 0.9 %fusion.9 = (bf16[512,256]{1,0:T(8,128)(2,1)}, bf16[512,256]{1,0:T(8,128)(2,1)}) fusion(f32[256,128]{1,0:T(8,128)S(1)} %get-tuple-element.26, f32[256,128]{1,0:T(8,128)S(1)} %get-tuple-element.25, f32[256,128]{1,0:T(8,128)S(1)} %fusion.48), kind=kLoop, calls=%fused_computation.32 | loop fusion | flops 917504 | bytes 917504 | tf_op jit(solution)/shard_map/convert_element_type | solution.py:72
  12.0 1.0 %fusion.40 = f32[256,256]{1,0:T(8,128)S(1)} fusion(), kind=kLoop, calls=%fused_computation.86 | loop fusion | flops 917504 | bytes 262144 | tf_op jit(solution)/shard_map/sin | solution.py:31
  13.0 0.2 reshape.48
  13.2 0.9 %fusion.10 = (bf16[512,256]{1,0:T(8,128)(2,1)}, bf16[512,256]{1,0:T(8,128)(2,1)}) fusion(f32[256,256]{1,0:T(8,128)S(1)} %get-tuple-element.21, f32[256,256]{1,0:T(8,128)S(1)} %fusion.40, f32[256,256]{1,0:T(8,128)S(1)} %get-tuple-element.22), kind=kLoop, calls=%fused_computation.33 | loop fusion | flops 1310720 | bytes 1310720 | tf_op jit(solution)/shard_map/convert_element_type | solution.py:72
  14.1 0.0 collective-permute-done.2
  14.1 0.0 copy-done.2
  14.1 0.2 fusion.34
  14.3 0.4 fusion.62
  14.7 1.4 %collective-permute-start.3 = (bf16[2,1,16,2,2048]{4,3,2,0,1:T(2,128)(2,1)S(1)}, bf16[2,1,16,2,2048]{4,3,2,0,1:T(2,128)(2,1)S(1)}, u32[]{:S(2)}, u32[]{:S(2)}) collective-permute-start(bf16[2,1,16,2,2048]{4,3,2,0,1:T(2,128)(2,1)S(1)} %fusion.62), channel_id=1, source_target_pairs={{0,2},{1,5},{2,0},{3,7},{4,6},{5,1},{6,4},{7,3},{8,10},{9,13},{10,... | collective-permute-start | bytes 786440 | tf_op jit(solution)/shard_map/ppermute | solution.py:196
  16.1 0.0 collective-permute-done
  16.1 0.2 pad_maximum_fusion.9
  16.3 0.5 collective-permute-start.1
  16.8 3.5 %collective-permute-done.3 = bf16[2,1,16,2,2048]{4,3,2,0,1:T(2,128)(2,1)S(1)} collective-permute-done((bf16[2,1,16,2,2048]{4,3,2,0,1:T(2,128)(2,1)S(1)}, bf16[2,1,16,2,2048]{4,3,2,0,1:T(2,128)(2,1)S(1)}, u32[]{:S(2)}, u32[]{:S(2)}) %collective-permute-start.3) | collective-permute-done | bytes 262176 | tf_op jit(solution)/shard_map/ppermute | solution.py:196
  20.3 0.5 fusion.23
  20.7 0.5 fusion.22
  21.2 0.7 %fusion.63 = bf16[2,2,1,16,2,2048]{5,4,3,1,0,2:T(2,128)(2,1)S(1)} fusion(bf16[1,2,1,16,2,2048]{5,4,3,1,2,0:T(2,128)(2,1)S(1)} %fusion.23, bf16[1,2,1,16,2,2048]{5,4,3,1,2,0:T(2,128)(2,1)S(1)} %fusion.22), kind=kLoop, calls=%fused_computation.112 | loop fusion | flops 262144 | bytes 1048576 | tf_op jit(solution)/shard_map/stack | solution.py:198
  21.9 1.4 %collective-permute-start.4 = (bf16[2,2,1,16,2,2048]{5,4,3,1,0,2:T(2,128)(2,1)S(1)}, bf16[2,2,1,16,2,2048]{5,4,3,1,0,2:T(2,128)(2,1)S(1)}, u32[]{:S(2)}, u32[]{:S(2)}) collective-permute-start(bf16[2,2,1,16,2,2048]{5,4,3,1,0,2:T(2,128)(2,1)S(1)} %fusion.63), channel_id=1, source_target_pairs={{0,4},{1,3},{2,6},{3,1},{4,0},{5,7},{6,2},{7,5},{8,12},{9,11},{10,... | collective-permute-start | bytes 1572872 | tf_op jit(solution)/shard_map/ppermute | solution.py:196
  23.3 0.0 collective-permute-done.1
  23.3 0.1 slice.50
  23.5 0.5 maximum_select_fusion
  24.0 0.2 fusion.65
  24.2 0.2 pad_maximum_fusion.7
  24.4 1.1 %fusion.4 = f32[4,256,512]{2,1,0:T(8,128)S(1)} fusion(f32[1,4,256,256]{3,1,2,0:T(4,128)S(1)} %bitcast.75, f32[256,256]{1,0:T(8,128)S(1)} %get-tuple-element.22, f32[256,256]{1,0:T(8,128)S(1)} %get-tuple-element.21), kind=kOutput, calls=%fused_computation.10 | convolution fusion | flops 805437440 | bytes 3670016 | tf_op jit(solution)/shard_map/bnm,nf->bmf/dot_general | solution.py:41
  25.5 0.0 copy-done
  25.5 0.0 copy-done.1
  25.5 0.3 multiply_add_fusion
  25.8 1.3 %fusion.3 = f32[4,128,512]{2,1,0:T(8,128)S(1)} fusion(f32[4,256,256]{2,1,0:T(8,128)S(1)} %get-tuple-element.8, f32[4,256,256]{2,1,0:T(8,128)S(1)} %get-tuple-element.7), kind=kOutput, calls=%fused_computation.5 | convolution fusion | flops 403636224 | bytes 3145728 | tf_op jit(solution)/shard_map/bnf,nk->bkf/dot_general | solution.py:54
  27.1 3.2 %collective-permute-done.4 = bf16[2,2,1,16,2,2048]{5,4,3,1,0,2:T(2,128)(2,1)S(1)} collective-permute-done((bf16[2,2,1,16,2,2048]{5,4,3,1,0,2:T(2,128)(2,1)S(1)}, bf16[2,2,1,16,2,2048]{5,4,3,1,0,2:T(2,128)(2,1)S(1)}, u32[]{:S(2)}, u32[]{:S(2)}) %collective-permute-start.4) | collective-permute-done | bytes 524320 | tf_op jit(solution)/shard_map/ppermute | solution.py:196
  30.3 1.1 %fusion.11 = bf16[1,2,2,1,16,2,2048]{6,5,4,2,1,3,0:T(2,128)(2,1)S(1)} fusion(bf16[2,2,1,16,2,2048]{5,4,3,1,0,2:T(2,128)(2,1)S(1)} %collective-permute-done.4, pred[]{:T(512)S(6)} %ne.103, bf16[1,2,1,16,2,2048]{5,4,3,1,2,0:T(2,128)(2,1)S(1)} %fusion.23, bf16[1,2,1,16,2,2048]{5,4,3,1,2,0:T(2,128)(2,1)S(1)} %fusion.22), kind=kLoop, calls=%fused_computation.34 | loop fusion | flops 524288 | bytes 1572865 | tf_op jit(solution)/shard_map/stack | solution.py:198
  31.5 1.0 %fusion.14 = bf16[1,2,2,1,16,2,2048]{6,5,4,2,1,3,0:T(2,128)(2,1)S(1)} fusion(pred[]{:T(512)S(6)} %ne.103, bf16[2,2,1,16,2,2048]{5,4,3,1,0,2:T(2,128)(2,1)S(1)} %collective-permute-done.4, bf16[1,2,1,16,2,2048]{5,4,3,1,2,0:T(2,128)(2,1)S(1)} %fusion.23, bf16[1,2,1,16,2,2048]{5,4,3,1,2,0:T(2,128)(2,1)S(1)} %fusion.22), kind=kLoop, calls=%fused_computation.37 | loop fusion | flops 524288 | bytes 1572865 | tf_op jit(solution)/shard_map/stack | solution.py:198
  32.4 0.8 %fusion.8 = bf16[2,2,2,1,8,2,2048]{6,5,4,2,1,3,0:T(2,128)(2,1)S(1)} fusion(s32[]{:T(128)S(6)} %select_n.185, bf16[1,2,2,1,16,2,2048]{6,5,4,2,1,3,0:T(2,128)(2,1)S(1)} %fusion.11, bf16[1,2,2,1,16,2,2048]{6,5,4,2,1,3,0:T(2,128)(2,1)S(1)} %fusion.14), kind=kLoop, calls=%fused_computation.31 | loop fusion | flops 262144 | bytes 1572868 | tf_op jit(solution)/shard_map/stack | solution.py:198
  33.2 0.4 copy.40
  33.6 1.4 %collective-permute-start.5 = (bf16[2,2,2,1,8,2,2048]{6,5,4,2,0,3,1:T(2,128)(2,1)S(1)}, bf16[2,2,2,1,8,2,2048]{6,5,4,2,0,3,1:T(2,128)(2,1)S(1)}, u32[]{:S(2)}, u32[]{:S(2)}) collective-permute-start(bf16[2,2,2,1,8,2,2048]{6,5,4,2,0,3,1:T(2,128)(2,1)S(1)} %copy.40), channel_id=1, source_target_pairs={{0,1},{1,0},{2,3},{3,2},{4,5},{5,4},{6,7},{7,6},{8,9},{9,8},{10,11... | collective-permute-start | bytes 1572872 | tf_op jit(solution)/shard_map/ppermute | solution.py:202
  35.0 1.3 %fusion.2 = f32[4,128,512]{2,1,0:T(8,128)S(1)} fusion(f32[4,256,256]{2,1,0:T(8,128)S(1)} %get-tuple-element.8, f32[4,256,256]{2,1,0:T(8,128)S(1)} %get-tuple-element.7), kind=kOutput, calls=%fused_computation.4 | convolution fusion | flops 403636224 | bytes 3145728 | tf_op jit(solution)/shard_map/bnf,nk->bkf/dot_general | solution.py:53
  36.3 0.1 slice_subtract_fusion
  36.5 1.1 %fusion.13 = (f32[2,128,512]{2,1,0:T(8,128)}, f32[2,128,512]{2,1,0:T(8,128)}) fusion(s32[]{:T(128)S(6)} %select_n.171, f32[4,128,256]{2,1,0:T(8,128)S(1)} %get-tuple-element.10, f32[4,128,256]{2,1,0:T(8,128)S(1)} %get-tuple-element.9, s32[]{:T(128)S(6)} %select_n.190), kind=kLoop, calls=%fused_computation.36 | loop fusion | flops 262144 | bytes 2097160 | tf_op jit(solution)/shard_map/concatenate | solution.py:55
  37.6 0.0 collective-permute-done.5
  37.6 1.2 %broadcast_select_fusion.1 = (bf16[2,2,2,1,8,2,2048]{6,5,4,2,1,3,0:T(2,128)(2,1)S(1)}, bf16[2,2,2,1,8,2,2048]{6,5,4,2,1,3,0:T(2,128)(2,1)S(1)}) fusion(pred[]{:T(512)S(6)} %ne.102, bf16[2,2,2,1,8,2,2048]{6,5,4,2,0,3,1:T(2,128)(2,1)S(1)} %collective-permute-done.5, s32[]{:T(128)S(6)} %select_n.186, bf16[1,2,2,1,16,2,2048]{6,5,4,2,1,3,0:T(2,128)(2,1)S(1)} %fusion.14, ...), kind=kLoop, calls=%fused_computation.20 | loop fusion | flops 524288 | bytes 2621445 | tf_op jit(solution)/shard_map/jit(_where)/select_n | solution.py:205
  38.8 0.5 broadcast_select_fusion.2
  39.4 0.3 stack.45
  39.7 0.3 stack.46
  40.1 1.3 %bitcast_select_fusion.1 = bf16[8,2,2,2,2,2,8,256]{7,6,5,4,3,2,1,0:T(8,128)(2,1)} fusion(bf16[2,2,2,2,8,2,8,256]{7,6,5,4,3,2,1,0:T(8,128)(2,1)S(1)} %constant_dynamic-update-slice_fusion, pred[]{:T(512)S(6)} %eq.19), kind=kLoop, calls=%fused_computation.15 | loop fusion | flops 524288 | bytes 2097153 | tf_op jit(solution)/shard_map/jit(_where)/select_n | solution.py:214
  41.4 10.3 %shard_map.38 = f32[8,2,128]{2,1,0:T(2,128)} custom-call(f32[2,128,512]{2,1,0:T(8,128)} %get-tuple-element.12.spec_ref, bf16[8,2,128,256]{3,2,1,0:T(8,128)(2,1)} %bitcast.76, bf16[512,256]{1,0:T(8,128)(2,1)} %get-tuple-element.18.fh_ref, bf16[512,256]{1,0:T(8,128)(2,1)} %get-tuple-element.17.fl_ref, f32[256,256]{1,0:T(8,128)} %copy-done.1, ...), custom_call_target="tpu_custom_call" | custom-call | flops 6442450944 | bytes 1581056 | tf_op jit(solution)/shard_map/pallas_call | solution.py:157
  51.7 0.7 %copy.52 = f32[1,8,2,128]{3,1,2,0:T(8,128)S(1)} copy(f32[1,8,2,128]{3,2,1,0:T(2,128)} %bitcast.84) | data formatting | bytes 16384
  52.4 0.0 collective-permute-start.6
  52.4 10.3 %shard_map.37 = f32[8,2,128]{2,1,0:T(2,128)} custom-call(f32[2,128,512]{2,1,0:T(8,128)} %get-tuple-element.11.spec_ref, bf16[8,2,128,256]{3,2,1,0:T(8,128)(2,1)} %bitcast.77, bf16[512,256]{1,0:T(8,128)(2,1)} %get-tuple-element.18.fh_ref, bf16[512,256]{1,0:T(8,128)(2,1)} %get-tuple-element.17.fl_ref, f32[256,256]{1,0:T(8,128)} %copy-done.1, ...), custom_call_target="tpu_custom_call" | custom-call | flops 6442450944 | bytes 1581056 | tf_op jit(solution)/shard_map/pallas_call | solution.py:157
  62.6 0.7 %copy.53 = f32[1,8,2,128]{3,1,2,0:T(8,128)S(1)} copy(f32[1,8,2,128]{3,2,1,0:T(2,128)} %bitcast.83) | data formatting | bytes 16384
  63.3 0.0 collective-permute-done.6
  63.3 0.6 maximum_select_fusion.1
  (3 shorter events, 0.1 us)
Async XLA Ops:
  1.1 15.0 %collective-permute-start = (f32[32768]{0:T(1024)S(1)}, f32[32768]{0:T(1024)S(1)}, u32[]{:S(2)}, u32[]{:S(2)}) collective-permute-start(f32[32768]{0:T(1024)S(1)} %slice.49), channel_id=1, source_target_pairs={{0,1},{1,2},{2,3},{3,4},{4,5},{5,6},{6,7},{7,8},{8,9},{9,10},{10,1... | collective-permute-start | bytes 393224 | tf_op jit(solution)/shard_map/ppermute | solution.py:23
  5.6 8.5 %collective-permute-start.2 = (bf16[1,16,2,2048]{3,2,1,0:T(2,128)(2,1)}, bf16[1,16,2,2048]{3,2,1,0:T(2,128)(2,1)S(1)}, u32[]{:S(2)}, u32[]{:S(2)}) collective-permute-start(bf16[1,16,2,2048]{3,2,1,0:T(2,128)(2,1)} %bitcast.80), channel_id=1, source_target_pairs={{0,8},{1,9},{2,10},{3,11},{4,12},{5,13},{6,14},{7,15},{8,0},{9,1},... | collective-permute-start | bytes 393224 | tf_op jit(solution)/shard_map/ppermute | solution.py:196
  9.0 5.1 %copy-start.2 = (bf16[16,2,2048]{2,1,0:T(2,128)(2,1)S(1)}, bf16[16,2,2048]{2,1,0:T(2,128)(2,1)}, u32[]{:S(2)}) copy-start(bf16[16,2,2048]{2,1,0:T(2,128)(2,1)} %param.5) | copy-start | bytes 393220
  10.1 15.4 %copy-start = (f32[256,256]{1,0:T(8,128)}, f32[256,256]{1,0:T(8,128)S(1)}, u32[]{:S(2)}) copy-start(f32[256,256]{1,0:T(8,128)S(1)} %get-tuple-element.23.ts_ref) | copy-start | bytes 786436
  10.1 15.4 %copy-start.1 = (f32[256,256]{1,0:T(8,128)}, f32[256,256]{1,0:T(8,128)S(1)}, u32[]{:S(2)}) copy-start(f32[256,256]{1,0:T(8,128)S(1)} %get-tuple-element.24.tc_ref) | copy-start | bytes 786436
  14.7 5.6 %collective-permute-start.3 = (bf16[2,1,16,2,2048]{4,3,2,0,1:T(2,128)(2,1)S(1)}, bf16[2,1,16,2,2048]{4,3,2,0,1:T(2,128)(2,1)S(1)}, u32[]{:S(2)}, u32[]{:S(2)}) collective-permute-start(bf16[2,1,16,2,2048]{4,3,2,0,1:T(2,128)(2,1)S(1)} %fusion.62), channel_id=1, source_target_pairs={{0,2},{1,5},{2,0},{3,7},{4,6},{5,1},{6,4},{7,3},{8,10},{9,13},{10,... | collective-permute-start | bytes 786440 | tf_op jit(solution)/shard_map/ppermute | solution.py:196
  16.3 7.0 %collective-permute-start.1 = (f32[3,32768]{1,0:T(4,128)S(1)}, f32[3,32768]{1,0:T(4,128)S(1)}, u32[]{:S(2)}, u32[]{:S(2)}) collective-permute-start(f32[3,32768]{1,0:T(4,128)S(1)} %pad_maximum_fusion.9), channel_id=1, source_target_pairs={{0,1},{1,0},{2,3},{3,2},{4,5},{5,4},{6,7},{7,6},{8,9},{9,8},{10,11... | collective-permute-start | bytes 1179656 | tf_op jit(solution)/shard_map/ppermute | solution.py:227
  21.9 8.4 %collective-permute-start.4 = (bf16[2,2,1,16,2,2048]{5,4,3,1,0,2:T(2,128)(2,1)S(1)}, bf16[2,2,1,16,2,2048]{5,4,3,1,0,2:T(2,128)(2,1)S(1)}, u32[]{:S(2)}, u32[]{:S(2)}) collective-permute-start(bf16[2,2,1,16,2,2048]{5,4,3,1,0,2:T(2,128)(2,1)S(1)} %fusion.63), channel_id=1, source_target_pairs={{0,4},{1,3},{2,6},{3,1},{4,0},{5,7},{6,2},{7,5},{8,12},{9,11},{10,... | collective-permute-start | bytes 1572872 | tf_op jit(solution)/shard_map/ppermute | solution.py:196
  33.6 4.0 %collective-permute-start.5 = (bf16[2,2,2,1,8,2,2048]{6,5,4,2,0,3,1:T(2,128)(2,1)S(1)}, bf16[2,2,2,1,8,2,2048]{6,5,4,2,0,3,1:T(2,128)(2,1)S(1)}, u32[]{:S(2)}, u32[]{:S(2)}) collective-permute-start(bf16[2,2,2,1,8,2,2048]{6,5,4,2,0,3,1:T(2,128)(2,1)S(1)} %copy.40), channel_id=1, source_target_pairs={{0,1},{1,0},{2,3},{3,2},{4,5},{5,4},{6,7},{7,6},{8,9},{9,8},{10,11... | collective-permute-start | bytes 1572872 | tf_op jit(solution)/shard_map/ppermute | solution.py:202
  52.4 11.0 %collective-permute-start.6 = (f32[8,256]{1,0:T(8,128)S(1)}, f32[8,256]{1,0:T(8,128)S(1)}, u32[]{:S(2)}, u32[]{:S(2)}) collective-permute-start(f32[8,256]{1,0:T(8,128)S(1)} %bitcast.82), channel_id=1, source_target_pairs={{0,1},{1,0},{2,3},{3,2},{4,5},{5,4},{6,7},{7,6},{8,9},{9,8},{10,11... | collective-permute-start | bytes 24584 | tf_op jit(solution)/shard_map/ppermute | solution.py:240

commit v17 on v15

--- a/solution.py
+++ b/solution.py
@@ -233,14 +233,15 @@
     partner_spectra = lax.dynamic_slice_in_dim(spectra, (1 - core) * block_total, block_total, axis=0)
     own_spectra = lax.dynamic_slice_in_dim(spectra, core * block_total, block_total, axis=0)
     half = bank.shape[0]
-    partner_peaks = window_peaks(partner_spectra, bank, tables).reshape(half, block_total * (RADIX // 2))
+    partner_peaks = window_peaks(partner_spectra, bank, tables)
     returned = lax.ppermute(partner_peaks, "seg", [(i, i ^ 1) for i in range(seg_total)])
-    own_peaks = window_peaks(own_spectra, bank, tables).reshape(half, block_total * (RADIX // 2))
-    return jnp.where(
+    own_peaks = window_peaks(own_spectra, bank, tables)
+    peaks = jnp.where(
         core == 0,
         jnp.concatenate([own_peaks, returned], axis=0),
         jnp.concatenate([returned, own_peaks], axis=0),
     )
+    return peaks.reshape(2 * half, block_total * (RADIX // 2))
 
 
 def solution(mesh):

time: 60.9 us -> 60.1 us (0.987)
  local copies, waits for them, and re-layouts: 3.13 us -> 2.44 us
    unnamed x7, local copies, waits for them, and re-layouts: 1.52 us -> 0.82 us
where the time goes in v17:
time: 60.1 us; the launch traced here: 59.8 us
  Pallas kernels  20.5 us (34%)
  starting transfers between devices  14.3 us (24%)
  other arithmetic  11.6 us (19%)
  waiting for transfers between devices  6.99 us (12%)
  matrix products  3.71 us (6%)
  local copies, waits for them, and re-layouts  2.44 us (4%)
    pallas_call x2, Pallas kernels, window_peaks(): pl.pallas_call(peaks_kernel, out_shape=jax.ShapeDtypeStruct((template_tot...  20.5 us
    ppermute x3, waiting for transfers between devices, gathered_half(): arrived = lax.ppermute(held, 'seg', pairs)  6.98 us
    ppermute x3, starting transfers between devices, gathered_half(): arrived = lax.ppermute(held, 'seg', pairs)  4.99 us
    ppermute x1, starting transfers between devices, passed_along(): return lax.ppermute(value, axis, pairs)  4.54 us
    ppermute x1, starting transfers between devices, local(): lax.ppermute(partner_peaks, 'seg', [(i, i ^ 1) for i in range(seg_total)])  3.04 us
    sin x3, other arithmetic, angle_table(): return (jnp.cos(angle_value), jnp.sin(angle_value))  2.54 us
    convert_element_type x2, other arithmetic, table_pair(): return (high.astype(jnp.bfloat16), (value - high).astype(jnp.bfloat16))  1.73 us
    ppermute x1, starting transfers between devices, local(): other = lax.ppermute(mine, 'seg', [(i, i ^ 1) for i in range(seg_total)])  1.68 us
  transfers between devices with their start and end apart: 7, of which 3 were waited for; matrix products, arithmetic and copies ran while one was open for 24% of the time, Pallas kernels for 17%

profile of v17, /device:TPU:1, one launch (start us, length us, event | category | flops | bytes accessed | tf_op | source)
XLA Modules:
  0.0 59.8 jit_solution(3153024263842349891)
XLA Ops:
  0.0 1.1 %convert_multiply_fusion = f32[65536]{0:T(1024)S(1)} fusion(f32[65536]{0:T(1024)} %param.3, s32[65536]{0:T(1024)} %param.4), kind=kLoop, calls=%fused_computation.59 | loop fusion | flops 131072 | bytes 786432 | tf_op jit(solution)/shard_map/mul | solution.py:219
  1.1 4.5 %collective-permute-start = (f32[32768]{0:T(1024)S(1)}, f32[32768]{0:T(1024)S(1)}, u32[]{:S(2)}, u32[]{:S(2)}) collective-permute-start(f32[32768]{0:T(1024)S(1)} %slice.49), channel_id=1, source_target_pairs={{0,1},{1,2},{2,3},{3,4},{4,5},{5,6},{6,7},{7,8},{8,9},{9,10},{10,1... | collective-permute-start | bytes 393224 | tf_op jit(solution)/shard_map/ppermute | solution.py:23
  5.6 1.0 %constant_dynamic-slice_fusion = (bf16[8,2,2048]{2,1,0:T(2,128)(2,1)S(1)}, bf16[8,2,2048]{2,1,0:T(2,128)(2,1)S(1)}) fusion(bf16[16,2,2048]{2,1,0:T(2,128)(2,1)} %param.5, s32[]{:T(128)S(6)} %select_n.181, s32[]{:T(128)S(6)} %select_n.180), kind=kLoop, calls=%fused_computation.94 | loop fusion | bytes 262152 | tf_op jit(solution)/shard_map/dynamic_slice | solution.py:187
  6.7 0.1 collective-permute-start.2
  6.7 1.0 %fusion.33 = (f32[256,256]{1,0:T(8,128)S(1)}, f32[256,256]{1,0:T(8,128)S(1)}) fusion(), kind=kLoop, calls=%fused_computation.76 | loop fusion | flops 983040 | bytes 524288 | tf_op jit(solution)/shard_map/cos | solution.py:31
  7.8 1.0 %fusion.30 = (f32[256,256]{1,0:T(8,128)S(1)}, f32[256,256]{1,0:T(8,128)S(1)}) fusion(), kind=kLoop, calls=%fused_computation.73 | loop fusion | flops 917504 | bytes 524288 | tf_op jit(solution)/shard_map/sin | solution.py:31
  8.8 0.0 copy-start
  8.8 0.0 copy-start.1
  8.8 0.5 fusion.40
  9.4 0.5 fusion.42
  9.9 0.9 %fusion.7 = (bf16[512,256]{1,0:T(8,128)(2,1)}, bf16[512,256]{1,0:T(8,128)(2,1)}) fusion(f32[256,128]{1,0:T(8,128)S(1)} %get-tuple-element.32, f32[256,128]{1,0:T(8,128)S(1)} %get-tuple-element.31, f32[256,128]{1,0:T(8,128)S(1)} %fusion.42), kind=kLoop, calls=%fused_computation.21 | loop fusion | flops 917504 | bytes 917504 | tf_op jit(solution)/shard_map/convert_element_type | solution.py:72
  10.7 0.0 collective-permute-done.2
  10.8 2.4 %collective-permute-start.3 = (bf16[2,1,8,2,2048]{4,2,3,0,1:T(8,128)(2,1)S(1)}, bf16[2,1,8,2,2048]{4,2,3,0,1:T(8,128)(2,1)S(1)}, u32[]{:S(2)}, u32[]{:S(2)}) collective-permute-start(bf16[2,1,8,2,2048]{4,2,3,0,1:T(8,128)(2,1)S(1)} %pad_maximum_fusion.12), channel_id=1, source_target_pairs={{0,8},{1,9},{2,10},{3,11},{4,12},{5,13},{6,14},{7,15},{8,0},{9,1},... | collective-permute-start | bytes 393224 | tf_op jit(solution)/shard_map/ppermute | solution.py:200
  13.2 1.0 %fusion.32 = f32[256,256]{1,0:T(8,128)S(1)} fusion(), kind=kLoop, calls=%fused_computation.75 | loop fusion | flops 917504 | bytes 262144 | tf_op jit(solution)/shard_map/sin | solution.py:31
  14.2 0.2 reshape.47
  14.3 0.9 %fusion.8 = (bf16[512,256]{1,0:T(8,128)(2,1)}, bf16[512,256]{1,0:T(8,128)(2,1)}) fusion(f32[256,256]{1,0:T(8,128)S(1)} %get-tuple-element.27, f32[256,256]{1,0:T(8,128)S(1)} %fusion.32, f32[256,256]{1,0:T(8,128)S(1)} %get-tuple-element.28), kind=kLoop, calls=%fused_computation.22 | loop fusion | flops 1310720 | bytes 1310720 | tf_op jit(solution)/shard_map/convert_element_type | solution.py:72
  15.2 3.9 %collective-permute-done.3 = bf16[2,1,8,2,2048]{4,2,3,0,1:T(8,128)(2,1)S(1)} collective-permute-done((bf16[2,1,8,2,2048]{4,2,3,0,1:T(8,128)(2,1)S(1)}, bf16[2,1,8,2,2048]{4,2,3,0,1:T(8,128)(2,1)S(1)}, u32[]{:S(2)}, u32[]{:S(2)}) %collective-permute-start.3) | collective-permute-done | bytes 131104 | tf_op jit(solution)/shard_map/ppermute | solution.py:200
  19.2 1.3 %collective-permute-start.4 = (bf16[2,2,1,8,2,2048]{5,3,4,1,0,2:T(8,128)(2,1)S(1)}, bf16[2,2,1,8,2,2048]{5,3,4,1,0,2:T(8,128)(2,1)S(1)}, u32[]{:S(2)}, u32[]{:S(2)}) collective-permute-start(bf16[2,2,1,8,2,2048]{5,3,4,1,0,2:T(8,128)(2,1)S(1)} %pad_maximum_fusion.11), channel_id=1, source_target_pairs={{0,2},{1,5},{2,0},{3,7},{4,6},{5,1},{6,4},{7,3},{8,10},{9,13},{10,... | collective-permute-start | bytes 786440 | tf_op jit(solution)/shard_map/ppermute | solution.py:200
  20.5 0.0 collective-permute-done
  20.5 0.2 pad_maximum_fusion.9
  20.8 1.7 %collective-permute-start.1 = (f32[3,32768]{1,0:T(4,128)S(1)}, f32[3,32768]{1,0:T(4,128)S(1)}, u32[]{:S(2)}, u32[]{:S(2)}) collective-permute-start(f32[3,32768]{1,0:T(4,128)S(1)} %pad_maximum_fusion.9), channel_id=1, source_target_pairs={{0,1},{1,0},{2,3},{3,2},{4,5},{5,4},{6,7},{7,6},{8,9},{9,8},{10,11... | collective-permute-start | bytes 1179656 | tf_op jit(solution)/shard_map/ppermute | solution.py:224
  22.4 2.3 %collective-permute-done.4 = bf16[2,2,1,8,2,2048]{5,3,4,1,0,2:T(8,128)(2,1)S(1)} collective-permute-done((bf16[2,2,1,8,2,2048]{5,3,4,1,0,2:T(8,128)(2,1)S(1)}, bf16[2,2,1,8,2,2048]{5,3,4,1,0,2:T(8,128)(2,1)S(1)}, u32[]{:S(2)}, u32[]{:S(2)}) %collective-permute-start.4) | collective-permute-done | bytes 262176 | tf_op jit(solution)/shard_map/ppermute | solution.py:200
  24.8 0.1 pad_maximum_fusion.10
  24.9 1.3 %collective-permute-start.5 = (bf16[2,2,2,1,8,2,2048]{6,4,5,3,2,1,0:T(8,128)(2,1)S(1)}, bf16[2,2,2,1,8,2,2048]{6,4,5,3,2,1,0:T(8,128)(2,1)S(1)}, u32[]{:S(2)}, u32[]{:S(2)}) collective-permute-start(bf16[2,2,2,1,8,2,2048]{6,4,5,3,2,1,0:T(8,128)(2,1)S(1)} %pad_maximum_fusion.10), channel_id=1, source_target_pairs={{0,4},{1,3},{2,6},{3,1},{4,0},{5,7},{6,2},{7,5},{8,12},{9,11},{10,... | collective-permute-start | bytes 1572872 | tf_op jit(solution)/shard_map/ppermute | solution.py:200
  26.2 0.0 collective-permute-done.1
  26.2 0.1 slice.50
  26.3 0.5 maximum_select_fusion
  26.8 0.2 fusion.56
  27.0 0.2 pad_maximum_fusion.7
  27.3 1.1 %fusion.4 = f32[4,256,512]{2,1,0:T(8,128)S(1)} fusion(f32[1,4,256,256]{3,1,2,0:T(4,128)S(1)} %bitcast.60, f32[256,256]{1,0:T(8,128)S(1)} %get-tuple-element.28, f32[256,256]{1,0:T(8,128)S(1)} %get-tuple-element.27), kind=kOutput, calls=%fused_computation.9 | convolution fusion | flops 805437440 | bytes 3670016 | tf_op jit(solution)/shard_map/bnm,nf->bmf/dot_general | solution.py:41
  28.4 0.0 copy-done
  28.4 0.0 copy-done.1
  28.4 0.3 multiply_add_fusion
  28.7 1.3 %fusion.3 = f32[4,128,512]{2,1,0:T(8,128)S(1)} fusion(f32[4,256,256]{2,1,0:T(8,128)S(1)} %get-tuple-element.6, f32[4,256,256]{2,1,0:T(8,128)S(1)} %get-tuple-element.5), kind=kOutput, calls=%fused_computation.4 | convolution fusion | flops 403636224 | bytes 3145728 | tf_op jit(solution)/shard_map/bnf,nk->bkf/dot_general | solution.py:54
  30.0 1.3 %fusion.2 = f32[4,128,512]{2,1,0:T(8,128)S(1)} fusion(f32[4,256,256]{2,1,0:T(8,128)S(1)} %get-tuple-element.6, f32[4,256,256]{2,1,0:T(8,128)S(1)} %get-tuple-element.5), kind=kOutput, calls=%fused_computation.3 | convolution fusion | flops 403636224 | bytes 3145728 | tf_op jit(solution)/shard_map/bnf,nk->bkf/dot_general | solution.py:53
  31.3 0.1 slice_subtract_fusion
  31.5 1.1 %fusion.10 = (f32[2,128,512]{2,1,0:T(8,128)}, f32[2,128,512]{2,1,0:T(8,128)}) fusion(s32[]{:T(128)S(6)} %select_n.172, f32[4,128,256]{2,1,0:T(8,128)S(1)} %get-tuple-element.8, f32[4,128,256]{2,1,0:T(8,128)S(1)} %get-tuple-element.7, s32[]{:T(128)S(6)} %select_n.191), kind=kLoop, calls=%fused_computation.24 | loop fusion | flops 262144 | bytes 2097160 | tf_op jit(solution)/shard_map/concatenate | solution.py:55
  32.6 0.7 %collective-permute-done.5 = bf16[2,2,2,1,8,2,2048]{6,4,5,3,2,1,0:T(8,128)(2,1)S(1)} collective-permute-done((bf16[2,2,2,1,8,2,2048]{6,4,5,3,2,1,0:T(8,128)(2,1)S(1)}, bf16[2,2,2,1,8,2,2048]{6,4,5,3,2,1,0:T(8,128)(2,1)S(1)}, u32[]{:S(2)}, u32[]{:S(2)}) %collective-permute-start.5) | collective-permute-done | bytes 524320 | tf_op jit(solution)/shard_map/ppermute | solution.py:200
  33.3 0.1 broadcast_select_fusion
  33.4 0.1 copy_dynamic-update-slice_fusion.1
  33.5 0.1 copy_dynamic-update-slice_fusion
  33.6 1.3 %bitcast_select_fusion = bf16[8,2,2,2,2,2,8,256]{7,6,5,4,3,2,1,0:T(8,128)(2,1)} fusion(bf16[2,2,2,2,8,2,8,256]{7,6,3,0,1,2,5,4:T(8,128)(2,1)S(1)} %copy_dynamic-update-slice_fusion, pred[]{:T(512)S(6)} %eq.19), kind=kLoop, calls=%fused_computation.14 | loop fusion | flops 524288 | bytes 2097153 | tf_op jit(solution)/shard_map/jit(_where)/select_n | solution.py:211
  34.9 10.3 %shard_map.38 = f32[8,2,128]{2,1,0:T(2,128)} custom-call(f32[2,128,512]{2,1,0:T(8,128)} %get-tuple-element.10.spec_ref, bf16[8,2,128,256]{3,2,1,0:T(8,128)(2,1)} %bitcast.63, bf16[512,256]{1,0:T(8,128)(2,1)} %get-tuple-element.20.fh_ref, bf16[512,256]{1,0:T(8,128)(2,1)} %get-tuple-element.19.fl_ref, f32[256,256]{1,0:T(8,128)} %copy-done.1, ...), custom_call_target="tpu_custom_call" | custom-call | flops 6442450944 | bytes 1581056 | tf_op jit(solution)/shard_map/pallas_call | solution.py:157
  45.2 3.0 %collective-permute-start.6 = (f32[8,2,128]{2,1,0:T(2,128)}, f32[8,2,128]{2,1,0:T(2,128)S(1)}, u32[]{:S(2)}, u32[]{:S(2)}) collective-permute-start(f32[8,2,128]{2,1,0:T(2,128)} %shard_map.38), channel_id=1, source_target_pairs={{0,1},{1,0},{2,3},{3,2},{4,5},{5,4},{6,7},{7,6},{8,9},{9,8},{10,11... | collective-permute-start | bytes 24584 | tf_op jit(solution)/shard_map/ppermute | solution.py:237
  48.2 10.3 %shard_map.37 = f32[8,2,128]{2,1,0:T(2,128)} custom-call(f32[2,128,512]{2,1,0:T(8,128)} %get-tuple-element.9.spec_ref, bf16[8,2,128,256]{3,2,1,0:T(8,128)(2,1)} %bitcast.64, bf16[512,256]{1,0:T(8,128)(2,1)} %get-tuple-element.20.fh_ref, bf16[512,256]{1,0:T(8,128)(2,1)} %get-tuple-element.19.fl_ref, f32[256,256]{1,0:T(8,128)} %copy-done.1, ...), custom_call_target="tpu_custom_call" | custom-call | flops 6442450944 | bytes 1581056 | tf_op jit(solution)/shard_map/pallas_call | solution.py:157
  58.5 0.7 %copy.46 = f32[1,8,2,128]{3,1,2,0:T(8,128)S(1)} copy(f32[1,8,2,128]{3,2,1,0:T(2,128)} %bitcast.71) | data formatting | bytes 16384
  59.2 0.0 collective-permute-done.6
  59.2 0.6 %maximum_select_fusion.1 = f32[16,256]{1,0:T(8,128)} fusion(f32[8,256]{1,0:T(8,128)S(1)} %bitcast.69, f32[8,256]{1,0:T(8,128)S(1)} %bitcast.68, pred[]{:T(512)S(6)} %eq.19), kind=kLoop, calls=%fused_computation.89 | loop fusion | flops 12288 | bytes 32769 | tf_op jit(solution)/shard_map/jit(_where)/select_n | solution.py:239
  (8 shorter events, 0.2 us)
Async XLA Ops:
  1.1 19.4 %collective-permute-start = (f32[32768]{0:T(1024)S(1)}, f32[32768]{0:T(1024)S(1)}, u32[]{:S(2)}, u32[]{:S(2)}) collective-permute-start(f32[32768]{0:T(1024)S(1)} %slice.49), channel_id=1, source_target_pairs={{0,1},{1,2},{2,3},{3,4},{4,5},{5,6},{6,7},{7,8},{8,9},{9,10},{10,1... | collective-permute-start | bytes 393224 | tf_op jit(solution)/shard_map/ppermute | solution.py:23
  6.7 4.1 %collective-permute-start.2 = (bf16[1,8,2,2048]{3,1,2,0:T(8,128)(2,1)S(1)}, bf16[1,8,2,2048]{3,1,2,0:T(8,128)(2,1)S(1)}, u32[]{:S(2)}, u32[]{:S(2)}) collective-permute-start(bf16[1,8,2,2048]{3,1,2,0:T(8,128)(2,1)S(1)} %bitcast.67), channel_id=1, source_target_pairs={{0,1},{1,0},{2,3},{3,2},{4,5},{5,4},{6,7},{7,6},{8,9},{9,8},{10,11... | collective-permute-start | bytes 196616 | tf_op jit(solution)/shard_map/ppermute | solution.py:189
  8.8 19.5 %copy-start = (f32[256,256]{1,0:T(8,128)}, f32[256,256]{1,0:T(8,128)S(1)}, u32[]{:S(2)}) copy-start(f32[256,256]{1,0:T(8,128)S(1)} %get-tuple-element.29.ts_ref) | copy-start | bytes 786436
  8.8 19.5 %copy-start.1 = (f32[256,256]{1,0:T(8,128)}, f32[256,256]{1,0:T(8,128)S(1)}, u32[]{:S(2)}) copy-start(f32[256,256]{1,0:T(8,128)S(1)} %get-tuple-element.30.tc_ref) | copy-start | bytes 786436
  10.8 8.3 %collective-permute-start.3 = (bf16[2,1,8,2,2048]{4,2,3,0,1:T(8,128)(2,1)S(1)}, bf16[2,1,8,2,2048]{4,2,3,0,1:T(8,128)(2,1)S(1)}, u32[]{:S(2)}, u32[]{:S(2)}) collective-permute-start(bf16[2,1,8,2,2048]{4,2,3,0,1:T(8,128)(2,1)S(1)} %pad_maximum_fusion.12), channel_id=1, source_target_pairs={{0,8},{1,9},{2,10},{3,11},{4,12},{5,13},{6,14},{7,15},{8,0},{9,1},... | collective-permute-start | bytes 393224 | tf_op jit(solution)/shard_map/ppermute | solution.py:200
  19.2 5.6 %collective-permute-start.4 = (bf16[2,2,1,8,2,2048]{5,3,4,1,0,2:T(8,128)(2,1)S(1)}, bf16[2,2,1,8,2,2048]{5,3,4,1,0,2:T(8,128)(2,1)S(1)}, u32[]{:S(2)}, u32[]{:S(2)}) collective-permute-start(bf16[2,2,1,8,2,2048]{5,3,4,1,0,2:T(8,128)(2,1)S(1)} %pad_maximum_fusion.11), channel_id=1, source_target_pairs={{0,2},{1,5},{2,0},{3,7},{4,6},{5,1},{6,4},{7,3},{8,10},{9,13},{10,... | collective-permute-start | bytes 786440 | tf_op jit(solution)/shard_map/ppermute | solution.py:200
  20.8 5.4 %collective-permute-start.1 = (f32[3,32768]{1,0:T(4,128)S(1)}, f32[3,32768]{1,0:T(4,128)S(1)}, u32[]{:S(2)}, u32[]{:S(2)}) collective-permute-start(f32[3,32768]{1,0:T(4,128)S(1)} %pad_maximum_fusion.9), channel_id=1, source_target_pairs={{0,1},{1,0},{2,3},{3,2},{4,5},{5,4},{6,7},{7,6},{8,9},{9,8},{10,11... | collective-permute-start | bytes 1179656 | tf_op jit(solution)/shard_map/ppermute | solution.py:224
  24.9 8.4 %collective-permute-start.5 = (bf16[2,2,2,1,8,2,2048]{6,4,5,3,2,1,0:T(8,128)(2,1)S(1)}, bf16[2,2,2,1,8,2,2048]{6,4,5,3,2,1,0:T(8,128)(2,1)S(1)}, u32[]{:S(2)}, u32[]{:S(2)}) collective-permute-start(bf16[2,2,2,1,8,2,2048]{6,4,5,3,2,1,0:T(8,128)(2,1)S(1)} %pad_maximum_fusion.10), channel_id=1, source_target_pairs={{0,4},{1,3},{2,6},{3,1},{4,0},{5,7},{6,2},{7,5},{8,12},{9,11},{10,... | collective-permute-start | bytes 1572872 | tf_op jit(solution)/shard_map/ppermute | solution.py:200
  45.2 14.0 %collective-permute-start.6 = (f32[8,2,128]{2,1,0:T(2,128)}, f32[8,2,128]{2,1,0:T(2,128)S(1)}, u32[]{:S(2)}, u32[]{:S(2)}) collective-permute-start(f32[8,2,128]{2,1,0:T(2,128)} %shard_map.38), channel_id=1, source_target_pairs={{0,1},{1,0},{2,3},{3,2},{4,5},{5,4},{6,7},{7,6},{8,9},{9,8},{10,11... | collective-permute-start | bytes 24584 | tf_op jit(solution)/shard_map/ppermute | solution.py:237

commit v18 on v17

--- a/solution.py
+++ b/solution.py
@@ -72,12 +72,6 @@
     return high.astype(jnp.bfloat16), (value - high).astype(jnp.bfloat16)
 
 
-def triple_dot(left_high, left_low, right_high, right_low):
-    total = jnp.dot(left_high, right_high, preferred_element_type=jnp.float32)
-    total = total + jnp.dot(left_high, right_low, preferred_element_type=jnp.float32)
-    return total + jnp.dot(left_low, right_high, preferred_element_type=jnp.float32)
-
-
 def inverse_tables(k_rows):
     half_radix = RADIX // 2
     cos_first, sin_first = angle_table(RADIX, k_rows, RADIX)
@@ -95,10 +89,12 @@
     second = jnp.concatenate([real_cols[:, half_radix:], imag_cols[:, half_radix:]], axis=1)
     first_high, first_low = table_pair(first)
     second_high, second_low = table_pair(second)
-    return first_high, first_low, cos_twist, sin_twist, second_high, second_low
-
-
-def peaks_kernel(spec_ref, bank_ref, fh_ref, fl_ref, tc_ref, ts_ref, sh_ref, sl_ref, out_ref):
+    first_cat = jnp.concatenate([first_high, first_high, first_low], axis=1)
+    second_cat = jnp.concatenate([second_high, second_low, second_high], axis=0)
+    return first_cat, cos_twist, sin_twist, second_cat
+
+
+def peaks_kernel(spec_ref, bank_ref, first_ref, tc_ref, ts_ref, second_ref, out_ref):
     half_radix = RADIX // 2
     block_total = spec_ref.shape[0]
     step_templates = bank_ref.shape[0]
@@ -119,7 +115,11 @@
             products.append(jnp.concatenate([prod_real, prod_imag], axis=0))
     stacked = jnp.concatenate(products, axis=1)
     stacked_high, stacked_low = split_pair(stacked)
-    first = triple_dot(fh_ref[...], fl_ref[...], stacked_high, stacked_low)
+    first = jnp.dot(
+        first_ref[...],
+        jnp.concatenate([stacked_high, stacked_low, stacked_high], axis=0),
+        preferred_element_type=jnp.float32,
+    )
     cos_twist = tc_ref[...]
     sin_twist = ts_ref[...]
     turned_rows = []
@@ -137,7 +137,11 @@
         )
     turned = jnp.concatenate(turned_rows, axis=0)
     turned_high, turned_low = split_pair(turned)
-    series = triple_dot(turned_high, turned_low, sh_ref[...], sl_ref[...])
+    series = jnp.dot(
+        jnp.concatenate([turned_high, turned_high, turned_low], axis=1),
+        second_ref[...],
+        preferred_element_type=jnp.float32,
+    )
     power_series = (
         series[:, :half_radix] * series[:, :half_radix]
         + series[:, half_radix:] * series[:, half_radix:]
@@ -161,12 +165,10 @@
         in_specs=[
             pl.BlockSpec((block_total, k_rows, 2 * RADIX), lambda k: (0, 0, 0)),
             pl.BlockSpec((step_templates, 2, k_rows, RADIX), lambda k: (k, 0, 0, 0)),
-            pl.BlockSpec((2 * RADIX, 2 * k_rows), fixed),
-            pl.BlockSpec((2 * RADIX, 2 * k_rows), fixed),
+            pl.BlockSpec((2 * RADIX, 6 * k_rows), fixed),
             pl.BlockSpec((RADIX, RADIX), fixed),
             pl.BlockSpec((RADIX, RADIX), fixed),
-            pl.BlockSpec((2 * RADIX, RADIX), fixed),
-            pl.BlockSpec((2 * RADIX, RADIX), fixed),
+            pl.BlockSpec((6 * RADIX, RADIX), fixed),
         ],
         out_specs=pl.BlockSpec((step_templates, block_total, RADIX // 2), lambda k: (k, 0, 0)),
         compiler_params=pltpu.CompilerParams(dimension_semantics=("arbitrary",)),

time: 60.1 us -> 61.8 us (1.028)
  waiting for transfers between devices: 6.99 us -> 8.08 us
    concatenate x0 -> x2, other arithmetic: none -> 1.9 us  [the longest x1 0.96 us: inverse_tables(): first_cat = jnp.concatenate([first_high, first_high, first_low], axis=1)]
    convert_element_type x2, other arithmetic: 1.73 us -> 0.14 us  [table_pair(): return (high.astype(jnp.bfloat16), (value - high).astype(jnp.bfloat16))]
    ppermute x3, waiting for transfers between devices: 6.98 us -> 8.07 us  [gathered_half(): arrived = lax.ppermute(held, 'seg', pairs)]
where the time goes in v18:
time: 61.8 us; the launch traced here: 61.5 us
  Pallas kernels  20.8 us (34%)
  starting transfers between devices  14.3 us (23%)
  other arithmetic  11.9 us (19%)
  waiting for transfers between devices  8.08 us (13%)
  matrix products  3.7 us (6%)
  local copies, waits for them, and re-layouts  2.44 us (4%)
    pallas_call x2, Pallas kernels, window_peaks(): pl.pallas_call(peaks_kernel, out_shape=jax.ShapeDtypeStruct((template_tot...  20.8 us
    ppermute x3, waiting for transfers between devices, gathered_half(): arrived = lax.ppermute(held, 'seg', pairs)  8.07 us
    ppermute x3, starting transfers between devices, gathered_half(): arrived = lax.ppermute(held, 'seg', pairs)  4.99 us
    ppermute x1, starting transfers between devices, passed_along(): return lax.ppermute(value, axis, pairs)  4.54 us
    ppermute x1, starting transfers between devices, local(): lax.ppermute(partner_peaks, 'seg', [(i, i ^ 1) for i in range(seg_total)])  3.05 us
    sin x3, other arithmetic, angle_table(): return (jnp.cos(angle_value), jnp.sin(angle_value))  2.54 us
    ppermute x1, starting transfers between devices, local(): other = lax.ppermute(mine, 'seg', [(i, i ^ 1) for i in range(seg_total)])  1.68 us
    dot_general x1, matrix products, forward(): sine_part = jnp.einsum('bnf,nk->bkf', turned, sin_second, precision=PRECISE)  1.33 us
  transfers between devices with their start and end apart: 7, of which 3 were waited for; matrix products, arithmetic and copies ran while one was open for 24% of the time, Pallas kernels for 17%

profile of v18, /device:TPU:1, one launch (start us, length us, event | category | flops | bytes accessed | tf_op | source)
XLA Modules:
  0.0 61.5 jit_solution(16414904380931670344)
XLA Ops:
  0.0 1.1 %convert_multiply_fusion = f32[65536]{0:T(1024)S(1)} fusion(f32[65536]{0:T(1024)} %param.3, s32[65536]{0:T(1024)} %param.4), kind=kLoop, calls=%fused_computation.61 | loop fusion | flops 131072 | bytes 786432 | tf_op jit(solution)/shard_map/mul | solution.py:221
  1.1 4.5 %collective-permute-start = (f32[32768]{0:T(1024)S(1)}, f32[32768]{0:T(1024)S(1)}, u32[]{:S(2)}, u32[]{:S(2)}) collective-permute-start(f32[32768]{0:T(1024)S(1)} %slice.49), channel_id=1, source_target_pairs={{0,1},{1,2},{2,3},{3,4},{4,5},{5,6},{6,7},{7,8},{8,9},{9,10},{10,1... | collective-permute-start | bytes 393224 | tf_op jit(solution)/shard_map/ppermute | solution.py:23
  5.6 1.0 %constant_dynamic-slice_fusion = (bf16[8,2,2048]{2,1,0:T(2,128)(2,1)S(1)}, bf16[8,2,2048]{2,1,0:T(2,128)(2,1)S(1)}) fusion(bf16[16,2,2048]{2,1,0:T(2,128)(2,1)} %param.5, s32[]{:T(128)S(6)} %select_n.181, s32[]{:T(128)S(6)} %select_n.180), kind=kLoop, calls=%fused_computation.96 | loop fusion | bytes 262152 | tf_op jit(solution)/shard_map/dynamic_slice | solution.py:189
  6.7 0.1 collective-permute-start.2
  6.7 0.2 reshape.47
  6.9 1.0 %fusion.33 = (f32[256,256]{1,0:T(8,128)S(1)}, f32[256,256]{1,0:T(8,128)S(1)}) fusion(), kind=kLoop, calls=%fused_computation.78 | loop fusion | flops 983040 | bytes 524288 | tf_op jit(solution)/shard_map/cos | solution.py:31
  8.0 1.0 %fusion.30 = (f32[256,256]{1,0:T(8,128)S(1)}, f32[256,256]{1,0:T(8,128)S(1)}) fusion(), kind=kLoop, calls=%fused_computation.75 | loop fusion | flops 917504 | bytes 524288 | tf_op jit(solution)/shard_map/sin | solution.py:31
  9.0 0.0 copy-start
  9.0 0.0 copy-start.1
  9.0 0.5 fusion.40
  9.6 0.5 fusion.42
  10.1 1.0 %fusion.32 = f32[256,256]{1,0:T(8,128)S(1)} fusion(), kind=kLoop, calls=%fused_computation.77 | loop fusion | flops 917504 | bytes 262144 | tf_op jit(solution)/shard_map/sin | solution.py:31
  11.1 0.1 fusion.8
  11.2 0.9 %pad_maximum_fusion.9.second_ref = bf16[1536,256]{1,0:T(8,128)(2,1)} fusion(bf16[512,256]{1,0:T(8,128)(2,1)S(1)} %get-tuple-element.16, bf16[512,256]{1,0:T(8,128)(2,1)S(1)} %get-tuple-element.15), kind=kLoop, calls=%fused_computation.18 | loop fusion | flops 2359296 | bytes 1310720 | tf_op jit(solution)/shard_map/concatenate | solution.py:93
  12.1 0.1 reduce-precision_convert_fusion.1
  12.2 0.0 collective-permute-done.2
  12.2 2.4 %collective-permute-start.3 = (bf16[2,1,8,2,2048]{4,2,3,0,1:T(8,128)(2,1)S(1)}, bf16[2,1,8,2,2048]{4,2,3,0,1:T(8,128)(2,1)S(1)}, u32[]{:S(2)}, u32[]{:S(2)}) collective-permute-start(bf16[2,1,8,2,2048]{4,2,3,0,1:T(8,128)(2,1)S(1)} %pad_maximum_fusion.14), channel_id=1, source_target_pairs={{0,8},{1,9},{2,10},{3,11},{4,12},{5,13},{6,14},{7,15},{8,0},{9,1},... | collective-permute-start | bytes 393224 | tf_op jit(solution)/shard_map/ppermute | solution.py:202
  14.6 1.0 %pad_maximum_fusion.8.first_ref = bf16[512,768]{1,0:T(8,128)(2,1)} fusion(bf16[512,256]{1,0:T(8,128)(2,1)S(1)} %get-tuple-element.20, bf16[512,256]{1,0:T(8,128)(2,1)S(1)} %get-tuple-element.19), kind=kLoop, calls=%fused_computation.17 | loop fusion | flops 2359296 | bytes 1310720 | tf_op jit(solution)/shard_map/concatenate | solution.py:92
  15.6 5.0 %collective-permute-done.3 = bf16[2,1,8,2,2048]{4,2,3,0,1:T(8,128)(2,1)S(1)} collective-permute-done((bf16[2,1,8,2,2048]{4,2,3,0,1:T(8,128)(2,1)S(1)}, bf16[2,1,8,2,2048]{4,2,3,0,1:T(8,128)(2,1)S(1)}, u32[]{:S(2)}, u32[]{:S(2)}) %collective-permute-start.3) | collective-permute-done | bytes 131104 | tf_op jit(solution)/shard_map/ppermute | solution.py:202
  20.7 1.3 %collective-permute-start.4 = (bf16[2,2,1,8,2,2048]{5,3,4,1,0,2:T(8,128)(2,1)S(1)}, bf16[2,2,1,8,2,2048]{5,3,4,1,0,2:T(8,128)(2,1)S(1)}, u32[]{:S(2)}, u32[]{:S(2)}) collective-permute-start(bf16[2,2,1,8,2,2048]{5,3,4,1,0,2:T(8,128)(2,1)S(1)} %pad_maximum_fusion.13), channel_id=1, source_target_pairs={{0,2},{1,5},{2,0},{3,7},{4,6},{5,1},{6,4},{7,3},{8,10},{9,13},{10,... | collective-permute-start | bytes 786440 | tf_op jit(solution)/shard_map/ppermute | solution.py:202
  22.0 0.0 collective-permute-done
  22.0 0.2 pad_maximum_fusion.11
  22.2 1.7 %collective-permute-start.1 = (f32[3,32768]{1,0:T(4,128)S(1)}, f32[3,32768]{1,0:T(4,128)S(1)}, u32[]{:S(2)}, u32[]{:S(2)}) collective-permute-start(f32[3,32768]{1,0:T(4,128)S(1)} %pad_maximum_fusion.11), channel_id=1, source_target_pairs={{0,1},{1,0},{2,3},{3,2},{4,5},{5,4},{6,7},{7,6},{8,9},{9,8},{10,11... | collective-permute-start | bytes 1179656 | tf_op jit(solution)/shard_map/ppermute | solution.py:226
  23.9 2.3 %collective-permute-done.4 = bf16[2,2,1,8,2,2048]{5,3,4,1,0,2:T(8,128)(2,1)S(1)} collective-permute-done((bf16[2,2,1,8,2,2048]{5,3,4,1,0,2:T(8,128)(2,1)S(1)}, bf16[2,2,1,8,2,2048]{5,3,4,1,0,2:T(8,128)(2,1)S(1)}, u32[]{:S(2)}, u32[]{:S(2)}) %collective-permute-start.4) | collective-permute-done | bytes 262176 | tf_op jit(solution)/shard_map/ppermute | solution.py:202
  26.3 0.1 pad_maximum_fusion.12
  26.3 1.3 %collective-permute-start.5 = (bf16[2,2,2,1,8,2,2048]{6,4,5,3,2,1,0:T(8,128)(2,1)S(1)}, bf16[2,2,2,1,8,2,2048]{6,4,5,3,2,1,0:T(8,128)(2,1)S(1)}, u32[]{:S(2)}, u32[]{:S(2)}) collective-permute-start(bf16[2,2,2,1,8,2,2048]{6,4,5,3,2,1,0:T(8,128)(2,1)S(1)} %pad_maximum_fusion.12), channel_id=1, source_target_pairs={{0,4},{1,3},{2,6},{3,1},{4,0},{5,7},{6,2},{7,5},{8,12},{9,11},{10,... | collective-permute-start | bytes 1572872 | tf_op jit(solution)/shard_map/ppermute | solution.py:202
  27.6 0.0 collective-permute-done.1
  27.6 0.1 slice.50
  27.8 0.5 maximum_select_fusion
  28.3 0.2 fusion.56
  28.5 0.2 pad_maximum_fusion.7
  28.7 1.1 %fusion.4 = f32[4,256,512]{2,1,0:T(8,128)S(1)} fusion(f32[1,4,256,256]{3,1,2,0:T(4,128)S(1)} %bitcast.60, f32[256,256]{1,0:T(8,128)S(1)} %get-tuple-element.28, f32[256,256]{1,0:T(8,128)S(1)} %get-tuple-element.27), kind=kOutput, calls=%fused_computation.9 | convolution fusion | flops 805437440 | bytes 3670016 | tf_op jit(solution)/shard_map/bnm,nf->bmf/dot_general | solution.py:41
  29.8 0.0 copy-done
  29.8 0.0 copy-done.1
  29.8 0.3 multiply_add_fusion
  30.1 1.3 %fusion.3 = f32[4,128,512]{2,1,0:T(8,128)S(1)} fusion(f32[4,256,256]{2,1,0:T(8,128)S(1)} %get-tuple-element.6, f32[4,256,256]{2,1,0:T(8,128)S(1)} %get-tuple-element.5), kind=kOutput, calls=%fused_computation.4 | convolution fusion | flops 403636224 | bytes 3145728 | tf_op jit(solution)/shard_map/bnf,nk->bkf/dot_general | solution.py:54
  31.4 1.3 %fusion.2 = f32[4,128,512]{2,1,0:T(8,128)S(1)} fusion(f32[4,256,256]{2,1,0:T(8,128)S(1)} %get-tuple-element.6, f32[4,256,256]{2,1,0:T(8,128)S(1)} %get-tuple-element.5), kind=kOutput, calls=%fused_computation.3 | convolution fusion | flops 403636224 | bytes 3145728 | tf_op jit(solution)/shard_map/bnf,nk->bkf/dot_general | solution.py:53
  32.7 0.1 slice_subtract_fusion
  32.9 1.1 %fusion.10 = (f32[2,128,512]{2,1,0:T(8,128)}, f32[2,128,512]{2,1,0:T(8,128)}) fusion(s32[]{:T(128)S(6)} %select_n.172, f32[4,128,256]{2,1,0:T(8,128)S(1)} %get-tuple-element.8, f32[4,128,256]{2,1,0:T(8,128)S(1)} %get-tuple-element.7, s32[]{:T(128)S(6)} %select_n.191), kind=kLoop, calls=%fused_computation.26 | loop fusion | flops 262144 | bytes 2097160 | tf_op jit(solution)/shard_map/concatenate | solution.py:55
  34.0 0.7 %collective-permute-done.5 = bf16[2,2,2,1,8,2,2048]{6,4,5,3,2,1,0:T(8,128)(2,1)S(1)} collective-permute-done((bf16[2,2,2,1,8,2,2048]{6,4,5,3,2,1,0:T(8,128)(2,1)S(1)}, bf16[2,2,2,1,8,2,2048]{6,4,5,3,2,1,0:T(8,128)(2,1)S(1)}, u32[]{:S(2)}, u32[]{:S(2)}) %collective-permute-start.5) | collective-permute-done | bytes 524320 | tf_op jit(solution)/shard_map/ppermute | solution.py:202
  34.7 0.1 broadcast_select_fusion
  34.8 0.1 copy_dynamic-update-slice_fusion.1
  34.9 0.1 copy_dynamic-update-slice_fusion
  35.0 1.3 %bitcast_select_fusion = bf16[8,2,2,2,2,2,8,256]{7,6,5,4,3,2,1,0:T(8,128)(2,1)} fusion(bf16[2,2,2,2,8,2,8,256]{7,6,3,0,1,2,5,4:T(8,128)(2,1)S(1)} %copy_dynamic-update-slice_fusion, pred[]{:T(512)S(6)} %eq.19), kind=kLoop, calls=%fused_computation.14 | loop fusion | flops 524288 | bytes 2097153 | tf_op jit(solution)/shard_map/jit(_where)/select_n | solution.py:213
  36.4 10.4 %shard_map.38 = f32[8,2,128]{2,1,0:T(2,128)} custom-call(f32[2,128,512]{2,1,0:T(8,128)} %get-tuple-element.10.spec_ref, bf16[8,2,128,256]{3,2,1,0:T(8,128)(2,1)} %bitcast.63, bf16[512,768]{1,0:T(8,128)(2,1)} %pad_maximum_fusion.8.first_ref, f32[256,256]{1,0:T(8,128)} %copy-done.1, f32[256,256]{1,0:T(8,128)} %copy-done, ...), custom_call_target="tpu_custom_call" | custom-call | flops 6442450944 | bytes 1581056 | tf_op jit(solution)/shard_map/pallas_call | solution.py:161
  46.8 3.0 %collective-permute-start.6 = (f32[8,2,128]{2,1,0:T(2,128)}, f32[8,2,128]{2,1,0:T(2,128)S(1)}, u32[]{:S(2)}, u32[]{:S(2)}) collective-permute-start(f32[8,2,128]{2,1,0:T(2,128)} %shard_map.38), channel_id=1, source_target_pairs={{0,1},{1,0},{2,3},{3,2},{4,5},{5,4},{6,7},{7,6},{8,9},{9,8},{10,11... | collective-permute-start | bytes 24584 | tf_op jit(solution)/shard_map/ppermute | solution.py:239
  49.8 10.4 %shard_map.37 = f32[8,2,128]{2,1,0:T(2,128)} custom-call(f32[2,128,512]{2,1,0:T(8,128)} %get-tuple-element.9.spec_ref, bf16[8,2,128,256]{3,2,1,0:T(8,128)(2,1)} %bitcast.64, bf16[512,768]{1,0:T(8,128)(2,1)} %pad_maximum_fusion.8.first_ref, f32[256,256]{1,0:T(8,128)} %copy-done.1, f32[256,256]{1,0:T(8,128)} %copy-done, ...), custom_call_target="tpu_custom_call" | custom-call | flops 6442450944 | bytes 1581056 | tf_op jit(solution)/shard_map/pallas_call | solution.py:161
  60.2 0.7 %copy.46 = f32[1,8,2,128]{3,1,2,0:T(8,128)S(1)} copy(f32[1,8,2,128]{3,2,1,0:T(2,128)} %bitcast.71) | data formatting | bytes 16384
  60.9 0.0 collective-permute-done.6
  60.9 0.6 maximum_select_fusion.1
  (8 shorter events, 0.2 us)
Async XLA Ops:
  1.1 20.9 %collective-permute-start = (f32[32768]{0:T(1024)S(1)}, f32[32768]{0:T(1024)S(1)}, u32[]{:S(2)}, u32[]{:S(2)}) collective-permute-start(f32[32768]{0:T(1024)S(1)} %slice.49), channel_id=1, source_target_pairs={{0,1},{1,2},{2,3},{3,4},{4,5},{5,6},{6,7},{7,8},{8,9},{9,10},{10,1... | collective-permute-start | bytes 393224 | tf_op jit(solution)/shard_map/ppermute | solution.py:23
  6.7 5.5 %collective-permute-start.2 = (bf16[1,8,2,2048]{3,1,2,0:T(8,128)(2,1)S(1)}, bf16[1,8,2,2048]{3,1,2,0:T(8,128)(2,1)S(1)}, u32[]{:S(2)}, u32[]{:S(2)}) collective-permute-start(bf16[1,8,2,2048]{3,1,2,0:T(8,128)(2,1)S(1)} %bitcast.67), channel_id=1, source_target_pairs={{0,1},{1,0},{2,3},{3,2},{4,5},{5,4},{6,7},{7,6},{8,9},{9,8},{10,11... | collective-permute-start | bytes 196616 | tf_op jit(solution)/shard_map/ppermute | solution.py:191
  9.0 20.8 %copy-start = (f32[256,256]{1,0:T(8,128)}, f32[256,256]{1,0:T(8,128)S(1)}, u32[]{:S(2)}) copy-start(f32[256,256]{1,0:T(8,128)S(1)} %get-tuple-element.29.ts_ref) | copy-start | bytes 786436
  9.0 20.8 %copy-start.1 = (f32[256,256]{1,0:T(8,128)}, f32[256,256]{1,0:T(8,128)S(1)}, u32[]{:S(2)}) copy-start(f32[256,256]{1,0:T(8,128)S(1)} %get-tuple-element.30.tc_ref) | copy-start | bytes 786436
  12.2 8.3 %collective-permute-start.3 = (bf16[2,1,8,2,2048]{4,2,3,0,1:T(8,128)(2,1)S(1)}, bf16[2,1,8,2,2048]{4,2,3,0,1:T(8,128)(2,1)S(1)}, u32[]{:S(2)}, u32[]{:S(2)}) collective-permute-start(bf16[2,1,8,2,2048]{4,2,3,0,1:T(8,128)(2,1)S(1)} %pad_maximum_fusion.14), channel_id=1, source_target_pairs={{0,8},{1,9},{2,10},{3,11},{4,12},{5,13},{6,14},{7,15},{8,0},{9,1},... | collective-permute-start | bytes 393224 | tf_op jit(solution)/shard_map/ppermute | solution.py:202
  20.7 5.6 %collective-permute-start.4 = (bf16[2,2,1,8,2,2048]{5,3,4,1,0,2:T(8,128)(2,1)S(1)}, bf16[2,2,1,8,2,2048]{5,3,4,1,0,2:T(8,128)(2,1)S(1)}, u32[]{:S(2)}, u32[]{:S(2)}) collective-permute-start(bf16[2,2,1,8,2,2048]{5,3,4,1,0,2:T(8,128)(2,1)S(1)} %pad_maximum_fusion.13), channel_id=1, source_target_pairs={{0,2},{1,5},{2,0},{3,7},{4,6},{5,1},{6,4},{7,3},{8,10},{9,13},{10,... | collective-permute-start | bytes 786440 | tf_op jit(solution)/shard_map/ppermute | solution.py:202
  22.2 5.4 %collective-permute-start.1 = (f32[3,32768]{1,0:T(4,128)S(1)}, f32[3,32768]{1,0:T(4,128)S(1)}, u32[]{:S(2)}, u32[]{:S(2)}) collective-permute-start(f32[3,32768]{1,0:T(4,128)S(1)} %pad_maximum_fusion.11), channel_id=1, source_target_pairs={{0,1},{1,0},{2,3},{3,2},{4,5},{5,4},{6,7},{7,6},{8,9},{9,8},{10,11... | collective-permute-start | bytes 1179656 | tf_op jit(solution)/shard_map/ppermute | solution.py:226
  26.3 8.4 %collective-permute-start.5 = (bf16[2,2,2,1,8,2,2048]{6,4,5,3,2,1,0:T(8,128)(2,1)S(1)}, bf16[2,2,2,1,8,2,2048]{6,4,5,3,2,1,0:T(8,128)(2,1)S(1)}, u32[]{:S(2)}, u32[]{:S(2)}) collective-permute-start(bf16[2,2,2,1,8,2,2048]{6,4,5,3,2,1,0:T(8,128)(2,1)S(1)} %pad_maximum_fusion.12), channel_id=1, source_target_pairs={{0,4},{1,3},{2,6},{3,1},{4,0},{5,7},{6,2},{7,5},{8,12},{9,11},{10,... | collective-permute-start | bytes 1572872 | tf_op jit(solution)/shard_map/ppermute | solution.py:202
  46.8 14.1 %collective-permute-start.6 = (f32[8,2,128]{2,1,0:T(2,128)}, f32[8,2,128]{2,1,0:T(2,128)S(1)}, u32[]{:S(2)}, u32[]{:S(2)}) collective-permute-start(f32[8,2,128]{2,1,0:T(2,128)} %shard_map.38), channel_id=1, source_target_pairs={{0,1},{1,0},{2,3},{3,2},{4,5},{5,4},{6,7},{7,6},{8,9},{9,8},{10,11... | collective-permute-start | bytes 24584 | tf_op jit(solution)/shard_map/ppermute | solution.py:239

commit v19 on v17

--- a/solution.py
+++ b/solution.py
@@ -187,6 +187,7 @@
     mine = lax.dynamic_slice_in_dim(template_bank, core * half, half, axis=0)
     theirs = lax.dynamic_slice_in_dim(template_bank, (1 - core) * half, half, axis=0)
     arrived = lax.ppermute(theirs[None], "seg", [(i, i ^ 1) for i in range(seg_total)])
+    first_arrived = arrived
     upper = core != 0
     held = jnp.stack([jnp.where(upper, arrived, mine[None]), jnp.where(upper, mine[None], arrived)], axis=0)
     odd_order = []
@@ -209,17 +210,18 @@
         return jnp.transpose(held, (steps, steps + 1) + bit_axes + (steps + 2, steps + 3))
 
     held = jnp.where(core == 0, in_bin_order(even_order), in_bin_order(odd_order))
-    return held.reshape(half, parts, seg_total * local_bins // RADIX, RADIX)
+    return held.reshape(half, parts, seg_total * local_bins // RADIX, RADIX), first_arrived
 
 
 def local(strain, gate_mask, template_bank):
     seg_total = lax.axis_size("seg")
     core = lax.axis_index("seg") % 2
-    bank = gathered_half(template_bank)
+    bank, first_arrived = gathered_half(template_bank)
     gated = strain * gate_mask.astype(jnp.float32)
     local_blocks = gated.reshape(-1, BLOCK)
     block_total = local_blocks.shape[0]
-    earlier = passed_along(local_blocks[block_total - 1], "seg", 1)
+    last_block, _ = lax.optimization_barrier((local_blocks[block_total - 1], first_arrived))
+    earlier = passed_along(last_block, "seg", 1)
     mine = jnp.concatenate([earlier[None], local_blocks], axis=0)
     other = lax.ppermute(mine, "seg", [(i, i ^ 1) for i in range(seg_total)])
     chip_blocks = jnp.where(

time: 60.1 us -> 57 us (0.948)
  waiting for transfers between devices: 6.99 us -> 5.01 us
  starting transfers between devices: 14.3 us -> 13.2 us
    ppermute x3, waiting for transfers between devices: 6.98 us -> 5 us  [gathered_half(): arrived = lax.ppermute(held, 'seg', pairs)]
    ppermute x1, starting transfers between devices: 4.54 us -> 3.5 us  [passed_along(): return lax.ppermute(value, axis, pairs)]
    ppermute x1, starting transfers between devices: 3.04 us -> 2.3 us  [local(): lax.ppermute(partner_peaks, 'seg', [(i, i ^ 1) for i in range(seg_total)])]
    ppermute x3, starting transfers between devices: 4.99 us -> 5.63 us  [gathered_half(): arrived = lax.ppermute(held, 'seg', pairs)]
  transfers between devices with their start and end apart: 7 -> 7, of which waited for: 3 -> 3; matrix products, arithmetic and copies ran while one was open for 24% -> 25% of each run, Pallas kernels for 17% -> 18%
where the time goes in v19:
time: 57 us; the launch traced here: 56.7 us
  Pallas kernels  20.5 us (36%)
  starting transfers between devices  13.2 us (23%)
  other arithmetic  11.6 us (20%)
  waiting for transfers between devices  5.01 us (9%)
  matrix products  3.71 us (7%)
  local copies, waits for them, and re-layouts  2.43 us (4%)
    pallas_call x2, Pallas kernels, window_peaks(): pl.pallas_call(peaks_kernel, out_shape=jax.ShapeDtypeStruct((template_tot...  20.5 us
    ppermute x3, starting transfers between devices, gathered_half(): arrived = lax.ppermute(held, 'seg', pairs)  5.63 us
    ppermute x3, waiting for transfers between devices, gathered_half(): arrived = lax.ppermute(held, 'seg', pairs)  5 us
    ppermute x1, starting transfers between devices, passed_along(): return lax.ppermute(value, axis, pairs)  3.5 us
    sin x3, other arithmetic, angle_table(): return (jnp.cos(angle_value), jnp.sin(angle_value))  2.54 us
    ppermute x1, starting transfers between devices, local(): lax.ppermute(partner_peaks, 'seg', [(i, i ^ 1) for i in range(seg_total)])  2.3 us
    convert_element_type x2, other arithmetic, table_pair(): return (high.astype(jnp.bfloat16), (value - high).astype(jnp.bfloat16))  1.72 us
    ppermute x1, starting transfers between devices, local(): other = lax.ppermute(mine, 'seg', [(i, i ^ 1) for i in range(seg_total)])  1.63 us
  transfers between devices with their start and end apart: 7, of which 3 were waited for; matrix products, arithmetic and copies ran while one was open for 25% of the time, Pallas kernels for 18%

profile of v19, /device:TPU:1, one launch (start us, length us, event | category | flops | bytes accessed | tf_op | source)
XLA Modules:
  0.0 56.7 jit_solution(742137434692364008)
XLA Ops:
  0.0 1.0 %constant_dynamic-slice_fusion = (bf16[8,2,2048]{2,1,0:T(2,128)(2,1)S(1)}, bf16[8,2,2048]{2,1,0:T(2,128)(2,1)S(1)}) fusion(bf16[16,2,2048]{2,1,0:T(2,128)(2,1)} %param.5, s32[]{:T(128)S(6)} %select_n.181, s32[]{:T(128)S(6)} %select_n.169), kind=kLoop, calls=%fused_computation.94 | loop fusion | bytes 262152 | tf_op jit(solution)/shard_map/dynamic_slice | solution.py:187
  1.0 0.1 collective-permute-start
  1.1 1.0 %fusion.33 = (f32[256,256]{1,0:T(8,128)S(1)}, f32[256,256]{1,0:T(8,128)S(1)}) fusion(), kind=kLoop, calls=%fused_computation.76 | loop fusion | flops 983040 | bytes 524288 | tf_op jit(solution)/shard_map/cos | solution.py:31
  2.2 1.0 %fusion.30 = (f32[256,256]{1,0:T(8,128)S(1)}, f32[256,256]{1,0:T(8,128)S(1)}) fusion(), kind=kLoop, calls=%fused_computation.73 | loop fusion | flops 917504 | bytes 524288 | tf_op jit(solution)/shard_map/sin | solution.py:31
  3.2 0.0 copy-start
  3.2 0.0 copy-start.1
  3.2 0.5 fusion.40
  3.8 0.5 fusion.42
  4.3 1.1 %convert_multiply_fusion = f32[65536]{0:T(1024)S(1)} fusion(f32[65536]{0:T(1024)} %param.3, s32[65536]{0:T(1024)} %param.4), kind=kLoop, calls=%fused_computation.59 | loop fusion | flops 131072 | bytes 786432 | tf_op jit(solution)/shard_map/mul | solution.py:220
  5.3 0.9 %fusion.7 = (bf16[512,256]{1,0:T(8,128)(2,1)}, bf16[512,256]{1,0:T(8,128)(2,1)}) fusion(f32[256,128]{1,0:T(8,128)S(1)} %get-tuple-element.34, f32[256,128]{1,0:T(8,128)S(1)} %get-tuple-element.33, f32[256,128]{1,0:T(8,128)S(1)} %fusion.42), kind=kLoop, calls=%fused_computation.21 | loop fusion | flops 917504 | bytes 917504 | tf_op jit(solution)/shard_map/convert_element_type | solution.py:72
  6.2 0.0 collective-permute-done
  6.3 3.8 %collective-permute-start.3 = (bf16[2,1,8,2,2048]{4,2,3,0,1:T(8,128)(2,1)S(1)}, bf16[2,1,8,2,2048]{4,2,3,0,1:T(8,128)(2,1)S(1)}, u32[]{:S(2)}, u32[]{:S(2)}) collective-permute-start(bf16[2,1,8,2,2048]{4,2,3,0,1:T(8,128)(2,1)S(1)} %pad_maximum_fusion.12), channel_id=1, source_target_pairs={{0,8},{1,9},{2,10},{3,11},{4,12},{5,13},{6,14},{7,15},{8,0},{9,1},... | collective-permute-start | bytes 393224 | tf_op jit(solution)/shard_map/ppermute | solution.py:201
  10.1 1.0 %fusion.32 = f32[256,256]{1,0:T(8,128)S(1)} fusion(), kind=kLoop, calls=%fused_computation.75 | loop fusion | flops 917504 | bytes 262144 | tf_op jit(solution)/shard_map/sin | solution.py:31
  11.0 0.2 reshape.47
  11.3 0.9 %fusion.8 = (bf16[512,256]{1,0:T(8,128)(2,1)}, bf16[512,256]{1,0:T(8,128)(2,1)}) fusion(f32[256,256]{1,0:T(8,128)S(1)} %get-tuple-element.29, f32[256,256]{1,0:T(8,128)S(1)} %fusion.32, f32[256,256]{1,0:T(8,128)S(1)} %get-tuple-element.30), kind=kLoop, calls=%fused_computation.22 | loop fusion | flops 1310720 | bytes 1310720 | tf_op jit(solution)/shard_map/convert_element_type | solution.py:72
  12.1 3.5 %collective-permute-start.1 = (f32[32768]{0:T(1024)S(1)}, f32[32768]{0:T(1024)S(1)}, u32[]{:S(2)}, u32[]{:S(2)}) collective-permute-start(f32[32768]{0:T(1024)S(1)} %slice.49), channel_id=1, source_target_pairs={{0,1},{1,2},{2,3},{3,4},{4,5},{5,6},{6,7},{7,8},{8,9},{9,10},{10,1... | collective-permute-start | bytes 393224 | tf_op jit(solution)/shard_map/ppermute | solution.py:23
  15.6 1.1 %collective-permute-done.3 = bf16[2,1,8,2,2048]{4,2,3,0,1:T(8,128)(2,1)S(1)} collective-permute-done((bf16[2,1,8,2,2048]{4,2,3,0,1:T(8,128)(2,1)S(1)}, bf16[2,1,8,2,2048]{4,2,3,0,1:T(8,128)(2,1)S(1)}, u32[]{:S(2)}, u32[]{:S(2)}) %collective-permute-start.3) | collective-permute-done | bytes 131104 | tf_op jit(solution)/shard_map/ppermute | solution.py:201
  16.8 0.7 %collective-permute-start.4 = (bf16[2,2,1,8,2,2048]{5,3,4,1,0,2:T(8,128)(2,1)S(1)}, bf16[2,2,1,8,2,2048]{5,3,4,1,0,2:T(8,128)(2,1)S(1)}, u32[]{:S(2)}, u32[]{:S(2)}) collective-permute-start(bf16[2,2,1,8,2,2048]{5,3,4,1,0,2:T(8,128)(2,1)S(1)} %pad_maximum_fusion.11), channel_id=1, source_target_pairs={{0,2},{1,5},{2,0},{3,7},{4,6},{5,1},{6,4},{7,3},{8,10},{9,13},{10,... | collective-permute-start | bytes 786440 | tf_op jit(solution)/shard_map/ppermute | solution.py:201
  17.5 0.0 collective-permute-done.1
  17.5 0.2 pad_maximum_fusion.9
  17.7 1.6 %collective-permute-start.2 = (f32[3,32768]{1,0:T(4,128)S(1)}, f32[3,32768]{1,0:T(4,128)S(1)}, u32[]{:S(2)}, u32[]{:S(2)}) collective-permute-start(f32[3,32768]{1,0:T(4,128)S(1)} %pad_maximum_fusion.9), channel_id=1, source_target_pairs={{0,1},{1,0},{2,3},{3,2},{4,5},{5,4},{6,7},{7,6},{8,9},{9,8},{10,11... | collective-permute-start | bytes 1179656 | tf_op jit(solution)/shard_map/ppermute | solution.py:226
  19.3 3.0 %collective-permute-done.4 = bf16[2,2,1,8,2,2048]{5,3,4,1,0,2:T(8,128)(2,1)S(1)} collective-permute-done((bf16[2,2,1,8,2,2048]{5,3,4,1,0,2:T(8,128)(2,1)S(1)}, bf16[2,2,1,8,2,2048]{5,3,4,1,0,2:T(8,128)(2,1)S(1)}, u32[]{:S(2)}, u32[]{:S(2)}) %collective-permute-start.4) | collective-permute-done | bytes 262176 | tf_op jit(solution)/shard_map/ppermute | solution.py:201
  22.4 0.1 pad_maximum_fusion.10
  22.5 1.2 %collective-permute-start.5 = (bf16[2,2,2,1,8,2,2048]{6,4,5,3,2,1,0:T(8,128)(2,1)S(1)}, bf16[2,2,2,1,8,2,2048]{6,4,5,3,2,1,0:T(8,128)(2,1)S(1)}, u32[]{:S(2)}, u32[]{:S(2)}) collective-permute-start(bf16[2,2,2,1,8,2,2048]{6,4,5,3,2,1,0:T(8,128)(2,1)S(1)} %pad_maximum_fusion.10), channel_id=1, source_target_pairs={{0,4},{1,3},{2,6},{3,1},{4,0},{5,7},{6,2},{7,5},{8,12},{9,11},{10,... | collective-permute-start | bytes 1572872 | tf_op jit(solution)/shard_map/ppermute | solution.py:201
  23.6 0.0 collective-permute-done.2
  23.6 0.1 slice.50
  23.8 0.5 maximum_select_fusion
  24.3 0.2 fusion.56
  24.5 0.2 pad_maximum_fusion.7
  24.7 1.1 %fusion.4 = f32[4,256,512]{2,1,0:T(8,128)S(1)} fusion(f32[1,4,256,256]{3,1,2,0:T(4,128)S(1)} %bitcast.60, f32[256,256]{1,0:T(8,128)S(1)} %get-tuple-element.30, f32[256,256]{1,0:T(8,128)S(1)} %get-tuple-element.29), kind=kOutput, calls=%fused_computation.9 | convolution fusion | flops 805437440 | bytes 3670016 | tf_op jit(solution)/shard_map/bnm,nf->bmf/dot_general | solution.py:41
  25.8 0.0 copy-done
  25.8 0.0 copy-done.1
  25.8 0.3 multiply_add_fusion
  26.1 1.3 %fusion.3 = f32[4,128,512]{2,1,0:T(8,128)S(1)} fusion(f32[4,256,256]{2,1,0:T(8,128)S(1)} %get-tuple-element.8, f32[4,256,256]{2,1,0:T(8,128)S(1)} %get-tuple-element.7), kind=kOutput, calls=%fused_computation.4 | convolution fusion | flops 403636224 | bytes 3145728 | tf_op jit(solution)/shard_map/bnf,nk->bkf/dot_general | solution.py:54
  27.4 1.3 %fusion.2 = f32[4,128,512]{2,1,0:T(8,128)S(1)} fusion(f32[4,256,256]{2,1,0:T(8,128)S(1)} %get-tuple-element.8, f32[4,256,256]{2,1,0:T(8,128)S(1)} %get-tuple-element.7), kind=kOutput, calls=%fused_computation.3 | convolution fusion | flops 403636224 | bytes 3145728 | tf_op jit(solution)/shard_map/bnf,nk->bkf/dot_general | solution.py:53
  28.7 0.1 slice_subtract_fusion
  28.9 1.1 %fusion.10 = (f32[2,128,512]{2,1,0:T(8,128)}, f32[2,128,512]{2,1,0:T(8,128)}) fusion(s32[]{:T(128)S(6)} %select_n.173, f32[4,128,256]{2,1,0:T(8,128)S(1)} %get-tuple-element.10, f32[4,128,256]{2,1,0:T(8,128)S(1)} %get-tuple-element.9, s32[]{:T(128)S(6)} %select_n.191), kind=kLoop, calls=%fused_computation.24 | loop fusion | flops 262144 | bytes 2097160 | tf_op jit(solution)/shard_map/concatenate | solution.py:55
  30.0 0.9 %collective-permute-done.5 = bf16[2,2,2,1,8,2,2048]{6,4,5,3,2,1,0:T(8,128)(2,1)S(1)} collective-permute-done((bf16[2,2,2,1,8,2,2048]{6,4,5,3,2,1,0:T(8,128)(2,1)S(1)}, bf16[2,2,2,1,8,2,2048]{6,4,5,3,2,1,0:T(8,128)(2,1)S(1)}, u32[]{:S(2)}, u32[]{:S(2)}) %collective-permute-start.5) | collective-permute-done | bytes 524320 | tf_op jit(solution)/shard_map/ppermute | solution.py:201
  30.9 0.1 broadcast_select_fusion
  31.0 0.1 copy_dynamic-update-slice_fusion.1
  31.1 0.1 copy_dynamic-update-slice_fusion
  31.2 1.3 %bitcast_select_fusion = bf16[8,2,2,2,2,2,8,256]{7,6,5,4,3,2,1,0:T(8,128)(2,1)} fusion(bf16[2,2,2,2,8,2,8,256]{7,6,3,0,1,2,5,4:T(8,128)(2,1)S(1)} %copy_dynamic-update-slice_fusion, pred[]{:T(512)S(6)} %eq.19), kind=kLoop, calls=%fused_computation.14 | loop fusion | flops 524288 | bytes 2097153 | tf_op jit(solution)/shard_map/jit(_where)/select_n | solution.py:212
  32.5 10.3 %shard_map.38 = f32[8,2,128]{2,1,0:T(2,128)} custom-call(f32[2,128,512]{2,1,0:T(8,128)} %get-tuple-element.12.spec_ref, bf16[8,2,128,256]{3,2,1,0:T(8,128)(2,1)} %bitcast.63, bf16[512,256]{1,0:T(8,128)(2,1)} %get-tuple-element.22.fh_ref, bf16[512,256]{1,0:T(8,128)(2,1)} %get-tuple-element.21.fl_ref, f32[256,256]{1,0:T(8,128)} %copy-done.1, ...), custom_call_target="tpu_custom_call" | custom-call | flops 6442450944 | bytes 1581056 | tf_op jit(solution)/shard_map/pallas_call | solution.py:157
  42.8 2.3 %collective-permute-start.6 = (f32[8,2,128]{2,1,0:T(2,128)}, f32[8,2,128]{2,1,0:T(2,128)S(1)}, u32[]{:S(2)}, u32[]{:S(2)}) collective-permute-start(f32[8,2,128]{2,1,0:T(2,128)} %shard_map.38), channel_id=1, source_target_pairs={{0,1},{1,0},{2,3},{3,2},{4,5},{5,4},{6,7},{7,6},{8,9},{9,8},{10,11... | collective-permute-start | bytes 24584 | tf_op jit(solution)/shard_map/ppermute | solution.py:239
  45.1 10.3 %shard_map.37 = f32[8,2,128]{2,1,0:T(2,128)} custom-call(f32[2,128,512]{2,1,0:T(8,128)} %get-tuple-element.11.spec_ref, bf16[8,2,128,256]{3,2,1,0:T(8,128)(2,1)} %bitcast.64, bf16[512,256]{1,0:T(8,128)(2,1)} %get-tuple-element.22.fh_ref, bf16[512,256]{1,0:T(8,128)(2,1)} %get-tuple-element.21.fl_ref, f32[256,256]{1,0:T(8,128)} %copy-done.1, ...), custom_call_target="tpu_custom_call" | custom-call | flops 6442450944 | bytes 1581056 | tf_op jit(solution)/shard_map/pallas_call | solution.py:157
  55.4 0.7 %copy.46 = f32[1,8,2,128]{3,1,2,0:T(8,128)S(1)} copy(f32[1,8,2,128]{3,2,1,0:T(2,128)} %bitcast.71) | data formatting | bytes 16384
  56.1 0.0 collective-permute-done.6
  56.1 0.6 %maximum_select_fusion.1 = f32[16,256]{1,0:T(8,128)} fusion(f32[8,256]{1,0:T(8,128)S(1)} %bitcast.69, f32[8,256]{1,0:T(8,128)S(1)} %bitcast.68, pred[]{:T(512)S(6)} %eq.19), kind=kLoop, calls=%fused_computation.89 | loop fusion | flops 12288 | bytes 32769 | tf_op jit(solution)/shard_map/jit(_where)/select_n | solution.py:241
  (8 shorter events, 0.2 us)
Async XLA Ops:
  1.0 5.2 %collective-permute-start = (bf16[1,8,2,2048]{3,1,2,0:T(8,128)(2,1)S(1)}, bf16[1,8,2,2048]{3,1,2,0:T(8,128)(2,1)S(1)}, u32[]{:S(2)}, u32[]{:S(2)}) collective-permute-start(bf16[1,8,2,2048]{3,1,2,0:T(8,128)(2,1)S(1)} %bitcast.67), channel_id=1, source_target_pairs={{0,1},{1,0},{2,3},{3,2},{4,5},{5,4},{6,7},{7,6},{8,9},{9,8},{10,11... | collective-permute-start | bytes 196616 | tf_op jit(solution)/shard_map/ppermute | solution.py:189
  3.2 22.6 %copy-start = (f32[256,256]{1,0:T(8,128)}, f32[256,256]{1,0:T(8,128)S(1)}, u32[]{:S(2)}) copy-start(f32[256,256]{1,0:T(8,128)S(1)} %get-tuple-element.31.ts_ref) | copy-start | bytes 786436
  3.2 22.6 %copy-start.1 = (f32[256,256]{1,0:T(8,128)}, f32[256,256]{1,0:T(8,128)S(1)}, u32[]{:S(2)}) copy-start(f32[256,256]{1,0:T(8,128)S(1)} %get-tuple-element.32.tc_ref) | copy-start | bytes 786436
  6.3 10.5 %collective-permute-start.3 = (bf16[2,1,8,2,2048]{4,2,3,0,1:T(8,128)(2,1)S(1)}, bf16[2,1,8,2,2048]{4,2,3,0,1:T(8,128)(2,1)S(1)}, u32[]{:S(2)}, u32[]{:S(2)}) collective-permute-start(bf16[2,1,8,2,2048]{4,2,3,0,1:T(8,128)(2,1)S(1)} %pad_maximum_fusion.12), channel_id=1, source_target_pairs={{0,8},{1,9},{2,10},{3,11},{4,12},{5,13},{6,14},{7,15},{8,0},{9,1},... | collective-permute-start | bytes 393224 | tf_op jit(solution)/shard_map/ppermute | solution.py:201
  12.1 5.3 %collective-permute-start.1 = (f32[32768]{0:T(1024)S(1)}, f32[32768]{0:T(1024)S(1)}, u32[]{:S(2)}, u32[]{:S(2)}) collective-permute-start(f32[32768]{0:T(1024)S(1)} %slice.49), channel_id=1, source_target_pairs={{0,1},{1,2},{2,3},{3,4},{4,5},{5,6},{6,7},{7,8},{8,9},{9,10},{10,1... | collective-permute-start | bytes 393224 | tf_op jit(solution)/shard_map/ppermute | solution.py:23
  16.8 5.6 %collective-permute-start.4 = (bf16[2,2,1,8,2,2048]{5,3,4,1,0,2:T(8,128)(2,1)S(1)}, bf16[2,2,1,8,2,2048]{5,3,4,1,0,2:T(8,128)(2,1)S(1)}, u32[]{:S(2)}, u32[]{:S(2)}) collective-permute-start(bf16[2,2,1,8,2,2048]{5,3,4,1,0,2:T(8,128)(2,1)S(1)} %pad_maximum_fusion.11), channel_id=1, source_target_pairs={{0,2},{1,5},{2,0},{3,7},{4,6},{5,1},{6,4},{7,3},{8,10},{9,13},{10,... | collective-permute-start | bytes 786440 | tf_op jit(solution)/shard_map/ppermute | solution.py:201
  17.7 5.9 %collective-permute-start.2 = (f32[3,32768]{1,0:T(4,128)S(1)}, f32[3,32768]{1,0:T(4,128)S(1)}, u32[]{:S(2)}, u32[]{:S(2)}) collective-permute-start(f32[3,32768]{1,0:T(4,128)S(1)} %pad_maximum_fusion.9), channel_id=1, source_target_pairs={{0,1},{1,0},{2,3},{3,2},{4,5},{5,4},{6,7},{7,6},{8,9},{9,8},{10,11... | collective-permute-start | bytes 1179656 | tf_op jit(solution)/shard_map/ppermute | solution.py:226
  22.5 8.4 %collective-permute-start.5 = (bf16[2,2,2,1,8,2,2048]{6,4,5,3,2,1,0:T(8,128)(2,1)S(1)}, bf16[2,2,2,1,8,2,2048]{6,4,5,3,2,1,0:T(8,128)(2,1)S(1)}, u32[]{:S(2)}, u32[]{:S(2)}) collective-permute-start(bf16[2,2,2,1,8,2,2048]{6,4,5,3,2,1,0:T(8,128)(2,1)S(1)} %pad_maximum_fusion.10), channel_id=1, source_target_pairs={{0,4},{1,3},{2,6},{3,1},{4,0},{5,7},{6,2},{7,5},{8,12},{9,11},{10,... | collective-permute-start | bytes 1572872 | tf_op jit(solution)/shard_map/ppermute | solution.py:201
  42.8 13.3 %collective-permute-start.6 = (f32[8,2,128]{2,1,0:T(2,128)}, f32[8,2,128]{2,1,0:T(2,128)S(1)}, u32[]{:S(2)}, u32[]{:S(2)}) collective-permute-start(f32[8,2,128]{2,1,0:T(2,128)} %shard_map.38), channel_id=1, source_target_pairs={{0,1},{1,0},{2,3},{3,2},{4,5},{5,4},{6,7},{7,6},{8,9},{9,8},{10,11... | collective-permute-start | bytes 24584 | tf_op jit(solution)/shard_map/ppermute | solution.py:239

commit v20 on v19

--- a/solution.py
+++ b/solution.py
@@ -199,6 +199,8 @@
     for even_distance, odd_distance in zip(even_order, odd_order):
         pairs = [(i, i ^ (even_distance if i % 2 == 0 else odd_distance)) for i in range(seg_total)]
         arrived = lax.ppermute(held, "seg", pairs)
+        if even_distance == odd_distance:
+            first_arrived = arrived
         upper = (me & jnp.where(core == 0, even_distance, odd_distance)) != 0
         held = jnp.stack([jnp.where(upper, arrived, held), jnp.where(upper, held, arrived)], axis=0)
     steps = len(odd_order) + 1

time: 57 us -> 59.6 us (1.046)
  waiting for transfers between devices: 5.01 us -> 10.4 us
  starting transfers between devices: 13.2 us -> 10 us
    ppermute x3, waiting for transfers between devices: 5 us -> 8.73 us  [gathered_half(): arrived = lax.ppermute(held, 'seg', pairs)]
    ppermute x1, waiting for transfers between devices: 0.01 us -> 1.65 us  [passed_along(): return lax.ppermute(value, axis, pairs)]
    ppermute x1, starting transfers between devices: 1.63 us -> 0.07 us  [local(): other = lax.ppermute(mine, 'seg', [(i, i ^ 1) for i in range(seg_total)])]
    ppermute x1, starting transfers between devices: 2.3 us -> 0.95 us  [local(): lax.ppermute(partner_peaks, 'seg', [(i, i ^ 1) for i in range(seg_total)])]
    ppermute x3, starting transfers between devices: 5.63 us -> 5.02 us  [gathered_half(): arrived = lax.ppermute(held, 'seg', pairs)]
  transfers between devices with their start and end apart: 7 -> 7, of which waited for: 3 -> 4; matrix products, arithmetic and copies ran while one was open for 25% -> 24% of each run, Pallas kernels for 18% -> 17%
where the time goes in v20:
time: 59.6 us; the launch traced here: 58.9 us
  Pallas kernels  20.5 us (34%)
  other arithmetic  11.6 us (19%)
  waiting for transfers between devices  10.4 us (17%)
  starting transfers between devices  10 us (17%)
  matrix products  3.71 us (6%)
  local copies, waits for them, and re-layouts  2.43 us (4%)
    pallas_call x2, Pallas kernels, window_peaks(): pl.pallas_call(peaks_kernel, out_shape=jax.ShapeDtypeStruct((template_tot...  20.5 us
    ppermute x3, waiting for transfers between devices, gathered_half(): arrived = lax.ppermute(held, 'seg', pairs)  8.73 us
    ppermute x3, starting transfers between devices, gathered_half(): arrived = lax.ppermute(held, 'seg', pairs)  5.02 us
    ppermute x1, starting transfers between devices, passed_along(): return lax.ppermute(value, axis, pairs)  3.85 us
    sin x3, other arithmetic, angle_table(): return (jnp.cos(angle_value), jnp.sin(angle_value))  2.54 us
    convert_element_type x2, other arithmetic, table_pair(): return (high.astype(jnp.bfloat16), (value - high).astype(jnp.bfloat16))  1.72 us
    ppermute x1, waiting for transfers between devices, passed_along(): return lax.ppermute(value, axis, pairs)  1.65 us
    dot_general x1, matrix products, forward(): sine_part = jnp.einsum('bnf,nk->bkf', turned, sin_second, precision=PRECISE)  1.33 us
  transfers between devices with their start and end apart: 7, of which 4 were waited for; matrix products, arithmetic and copies ran while one was open for 24% of the time, Pallas kernels for 17%

profile of v20, /device:TPU:1, one launch (start us, length us, event | category | flops | bytes accessed | tf_op | source)
XLA Modules:
  0.0 58.9 jit_solution(17654441639395835162)
XLA Ops:
  0.0 1.0 %constant_dynamic-slice_fusion = (bf16[8,2,2048]{2,1,0:T(2,128)(2,1)S(1)}, bf16[8,2,2048]{2,1,0:T(2,128)(2,1)S(1)}) fusion(bf16[16,2,2048]{2,1,0:T(2,128)(2,1)} %param.5, s32[]{:T(128)S(6)} %select_n.171, s32[]{:T(128)S(6)} %select_n.170), kind=kLoop, calls=%fused_computation.94 | loop fusion | bytes 262152 | tf_op jit(solution)/shard_map/dynamic_slice | solution.py:187
  1.0 0.1 collective-permute-start
  1.1 1.0 %fusion.33 = (f32[256,256]{1,0:T(8,128)S(1)}, f32[256,256]{1,0:T(8,128)S(1)}) fusion(), kind=kLoop, calls=%fused_computation.76 | loop fusion | flops 983040 | bytes 524288 | tf_op jit(solution)/shard_map/cos | solution.py:31
  2.2 1.0 %fusion.30 = (f32[256,256]{1,0:T(8,128)S(1)}, f32[256,256]{1,0:T(8,128)S(1)}) fusion(), kind=kLoop, calls=%fused_computation.73 | loop fusion | flops 917504 | bytes 524288 | tf_op jit(solution)/shard_map/sin | solution.py:31
  3.2 0.0 copy-start
  3.2 0.0 copy-start.1
  3.2 0.5 fusion.40
  3.8 0.5 fusion.42
  4.3 1.1 %convert_multiply_fusion = f32[65536]{0:T(1024)S(1)} fusion(f32[65536]{0:T(1024)} %param.3, s32[65536]{0:T(1024)} %param.4), kind=kLoop, calls=%fused_computation.59 | loop fusion | flops 131072 | bytes 786432 | tf_op jit(solution)/shard_map/mul | solution.py:222
  5.3 0.9 %fusion.7 = (bf16[512,256]{1,0:T(8,128)(2,1)}, bf16[512,256]{1,0:T(8,128)(2,1)}) fusion(f32[256,128]{1,0:T(8,128)S(1)} %get-tuple-element.34, f32[256,128]{1,0:T(8,128)S(1)} %get-tuple-element.33, f32[256,128]{1,0:T(8,128)S(1)} %fusion.42), kind=kLoop, calls=%fused_computation.21 | loop fusion | flops 917504 | bytes 917504 | tf_op jit(solution)/shard_map/convert_element_type | solution.py:72
  6.2 0.0 collective-permute-done
  6.2 3.8 %collective-permute-start.1 = (bf16[2,1,8,2,2048]{4,2,3,0,1:T(8,128)(2,1)S(1)}, bf16[2,1,8,2,2048]{4,2,3,0,1:T(8,128)(2,1)S(1)}, u32[]{:S(2)}, u32[]{:S(2)}) collective-permute-start(bf16[2,1,8,2,2048]{4,2,3,0,1:T(8,128)(2,1)S(1)} %pad_maximum_fusion.12), channel_id=1, source_target_pairs={{0,8},{1,9},{2,10},{3,11},{4,12},{5,13},{6,14},{7,15},{8,0},{9,1},... | collective-permute-start | bytes 393224 | tf_op jit(solution)/shard_map/ppermute | solution.py:201
  10.1 1.0 %fusion.32 = f32[256,256]{1,0:T(8,128)S(1)} fusion(), kind=kLoop, calls=%fused_computation.75 | loop fusion | flops 917504 | bytes 262144 | tf_op jit(solution)/shard_map/sin | solution.py:31
  11.0 0.2 reshape.47
  11.3 0.9 %fusion.8 = (bf16[512,256]{1,0:T(8,128)(2,1)}, bf16[512,256]{1,0:T(8,128)(2,1)}) fusion(f32[256,256]{1,0:T(8,128)S(1)} %get-tuple-element.29, f32[256,256]{1,0:T(8,128)S(1)} %fusion.32, f32[256,256]{1,0:T(8,128)S(1)} %get-tuple-element.30), kind=kLoop, calls=%fused_computation.22 | loop fusion | flops 1310720 | bytes 1310720 | tf_op jit(solution)/shard_map/convert_element_type | solution.py:72
  12.1 4.6 %collective-permute-done.1 = bf16[2,1,8,2,2048]{4,2,3,0,1:T(8,128)(2,1)S(1)} collective-permute-done((bf16[2,1,8,2,2048]{4,2,3,0,1:T(8,128)(2,1)S(1)}, bf16[2,1,8,2,2048]{4,2,3,0,1:T(8,128)(2,1)S(1)}, u32[]{:S(2)}, u32[]{:S(2)}) %collective-permute-start.1) | collective-permute-done | bytes 131104 | tf_op jit(solution)/shard_map/ppermute | solution.py:201
  16.7 3.9 %collective-permute-start.2 = (f32[32768]{0:T(1024)S(1)}, f32[32768]{0:T(1024)S(1)}, u32[]{:S(2)}, u32[]{:S(2)}) collective-permute-start(f32[32768]{0:T(1024)S(1)} %slice.49), channel_id=1, source_target_pairs={{0,1},{1,2},{2,3},{3,4},{4,5},{5,6},{6,7},{7,8},{8,9},{9,10},{10,1... | collective-permute-start | bytes 393224 | tf_op jit(solution)/shard_map/ppermute | solution.py:23
  20.7 0.5 collective-permute-start.4
  21.1 1.6 %collective-permute-done.2 = f32[32768]{0:T(1024)S(1)} collective-permute-done((f32[32768]{0:T(1024)S(1)}, f32[32768]{0:T(1024)S(1)}, u32[]{:S(2)}, u32[]{:S(2)}) %collective-permute-start.2) | collective-permute-done | bytes 131104 | tf_op jit(solution)/shard_map/ppermute | solution.py:23
  22.8 0.2 pad_maximum_fusion.9
  23.0 0.1 collective-permute-start.3
  23.1 2.8 %collective-permute-done.4 = bf16[2,2,1,8,2,2048]{5,3,4,1,0,2:T(8,128)(2,1)S(1)} collective-permute-done((bf16[2,2,1,8,2,2048]{5,3,4,1,0,2:T(8,128)(2,1)S(1)}, bf16[2,2,1,8,2,2048]{5,3,4,1,0,2:T(8,128)(2,1)S(1)}, u32[]{:S(2)}, u32[]{:S(2)}) %collective-permute-start.4) | collective-permute-done | bytes 262176 | tf_op jit(solution)/shard_map/ppermute | solution.py:201
  26.0 0.1 pad_maximum_fusion.10
  26.1 0.7 %collective-permute-start.5 = (bf16[2,2,2,1,8,2,2048]{6,4,5,3,2,1,0:T(8,128)(2,1)S(1)}, bf16[2,2,2,1,8,2,2048]{6,4,5,3,2,1,0:T(8,128)(2,1)S(1)}, u32[]{:S(2)}, u32[]{:S(2)}) collective-permute-start(bf16[2,2,2,1,8,2,2048]{6,4,5,3,2,1,0:T(8,128)(2,1)S(1)} %pad_maximum_fusion.10), channel_id=1, source_target_pairs={{0,4},{1,3},{2,6},{3,1},{4,0},{5,7},{6,2},{7,5},{8,12},{9,11},{10,... | collective-permute-start | bytes 1572872 | tf_op jit(solution)/shard_map/ppermute | solution.py:201
  26.8 0.0 collective-permute-done.3
  26.8 0.1 slice.50
  26.9 0.5 maximum_select_fusion
  27.4 0.2 fusion.56
  27.6 0.2 pad_maximum_fusion.7
  27.9 1.1 %fusion.4 = f32[4,256,512]{2,1,0:T(8,128)S(1)} fusion(f32[1,4,256,256]{3,1,2,0:T(4,128)S(1)} %bitcast.60, f32[256,256]{1,0:T(8,128)S(1)} %get-tuple-element.30, f32[256,256]{1,0:T(8,128)S(1)} %get-tuple-element.29), kind=kOutput, calls=%fused_computation.9 | convolution fusion | flops 805437440 | bytes 3670016 | tf_op jit(solution)/shard_map/bnm,nf->bmf/dot_general | solution.py:41
  28.9 0.0 copy-done
  28.9 0.0 copy-done.1
  29.0 0.3 multiply_add_fusion
  29.2 1.3 %fusion.3 = f32[4,128,512]{2,1,0:T(8,128)S(1)} fusion(f32[4,256,256]{2,1,0:T(8,128)S(1)} %get-tuple-element.8, f32[4,256,256]{2,1,0:T(8,128)S(1)} %get-tuple-element.7), kind=kOutput, calls=%fused_computation.4 | convolution fusion | flops 403636224 | bytes 3145728 | tf_op jit(solution)/shard_map/bnf,nk->bkf/dot_general | solution.py:54
  30.6 1.3 %fusion.2 = f32[4,128,512]{2,1,0:T(8,128)S(1)} fusion(f32[4,256,256]{2,1,0:T(8,128)S(1)} %get-tuple-element.8, f32[4,256,256]{2,1,0:T(8,128)S(1)} %get-tuple-element.7), kind=kOutput, calls=%fused_computation.3 | convolution fusion | flops 403636224 | bytes 3145728 | tf_op jit(solution)/shard_map/bnf,nk->bkf/dot_general | solution.py:53
  31.9 0.1 slice_subtract_fusion
  32.0 1.1 %fusion.10 = (f32[2,128,512]{2,1,0:T(8,128)}, f32[2,128,512]{2,1,0:T(8,128)}) fusion(s32[]{:T(128)S(6)} %select_n.177, f32[4,128,256]{2,1,0:T(8,128)S(1)} %get-tuple-element.10, f32[4,128,256]{2,1,0:T(8,128)S(1)} %get-tuple-element.9, s32[]{:T(128)S(6)} %select_n.191), kind=kLoop, calls=%fused_computation.24 | loop fusion | flops 262144 | bytes 2097160 | tf_op jit(solution)/shard_map/concatenate | solution.py:55
  33.2 1.3 %collective-permute-done.5 = bf16[2,2,2,1,8,2,2048]{6,4,5,3,2,1,0:T(8,128)(2,1)S(1)} collective-permute-done((bf16[2,2,2,1,8,2,2048]{6,4,5,3,2,1,0:T(8,128)(2,1)S(1)}, bf16[2,2,2,1,8,2,2048]{6,4,5,3,2,1,0:T(8,128)(2,1)S(1)}, u32[]{:S(2)}, u32[]{:S(2)}) %collective-permute-start.5) | collective-permute-done | bytes 524320 | tf_op jit(solution)/shard_map/ppermute | solution.py:201
  34.4 0.1 broadcast_select_fusion
  34.5 0.1 copy_dynamic-update-slice_fusion.1
  34.6 0.1 copy_dynamic-update-slice_fusion
  34.8 1.3 %bitcast_select_fusion = bf16[8,2,2,2,2,2,8,256]{7,6,5,4,3,2,1,0:T(8,128)(2,1)} fusion(bf16[2,2,2,2,8,2,8,256]{7,6,3,0,1,2,5,4:T(8,128)(2,1)S(1)} %copy_dynamic-update-slice_fusion, pred[]{:T(512)S(6)} %eq.19), kind=kLoop, calls=%fused_computation.14 | loop fusion | flops 524288 | bytes 2097153 | tf_op jit(solution)/shard_map/jit(_where)/select_n | solution.py:214
  36.1 10.3 %shard_map.38 = f32[8,2,128]{2,1,0:T(2,128)} custom-call(f32[2,128,512]{2,1,0:T(8,128)} %get-tuple-element.12.spec_ref, bf16[8,2,128,256]{3,2,1,0:T(8,128)(2,1)} %bitcast.63, bf16[512,256]{1,0:T(8,128)(2,1)} %get-tuple-element.22.fh_ref, bf16[512,256]{1,0:T(8,128)(2,1)} %get-tuple-element.21.fl_ref, f32[256,256]{1,0:T(8,128)} %copy-done.1, ...), custom_call_target="tpu_custom_call" | custom-call | flops 6442450944 | bytes 1581056 | tf_op jit(solution)/shard_map/pallas_call | solution.py:157
  46.4 1.0 %collective-permute-start.6 = (f32[8,2,128]{2,1,0:T(2,128)}, f32[8,2,128]{2,1,0:T(2,128)S(1)}, u32[]{:S(2)}, u32[]{:S(2)}) collective-permute-start(f32[8,2,128]{2,1,0:T(2,128)} %shard_map.38), channel_id=1, source_target_pairs={{0,1},{1,0},{2,3},{3,2},{4,5},{5,4},{6,7},{7,6},{8,9},{9,8},{10,11... | collective-permute-start | bytes 24584 | tf_op jit(solution)/shard_map/ppermute | solution.py:241
  47.3 10.3 %shard_map.37 = f32[8,2,128]{2,1,0:T(2,128)} custom-call(f32[2,128,512]{2,1,0:T(8,128)} %get-tuple-element.11.spec_ref, bf16[8,2,128,256]{3,2,1,0:T(8,128)(2,1)} %bitcast.64, bf16[512,256]{1,0:T(8,128)(2,1)} %get-tuple-element.22.fh_ref, bf16[512,256]{1,0:T(8,128)(2,1)} %get-tuple-element.21.fl_ref, f32[256,256]{1,0:T(8,128)} %copy-done.1, ...), custom_call_target="tpu_custom_call" | custom-call | flops 6442450944 | bytes 1581056 | tf_op jit(solution)/shard_map/pallas_call | solution.py:157
  57.6 0.7 %copy.46 = f32[1,8,2,128]{3,1,2,0:T(8,128)S(1)} copy(f32[1,8,2,128]{3,2,1,0:T(2,128)} %bitcast.71) | data formatting | bytes 16384
  58.3 0.0 collective-permute-done.6
  58.3 0.6 %maximum_select_fusion.1 = f32[16,256]{1,0:T(8,128)} fusion(f32[8,256]{1,0:T(8,128)S(1)} %bitcast.69, f32[8,256]{1,0:T(8,128)S(1)} %bitcast.68, pred[]{:T(512)S(6)} %eq.19), kind=kLoop, calls=%fused_computation.89 | loop fusion | flops 12288 | bytes 32769 | tf_op jit(solution)/shard_map/jit(_where)/select_n | solution.py:243
  (8 shorter events, 0.2 us)
Async XLA Ops:
  1.0 5.2 %collective-permute-start = (bf16[1,8,2,2048]{3,1,2,0:T(8,128)(2,1)S(1)}, bf16[1,8,2,2048]{3,1,2,0:T(8,128)(2,1)S(1)}, u32[]{:S(2)}, u32[]{:S(2)}) collective-permute-start(bf16[1,8,2,2048]{3,1,2,0:T(8,128)(2,1)S(1)} %bitcast.67), channel_id=1, source_target_pairs={{0,1},{1,0},{2,3},{3,2},{4,5},{5,4},{6,7},{7,6},{8,9},{9,8},{10,11... | collective-permute-start | bytes 196616 | tf_op jit(solution)/shard_map/ppermute | solution.py:189
  3.2 25.7 %copy-start = (f32[256,256]{1,0:T(8,128)}, f32[256,256]{1,0:T(8,128)S(1)}, u32[]{:S(2)}) copy-start(f32[256,256]{1,0:T(8,128)S(1)} %get-tuple-element.31.ts_ref) | copy-start | bytes 786436
  3.2 25.7 %copy-start.1 = (f32[256,256]{1,0:T(8,128)}, f32[256,256]{1,0:T(8,128)S(1)}, u32[]{:S(2)}) copy-start(f32[256,256]{1,0:T(8,128)S(1)} %get-tuple-element.32.tc_ref) | copy-start | bytes 786436
  6.2 10.5 %collective-permute-start.1 = (bf16[2,1,8,2,2048]{4,2,3,0,1:T(8,128)(2,1)S(1)}, bf16[2,1,8,2,2048]{4,2,3,0,1:T(8,128)(2,1)S(1)}, u32[]{:S(2)}, u32[]{:S(2)}) collective-permute-start(bf16[2,1,8,2,2048]{4,2,3,0,1:T(8,128)(2,1)S(1)} %pad_maximum_fusion.12), channel_id=1, source_target_pairs={{0,8},{1,9},{2,10},{3,11},{4,12},{5,13},{6,14},{7,15},{8,0},{9,1},... | collective-permute-start | bytes 393224 | tf_op jit(solution)/shard_map/ppermute | solution.py:201
  16.7 6.1 %collective-permute-start.2 = (f32[32768]{0:T(1024)S(1)}, f32[32768]{0:T(1024)S(1)}, u32[]{:S(2)}, u32[]{:S(2)}) collective-permute-start(f32[32768]{0:T(1024)S(1)} %slice.49), channel_id=1, source_target_pairs={{0,1},{1,2},{2,3},{3,4},{4,5},{5,6},{6,7},{7,8},{8,9},{9,10},{10,1... | collective-permute-start | bytes 393224 | tf_op jit(solution)/shard_map/ppermute | solution.py:23
  20.7 5.3 %collective-permute-start.4 = (bf16[2,2,1,8,2,2048]{5,3,4,1,0,2:T(8,128)(2,1)S(1)}, bf16[2,2,1,8,2,2048]{5,3,4,1,0,2:T(8,128)(2,1)S(1)}, u32[]{:S(2)}, u32[]{:S(2)}) collective-permute-start(bf16[2,2,1,8,2,2048]{5,3,4,1,0,2:T(8,128)(2,1)S(1)} %pad_maximum_fusion.11), channel_id=1, source_target_pairs={{0,2},{1,5},{2,0},{3,7},{4,6},{5,1},{6,4},{7,3},{8,10},{9,13},{10,... | collective-permute-start | bytes 786440 | tf_op jit(solution)/shard_map/ppermute | solution.py:201
  23.0 3.7 %collective-permute-start.3 = (f32[3,32768]{1,0:T(4,128)S(1)}, f32[3,32768]{1,0:T(4,128)S(1)}, u32[]{:S(2)}, u32[]{:S(2)}) collective-permute-start(f32[3,32768]{1,0:T(4,128)S(1)} %pad_maximum_fusion.9), channel_id=1, source_target_pairs={{0,1},{1,0},{2,3},{3,2},{4,5},{5,4},{6,7},{7,6},{8,9},{9,8},{10,11... | collective-permute-start | bytes 1179656 | tf_op jit(solution)/shard_map/ppermute | solution.py:228
  26.1 8.4 %collective-permute-start.5 = (bf16[2,2,2,1,8,2,2048]{6,4,5,3,2,1,0:T(8,128)(2,1)S(1)}, bf16[2,2,2,1,8,2,2048]{6,4,5,3,2,1,0:T(8,128)(2,1)S(1)}, u32[]{:S(2)}, u32[]{:S(2)}) collective-permute-start(bf16[2,2,2,1,8,2,2048]{6,4,5,3,2,1,0:T(8,128)(2,1)S(1)} %pad_maximum_fusion.10), channel_id=1, source_target_pairs={{0,4},{1,3},{2,6},{3,1},{4,0},{5,7},{6,2},{7,5},{8,12},{9,11},{10,... | collective-permute-start | bytes 1572872 | tf_op jit(solution)/shard_map/ppermute | solution.py:201
  46.4 11.9 %collective-permute-start.6 = (f32[8,2,128]{2,1,0:T(2,128)}, f32[8,2,128]{2,1,0:T(2,128)S(1)}, u32[]{:S(2)}, u32[]{:S(2)}) collective-permute-start(f32[8,2,128]{2,1,0:T(2,128)} %shard_map.38), channel_id=1, source_target_pairs={{0,1},{1,0},{2,3},{3,2},{4,5},{5,4},{6,7},{7,6},{8,9},{9,8},{10,11... | collective-permute-start | bytes 24584 | tf_op jit(solution)/shard_map/ppermute | solution.py:241

commit v21 on v19

--- a/solution.py
+++ b/solution.py
@@ -10,7 +10,7 @@
 RADIX = 256
 BLOCK = 32768
 SUBBANK = 8
-STEP_TEMPLATES = 2
+STEP_TEMPLATES = 4
 
 
 PRECISE = lax.Precision.HIGH

time: 57 us -> 57.2 us (level)
  no operation moved by 1% of the time
where the time goes in v21:
time: 57.2 us; the launch traced here: 57 us
  Pallas kernels  20.8 us (36%)
  starting transfers between devices  13 us (23%)
  other arithmetic  11.6 us (20%)
  waiting for transfers between devices  5.19 us (9%)
  matrix products  3.71 us (6%)
  local copies, waits for them, and re-layouts  2.43 us (4%)
    pallas_call x2, Pallas kernels, window_peaks(): pl.pallas_call(peaks_kernel, out_shape=jax.ShapeDtypeStruct((template_tot...  20.8 us
    ppermute x3, starting transfers between devices, gathered_half(): arrived = lax.ppermute(held, 'seg', pairs)  5.63 us
    ppermute x3, waiting for transfers between devices, gathered_half(): arrived = lax.ppermute(held, 'seg', pairs)  5.18 us
    ppermute x1, starting transfers between devices, passed_along(): return lax.ppermute(value, axis, pairs)  3.32 us
    sin x3, other arithmetic, angle_table(): return (jnp.cos(angle_value), jnp.sin(angle_value))  2.54 us
    ppermute x1, starting transfers between devices, local(): lax.ppermute(partner_peaks, 'seg', [(i, i ^ 1) for i in range(seg_total)])  2.31 us
    convert_element_type x2, other arithmetic, table_pair(): return (high.astype(jnp.bfloat16), (value - high).astype(jnp.bfloat16))  1.72 us
    ppermute x1, starting transfers between devices, local(): other = lax.ppermute(mine, 'seg', [(i, i ^ 1) for i in range(seg_total)])  1.63 us
  transfers between devices with their start and end apart: 7, of which 3 were waited for; matrix products, arithmetic and copies ran while one was open for 25% of the time, Pallas kernels for 18%

profile of v21, /device:TPU:1, one launch (start us, length us, event | category | flops | bytes accessed | tf_op | source)
XLA Modules:
  0.0 57.0 jit_solution(11887226192537824981)
XLA Ops:
  0.0 1.0 %constant_dynamic-slice_fusion = (bf16[8,2,2048]{2,1,0:T(2,128)(2,1)S(1)}, bf16[8,2,2048]{2,1,0:T(2,128)(2,1)S(1)}) fusion(bf16[16,2,2048]{2,1,0:T(2,128)(2,1)} %param.5, s32[]{:T(128)S(6)} %select_n.181, s32[]{:T(128)S(6)} %select_n.169), kind=kLoop, calls=%fused_computation.94 | loop fusion | bytes 262152 | tf_op jit(solution)/shard_map/dynamic_slice | solution.py:187
  1.0 0.1 collective-permute-start
  1.1 1.0 %fusion.33 = (f32[256,256]{1,0:T(8,128)S(1)}, f32[256,256]{1,0:T(8,128)S(1)}) fusion(), kind=kLoop, calls=%fused_computation.76 | loop fusion | flops 983040 | bytes 524288 | tf_op jit(solution)/shard_map/cos | solution.py:31
  2.2 1.0 %fusion.30 = (f32[256,256]{1,0:T(8,128)S(1)}, f32[256,256]{1,0:T(8,128)S(1)}) fusion(), kind=kLoop, calls=%fused_computation.73 | loop fusion | flops 917504 | bytes 524288 | tf_op jit(solution)/shard_map/sin | solution.py:31
  3.2 0.0 copy-start
  3.2 0.0 copy-start.1
  3.2 0.5 fusion.40
  3.8 0.5 fusion.42
  4.3 1.1 %convert_multiply_fusion = f32[65536]{0:T(1024)S(1)} fusion(f32[65536]{0:T(1024)} %param.3, s32[65536]{0:T(1024)} %param.4), kind=kLoop, calls=%fused_computation.59 | loop fusion | flops 131072 | bytes 786432 | tf_op jit(solution)/shard_map/mul | solution.py:220
  5.3 0.9 %fusion.7 = (bf16[512,256]{1,0:T(8,128)(2,1)}, bf16[512,256]{1,0:T(8,128)(2,1)}) fusion(f32[256,128]{1,0:T(8,128)S(1)} %get-tuple-element.34, f32[256,128]{1,0:T(8,128)S(1)} %get-tuple-element.33, f32[256,128]{1,0:T(8,128)S(1)} %fusion.42), kind=kLoop, calls=%fused_computation.21 | loop fusion | flops 917504 | bytes 917504 | tf_op jit(solution)/shard_map/convert_element_type | solution.py:72
  6.2 0.0 collective-permute-done
  6.3 3.8 %collective-permute-start.3 = (bf16[2,1,8,2,2048]{4,2,3,0,1:T(8,128)(2,1)S(1)}, bf16[2,1,8,2,2048]{4,2,3,0,1:T(8,128)(2,1)S(1)}, u32[]{:S(2)}, u32[]{:S(2)}) collective-permute-start(bf16[2,1,8,2,2048]{4,2,3,0,1:T(8,128)(2,1)S(1)} %pad_maximum_fusion.12), channel_id=1, source_target_pairs={{0,8},{1,9},{2,10},{3,11},{4,12},{5,13},{6,14},{7,15},{8,0},{9,1},... | collective-permute-start | bytes 393224 | tf_op jit(solution)/shard_map/ppermute | solution.py:201
  10.1 1.0 %fusion.32 = f32[256,256]{1,0:T(8,128)S(1)} fusion(), kind=kLoop, calls=%fused_computation.75 | loop fusion | flops 917504 | bytes 262144 | tf_op jit(solution)/shard_map/sin | solution.py:31
  11.0 0.2 reshape.47
  11.3 0.9 %fusion.8 = (bf16[512,256]{1,0:T(8,128)(2,1)}, bf16[512,256]{1,0:T(8,128)(2,1)}) fusion(f32[256,256]{1,0:T(8,128)S(1)} %get-tuple-element.29, f32[256,256]{1,0:T(8,128)S(1)} %fusion.32, f32[256,256]{1,0:T(8,128)S(1)} %get-tuple-element.30), kind=kLoop, calls=%fused_computation.22 | loop fusion | flops 1310720 | bytes 1310720 | tf_op jit(solution)/shard_map/convert_element_type | solution.py:72
  12.1 3.3 %collective-permute-start.1 = (f32[32768]{0:T(1024)S(1)}, f32[32768]{0:T(1024)S(1)}, u32[]{:S(2)}, u32[]{:S(2)}) collective-permute-start(f32[32768]{0:T(1024)S(1)} %slice.49), channel_id=1, source_target_pairs={{0,1},{1,2},{2,3},{3,4},{4,5},{5,6},{6,7},{7,8},{8,9},{9,10},{10,1... | collective-permute-start | bytes 393224 | tf_op jit(solution)/shard_map/ppermute | solution.py:23
  15.5 1.3 %collective-permute-done.3 = bf16[2,1,8,2,2048]{4,2,3,0,1:T(8,128)(2,1)S(1)} collective-permute-done((bf16[2,1,8,2,2048]{4,2,3,0,1:T(8,128)(2,1)S(1)}, bf16[2,1,8,2,2048]{4,2,3,0,1:T(8,128)(2,1)S(1)}, u32[]{:S(2)}, u32[]{:S(2)}) %collective-permute-start.3) | collective-permute-done | bytes 131104 | tf_op jit(solution)/shard_map/ppermute | solution.py:201
  16.8 0.7 %collective-permute-start.4 = (bf16[2,2,1,8,2,2048]{5,3,4,1,0,2:T(8,128)(2,1)S(1)}, bf16[2,2,1,8,2,2048]{5,3,4,1,0,2:T(8,128)(2,1)S(1)}, u32[]{:S(2)}, u32[]{:S(2)}) collective-permute-start(bf16[2,2,1,8,2,2048]{5,3,4,1,0,2:T(8,128)(2,1)S(1)} %pad_maximum_fusion.11), channel_id=1, source_target_pairs={{0,2},{1,5},{2,0},{3,7},{4,6},{5,1},{6,4},{7,3},{8,10},{9,13},{10,... | collective-permute-start | bytes 786440 | tf_op jit(solution)/shard_map/ppermute | solution.py:201
  17.5 0.0 collective-permute-done.1
  17.5 0.2 pad_maximum_fusion.9
  17.7 1.6 %collective-permute-start.2 = (f32[3,32768]{1,0:T(4,128)S(1)}, f32[3,32768]{1,0:T(4,128)S(1)}, u32[]{:S(2)}, u32[]{:S(2)}) collective-permute-start(f32[3,32768]{1,0:T(4,128)S(1)} %pad_maximum_fusion.9), channel_id=1, source_target_pairs={{0,1},{1,0},{2,3},{3,2},{4,5},{5,4},{6,7},{7,6},{8,9},{9,8},{10,11... | collective-permute-start | bytes 1179656 | tf_op jit(solution)/shard_map/ppermute | solution.py:226
  19.3 3.0 %collective-permute-done.4 = bf16[2,2,1,8,2,2048]{5,3,4,1,0,2:T(8,128)(2,1)S(1)} collective-permute-done((bf16[2,2,1,8,2,2048]{5,3,4,1,0,2:T(8,128)(2,1)S(1)}, bf16[2,2,1,8,2,2048]{5,3,4,1,0,2:T(8,128)(2,1)S(1)}, u32[]{:S(2)}, u32[]{:S(2)}) %collective-permute-start.4) | collective-permute-done | bytes 262176 | tf_op jit(solution)/shard_map/ppermute | solution.py:201
  22.4 0.1 pad_maximum_fusion.10
  22.5 1.2 %collective-permute-start.5 = (bf16[2,2,2,1,8,2,2048]{6,4,5,3,2,1,0:T(8,128)(2,1)S(1)}, bf16[2,2,2,1,8,2,2048]{6,4,5,3,2,1,0:T(8,128)(2,1)S(1)}, u32[]{:S(2)}, u32[]{:S(2)}) collective-permute-start(bf16[2,2,2,1,8,2,2048]{6,4,5,3,2,1,0:T(8,128)(2,1)S(1)} %pad_maximum_fusion.10), channel_id=1, source_target_pairs={{0,4},{1,3},{2,6},{3,1},{4,0},{5,7},{6,2},{7,5},{8,12},{9,11},{10,... | collective-permute-start | bytes 1572872 | tf_op jit(solution)/shard_map/ppermute | solution.py:201
  23.6 0.0 collective-permute-done.2
  23.6 0.1 slice.50
  23.8 0.5 maximum_select_fusion
  24.3 0.2 fusion.56
  24.5 0.2 pad_maximum_fusion.7
  24.7 1.1 %fusion.4 = f32[4,256,512]{2,1,0:T(8,128)S(1)} fusion(f32[1,4,256,256]{3,1,2,0:T(4,128)S(1)} %bitcast.60, f32[256,256]{1,0:T(8,128)S(1)} %get-tuple-element.30, f32[256,256]{1,0:T(8,128)S(1)} %get-tuple-element.29), kind=kOutput, calls=%fused_computation.9 | convolution fusion | flops 805437440 | bytes 3670016 | tf_op jit(solution)/shard_map/bnm,nf->bmf/dot_general | solution.py:41
  25.8 0.0 copy-done
  25.8 0.0 copy-done.1
  25.8 0.3 multiply_add_fusion
  26.1 1.3 %fusion.3 = f32[4,128,512]{2,1,0:T(8,128)S(1)} fusion(f32[4,256,256]{2,1,0:T(8,128)S(1)} %get-tuple-element.8, f32[4,256,256]{2,1,0:T(8,128)S(1)} %get-tuple-element.7), kind=kOutput, calls=%fused_computation.4 | convolution fusion | flops 403636224 | bytes 3145728 | tf_op jit(solution)/shard_map/bnf,nk->bkf/dot_general | solution.py:54
  27.4 1.3 %fusion.2 = f32[4,128,512]{2,1,0:T(8,128)S(1)} fusion(f32[4,256,256]{2,1,0:T(8,128)S(1)} %get-tuple-element.8, f32[4,256,256]{2,1,0:T(8,128)S(1)} %get-tuple-element.7), kind=kOutput, calls=%fused_computation.3 | convolution fusion | flops 403636224 | bytes 3145728 | tf_op jit(solution)/shard_map/bnf,nk->bkf/dot_general | solution.py:53
  28.7 0.1 slice_subtract_fusion
  28.9 1.1 %fusion.10 = (f32[2,128,512]{2,1,0:T(8,128)}, f32[2,128,512]{2,1,0:T(8,128)}) fusion(s32[]{:T(128)S(6)} %select_n.173, f32[4,128,256]{2,1,0:T(8,128)S(1)} %get-tuple-element.10, f32[4,128,256]{2,1,0:T(8,128)S(1)} %get-tuple-element.9, s32[]{:T(128)S(6)} %select_n.191), kind=kLoop, calls=%fused_computation.24 | loop fusion | flops 262144 | bytes 2097160 | tf_op jit(solution)/shard_map/concatenate | solution.py:55
  30.0 0.9 %collective-permute-done.5 = bf16[2,2,2,1,8,2,2048]{6,4,5,3,2,1,0:T(8,128)(2,1)S(1)} collective-permute-done((bf16[2,2,2,1,8,2,2048]{6,4,5,3,2,1,0:T(8,128)(2,1)S(1)}, bf16[2,2,2,1,8,2,2048]{6,4,5,3,2,1,0:T(8,128)(2,1)S(1)}, u32[]{:S(2)}, u32[]{:S(2)}) %collective-permute-start.5) | collective-permute-done | bytes 524320 | tf_op jit(solution)/shard_map/ppermute | solution.py:201
  30.9 0.1 broadcast_select_fusion
  31.0 0.1 copy_dynamic-update-slice_fusion.1
  31.1 0.1 copy_dynamic-update-slice_fusion
  31.2 1.3 %bitcast_select_fusion = bf16[8,2,2,2,2,2,8,256]{7,6,5,4,3,2,1,0:T(8,128)(2,1)} fusion(bf16[2,2,2,2,8,2,8,256]{7,6,3,0,1,2,5,4:T(8,128)(2,1)S(1)} %copy_dynamic-update-slice_fusion, pred[]{:T(512)S(6)} %eq.19), kind=kLoop, calls=%fused_computation.14 | loop fusion | flops 524288 | bytes 2097153 | tf_op jit(solution)/shard_map/jit(_where)/select_n | solution.py:212
  32.5 10.4 %shard_map.38 = f32[8,2,128]{2,1,0:T(2,128)} custom-call(f32[2,128,512]{2,1,0:T(8,128)} %get-tuple-element.12.spec_ref, bf16[8,2,128,256]{3,2,1,0:T(8,128)(2,1)} %bitcast.63, bf16[512,256]{1,0:T(8,128)(2,1)} %get-tuple-element.22.fh_ref, bf16[512,256]{1,0:T(8,128)(2,1)} %get-tuple-element.21.fl_ref, f32[256,256]{1,0:T(8,128)} %copy-done.1, ...), custom_call_target="tpu_custom_call" | custom-call | flops 6442450944 | bytes 1581056 | tf_op jit(solution)/shard_map/pallas_call | solution.py:157
  42.9 2.3 %collective-permute-start.6 = (f32[8,2,128]{2,1,0:T(2,128)}, f32[8,2,128]{2,1,0:T(2,128)S(1)}, u32[]{:S(2)}, u32[]{:S(2)}) collective-permute-start(f32[8,2,128]{2,1,0:T(2,128)} %shard_map.38), channel_id=1, source_target_pairs={{0,1},{1,0},{2,3},{3,2},{4,5},{5,4},{6,7},{7,6},{8,9},{9,8},{10,11... | collective-permute-start | bytes 24584 | tf_op jit(solution)/shard_map/ppermute | solution.py:239
  45.2 10.4 %shard_map.37 = f32[8,2,128]{2,1,0:T(2,128)} custom-call(f32[2,128,512]{2,1,0:T(8,128)} %get-tuple-element.11.spec_ref, bf16[8,2,128,256]{3,2,1,0:T(8,128)(2,1)} %bitcast.64, bf16[512,256]{1,0:T(8,128)(2,1)} %get-tuple-element.22.fh_ref, bf16[512,256]{1,0:T(8,128)(2,1)} %get-tuple-element.21.fl_ref, f32[256,256]{1,0:T(8,128)} %copy-done.1, ...), custom_call_target="tpu_custom_call" | custom-call | flops 6442450944 | bytes 1581056 | tf_op jit(solution)/shard_map/pallas_call | solution.py:157
  55.7 0.7 %copy.46 = f32[1,8,2,128]{3,1,2,0:T(8,128)S(1)} copy(f32[1,8,2,128]{3,2,1,0:T(2,128)} %bitcast.71) | data formatting | bytes 16384
  56.4 0.0 collective-permute-done.6
  56.4 0.6 %maximum_select_fusion.1 = f32[16,256]{1,0:T(8,128)} fusion(f32[8,256]{1,0:T(8,128)S(1)} %bitcast.69, f32[8,256]{1,0:T(8,128)S(1)} %bitcast.68, pred[]{:T(512)S(6)} %eq.19), kind=kLoop, calls=%fused_computation.89 | loop fusion | flops 12288 | bytes 32769 | tf_op jit(solution)/shard_map/jit(_where)/select_n | solution.py:241
  (8 shorter events, 0.2 us)
Async XLA Ops:
  1.0 5.2 %collective-permute-start = (bf16[1,8,2,2048]{3,1,2,0:T(8,128)(2,1)S(1)}, bf16[1,8,2,2048]{3,1,2,0:T(8,128)(2,1)S(1)}, u32[]{:S(2)}, u32[]{:S(2)}) collective-permute-start(bf16[1,8,2,2048]{3,1,2,0:T(8,128)(2,1)S(1)} %bitcast.67), channel_id=1, source_target_pairs={{0,1},{1,0},{2,3},{3,2},{4,5},{5,4},{6,7},{7,6},{8,9},{9,8},{10,11... | collective-permute-start | bytes 196616 | tf_op jit(solution)/shard_map/ppermute | solution.py:189
  3.2 22.6 %copy-start = (f32[256,256]{1,0:T(8,128)}, f32[256,256]{1,0:T(8,128)S(1)}, u32[]{:S(2)}) copy-start(f32[256,256]{1,0:T(8,128)S(1)} %get-tuple-element.31.ts_ref) | copy-start | bytes 786436
  3.2 22.6 %copy-start.1 = (f32[256,256]{1,0:T(8,128)}, f32[256,256]{1,0:T(8,128)S(1)}, u32[]{:S(2)}) copy-start(f32[256,256]{1,0:T(8,128)S(1)} %get-tuple-element.32.tc_ref) | copy-start | bytes 786436
  6.3 10.5 %collective-permute-start.3 = (bf16[2,1,8,2,2048]{4,2,3,0,1:T(8,128)(2,1)S(1)}, bf16[2,1,8,2,2048]{4,2,3,0,1:T(8,128)(2,1)S(1)}, u32[]{:S(2)}, u32[]{:S(2)}) collective-permute-start(bf16[2,1,8,2,2048]{4,2,3,0,1:T(8,128)(2,1)S(1)} %pad_maximum_fusion.12), channel_id=1, source_target_pairs={{0,8},{1,9},{2,10},{3,11},{4,12},{5,13},{6,14},{7,15},{8,0},{9,1},... | collective-permute-start | bytes 393224 | tf_op jit(solution)/shard_map/ppermute | solution.py:201
  12.1 5.3 %collective-permute-start.1 = (f32[32768]{0:T(1024)S(1)}, f32[32768]{0:T(1024)S(1)}, u32[]{:S(2)}, u32[]{:S(2)}) collective-permute-start(f32[32768]{0:T(1024)S(1)} %slice.49), channel_id=1, source_target_pairs={{0,1},{1,2},{2,3},{3,4},{4,5},{5,6},{6,7},{7,8},{8,9},{9,10},{10,1... | collective-permute-start | bytes 393224 | tf_op jit(solution)/shard_map/ppermute | solution.py:23
  16.8 5.6 %collective-permute-start.4 = (bf16[2,2,1,8,2,2048]{5,3,4,1,0,2:T(8,128)(2,1)S(1)}, bf16[2,2,1,8,2,2048]{5,3,4,1,0,2:T(8,128)(2,1)S(1)}, u32[]{:S(2)}, u32[]{:S(2)}) collective-permute-start(bf16[2,2,1,8,2,2048]{5,3,4,1,0,2:T(8,128)(2,1)S(1)} %pad_maximum_fusion.11), channel_id=1, source_target_pairs={{0,2},{1,5},{2,0},{3,7},{4,6},{5,1},{6,4},{7,3},{8,10},{9,13},{10,... | collective-permute-start | bytes 786440 | tf_op jit(solution)/shard_map/ppermute | solution.py:201
  17.7 5.9 %collective-permute-start.2 = (f32[3,32768]{1,0:T(4,128)S(1)}, f32[3,32768]{1,0:T(4,128)S(1)}, u32[]{:S(2)}, u32[]{:S(2)}) collective-permute-start(f32[3,32768]{1,0:T(4,128)S(1)} %pad_maximum_fusion.9), channel_id=1, source_target_pairs={{0,1},{1,0},{2,3},{3,2},{4,5},{5,4},{6,7},{7,6},{8,9},{9,8},{10,11... | collective-permute-start | bytes 1179656 | tf_op jit(solution)/shard_map/ppermute | solution.py:226
  22.5 8.4 %collective-permute-start.5 = (bf16[2,2,2,1,8,2,2048]{6,4,5,3,2,1,0:T(8,128)(2,1)S(1)}, bf16[2,2,2,1,8,2,2048]{6,4,5,3,2,1,0:T(8,128)(2,1)S(1)}, u32[]{:S(2)}, u32[]{:S(2)}) collective-permute-start(bf16[2,2,2,1,8,2,2048]{6,4,5,3,2,1,0:T(8,128)(2,1)S(1)} %pad_maximum_fusion.10), channel_id=1, source_target_pairs={{0,4},{1,3},{2,6},{3,1},{4,0},{5,7},{6,2},{7,5},{8,12},{9,11},{10,... | collective-permute-start | bytes 1572872 | tf_op jit(solution)/shard_map/ppermute | solution.py:201
  42.9 13.4 %collective-permute-start.6 = (f32[8,2,128]{2,1,0:T(2,128)}, f32[8,2,128]{2,1,0:T(2,128)S(1)}, u32[]{:S(2)}, u32[]{:S(2)}) collective-permute-start(f32[8,2,128]{2,1,0:T(2,128)} %shard_map.38), channel_id=1, source_target_pairs={{0,1},{1,0},{2,3},{3,2},{4,5},{5,4},{6,7},{7,6},{8,9},{9,8},{10,11... | collective-permute-start | bytes 24584 | tf_op jit(solution)/shard_map/ppermute | solution.py:239
